TPU v7x, 128 devices: a whole 4x4x4 slice. The times are simulated.
128 devices in a mesh: req: 16 (over y, x), kvh: 8 (over z, core).
Axes of the slice: x: 4, y: 4, z: 4, core: 2. Of those that a mesh axis runs over, the one named last changes fastest.
Arguments:
- states: bfloat16 [128, 2560], P('req', 'kvh'), may hold values from -6 to 6
- attn_gain: bfloat16 [2560], replicated, may hold values from 0.099609375 to 1.8984375
- w_query: bfloat16 [2560, 4096], P(None, 'kvh'), may hold values from -0.125 to 0.125
- w_key: bfloat16 [2560, 1024], P(None, 'kvh'), may hold values from -0.125 to 0.125
- w_value: bfloat16 [2560, 1024], P(None, 'kvh'), may hold values from -0.125 to 0.125
- query_gain: bfloat16 [128], replicated, may hold values from 0.5 to 2
- key_gain: bfloat16 [128], replicated, may hold values from 0.5 to 2
- w_output: bfloat16 [4096, 2560], P('kvh'), may hold values from -0.25 to 0.25
- ffn_gain: bfloat16 [2560], P('kvh'), may hold values from 0.099609375 to 1.8984375
- w_gate: bfloat16 [2560, 9728], P('kvh', 'req'), may hold values from -0.125 to 0.125
- w_up: bfloat16 [2560, 9728], P('kvh', 'req'), may hold values from -0.125 to 0.125
- w_down: bfloat16 [9728, 2560], P('req', 'kvh'), may hold values from -0.0625 to 0.0625
- kv_pool: bfloat16 [1024, 8, 128, 256], P('req', 'kvh'), may hold values from -6 to 6
- lengths: int32 [128], replicated, may hold values from 1 to 1023, as said below
- page_table: int32 [128, 8], P('req'), may hold values from 0 to 63, as said below
- new_order: int32 [128], replicated, may hold values from 0 to 127, as said below
Outputs:
- output: bfloat16 [128, 2560], P('req', 'kvh')
- new_pool: bfloat16 [1024, 8, 128, 256], P('req', 'kvh')
Inputs may be any that keep to these rules, and one draw needn't show every extreme that they name: `lengths`: each request has at least one cached position and room for the new one; some request has exactly 1023. `page_table`: the 8 rows of one device name each of its 64 pool rows exactly once. `new_order`: A permutation of the requests; slot s lies on the device s // 8. The 8 requests of one device go to 8 different devices, and each device receives its 8 requests from 8 different devices.
All inputs are finite; a program needn't handle non-finite values.
Results may differ from a plain program's by a relative error of at most 0.0087.
Values may be sent and summed in bfloat16 or wider, within the bound.
No kernel may reach another device: no remote copies, remote signals or barrier semaphores. Data moves between devices by JAX's collectives and lax.ppermute only.
A program may use at most 128 MiB of HBM per device.

v0:
```python
import math

import jax
import jax.numpy as jnp
from jax import lax
from jax.sharding import PartitionSpec as P

D = 2560


EPSILON = 1e-06


def rms_norm(values, norm_gain):
    mean_sq = jnp.mean(values * values, axis=-1, keepdims=True)
    return values * lax.rsqrt(mean_sq + EPSILON) * norm_gain


def rotary(values, positions):
    half_dim = values.shape[-1] // 2
    frequency = jnp.exp(
        jnp.arange(half_dim, dtype=jnp.float32) * (-2.0 * math.log(1000000.0) / values.shape[-1])
    )
    angles = positions.astype(jnp.float32)[:, None, None] * frequency
    cosine = jnp.cos(angles)
    sine_part = jnp.sin(angles)
    first_half = values[..., :half_dim]
    second_half = values[..., half_dim:]
    return jnp.concatenate(
        [
            first_half * cosine - second_half * sine_part,
            second_half * cosine + first_half * sine_part,
        ],
        axis=-1,
    )


def by_peer(rows, owners, peer_ids):
    matches = owners[None, :] == peer_ids[:, None]
    picked = jnp.argmax(matches.astype(jnp.int32), axis=1)
    present = jnp.any(matches, axis=1)
    shape_tail = (1,) * (rows.ndim - 1)
    return jnp.where(present.reshape((-1,) + shape_tail), rows[picked], jnp.zeros((), rows.dtype))


def send_pages(blocks, destination, source_owner, peer_ids):
    parcels = by_peer(blocks, destination, peer_ids)
    received = lax.all_to_all(parcels, "req", split_axis=0, concat_axis=0, tiled=True)
    return received[source_owner]


def build_sequence(blocks, lengths_now, fresh):
    row_count, pages_per, kv_local, page_len, channels = blocks.shape
    span_len = pages_per * page_len
    sequence = blocks.transpose(0, 2, 1, 3, 4).reshape(row_count, kv_local, span_len, channels)
    positions = jnp.arange(span_len, dtype=jnp.int32)
    lengths_col = lengths_now[:, None, None, None]
    kept = positions[None, None, :, None] < lengths_col
    placed = positions[None, None, :, None] == lengths_col
    return jnp.where(
        kept, sequence, jnp.where(placed, fresh[:, :, None, :], jnp.zeros((), jnp.bfloat16))
    )


def to_blocks(sequence, pages_per):
    row_count, kv_local, span_len, channels = sequence.shape
    page_len = span_len // pages_per
    return sequence.reshape(row_count, kv_local, pages_per, page_len, channels).transpose(
        0, 2, 1, 3, 4
    )


def attend(query, sequence, lengths_now):
    row_count, kv_local, span_len, channels = sequence.shape
    head_dim = channels // 2
    q_local = query.shape[1]
    group_size = q_local // kv_local
    grouped = query.reshape(row_count, kv_local, group_size, head_dim)
    scores = jnp.einsum(
        "rkgd,rktd->rkgt", grouped, sequence[..., :head_dim], preferred_element_type=jnp.float32
    ) * (1.0 / math.sqrt(head_dim))
    positions = jnp.arange(span_len, dtype=jnp.int32)
    valid = positions[None, None, None, :] <= lengths_now[:, None, None, None]
    scores = jnp.where(valid, scores, -jnp.inf)
    weights = jax.nn.softmax(scores, axis=-1).astype(jnp.bfloat16)
    mixed = jnp.einsum(
        "rkgt,rktd->rkgd", weights, sequence[..., head_dim:], preferred_element_type=jnp.float32
    )
    return mixed.reshape(row_count, q_local * head_dim).astype(jnp.bfloat16)


def per_device(
    states,
    attn_gain,
    w_query,
    w_key,
    w_value,
    query_gain,
    key_gain,
    w_output,
    ffn_gain,
    w_gate,
    w_up,
    w_down,
    kv_pool,
    lengths,
    page_table,
    new_order,
):
    devices_req = lax.axis_size("req")
    my_index = lax.axis_index("req")
    row_count = states.shape[0]
    head_dim = query_gain.shape[0]
    kv_local = w_key.shape[1] // head_dim
    q_local = w_query.shape[1] // head_dim
    pages_per = page_table.shape[1]
    page_len = kv_pool.shape[2]
    channels = 2 * head_dim
    total_rows = new_order.shape[0]
    everyone = jnp.arange(total_rows, dtype=jnp.int32)
    new_position = jnp.zeros((total_rows,), jnp.int32).at[new_order].set(everyone)
    arriving = lax.dynamic_slice_in_dim(new_order, my_index * row_count, row_count)
    leaving = my_index * row_count + jnp.arange(row_count, dtype=jnp.int32)
    destination = new_position[leaving] // row_count
    source_owner = arriving // row_count
    peer_ids = jnp.arange(devices_req, dtype=jnp.int32)
    all_states = lax.all_gather(states, "req", axis=0, tiled=True)
    own_states = all_states[arriving]
    full_states = lax.all_gather(own_states, "kvh", axis=1, tiled=True)
    normed = rms_norm(full_states.astype(jnp.float32), attn_gain.astype(jnp.float32)).astype(
        jnp.bfloat16
    )
    query = jnp.dot(normed, w_query, preferred_element_type=jnp.float32).reshape(
        row_count, q_local, head_dim
    )
    key_new = jnp.dot(normed, w_key, preferred_element_type=jnp.float32).reshape(
        row_count, kv_local, head_dim
    )
    value_new = jnp.dot(normed, w_value, preferred_element_type=jnp.float32).reshape(
        row_count, kv_local, head_dim
    )
    positions_now = lengths[arriving]
    query = rotary(rms_norm(query, query_gain.astype(jnp.float32)), positions_now).astype(
        jnp.bfloat16
    )
    key_new = rotary(rms_norm(key_new, key_gain.astype(jnp.float32)), positions_now).astype(
        jnp.bfloat16
    )
    fresh = jnp.concatenate([key_new, value_new.astype(jnp.bfloat16)], axis=-1)
    outgoing_blocks = kv_pool[page_table]
    arrived = send_pages(outgoing_blocks, destination, source_owner, peer_ids)
    sequence = build_sequence(arrived, positions_now, fresh)
    new_pool = to_blocks(sequence, pages_per).reshape(
        row_count * pages_per, kv_local, page_len, channels
    )
    mixed = attend(query, sequence, positions_now)
    partial_out = jnp.dot(mixed, w_output, preferred_element_type=jnp.float32)
    attn_out = lax.psum_scatter(partial_out, "kvh", scatter_dimension=1, tiled=True)
    residual = (own_states.astype(jnp.float32) + attn_out).astype(jnp.bfloat16)
    residual_wide = residual.astype(jnp.float32)
    total_sq = lax.psum(jnp.sum(residual_wide * residual_wide, axis=-1, keepdims=True), "kvh")
    normed_two = (
        residual_wide * lax.rsqrt(total_sq / D + EPSILON) * ffn_gain.astype(jnp.float32)
    ).astype(jnp.bfloat16)
    ffn_width = w_gate.shape[1]
    joined = jnp.concatenate([w_gate, w_up], axis=1)
    partial_both = jnp.dot(
        lax.all_gather(normed_two, "req", axis=0, tiled=True),
        joined,
        preferred_element_type=jnp.float32,
    )
    summed = lax.psum(partial_both, "kvh")
    hidden = (jax.nn.silu(summed[:, :ffn_width]) * summed[:, ffn_width:]).astype(jnp.bfloat16)
    lowered = lax.psum_scatter(
        jnp.dot(hidden, w_down, preferred_element_type=jnp.float32),
        "req",
        scatter_dimension=0,
        tiled=True,
    )
    finished = (residual_wide + lowered).astype(jnp.bfloat16)
    gathered = lax.all_gather(finished, "req", axis=0, tiled=True)
    result = gathered[new_position[leaving]]
    return (result, new_pool)


def solution(mesh):
    in_specs = (
        P("req", "kvh"),
        P(),
        P(None, "kvh"),
        P(None, "kvh"),
        P(None, "kvh"),
        P(),
        P(),
        P("kvh", None),
        P("kvh"),
        P("kvh", "req"),
        P("kvh", "req"),
        P("req", "kvh"),
        P("req", "kvh", None, None),
        P(),
        P("req", None),
        P(),
    )
    out_specs = (P("req", "kvh"), P("req", "kvh", None, None))
    return jax.shard_map(
        per_device, mesh=mesh, in_specs=in_specs, out_specs=out_specs, check_vma=False
    )
```

profile of v0, /device:TPU:0, one launch (start us, length us, event | category | flops | bytes accessed | tf_op | source)
XLA Modules:
  0.0 463.7 jit_solution(13554562346039470376)
XLA Ops:
  7.2 0.8 compare_select_fusion.5
  8.0 1.0 scatter_custom_fusion
  9.0 0.6 gather_fusion.2
  9.7 0.6 iota_reduce_fusion
  10.3 0.7 compare_select_fusion
  11.2 5.0 %gather_fusion.3 = bf16[64,128,256]{2,1,0:T(8,128)(2,1)} fusion(bf16[64,128,256]{2,1,0:T(8,128)(2,1)} %bitcast.76, s32[1024]{0:T(1024)S(1)} %pad_clamp_fusion.3), kind=kCustom, calls=%fused_computation.3 | custom fusion | bytes 8388864 | tf_op jit(solution)/shard_map/gather | solution.py:150
  16.2 6.9 %gather_fusion.4 = bf16[16,8,128,256]{3,2,1,0:T(8,128)(2,1)} fusion(bf16[8,8,128,256]{3,2,1,0:T(8,128)(2,1)} %bitcast.73, s32[1024]{0:T(1024)S(1)} %pad_clamp_fusion.2), kind=kCustom, calls=%fused_computation.4 | custom fusion | bytes 16777280 | tf_op jit(solution)/shard_map/gather | solution.py:43
  23.0 7.2 %bitcast_select_fusion = bf16[16,8,1,128,256]{4,3,1,2,0:T(8,128)(2,1)} fusion(bf16[16,8,128,256]{3,2,1,0:T(8,128)(2,1)} %gather_fusion.4, pred[16]{0:T(512)(128)(4,1)S(1)} %fusion.36), kind=kLoop, calls=%fused_computation.9 | loop fusion | flops 4194304 | bytes 16777232 | tf_op jit(solution)/shard_map/jit(_where)/select_n | solution.py:43
  30.3 7.3 %all-to-all-start = ((bf16[16,8,1,128,256]{4,3,1,2,0:T(8,128)(2,1)}), bf16[16,8,1,128,256]{4,3,1,2,0:T(8,128)(2,1)}, u32[]{:S(2)}, u32[]{:S(2)}) async-start(bf16[16,8,1,128,256]{4,3,1,2,0:T(8,128)(2,1)} %bitcast_select_fusion), calls=%async_computation | async-start | bytes 16777216 | tf_op jit(solution)/shard_map/all_to_all | solution.py:48
  37.8 0.6 gather_fusion.1
  38.4 138.1 %all_gather.12 = bf16[128,320]{1,0:T(8,128)(2,1)S(1)} all-gather(bf16[8,320]{1,0:T(8,128)(2,1)S(1)} %copy-done.6), channel_id=1, replica_groups=mesh['req'=16,'kvh'=8] {'req'}, dimensions={0}, use_global_device_ids=true | all-gather | bytes 87040 | tf_op jit(solution)/shard_map/all_gather | solution.py:127
  177.1 14.0 %all-gather.1 = bf16[8,320,8]{1,2,0:T(8,128)(2,1)S(1)} all-gather(bf16[1,320,8]{1,2,0:T(8,128)(2,1)S(1)} %bitcast.78), channel_id=2, replica_groups=mesh['req'=16,'kvh'=8] {'kvh'}, dimensions={0}, use_global_device_ids=true | all-gather | bytes 46080 | tf_op jit(solution)/shard_map/all_gather | solution.py:129
  191.5 2.3 multiply_reduce_fusion.1
  194.2 1.4 multiply_reduce_fusion.2
  196.2 6.2 %gather_fusion.5 = bf16[8,8,128,256]{3,2,1,0:T(8,128)(2,1)} fusion(bf16[16,8,128,256]{3,2,1,0:T(8,128)(2,1)} %bitcast.7, s32[1024]{0:T(1024)S(1)} %pad_clamp_fusion.1), kind=kCustom, calls=%fused_computation.5 | custom fusion | bytes 8388640 | tf_op jit(solution)/shard_map/gather | solution.py:49
  202.4 7.6 %bitcast_select_fusion.1 = bf16[8,1,1024,256]{3,2,0,1:T(8,128)(2,1)} fusion(bf16[8,8,128,256]{3,2,1,0:T(8,128)(2,1)} %gather_fusion.5, pred[8,1024]{1,0:T(8,128)(4,1)S(1)} %get-tuple-element.16, pred[8,1024]{1,0:T(8,128)(4,1)S(1)} %get-tuple-element.15, bf16[8,256]{1,0:T(8,128)(2,1)S(1)} %maximum_bitcast_fusion), kind=kLoop, calls=%fused_computation.10 | loop fusion | flops 4194304 | bytes 8409088 | tf_op jit(solution)/shard_map/jit(_where)/select_n | solution.py:60
  210.1 3.0 fusion.44
  213.1 2.2 fusion.8
  215.3 2.2 convolution_bitcast_fusion
  219.0 29.7 %reduce-scatter.4.cloned.1.call-done = f32[320,8]{1,0:T(8,128)} async-done(((f32[2560,8]{1,0:T(8,128)}), f32[320,8]{1,0:T(8,128)}) %reduce-scatter.4.cloned.1.call-update) | async-done | bytes 10256
  248.7 1.0 copy.34
  249.8 12.6 %psum.14 = f32[8,1]{0,1:T(1,128)S(1)} all-reduce(f32[8,1]{0,1:T(1,128)S(1)} %bitcast.79), channel_id=1, replica_groups=mesh['req'=16,'kvh'=8] {'kvh'}, use_global_device_ids=true, to_apply=%region_10.11 | all-reduce | flops 8 | bytes 64 | tf_op jit(solution)/shard_map/psum | solution.py:161
  262.4 23.8 %all_gather.14 = bf16[128,320]{1,0:T(8,128)(2,1)S(1)} all-gather(bf16[8,320]{1,0:T(8,128)(2,1)S(1)} %fusion.21), channel_id=1, replica_groups=mesh['req'=16,'kvh'=8] {'req'}, dimensions={0}, use_global_device_ids=true | all-gather | bytes 87040 | tf_op jit(solution)/shard_map/all_gather | solution.py:168
  286.3 1.7 fusion.10
  288.0 58.4 %all-reduce.4.cloned.1.call-done = f32[128,1216]{0,1:T(8,128)} async-done(((f32[128,1216]{0,1:T(8,128)}), f32[128,1216]{0,1:T(8,128)}) %all-reduce.4.cloned.1.call-update) | async-done | bytes 622608 | tf_op jit(solution)/shard_map/psum | solution.py:172
  346.4 2.2 fusion.15
  348.9 1.9 copy-done.2
  350.8 4.9 %select_select_fusion = bf16[64,1,128,256]{3,2,1,0:T(8,128)(2,1)} fusion(bf16[64,1,128,256]{3,2,1,0:T(8,128)(2,1)S(1)} %bitcast.74, bf16[64,1,128,256]{3,2,1,0:T(8,128)(2,1)S(1)} %bitcast.75, pred[64,128]{1,0:T(8,128)(4,1)S(1)} %eq.40, pred[64,128]{1,0:T(8,128)(4,1)S(1)} %lt.90), kind=kLoop, calls=%fused_computation.11 | loop fusion | flops 4194304 | bytes 12599296 | tf_op jit(solution)/shard_map/jit(_where)/select_n | solution.py:60
  355.7 76.5 %all-reduce.6.cloned.1.call-done = f32[128,320]{1,0:T(8,128)} async-done(((f32[128,320]{1,0:T(8,128)}), f32[128,320]{1,0:T(8,128)}) %all-reduce.6.cloned.1.call-update) | async-done | bytes 163856
  432.3 0.7 fusion.22
  433.0 23.0 %all_gather.15 = bf16[128,320]{1,0:T(8,128)(2,1)S(1)} all-gather(bf16[8,320]{1,0:T(8,128)(2,1)S(1)} %fusion.22), channel_id=1, replica_groups=mesh['req'=16,'kvh'=8] {'req'}, dimensions={0}, use_global_device_ids=true | all-gather | bytes 87040 | tf_op jit(solution)/shard_map/all_gather | solution.py:181
  456.0 1.2 gather_fusion.6
  (77 shorter events, 3.6 us)
Async XLA Ops:
  7.2 208.1 %copy-start = (bf16[512,2560]{1,0:T(8,128)(2,1)S(1)}, bf16[512,2560]{1,0:T(8,128)(2,1)}, u32[]{:S(2)}) copy-start(bf16[512,2560]{1,0:T(8,128)(2,1)} %param.23) | copy-start | bytes 7864324
  30.2 7.4 %copy-start.9 = (s32[128]{0:T(128)S(1)}, s32[128]{0:T(128)}, u32[]{:S(2)}) copy-start(s32[128]{0:T(128)} %param.31) | copy-start | bytes 1540
  30.2 7.5 %copy-start.1 = (s32[128]{0:T(128)S(1)}, s32[128]{0:T(128)}, u32[]{:S(2)}) copy-start(s32[128]{0:T(128)} %param.29) | copy-start | bytes 1540
  30.2 8.2 %copy-start.6 = (bf16[8,320]{1,0:T(8,128)(2,1)S(1)}, bf16[8,320]{1,0:T(8,128)(2,1)}, u32[]{:S(2)}) copy-start(bf16[8,320]{1,0:T(8,128)(2,1)} %param.16) | copy-start | bytes 15364
  30.2 161.0 %copy-start.7 = (bf16[2560]{0:T(1024)(128)(2,1)S(1)}, bf16[2560]{0:T(1024)(128)(2,1)}, u32[]{:S(2)}) copy-start(bf16[2560]{0:T(1024)(128)(2,1)} %param.17) | copy-start | bytes 15364
  30.2 161.0 %copy-start.10 = (bf16[128]{0:T(256)(128)(2,1)S(1)}, bf16[128]{0:T(256)(128)(2,1)}, u32[]{:S(2)}) copy-start(bf16[128]{0:T(256)(128)(2,1)} %param.22) | copy-start | bytes 772
  30.3 161.0 %copy-start.11 = (bf16[128]{0:T(256)(128)(2,1)S(1)}, bf16[128]{0:T(256)(128)(2,1)}, u32[]{:S(2)}) copy-start(bf16[128]{0:T(256)(128)(2,1)} %param.21) | copy-start | bytes 772
  30.3 163.6 %copy-start.8 = (bf16[320]{0:T(512)(128)(2,1)S(1)}, bf16[320]{0:T(512)(128)(2,1)}, u32[]{:S(2)}) copy-start(bf16[320]{0:T(512)(128)(2,1)} %param.24) | copy-start | bytes 1924
  30.3 163.7 %copy-start.3 = (bf16[2560,128]{1,0:T(8,128)(2,1)S(1)}, bf16[2560,128]{1,0:T(8,128)(2,1)}, u32[]{:S(2)}) copy-start(bf16[2560,128]{1,0:T(8,128)(2,1)} %param.20) | copy-start | bytes 1966084
  30.3 165.9 %all-to-all-start = ((bf16[16,8,1,128,256]{4,3,1,2,0:T(8,128)(2,1)}), bf16[16,8,1,128,256]{4,3,1,2,0:T(8,128)(2,1)}, u32[]{:S(2)}, u32[]{:S(2)}) async-start(bf16[16,8,1,128,256]{4,3,1,2,0:T(8,128)(2,1)} %bitcast_select_fusion), calls=%async_computation | async-start | bytes 16777216 | tf_op jit(solution)/shard_map/all_to_all | solution.py:48
  37.6 211.1 %reduce-scatter.4.cloned.1.call-start = ((), (), s32[]{:S(2)}) async-start(), calls=%async_computation.3 | async-start | bytes 1474560
  213.1 4.6 copy-start.12
  213.1 73.2 %copy-start.4 = (bf16[320,608]{1,0:T(8,128)(2,1)S(1)}, bf16[320,608]{1,0:T(8,128)(2,1)}, u32[]{:S(2)}) copy-start(bf16[320,608]{1,0:T(8,128)(2,1)} %param.26) | copy-start | bytes 1167364
  213.1 73.2 %copy-start.5 = (bf16[320,608]{1,0:T(8,128)(2,1)S(1)}, bf16[320,608]{1,0:T(8,128)(2,1)}, u32[]{:S(2)}) copy-start(bf16[320,608]{1,0:T(8,128)(2,1)} %param.25) | copy-start | bytes 1167364
  217.5 128.9 %all-reduce.4.cloned.1.call-start = ((), (), s32[]{:S(2)}) async-start(), calls=%async_computation.2 | async-start | bytes 1245184 | tf_op jit(solution)/shard_map/psum | solution.py:172
  288.0 144.3 %all-reduce.6.cloned.1.call-start = ((), (), s32[]{:S(2)}) async-start(), calls=%async_computation.4 | async-start | bytes 393216
  348.6 2.2 copy-start.2
Sparse Core Ops, SparseCore 0:
  217.6 30.9 reduce-scatter.3
  288.1 58.3 all-reduce.3
  349.6 82.5 all-reduce.5
where the time goes:
time: 465 us; the launch traced here: 464 us
  blocking collectives  212 us (46%)
  waiting for transfers between devices  165 us (35%)
  local copies, waits for them, and re-layouts  26.2 us (6%)
  other arithmetic  24 us (5%)
  matrix products  15.1 us (3%)
  between operations  14.7 us (3%)
  starting transfers between devices  7.43 us (2%)
    all_gather x1, blocking collectives, per_device(): all_states = lax.all_gather(states, 'req', axis=0, tiled=True)  138 us
    unnamed x5, waiting for transfers between devices  106 us
    psum x1, waiting for transfers between devices, per_device(): summed = lax.psum(partial_both, 'kvh')  58.4 us
    all_gather x1, blocking collectives, per_device(): lax.all_gather(normed_two, 'req', axis=0, tiled=True)  23.8 us
    all_gather x1, blocking collectives, per_device(): gathered = lax.all_gather(finished, 'req', axis=0, tiled=True)  23 us
    all_gather x1, blocking collectives, per_device(): full_states = lax.all_gather(own_states, 'kvh', axis=1, tiled=True)  14 us
    psum x1, blocking collectives, per_device(): lax.psum(jnp.sum(residual_wide * residual_wide, axis=-1, keepdims=True),...  12.6 us
    select_n x2, other arithmetic, build_sequence(): jnp.where(kept, sequence, jnp.where(placed, fresh[:, :, None, :], jnp.zer...  12.5 us
  transfers between devices with their start and end apart: 4, of which 3 were waited for; matrix products, arithmetic and copies ran while one was open for 3% of the time, Pallas kernels for 0%

commit v1 on v0

v1 whole, which is shorter than its diff:
```python
import math

import jax
import jax.numpy as jnp
from jax import lax
from jax.sharding import PartitionSpec as P

D = 2560


EPSILON = 1e-06


def rms_norm(values, norm_gain):
    mean_sq = jnp.mean(values * values, axis=-1, keepdims=True)
    return values * lax.rsqrt(mean_sq + EPSILON) * norm_gain


def rotary(values, positions):
    half_dim = values.shape[-1] // 2
    frequency = jnp.exp(
        jnp.arange(half_dim, dtype=jnp.float32) * (-2.0 * math.log(1000000.0) / values.shape[-1])
    )
    angles = positions.astype(jnp.float32)[:, None, None] * frequency
    cosine = jnp.cos(angles)
    sine_part = jnp.sin(angles)
    first_half = values[..., :half_dim]
    second_half = values[..., half_dim:]
    return jnp.concatenate(
        [
            first_half * cosine - second_half * sine_part,
            second_half * cosine + first_half * sine_part,
        ],
        axis=-1,
    )


def mask_blocks(blocks, lengths_now, fresh):
    row_count, pages_per, kv_local, page_len, channels = blocks.shape
    positions = (
        jnp.arange(pages_per, dtype=jnp.int32)[:, None] * page_len
        + jnp.arange(page_len, dtype=jnp.int32)[None, :]
    )
    positions = positions[None, :, None, :, None]
    lengths_col = lengths_now[:, None, None, None, None]
    kept = positions < lengths_col
    placed = positions == lengths_col
    return jnp.where(
        kept,
        blocks,
        jnp.where(placed, fresh[:, None, :, None, :], jnp.zeros((), jnp.bfloat16)),
    )


def attend(query, sequence, lengths_now):
    row_count, kv_local, span_len, channels = sequence.shape
    head_dim = channels // 2
    q_local = query.shape[1]
    group_size = q_local // kv_local
    grouped = query.reshape(row_count, kv_local, group_size, head_dim)
    scores = jnp.einsum(
        "rkgd,rktd->rkgt", grouped, sequence[..., :head_dim], preferred_element_type=jnp.float32
    ) * (1.0 / math.sqrt(head_dim))
    positions = jnp.arange(span_len, dtype=jnp.int32)
    valid = positions[None, None, None, :] <= lengths_now[:, None, None, None]
    scores = jnp.where(valid, scores, -jnp.inf)
    weights = jax.nn.softmax(scores, axis=-1).astype(jnp.bfloat16)
    mixed = jnp.einsum(
        "rkgt,rktd->rkgd", weights, sequence[..., head_dim:], preferred_element_type=jnp.float32
    )
    return mixed.reshape(row_count, q_local * head_dim).astype(jnp.bfloat16)


def per_device(
    states,
    attn_gain,
    w_query,
    w_key,
    w_value,
    query_gain,
    key_gain,
    w_output,
    ffn_gain,
    w_gate,
    w_up,
    w_down,
    kv_pool,
    lengths,
    page_table,
    new_order,
):
    devices_req = lax.axis_size("req")
    my_index = lax.axis_index("req")
    kvh_index = lax.axis_index("kvh")
    row_count = states.shape[0]
    width_local = states.shape[1]
    head_dim = query_gain.shape[0]
    kv_local = w_key.shape[1] // head_dim
    q_local = w_query.shape[1] // head_dim
    pages_per = page_table.shape[1]
    page_len = kv_pool.shape[2]
    channels = 2 * head_dim
    total_rows = new_order.shape[0]

    everyone = jnp.arange(total_rows, dtype=jnp.int32)
    new_position = jnp.zeros((total_rows,), jnp.int32).at[new_order].set(everyone)
    home = my_index * row_count + jnp.arange(row_count, dtype=jnp.int32)
    destination = new_position[home] // row_count
    peer_ids = jnp.arange(devices_req, dtype=jnp.int32)
    matches = destination[None, :] == peer_ids[:, None]
    picked = jnp.argmax(matches.astype(jnp.int32), axis=1)
    parcels = kv_pool[page_table[picked]]
    received = lax.all_to_all(parcels, "req", split_axis=0, concat_axis=0, tiled=True)
    arriving = lax.dynamic_slice_in_dim(new_order, my_index * row_count, row_count)
    source_owner = arriving // row_count

    full_states = lax.all_gather(states, "kvh", axis=1, tiled=True)
    normed = rms_norm(full_states.astype(jnp.float32), attn_gain.astype(jnp.float32)).astype(
        jnp.bfloat16
    )
    query = jnp.dot(normed, w_query, preferred_element_type=jnp.float32).reshape(
        row_count, q_local, head_dim
    )
    key_new = jnp.dot(normed, w_key, preferred_element_type=jnp.float32).reshape(
        row_count, kv_local, head_dim
    )
    value_new = jnp.dot(normed, w_value, preferred_element_type=jnp.float32).reshape(
        row_count, kv_local, head_dim
    )
    positions_home = lengths[home]
    query = rotary(rms_norm(query, query_gain.astype(jnp.float32)), positions_home).astype(
        jnp.bfloat16
    )
    key_new = rotary(rms_norm(key_new, key_gain.astype(jnp.float32)), positions_home).astype(
        jnp.bfloat16
    )
    fresh = jnp.concatenate([key_new, value_new.astype(jnp.bfloat16)], axis=-1)
    home_blocks = mask_blocks(kv_pool[page_table], positions_home, fresh)
    sequence = home_blocks.transpose(0, 2, 1, 3, 4).reshape(
        row_count, kv_local, pages_per * page_len, channels
    )
    mixed = attend(query, sequence, positions_home)
    partial_out = jnp.dot(mixed, w_output, preferred_element_type=jnp.float32)
    attn_out = lax.psum(partial_out, "kvh")
    residual_full = (full_states.astype(jnp.float32) + attn_out).astype(jnp.bfloat16)
    residual_wide_full = residual_full.astype(jnp.float32)
    total_sq = jnp.sum(residual_wide_full * residual_wide_full, axis=-1, keepdims=True)
    residual_wide = lax.dynamic_slice_in_dim(
        residual_wide_full, kvh_index * width_local, width_local, axis=1
    )
    normed_two = (
        residual_wide * lax.rsqrt(total_sq / D + EPSILON) * ffn_gain.astype(jnp.float32)
    ).astype(jnp.bfloat16)

    fresh_flat = fresh.reshape(row_count, kv_local * channels)
    gathered = lax.all_gather(
        jnp.concatenate([normed_two, fresh_flat], axis=1), "req", axis=0, tiled=True
    )
    normed_all = gathered[:, :width_local]
    fresh_all = gathered[:, width_local:].reshape(total_rows, kv_local, channels)
    ffn_width = w_gate.shape[1]
    joined = jnp.concatenate([w_gate, w_up], axis=1)
    partial_both = jnp.dot(normed_all, joined, preferred_element_type=jnp.float32)
    summed = lax.psum(partial_both, "kvh")
    hidden = (jax.nn.silu(summed[:, :ffn_width]) * summed[:, ffn_width:]).astype(jnp.bfloat16)
    lowered = lax.psum_scatter(
        jnp.dot(hidden, w_down, preferred_element_type=jnp.float32),
        "req",
        scatter_dimension=0,
        tiled=True,
    )
    result = (residual_wide + lowered).astype(jnp.bfloat16)

    arrived = received[source_owner]
    new_blocks = mask_blocks(arrived, lengths[arriving], fresh_all[arriving])
    new_pool = new_blocks.reshape(row_count * pages_per, kv_local, page_len, channels)
    return (result, new_pool)


def solution(mesh):
    in_specs = (
        P("req", "kvh"),
        P(),
        P(None, "kvh"),
        P(None, "kvh"),
        P(None, "kvh"),
        P(),
        P(),
        P("kvh", None),
        P("kvh"),
        P("kvh", "req"),
        P("kvh", "req"),
        P("req", "kvh"),
        P("req", "kvh", None, None),
        P(),
        P("req", None),
        P(),
    )
    out_specs = (P("req", "kvh"), P("req", "kvh", None, None))
    return jax.shard_map(
        per_device, mesh=mesh, in_specs=in_specs, out_specs=out_specs, check_vma=False
    )
```

time: 465 us -> 342 us (0.74)
  blocking collectives: 212 us -> 55.1 us
  waiting for transfers between devices: 165 us -> 203 us
    all_gather x4 -> x2, blocking collectives: 199 us -> 55.1 us  [the longest x1 41 us: per_device(): lax.all_gather(jnp.concatenate([normed_two, fresh_flat], axis=1), 'req',...]
    psum x0 -> x1, waiting for transfers between devices: none -> 56.2 us  [per_device(): attn_out = lax.psum(partial_out, 'kvh')]
    unnamed x5 -> x4, waiting for transfers between devices: 106 us -> 84.2 us
    psum x1 -> x0, blocking collectives: 12.6 us -> none  [per_device(): lax.psum(jnp.sum(residual_wide * residual_wide, axis=-1, keepdims=True),...]
    select_n x9 -> x8, other arithmetic: 20.5 us -> 15.4 us  [the longest x2 15.3 us: mask_blocks(): jnp.where(kept, blocks, jnp.where(placed, fresh[:, None, :, None, :], jnp...]
    gather x7 -> x9, local copies, waits for them, and re-layouts: 21.1 us -> 23.8 us  [the longest x3 9.99 us: per_device(): parcels = kv_pool[page_table[picked]]]
  transfers between devices with their start and end apart: 4 -> 4, of which waited for: 3 -> 3; matrix products, arithmetic and copies ran while one was open for 3% -> 10% of each run, Pallas kernels for 0% -> 0%
where the time goes in v1:
time: 342 us; the launch traced here: 341 us
  waiting for transfers between devices  203 us (59%)
  blocking collectives  55.1 us (16%)
  local copies, waits for them, and re-layouts  26.1 us (8%)
  other arithmetic  20.4 us (6%)
  between operations  14.7 us (4%)
  matrix products  14.4 us (4%)
  starting transfers between devices  7.42 us (2%)
    unnamed x4, waiting for transfers between devices  84.2 us
    psum x1, waiting for transfers between devices, per_device(): summed = lax.psum(partial_both, 'kvh')  62.3 us
    psum x1, waiting for transfers between devices, per_device(): attn_out = lax.psum(partial_out, 'kvh')  56.2 us
    all_gather x1, blocking collectives, per_device(): lax.all_gather(jnp.concatenate([normed_two, fresh_flat], axis=1), 'req',...  41 us
    select_n x2, other arithmetic, mask_blocks(): jnp.where(kept, blocks, jnp.where(placed, fresh[:, None, :, None, :], jnp...  15.3 us
    all_gather x1, blocking collectives, per_device(): full_states = lax.all_gather(states, 'kvh', axis=1, tiled=True)  14 us
    gather x3, local copies, waits for them, and re-layouts, per_device(): parcels = kv_pool[page_table[picked]]  9.99 us
    all_to_all x1, starting transfers between devices, per_device(): lax.all_to_all(parcels, 'req', split_axis=0, concat_axis=0, tiled=True)  7.3 us
  transfers between devices with their start and end apart: 4, of which 3 were waited for; matrix products, arithmetic and copies ran while one was open for 10% of the time, Pallas kernels for 0%

profile of v1, /device:TPU:0, one launch (start us, length us, event | category | flops | bytes accessed | tf_op | source)
XLA Modules:
  0.0 340.9 jit_solution(16654045882225741350)
XLA Ops:
  7.2 0.8 compare_select_fusion.4
  8.0 1.0 scatter_custom_fusion
  9.0 0.6 gather_fusion.3
  9.7 0.6 iota_reduce_fusion
  10.3 1.2 gather_fusion.4
  11.8 8.7 %gather_fusion.5 = bf16[128,128,256]{2,1,0:T(8,128)(2,1)} fusion(bf16[64,128,256]{2,1,0:T(8,128)(2,1)} %bitcast.79, s32[1024]{0:T(1024)S(1)} %pad_clamp_fusion.1), kind=kCustom, calls=%fused_computation.5 | custom fusion | bytes 16777728 | tf_op jit(solution)/shard_map/gather | solution.py:112
  20.5 7.3 %all-to-all-start = ((bf16[16,8,1,128,256]{4,3,1,2,0:T(8,128)(2,1)}), bf16[16,8,1,128,256]{4,3,1,2,0:T(8,128)(2,1)}, u32[]{:S(2)}, u32[]{:S(2)}) async-start(bf16[16,8,1,128,256]{4,3,1,2,0:T(8,128)(2,1)} %bitcast.81), calls=%async_computation | async-start | bytes 16777216 | tf_op jit(solution)/shard_map/all_to_all | solution.py:113
  27.9 0.6 gather_fusion
  28.7 14.0 %all-gather = bf16[8,320,8]{1,2,0:T(8,128)(2,1)S(1)} all-gather(bf16[1,320,8]{1,2,0:T(8,128)(2,1)S(1)} %bitcast.84), channel_id=1, replica_groups=mesh['req'=16,'kvh'=8] {'kvh'}, dimensions={0}, use_global_device_ids=true | all-gather | bytes 46080 | tf_op jit(solution)/shard_map/all_gather | solution.py:117
  42.8 0.1 fusion.18
  43.0 2.3 multiply_reduce_fusion.1
  45.4 5.1 %gather_fusion.1 = bf16[64,128,256]{2,1,0:T(8,128)(2,1)} fusion(bf16[64,128,256]{2,1,0:T(8,128)(2,1)} %bitcast.80, s32[1024]{0:T(1024)S(1)} %pad_clamp_fusion.4), kind=kCustom, calls=%fused_computation.1 | custom fusion | bytes 8388864 | tf_op jit(solution)/shard_map/gather | solution.py:138
  50.5 0.2 fusion.9
  50.7 1.4 multiply_reduce_fusion.2
  52.2 0.1 fusion.37
  52.9 7.6 %select_select_fusion.1 = bf16[8,1,1024,256]{3,2,0,1:T(8,128)(2,1)} fusion(bf16[8,1,1024,256]{3,2,0,1:T(8,128)(2,1)} %bitcast.83, pred[8,1024]{1,0:T(8,128)(4,1)S(1)} %get-tuple-element.13, pred[8,1024]{1,0:T(8,128)(4,1)S(1)} %get-tuple-element.12, bf16[8,256]{1,0:T(8,128)(2,1)S(1)} %maximum_bitcast_fusion), kind=kLoop, calls=%fused_computation.11 | loop fusion | flops 4194304 | bytes 8409088 | tf_op jit(solution)/shard_map/jit(_where)/select_n | solution.py:48
  60.5 2.5 fusion.48
  63.0 2.0 fusion.8
  65.1 1.1 fusion.26
  66.4 0.6 gather_fusion.2
  67.2 0.6 dynamic-slice
  68.4 56.2 %all-reduce.5.cloned.1.call-done = f32[8,2560]{1,0:T(8,128)} async-done(((f32[8,2560]{1,0:T(8,128)}), f32[8,2560]{1,0:T(8,128)}) %all-reduce.5.cloned.1.call-update) | async-done | bytes 81936 | tf_op jit(solution)/shard_map/psum | solution.py:144
  124.6 1.0 multiply_reduce_fusion
  125.8 41.0 %all_gather.7 = bf16[128,576]{1,0:T(8,128)(2,1)S(1)} all-gather(bf16[8,576]{1,0:T(8,128)(2,1)S(1)} %pad_maximum_fusion), channel_id=1, replica_groups=mesh['req'=16,'kvh'=8] {'req'}, dimensions={0}, use_global_device_ids=true | all-gather | bytes 156672 | tf_op jit(solution)/shard_map/all_gather | solution.py:156
  166.9 2.7 fusion.10
  169.8 0.6 gather_fusion.7
  170.4 62.3 %all-reduce.7.cloned.1.call-done = f32[128,1216]{0,1:T(8,128)} async-done(((f32[128,1216]{0,1:T(8,128)}), f32[128,1216]{0,1:T(8,128)}) %all-reduce.7.cloned.1.call-update) | async-done | bytes 622608 | tf_op jit(solution)/shard_map/psum | solution.py:164
  232.7 2.2 fusion.15
  234.9 84.2 %all-reduce.9.cloned.1.call-done = f32[128,320]{1,0:T(8,128)} async-done(((f32[128,320]{1,0:T(8,128)}), f32[128,320]{1,0:T(8,128)}) %all-reduce.9.cloned.1.call-update) | async-done | bytes 163856
  319.1 1.4 fusion.25
  320.5 6.2 %gather_fusion.6 = bf16[8,8,128,256]{3,2,1,0:T(8,128)(2,1)} fusion(bf16[16,8,128,256]{3,2,1,0:T(8,128)(2,1)} %bitcast.16, s32[1024]{0:T(1024)S(1)} %pad_clamp_fusion), kind=kCustom, calls=%fused_computation.6 | custom fusion | bytes 8388640 | tf_op jit(solution)/shard_map/gather | solution.py:174
  326.7 7.6 %select_select_fusion = bf16[64,1,128,256]{3,2,1,0:T(8,128)(2,1)} fusion(bf16[64,1,128,256]{3,2,1,0:T(8,128)(2,1)} %bitcast.82, pred[64,128]{1,0:T(8,128)(4,1)S(1)} %get-tuple-element.11, pred[64,128]{1,0:T(8,128)(4,1)S(1)} %get-tuple-element.10, bf16[64,256]{1,0:T(8,128)(2,1)S(1)} %broadcast_bitcast_fusion), kind=kLoop, calls=%fused_computation.10 | loop fusion | flops 4194304 | bytes 8437760 | tf_op jit(solution)/shard_map/jit(_where)/select_n | solution.py:48
  (77 shorter events, 2.1 us)
Async XLA Ops:
  7.2 57.9 %copy-start = (bf16[512,2560]{1,0:T(8,128)(2,1)S(1)}, bf16[512,2560]{1,0:T(8,128)(2,1)}, u32[]{:S(2)}) copy-start(bf16[512,2560]{1,0:T(8,128)(2,1)} %param.23) | copy-start | bytes 7864324
  20.5 7.4 %copy-start.9 = (bf16[128]{0:T(256)(128)(2,1)S(1)}, bf16[128]{0:T(256)(128)(2,1)}, u32[]{:S(2)}) copy-start(bf16[128]{0:T(256)(128)(2,1)} %param.21) | copy-start | bytes 772
  20.5 7.4 %copy-start.10 = (bf16[128]{0:T(256)(128)(2,1)S(1)}, bf16[128]{0:T(256)(128)(2,1)}, u32[]{:S(2)}) copy-start(bf16[128]{0:T(256)(128)(2,1)} %param.22) | copy-start | bytes 772
  20.5 7.4 %copy-start.1 = (s32[128]{0:T(128)S(1)}, s32[128]{0:T(128)}, u32[]{:S(2)}) copy-start(s32[128]{0:T(128)} %param.29) | copy-start | bytes 1540
  20.5 8.1 %copy-start.2 = (s32[8,8]{1,0:T(8,128)S(1)}, s32[8,8]{1,0:T(8,128)}, u32[]{:S(2)}) copy-start(s32[8,8]{1,0:T(8,128)} %param.30) | copy-start | bytes 772
  20.5 8.2 %copy-start.5 = (bf16[2560]{0:T(1024)(128)(2,1)S(1)}, bf16[2560]{0:T(1024)(128)(2,1)}, u32[]{:S(2)}) copy-start(bf16[2560]{0:T(1024)(128)(2,1)} %param.17) | copy-start | bytes 15364
  20.5 8.2 %copy-start.4 = (bf16[8,320]{1,0:T(8,128)(2,1)S(1)}, bf16[8,320]{1,0:T(8,128)(2,1)}, u32[]{:S(2)}) copy-start(bf16[8,320]{1,0:T(8,128)(2,1)} %param.16) | copy-start | bytes 15364
  20.5 300.0 %all-to-all-start = ((bf16[16,8,1,128,256]{4,3,1,2,0:T(8,128)(2,1)}), bf16[16,8,1,128,256]{4,3,1,2,0:T(8,128)(2,1)}, u32[]{:S(2)}, u32[]{:S(2)}) async-start(bf16[16,8,1,128,256]{4,3,1,2,0:T(8,128)(2,1)} %bitcast.81), calls=%async_computation | async-start | bytes 16777216 | tf_op jit(solution)/shard_map/all_to_all | solution.py:113
  27.8 96.8 %all-reduce.5.cloned.1.call-start = ((), (), s32[]{:S(2)}) async-start(), calls=%async_computation.1 | async-start | bytes 163840 | tf_op jit(solution)/shard_map/psum | solution.py:144
  45.4 5.1 %copy-start.3 = (bf16[2560,128]{1,0:T(8,128)(2,1)S(1)}, bf16[2560,128]{1,0:T(8,128)(2,1)}, u32[]{:S(2)}) copy-start(bf16[2560,128]{1,0:T(8,128)(2,1)} %param.20) | copy-start | bytes 1966084
  60.5 5.7 %copy-start.7 = (s32[128]{0:T(128)S(1)}, s32[128]{0:T(128)}, u32[]{:S(2)}) copy-start(s32[128]{0:T(128)} %param.31) | copy-start | bytes 1540
  60.5 5.9 %copy-start.6 = (bf16[320]{0:T(512)(128)(2,1)S(1)}, bf16[320]{0:T(512)(128)(2,1)}, u32[]{:S(2)}) copy-start(bf16[320]{0:T(512)(128)(2,1)} %param.24) | copy-start | bytes 1924
  60.5 6.7 %copy-start.11 = (u32[128]{0:T(128)S(1)}, u32[128]{0:T(128)}, u32[]{:S(2)}) copy-start(u32[128]{0:T(128)} %constant.91) | copy-start | bytes 1540
  60.5 106.4 %copy-start.8 = (bf16[320,608]{1,0:T(8,128)(2,1)S(1)}, bf16[320,608]{1,0:T(8,128)(2,1)}, u32[]{:S(2)}) copy-start(bf16[320,608]{1,0:T(8,128)(2,1)} %param.26) | copy-start | bytes 1167364
  66.2 166.5 %all-reduce.7.cloned.1.call-start = ((), (), s32[]{:S(2)}) async-start(), calls=%async_computation.2 | async-start | bytes 1245184 | tf_op jit(solution)/shard_map/psum | solution.py:164
  169.6 149.6 %all-reduce.9.cloned.1.call-start = ((), (), s32[]{:S(2)}) async-start(), calls=%async_computation.3 | async-start | bytes 393216
Sparse Core Ops, SparseCore 0:
  66.3 58.2 all-reduce.4
  169.7 62.9 all-reduce.6
  236.5 82.5 all-reduce.8

commit v2 on v1

--- a/solution.py
+++ b/solution.py
@@ -141,7 +141,17 @@
     )
     mixed = attend(query, sequence, positions_home)
     partial_out = jnp.dot(mixed, w_output, preferred_element_type=jnp.float32)
-    attn_out = lax.psum(partial_out, "kvh")
+    devices_kvh = lax.axis_size("kvh")
+    attn_out = jnp.sum(
+        lax.all_to_all(
+            jnp.broadcast_to(partial_out[None], (devices_kvh,) + partial_out.shape),
+            "kvh",
+            split_axis=0,
+            concat_axis=0,
+            tiled=True,
+        ),
+        axis=0,
+    )
     residual_full = (full_states.astype(jnp.float32) + attn_out).astype(jnp.bfloat16)
     residual_wide_full = residual_full.astype(jnp.float32)
     total_sq = jnp.sum(residual_wide_full * residual_wide_full, axis=-1, keepdims=True)
@@ -161,13 +171,31 @@
     ffn_width = w_gate.shape[1]
     joined = jnp.concatenate([w_gate, w_up], axis=1)
     partial_both = jnp.dot(normed_all, joined, preferred_element_type=jnp.float32)
-    summed = lax.psum(partial_both, "kvh")
-    hidden = (jax.nn.silu(summed[:, :ffn_width]) * summed[:, ffn_width:]).astype(jnp.bfloat16)
-    lowered = lax.psum_scatter(
-        jnp.dot(hidden, w_down, preferred_element_type=jnp.float32),
-        "req",
-        scatter_dimension=0,
-        tiled=True,
+    group_rows = total_rows // devices_kvh
+    summed = jnp.sum(
+        lax.all_to_all(
+            partial_both.reshape(devices_kvh, group_rows, 2 * ffn_width),
+            "kvh",
+            split_axis=0,
+            concat_axis=0,
+            tiled=True,
+        ),
+        axis=0,
+    )
+    hidden_part = (jax.nn.silu(summed[:, :ffn_width]) * summed[:, ffn_width:]).astype(
+        jnp.bfloat16
+    )
+    hidden = lax.all_gather(hidden_part, "kvh", axis=0, tiled=True)
+    lowered_parts = jnp.dot(hidden, w_down, preferred_element_type=jnp.float32)
+    lowered = jnp.sum(
+        lax.all_to_all(
+            lowered_parts.reshape(devices_req, row_count, width_local),
+            "req",
+            split_axis=0,
+            concat_axis=0,
+            tiled=True,
+        ),
+        axis=0,
     )
     result = (residual_wide + lowered).astype(jnp.bfloat16)
 

time: 342 us -> 277 us (0.81)
  waiting for transfers between devices: 203 us -> 141 us
  between operations: 14.7 us -> 0.89 us
  starting transfers between devices: 7.42 us -> 19.8 us
  blocking collectives: 55.1 us -> 51.2 us
    all_to_all x1, waiting for transfers between devices: 0.01 us -> 121 us  [per_device(): lax.all_to_all(parcels, 'req', split_axis=0, concat_axis=0, tiled=True)]
    psum x2 -> x0, waiting for transfers between devices: 119 us -> none  [the longest x1 62.3 us: per_device(): summed = lax.psum(partial_both, 'kvh')]
    unnamed x4 -> x0, waiting for transfers between devices: 84.2 us -> none
    all_to_all x0 -> x3, waiting for transfers between devices: none -> 20.4 us  [the longest x1 10.4 us: per_device(): lax.all_to_all(partial_both.reshape(devices_kvh, group_rows, 2 * ffn_widt...]
    all_gather x1, blocking collectives: 41 us -> 24.1 us  [per_device(): lax.all_gather(jnp.concatenate([normed_two, fresh_flat], axis=1), 'req',...]
    all_gather x0 -> x1, blocking collectives: none -> 12.8 us  [per_device(): hidden = lax.all_gather(hidden_part, 'kvh', axis=0, tiled=True)]
    all_to_all x0 -> x3, starting transfers between devices: none -> 12.4 us  [the longest x1 4.85 us: per_device(): lax.all_to_all(lowered_parts.reshape(devices_req, row_count, width_local)...]
  transfers between devices with their start and end apart: 4 -> 4, of which waited for: 3 -> 3; matrix products, arithmetic and copies ran while one was open for 10% -> 5% of each run, Pallas kernels for 0% -> 0%
where the time goes in v2:
time: 277 us; the launch traced here: 276 us
  waiting for transfers between devices  141 us (51%)
  blocking collectives  51.2 us (18%)
  local copies, waits for them, and re-layouts  26.8 us (10%)
  other arithmetic  21.8 us (8%)
  starting transfers between devices  19.8 us (7%)
  matrix products  14.2 us (5%)
    all_to_all x1, waiting for transfers between devices, per_device(): lax.all_to_all(parcels, 'req', split_axis=0, concat_axis=0, tiled=True)  121 us
    all_gather x1, blocking collectives, per_device(): lax.all_gather(jnp.concatenate([normed_two, fresh_flat], axis=1), 'req',...  24.1 us
    select_n x2, other arithmetic, mask_blocks(): jnp.where(kept, blocks, jnp.where(placed, fresh[:, None, :, None, :], jnp...  15.3 us
    all_gather x1, blocking collectives, per_device(): full_states = lax.all_gather(states, 'kvh', axis=1, tiled=True)  14.4 us
    all_gather x1, blocking collectives, per_device(): hidden = lax.all_gather(hidden_part, 'kvh', axis=0, tiled=True)  12.8 us
    all_to_all x1, waiting for transfers between devices, per_device(): lax.all_to_all(partial_both.reshape(devices_kvh, group_rows, 2 * ffn_widt...  10.4 us
    all_to_all x1, waiting for transfers between devices, per_device(): lax.all_to_all(jnp.broadcast_to(partial_out[None], (devices_kvh,) + parti...  10 us
    gather x3, local copies, waits for them, and re-layouts, per_device(): parcels = kv_pool[page_table[picked]]  9.29 us
  transfers between devices with their start and end apart: 4, of which 3 were waited for; matrix products, arithmetic and copies ran while one was open for 5% of the time, Pallas kernels for 0%

profile of v2, /device:TPU:0, one launch (start us, length us, event | category | flops | bytes accessed | tf_op | source)
XLA Modules:
  0.0 276.1 jit_solution(8201473199355241806)
XLA Ops:
  0.7 0.8 convert_element_type.76
  1.5 0.7 convert_element_type.78
  2.2 1.3 gather_fusion
  3.5 0.7 compare_select_fusion.1
  4.3 0.7 convert_element_type.74
  5.1 14.4 %all-gather = bf16[8,320,8]{1,2,0:T(8,128)(2,1)S(1)} all-gather(bf16[1,320,8]{1,2,0:T(8,128)(2,1)} %bitcast.88), channel_id=1, replica_groups=mesh['req'=16,'kvh'=8] {'kvh'}, dimensions={0}, use_global_device_ids=true | all-gather | bytes 46080 | tf_op jit(solution)/shard_map/all_gather | solution.py:117
  19.8 1.3 fusion.9
  21.1 1.4 multiply_reduce_fusion.2
  22.5 2.3 multiply_reduce_fusion.1
  25.2 5.0 %gather_fusion.1 = bf16[64,128,256]{2,1,0:T(8,128)(2,1)} fusion(bf16[64,128,256]{2,1,0:T(8,128)(2,1)} %bitcast.82, s32[1024]{0:T(1024)S(1)} %pad_clamp_fusion.4), kind=kCustom, calls=%fused_computation.1 | custom fusion | bytes 8388864 | tf_op jit(solution)/shard_map/gather | solution.py:138
  30.4 7.6 %select_select_fusion.1 = bf16[8,1,1024,256]{3,2,0,1:T(8,128)(2,1)} fusion(bf16[8,1,1024,256]{3,2,0,1:T(8,128)(2,1)} %bitcast.86, pred[8,1024]{1,0:T(8,128)(4,1)S(1)} %get-tuple-element.13, pred[8,1024]{1,0:T(8,128)(4,1)S(1)} %get-tuple-element.12, bf16[8,256]{1,0:T(8,128)(2,1)S(1)} %maximum_bitcast_fusion), kind=kLoop, calls=%fused_computation.11 | loop fusion | flops 4194304 | bytes 8409088 | tf_op jit(solution)/shard_map/jit(_where)/select_n | solution.py:48
  38.1 2.5 fusion.44
  40.5 2.1 fusion.8
  43.1 0.9 broadcast_in_dim.127
  43.9 4.0 %all-to-all-start = ((f32[8,8,2560]{2,1,0:T(8,128)}), f32[8,8,2560]{2,1,0:T(8,128)S(1)}, u32[]{:S(2)}, u32[]{:S(2)}) async-start(f32[8,8,2560]{2,1,0:T(8,128)} %broadcast_in_dim.127), calls=%async_computation | async-start | bytes 1310720 | tf_op jit(solution)/shard_map/all_to_all | solution.py:146
  48.0 1.0 scatter_custom_fusion
  49.0 0.6 gather_fusion.3
  49.7 10.0 %all-to-all-done = f32[8,8,2560]{2,1,0:T(8,128)S(1)} async-done(((f32[8,8,2560]{2,1,0:T(8,128)}), f32[8,8,2560]{2,1,0:T(8,128)S(1)}, u32[]{:S(2)}, u32[]{:S(2)}) %all-to-all-start) | async-done | bytes 655392 | tf_op jit(solution)/shard_map/all_to_all | solution.py:146
  60.6 24.1 %all_gather.10 = bf16[128,576]{1,0:T(8,128)(2,1)S(1)} all-gather(bf16[8,576]{1,0:T(8,128)(2,1)S(1)} %pad_maximum_fusion), channel_id=1, replica_groups=mesh['req'=16,'kvh'=8] {'req'}, dimensions={0}, use_global_device_ids=true | all-gather | bytes 156672 | tf_op jit(solution)/shard_map/all_gather | solution.py:166
  84.7 2.4 fusion.10
  87.1 3.5 %all-to-all-start.1 = ((f32[8,16,1216]{2,1,0:T(8,128)}), f32[8,16,1216]{2,1,0:T(8,128)S(1)}, u32[]{:S(2)}, u32[]{:S(2)}) async-start(f32[8,16,1216]{2,1,0:T(8,128)} %bitcast.87), calls=%async_computation.1 | async-start | bytes 1310720 | tf_op jit(solution)/shard_map/all_to_all | solution.py:176
  91.9 10.4 %all-to-all-done.1 = f32[8,16,1216]{2,1,0:T(8,128)S(1)} async-done(((f32[8,16,1216]{2,1,0:T(8,128)}), f32[8,16,1216]{2,1,0:T(8,128)S(1)}, u32[]{:S(2)}, u32[]{:S(2)}) %all-to-all-start.1) | async-done | bytes 622624 | tf_op jit(solution)/shard_map/all_to_all | solution.py:176
  102.4 12.8 %all_gather.11 = bf16[128,608]{1,0:T(8,128)(2,1)S(1)} all-gather(bf16[16,608]{1,0:T(8,128)(2,1)S(1)} %fusion.21), channel_id=1, replica_groups=mesh['req'=16,'kvh'=8] {'kvh'}, dimensions={0}, use_global_device_ids=true | all-gather | bytes 175104 | tf_op jit(solution)/shard_map/all_gather | solution.py:188
  115.1 2.0 convolution_bitcast_fusion
  117.1 4.8 %all-to-all-start.2 = ((f32[16,8,320]{2,1,0:T(8,128)}), f32[16,8,320]{2,1,0:T(8,128)S(1)}, u32[]{:S(2)}, u32[]{:S(2)}) async-start(f32[16,8,320]{2,1,0:T(8,128)} %convolution_bitcast_fusion), calls=%async_computation.2 | async-start | bytes 393216 | tf_op jit(solution)/shard_map/all_to_all | solution.py:191
  122.1 8.7 %gather_fusion.5 = bf16[128,128,256]{2,1,0:T(8,128)(2,1)} fusion(bf16[64,128,256]{2,1,0:T(8,128)(2,1)} %bitcast.83, s32[1024]{0:T(1024)S(1)} %pad_clamp_fusion.1), kind=kCustom, calls=%fused_computation.5 | custom fusion | bytes 16777728 | tf_op jit(solution)/shard_map/gather | solution.py:112
  130.8 7.4 %all-to-all-start.3 = ((bf16[16,8,1,128,256]{4,3,1,2,0:T(8,128)(2,1)}), bf16[16,8,1,128,256]{4,3,1,2,0:T(8,128)(2,1)}, u32[]{:S(2)}, u32[]{:S(2)}) async-start(bf16[16,8,1,128,256]{4,3,1,2,0:T(8,128)(2,1)} %bitcast.84), calls=%async_computation.3 | async-start | bytes 16777216 | tf_op jit(solution)/shard_map/all_to_all | solution.py:113
  138.3 0.6 gather_fusion.2
  139.9 1.4 add_convert_fusion.1
  141.3 120.9 %all-to-all-done.3 = bf16[16,8,1,128,256]{4,3,1,2,0:T(8,128)(2,1)} async-done(((bf16[16,8,1,128,256]{4,3,1,2,0:T(8,128)(2,1)}), bf16[16,8,1,128,256]{4,3,1,2,0:T(8,128)(2,1)}, u32[]{:S(2)}, u32[]{:S(2)}) %all-to-all-start.3) | async-done | bytes 8388640 | tf_op jit(solution)/shard_map/all_to_all | solution.py:113
  262.2 6.2 %gather_fusion.6 = bf16[8,8,128,256]{3,2,1,0:T(8,128)(2,1)} fusion(bf16[16,8,128,256]{3,2,1,0:T(8,128)(2,1)} %bitcast.18, s32[1024]{0:T(1024)S(1)} %pad_clamp_fusion), kind=kCustom, calls=%fused_computation.6 | custom fusion | bytes 8388640 | tf_op jit(solution)/shard_map/gather | solution.py:202
  268.4 7.6 %select_select_fusion = bf16[64,1,128,256]{3,2,1,0:T(8,128)(2,1)} fusion(bf16[64,1,128,256]{3,2,1,0:T(8,128)(2,1)} %bitcast.85, pred[64,128]{1,0:T(8,128)(4,1)S(1)} %get-tuple-element.11, pred[64,128]{1,0:T(8,128)(4,1)S(1)} %get-tuple-element.10, bf16[64,256]{1,0:T(8,128)(2,1)S(1)} %broadcast_bitcast_fusion), kind=kLoop, calls=%fused_computation.10 | loop fusion | flops 4194304 | bytes 8437760 | tf_op jit(solution)/shard_map/jit(_where)/select_n | solution.py:48
  (67 shorter events, 5.1 us)
Async XLA Ops:
  0.6 42.0 %copy-start = (bf16[512,2560]{1,0:T(8,128)(2,1)S(1)}, bf16[512,2560]{1,0:T(8,128)(2,1)}, u32[]{:S(2)}) copy-start(bf16[512,2560]{1,0:T(8,128)(2,1)} %param.23) | copy-start | bytes 7864324
  40.5 7.5 %copy-start.4 = (bf16[320]{0:T(512)(128)(2,1)S(1)}, bf16[320]{0:T(512)(128)(2,1)}, u32[]{:S(2)}) copy-start(bf16[320]{0:T(512)(128)(2,1)} %param.24) | copy-start | bytes 1924
  40.5 7.5 %copy-start.5 = (s32[128]{0:T(128)S(1)}, s32[128]{0:T(128)}, u32[]{:S(2)}) copy-start(s32[128]{0:T(128)} %param.31) | copy-start | bytes 1540
  42.6 48.6 %copy-start.2 = (s32[8,8]{1,0:T(8,128)S(1)}, s32[8,8]{1,0:T(8,128)}, u32[]{:S(2)}) copy-start(s32[8,8]{1,0:T(8,128)} %param.30) | copy-start | bytes 772
  43.9 15.8 %all-to-all-start = ((f32[8,8,2560]{2,1,0:T(8,128)}), f32[8,8,2560]{2,1,0:T(8,128)S(1)}, u32[]{:S(2)}, u32[]{:S(2)}) async-start(f32[8,8,2560]{2,1,0:T(8,128)} %broadcast_in_dim.127), calls=%async_computation | async-start | bytes 1310720 | tf_op jit(solution)/shard_map/all_to_all | solution.py:146
  59.9 0.6 copy-start.3
  87.1 15.2 %all-to-all-start.1 = ((f32[8,16,1216]{2,1,0:T(8,128)}), f32[8,16,1216]{2,1,0:T(8,128)S(1)}, u32[]{:S(2)}, u32[]{:S(2)}) async-start(f32[8,16,1216]{2,1,0:T(8,128)} %bitcast.87), calls=%async_computation.1 | async-start | bytes 1310720 | tf_op jit(solution)/shard_map/all_to_all | solution.py:176
  117.1 13.7 %all-to-all-start.2 = ((f32[16,8,320]{2,1,0:T(8,128)}), f32[16,8,320]{2,1,0:T(8,128)S(1)}, u32[]{:S(2)}, u32[]{:S(2)}) async-start(f32[16,8,320]{2,1,0:T(8,128)} %convolution_bitcast_fusion), calls=%async_computation.2 | async-start | bytes 393216 | tf_op jit(solution)/shard_map/all_to_all | solution.py:191
  130.8 7.5 %copy-start.1 = (s32[128]{0:T(128)S(1)}, s32[128]{0:T(128)}, u32[]{:S(2)}) copy-start(s32[128]{0:T(128)} %param.29) | copy-start | bytes 1540
  130.8 131.4 %all-to-all-start.3 = ((bf16[16,8,1,128,256]{4,3,1,2,0:T(8,128)(2,1)}), bf16[16,8,1,128,256]{4,3,1,2,0:T(8,128)(2,1)}, u32[]{:S(2)}, u32[]{:S(2)}) async-start(bf16[16,8,1,128,256]{4,3,1,2,0:T(8,128)(2,1)} %bitcast.84), calls=%async_computation.3 | async-start | bytes 16777216 | tf_op jit(solution)/shard_map/all_to_all | solution.py:113

commit v3 on v2

--- a/solution.py
+++ b/solution.py
@@ -4,6 +4,7 @@
 import jax.numpy as jnp
 from jax import lax
 from jax.sharding import PartitionSpec as P
+
 
 D = 2560
 
@@ -36,7 +37,7 @@
 
 
 def mask_blocks(blocks, lengths_now, fresh):
-    row_count, pages_per, kv_local, page_len, channels = blocks.shape
+    _, pages_per, _, page_len, _ = blocks.shape
     positions = (
         jnp.arange(pages_per, dtype=jnp.int32)[:, None] * page_len
         + jnp.arange(page_len, dtype=jnp.int32)[None, :]
@@ -109,8 +110,11 @@
     peer_ids = jnp.arange(devices_req, dtype=jnp.int32)
     matches = destination[None, :] == peer_ids[:, None]
     picked = jnp.argmax(matches.astype(jnp.int32), axis=1)
-    parcels = kv_pool[page_table[picked]]
-    received = lax.all_to_all(parcels, "req", split_axis=0, concat_axis=0, tiled=True)
+    shift_parcels = [
+        kv_pool[page_table[picked[(my_index + shift) % devices_req]]]
+        for shift in range(devices_req)
+    ]
+    early_shifts = devices_req // 3
     arriving = lax.dynamic_slice_in_dim(new_order, my_index * row_count, row_count)
     source_owner = arriving // row_count
 
@@ -166,6 +170,9 @@
     gathered = lax.all_gather(
         jnp.concatenate([normed_two, fresh_flat], axis=1), "req", axis=0, tiled=True
     )
+    late_parcels = shift_parcels[early_shifts + 1 :]
+    gathered, late_parcels = lax.optimization_barrier((gathered, late_parcels))
+    shift_parcels = shift_parcels[: early_shifts + 1] + list(late_parcels)
     normed_all = gathered[:, :width_local]
     fresh_all = gathered[:, width_local:].reshape(total_rows, kv_local, channels)
     ffn_width = w_gate.shape[1]
@@ -187,19 +194,26 @@
     )
     hidden = lax.all_gather(hidden_part, "kvh", axis=0, tiled=True)
     lowered_parts = jnp.dot(hidden, w_down, preferred_element_type=jnp.float32)
-    lowered = jnp.sum(
-        lax.all_to_all(
-            lowered_parts.reshape(devices_req, row_count, width_local),
-            "req",
-            split_axis=0,
-            concat_axis=0,
-            tiled=True,
-        ),
-        axis=0,
-    )
-    result = (residual_wide + lowered).astype(jnp.bfloat16)
-
-    arrived = received[source_owner]
+    lowered_all = lax.all_to_all(
+        lowered_parts.reshape(devices_req, row_count, width_local),
+        "req",
+        split_axis=0,
+        concat_axis=0,
+        tiled=True,
+    )
+    result = (residual_wide + jnp.sum(lowered_all, axis=0)).astype(jnp.bfloat16)
+
+    moved = [shift_parcels[0]]
+    for shift in range(1, devices_req):
+        moved.append(
+            lax.ppermute(
+                shift_parcels[shift],
+                "req",
+                [(i, (i + shift) % devices_req) for i in range(devices_req)],
+            )
+        )
+    received = jnp.stack(moved)
+    arrived = received[(my_index - source_owner) % devices_req]
     new_blocks = mask_blocks(arrived, lengths[arriving], fresh_all[arriving])
     new_pool = new_blocks.reshape(row_count * pages_per, kv_local, page_len, channels)
     return (result, new_pool)
@@ -225,6 +239,7 @@
         P(),
     )
     out_specs = (P("req", "kvh"), P("req", "kvh", None, None))
+
     return jax.shard_map(
         per_device, mesh=mesh, in_specs=in_specs, out_specs=out_specs, check_vma=False
     )

time: 277 us -> 332 us (1.20)
  waiting for transfers between devices: 141 us -> 35.3 us
  local copies, waits for them, and re-layouts: 26.8 us -> 98.9 us
  starting transfers between devices: 19.8 us -> 79.2 us
  between operations: 0.89 us -> 30.9 us
    all_to_all x1 -> x0, waiting for transfers between devices: 121 us -> none  [per_device(): lax.all_to_all(parcels, 'req', split_axis=0, concat_axis=0, tiled=True)]
    ppermute x0 -> x15, starting transfers between devices: none -> 57.7 us  [per_device(): lax.ppermute(shift_parcels[shift], 'req', [(i, (i + shift) % devices_req)...]
    gather x4 -> x17, local copies, waits for them, and re-layouts: 15.5 us -> 63.4 us  [the longest x16 57.2 us: per_device(): kv_pool[page_table[picked[(my_index + shift) % devices_req]]]]
    ppermute x0 -> x15, waiting for transfers between devices: none -> 34.4 us  [per_device(): lax.ppermute(shift_parcels[shift], 'req', [(i, (i + shift) % devices_req)...]
    unnamed x12 -> x35, local copies, waits for them, and re-layouts: 0.56 us -> 24 us
    all_to_all x1, waiting for transfers between devices: 10.4 us -> 0.01 us  [per_device(): lax.all_to_all(partial_both.reshape(devices_kvh, group_rows, 2 * ffn_widt...]
    all_to_all x1, waiting for transfers between devices: 10 us -> 0.01 us  [per_device(): lax.all_to_all(jnp.broadcast_to(partial_out[None], (devices_kvh,) + parti...]
    all_to_all x1, starting transfers between devices: 4.85 us -> 12.5 us  [per_device(): lax.all_to_all(lowered_parts.reshape(devices_req, row_count, width_local)...]
  transfers between devices with their start and end apart: 4 -> 18, of which waited for: 3 -> 4; matrix products, arithmetic and copies ran while one was open for 5% -> 37% of each run, Pallas kernels for 0% -> 0%
where the time goes in v3:
time: 332 us; the launch traced here: 329 us
  local copies, waits for them, and re-layouts  98.9 us (30%)
  starting transfers between devices  79.2 us (24%)
  blocking collectives  51 us (15%)
  waiting for transfers between devices  35.3 us (11%)
  between operations  30.9 us (9%)
  other arithmetic  21 us (6%)
  matrix products  13.2 us (4%)
    ppermute x15, starting transfers between devices, per_device(): lax.ppermute(shift_parcels[shift], 'req', [(i, (i + shift) % devices_req)...  57.7 us
    gather x16, local copies, waits for them, and re-layouts, per_device(): kv_pool[page_table[picked[(my_index + shift) % devices_req]]]  57.2 us
    ppermute x15, waiting for transfers between devices, per_device(): lax.ppermute(shift_parcels[shift], 'req', [(i, (i + shift) % devices_req)...  34.4 us
    unnamed x35, local copies, waits for them, and re-layouts  24 us
    all_gather x1, blocking collectives, per_device(): lax.all_gather(jnp.concatenate([normed_two, fresh_flat], axis=1), 'req',...  23.8 us
    select_n x2, other arithmetic, mask_blocks(): jnp.where(kept, blocks, jnp.where(placed, fresh[:, None, :, None, :], jnp...  15.3 us
    all_gather x1, blocking collectives, per_device(): full_states = lax.all_gather(states, 'kvh', axis=1, tiled=True)  14 us
    all_gather x1, blocking collectives, per_device(): hidden = lax.all_gather(hidden_part, 'kvh', axis=0, tiled=True)  13.1 us
  transfers between devices with their start and end apart: 18, of which 4 were waited for; matrix products, arithmetic and copies ran while one was open for 37% of the time, Pallas kernels for 0%

profile of v3, /device:TPU:0, one launch (start us, length us, event | category | flops | bytes accessed | tf_op | source)
XLA Modules:
  0.0 329.4 jit_solution(1935581721038881123)
XLA Ops:
  36.4 3.6 %gather_fusion.15 = bf16[8,128,256]{2,1,0:T(8,128)(2,1)} fusion(bf16[64,128,256]{2,1,0:T(8,128)(2,1)} %bitcast.233, s32[1024]{0:T(1024)S(1)} %pad_clamp_fusion.5), kind=kCustom, calls=%fused_computation.15 | custom fusion | bytes 1048608 | tf_op jit(solution)/shard_map/gather | solution.py:114
  41.6 3.6 %gather_fusion.16 = bf16[8,128,256]{2,1,0:T(8,128)(2,1)} fusion(bf16[64,128,256]{2,1,0:T(8,128)(2,1)} %bitcast.234, s32[1024]{0:T(1024)S(1)} %pad_clamp_fusion.4), kind=kCustom, calls=%fused_computation.16 | custom fusion | bytes 1048608 | tf_op jit(solution)/shard_map/gather | solution.py:114
  47.9 3.6 %gather_fusion.17 = bf16[8,128,256]{2,1,0:T(8,128)(2,1)} fusion(bf16[64,128,256]{2,1,0:T(8,128)(2,1)} %bitcast.235, s32[1024]{0:T(1024)S(1)} %pad_clamp_fusion.3), kind=kCustom, calls=%fused_computation.17 | custom fusion | bytes 1048608 | tf_op jit(solution)/shard_map/gather | solution.py:114
  53.9 3.6 %gather_fusion.18 = bf16[8,128,256]{2,1,0:T(8,128)(2,1)} fusion(bf16[64,128,256]{2,1,0:T(8,128)(2,1)} %bitcast.236, s32[1024]{0:T(1024)S(1)} %pad_clamp_fusion.2), kind=kCustom, calls=%fused_computation.18 | custom fusion | bytes 1048608 | tf_op jit(solution)/shard_map/gather | solution.py:114
  59.1 3.6 %gather_fusion.19 = bf16[8,128,256]{2,1,0:T(8,128)(2,1)} fusion(bf16[64,128,256]{2,1,0:T(8,128)(2,1)} %bitcast.237, s32[1024]{0:T(1024)S(1)} %pad_clamp_fusion.1), kind=kCustom, calls=%fused_computation.19 | custom fusion | bytes 1048608 | tf_op jit(solution)/shard_map/gather | solution.py:114
  64.7 14.0 %all-gather = bf16[8,320,8]{1,2,0:T(8,128)(2,1)S(1)} all-gather(bf16[1,320,8]{1,2,0:T(8,128)(2,1)S(1)} %bitcast.269), channel_id=1, replica_groups=mesh['req'=16,'kvh'=8] {'kvh'}, dimensions={0}, use_global_device_ids=true | all-gather | bytes 46080 | tf_op jit(solution)/shard_map/all_gather | solution.py:121
  81.3 5.0 %gather_fusion.1 = bf16[64,128,256]{2,1,0:T(8,128)(2,1)} fusion(bf16[64,128,256]{2,1,0:T(8,128)(2,1)} %bitcast.238, s32[1024]{0:T(1024)S(1)} %pad_clamp_fusion.18), kind=kCustom, calls=%fused_computation.1 | custom fusion | bytes 8388864 | tf_op jit(solution)/shard_map/gather | solution.py:142
  88.9 7.6 %select_select_fusion.1 = bf16[8,1,1024,256]{3,2,0,1:T(8,128)(2,1)} fusion(bf16[8,1,1024,256]{3,2,0,1:T(8,128)(2,1)} %bitcast.251, pred[8,1024]{1,0:T(8,128)(4,1)S(1)} %get-tuple-element.35, pred[8,1024]{1,0:T(8,128)(4,1)S(1)} %get-tuple-element.34, bf16[8,256]{1,0:T(8,128)(2,1)S(1)} %maximum_bitcast_fusion), kind=kLoop, calls=%fused_computation.25 | loop fusion | flops 4194304 | bytes 8409088 | tf_op jit(solution)/shard_map/jit(_where)/select_n | solution.py:49
  102.4 4.1 %all-to-all-start = ((f32[8,8,2560]{2,1,0:T(8,128)}), f32[8,8,2560]{2,1,0:T(8,128)S(1)}, u32[]{:S(2)}, u32[]{:S(2)}) async-start(f32[8,8,2560]{2,1,0:T(8,128)} %broadcast_in_dim.139), calls=%async_computation | async-start | bytes 1310720 | tf_op jit(solution)/shard_map/all_to_all | solution.py:150
  106.5 3.6 %gather_fusion.14 = bf16[8,128,256]{2,1,0:T(8,128)(2,1)} fusion(bf16[64,128,256]{2,1,0:T(8,128)(2,1)} %bitcast.239, s32[1024]{0:T(1024)S(1)} %pad_clamp_fusion.6), kind=kCustom, calls=%fused_computation.14 | custom fusion | bytes 1048608 | tf_op jit(solution)/shard_map/gather | solution.py:114
  113.0 3.6 %gather_fusion.3 = bf16[8,128,256]{2,1,0:T(8,128)(2,1)} fusion(bf16[64,128,256]{2,1,0:T(8,128)(2,1)} %bitcast.240, s32[1024]{0:T(1024)S(1)} %pad_clamp_fusion.17), kind=kCustom, calls=%fused_computation.3 | custom fusion | bytes 1048608 | tf_op jit(solution)/shard_map/gather | solution.py:114
  116.6 3.6 %gather_fusion.4 = bf16[8,128,256]{2,1,0:T(8,128)(2,1)} fusion(bf16[64,128,256]{2,1,0:T(8,128)(2,1)} %bitcast.241, s32[1024]{0:T(1024)S(1)} %pad_clamp_fusion.16), kind=kCustom, calls=%fused_computation.4 | custom fusion | bytes 1048608 | tf_op jit(solution)/shard_map/gather | solution.py:114
  120.2 3.6 %gather_fusion.5 = bf16[8,128,256]{2,1,0:T(8,128)(2,1)} fusion(bf16[64,128,256]{2,1,0:T(8,128)(2,1)} %bitcast.242, s32[1024]{0:T(1024)S(1)} %pad_clamp_fusion.15), kind=kCustom, calls=%fused_computation.5 | custom fusion | bytes 1048608 | tf_op jit(solution)/shard_map/gather | solution.py:114
  123.8 3.6 %gather_fusion.6 = bf16[8,128,256]{2,1,0:T(8,128)(2,1)} fusion(bf16[64,128,256]{2,1,0:T(8,128)(2,1)} %bitcast.243, s32[1024]{0:T(1024)S(1)} %pad_clamp_fusion.14), kind=kCustom, calls=%fused_computation.6 | custom fusion | bytes 1048608 | tf_op jit(solution)/shard_map/gather | solution.py:114
  127.3 3.6 %gather_fusion.7 = bf16[8,128,256]{2,1,0:T(8,128)(2,1)} fusion(bf16[64,128,256]{2,1,0:T(8,128)(2,1)} %bitcast.244, s32[1024]{0:T(1024)S(1)} %pad_clamp_fusion.13), kind=kCustom, calls=%fused_computation.7 | custom fusion | bytes 1048608 | tf_op jit(solution)/shard_map/gather | solution.py:114
  130.9 3.6 %gather_fusion.8 = bf16[8,128,256]{2,1,0:T(8,128)(2,1)} fusion(bf16[64,128,256]{2,1,0:T(8,128)(2,1)} %bitcast.245, s32[1024]{0:T(1024)S(1)} %pad_clamp_fusion.12), kind=kCustom, calls=%fused_computation.8 | custom fusion | bytes 1048608 | tf_op jit(solution)/shard_map/gather | solution.py:114
  134.5 3.6 %gather_fusion.9 = bf16[8,128,256]{2,1,0:T(8,128)(2,1)} fusion(bf16[64,128,256]{2,1,0:T(8,128)(2,1)} %bitcast.246, s32[1024]{0:T(1024)S(1)} %pad_clamp_fusion.11), kind=kCustom, calls=%fused_computation.9 | custom fusion | bytes 1048608 | tf_op jit(solution)/shard_map/gather | solution.py:114
  138.0 3.6 %gather_fusion.10 = bf16[8,128,256]{2,1,0:T(8,128)(2,1)} fusion(bf16[64,128,256]{2,1,0:T(8,128)(2,1)} %bitcast.247, s32[1024]{0:T(1024)S(1)} %pad_clamp_fusion.10), kind=kCustom, calls=%fused_computation.10 | custom fusion | bytes 1048608 | tf_op jit(solution)/shard_map/gather | solution.py:114
  141.6 3.6 %gather_fusion.11 = bf16[8,128,256]{2,1,0:T(8,128)(2,1)} fusion(bf16[64,128,256]{2,1,0:T(8,128)(2,1)} %bitcast.248, s32[1024]{0:T(1024)S(1)} %pad_clamp_fusion.9), kind=kCustom, calls=%fused_computation.11 | custom fusion | bytes 1048608 | tf_op jit(solution)/shard_map/gather | solution.py:114
  145.2 3.6 %gather_fusion.12 = bf16[8,128,256]{2,1,0:T(8,128)(2,1)} fusion(bf16[64,128,256]{2,1,0:T(8,128)(2,1)} %bitcast.249, s32[1024]{0:T(1024)S(1)} %pad_clamp_fusion.8), kind=kCustom, calls=%fused_computation.12 | custom fusion | bytes 1048608 | tf_op jit(solution)/shard_map/gather | solution.py:114
  156.6 23.8 %all_gather.10 = bf16[128,576]{1,0:T(8,128)(2,1)S(1)} all-gather(bf16[8,576]{1,0:T(8,128)(2,1)S(1)} %pad_maximum_fusion), channel_id=1, replica_groups=mesh['req'=16,'kvh'=8] {'req'}, dimensions={0}, use_global_device_ids=true | all-gather | bytes 156672 | tf_op jit(solution)/shard_map/all_gather | solution.py:170
  197.7 4.8 %all-to-all-start.1 = ((f32[8,16,1216]{2,1,0:T(8,128)}), f32[8,16,1216]{2,1,0:T(8,128)S(1)}, u32[]{:S(2)}, u32[]{:S(2)}) async-start(f32[8,16,1216]{2,1,0:T(8,128)} %bitcast.253), calls=%async_computation.1 | async-start | bytes 1310720 | tf_op jit(solution)/shard_map/all_to_all | solution.py:183
  202.5 9.6 %collective-permute-start.10 = (bf16[8,1,128,256]{3,2,0,1:T(8,128)(2,1)}, bf16[8,1,128,256]{3,2,0,1:T(8,128)(2,1)S(1)}, u32[]{:S(2)}, u32[]{:S(2)}) collective-permute-start(bf16[8,1,128,256]{3,2,0,1:T(8,128)(2,1)} %bitcast.263), channel_id=1, source_target_pairs={{0,88},{8,96},{16,104},{24,112},{32,120},{40,0},{48,8},{56,16},{64... | collective-permute-start | bytes 1572872 | tf_op jit(solution)/shard_map/ppermute | solution.py:209
  213.9 18.7 %collective-permute-done.6 = bf16[8,1,128,256]{3,2,0,1:T(8,128)(2,1)} collective-permute-done((bf16[8,1,128,256]{3,2,0,1:T(8,128)(2,1)}, bf16[8,1,128,256]{3,2,0,1:T(8,128)(2,1)}, u32[]{:S(2)}, u32[]{:S(2)}) %collective-permute-start.6) | collective-permute-done | bytes 524320 | tf_op jit(solution)/shard_map/ppermute | solution.py:209
  234.5 17.4 %collective-permute-start.12 = (bf16[8,1,128,256]{3,2,0,1:T(8,128)(2,1)}, bf16[8,1,128,256]{3,2,0,1:T(8,128)(2,1)S(1)}, u32[]{:S(2)}, u32[]{:S(2)}) collective-permute-start(bf16[8,1,128,256]{3,2,0,1:T(8,128)(2,1)} %bitcast.261), channel_id=1, source_target_pairs={{0,104},{8,112},{16,120},{24,0},{32,8},{40,16},{48,24},{56,32},{64... | collective-permute-start | bytes 1572872 | tf_op jit(solution)/shard_map/ppermute | solution.py:209
  253.8 8.8 %collective-permute-start.13 = (bf16[8,1,128,256]{3,2,0,1:T(8,128)(2,1)}, bf16[8,1,128,256]{3,2,0,1:T(8,128)(2,1)S(1)}, u32[]{:S(2)}, u32[]{:S(2)}) collective-permute-start(bf16[8,1,128,256]{3,2,0,1:T(8,128)(2,1)} %bitcast.260), channel_id=1, source_target_pairs={{0,112},{8,120},{16,0},{24,8},{32,16},{40,24},{48,32},{56,40},{64,... | collective-permute-start | bytes 1572872 | tf_op jit(solution)/shard_map/ppermute | solution.py:209
  268.1 12.1 %collective-permute-done.12 = bf16[8,1,128,256]{3,2,0,1:T(8,128)(2,1)S(1)} collective-permute-done((bf16[8,1,128,256]{3,2,0,1:T(8,128)(2,1)}, bf16[8,1,128,256]{3,2,0,1:T(8,128)(2,1)S(1)}, u32[]{:S(2)}, u32[]{:S(2)}) %collective-permute-start.12) | collective-permute-done | bytes 524320 | tf_op jit(solution)/shard_map/ppermute | solution.py:209
  281.9 3.6 %collective-permute-done.14 = bf16[8,1,128,256]{3,2,0,1:T(8,128)(2,1)S(1)} collective-permute-done((bf16[8,1,128,256]{3,2,0,1:T(8,128)(2,1)S(1)}, bf16[8,1,128,256]{3,2,0,1:T(8,128)(2,1)S(1)}, u32[]{:S(2)}, u32[]{:S(2)}) %collective-permute-start.14) | collective-permute-done | bytes 524320 | tf_op jit(solution)/shard_map/ppermute | solution.py:209
  286.3 6.2 %gather_fusion.20 = bf16[8,8,128,256]{3,2,1,0:T(8,128)(2,1)} fusion(bf16[16,8,128,256]{3,2,1,0:T(8,128)(2,1)} %bitcast.252, s32[1024]{0:T(1024)S(1)} %pad_clamp_fusion), kind=kCustom, calls=%fused_computation.20 | custom fusion | bytes 8388640 | tf_op jit(solution)/shard_map/gather | solution.py:216
  292.7 13.1 %all_gather.11 = bf16[128,608]{1,0:T(8,128)(2,1)S(1)} all-gather(bf16[16,608]{1,0:T(8,128)(2,1)S(1)} %fusion.21), channel_id=1, replica_groups=mesh['req'=16,'kvh'=8] {'kvh'}, dimensions={0}, use_global_device_ids=true | all-gather | bytes 175104 | tf_op jit(solution)/shard_map/all_gather | solution.py:195
  307.7 12.5 %all-to-all-start.2 = ((f32[16,8,320]{2,1,0:T(8,128)}), f32[16,8,320]{2,1,0:T(8,128)S(1)}, u32[]{:S(2)}, u32[]{:S(2)}) async-start(f32[16,8,320]{2,1,0:T(8,128)} %convolution_bitcast_fusion), calls=%async_computation.2 | async-start | bytes 393216 | tf_op jit(solution)/shard_map/all_to_all | solution.py:197
  320.3 7.6 %select_select_fusion = bf16[64,1,128,256]{3,2,1,0:T(8,128)(2,1)} fusion(bf16[64,1,128,256]{3,2,1,0:T(8,128)(2,1)} %bitcast.250, pred[64,128]{1,0:T(8,128)(4,1)S(1)} %get-tuple-element.33, pred[64,128]{1,0:T(8,128)(4,1)S(1)} %get-tuple-element.32, bf16[64,256]{1,0:T(8,128)(2,1)S(1)} %broadcast_bitcast_fusion), kind=kLoop, calls=%fused_computation.24 | loop fusion | flops 4194304 | bytes 8437760 | tf_op jit(solution)/shard_map/jit(_where)/select_n | solution.py:49
  (143 shorter events, 72.2 us)
Async XLA Ops:
  0.6 100.4 %copy-start = (bf16[512,2560]{1,0:T(8,128)(2,1)S(1)}, bf16[512,2560]{1,0:T(8,128)(2,1)}, u32[]{:S(2)}) copy-start(bf16[512,2560]{1,0:T(8,128)(2,1)} %param.23) | copy-start | bytes 7864324
  0.6 63.3 %copy-start.4 = (s32[8,8]{1,0:T(8,128)S(1)}, s32[8,8]{1,0:T(8,128)}, u32[]{:S(2)}) copy-start(s32[8,8]{1,0:T(8,128)} %param.30) | copy-start | bytes 772
  0.7 63.3 %copy-start.1 = (s32[128]{0:T(128)S(1)}, s32[128]{0:T(128)}, u32[]{:S(2)}) copy-start(s32[128]{0:T(128)} %param.29) | copy-start | bytes 1540
  0.7 64.0 %copy-start.5 = (bf16[8,320]{1,0:T(8,128)(2,1)S(1)}, bf16[8,320]{1,0:T(8,128)(2,1)}, u32[]{:S(2)}) copy-start(bf16[8,320]{1,0:T(8,128)(2,1)} %param.16) | copy-start | bytes 15364
  0.7 78.3 %copy-start.6 = (bf16[2560]{0:T(1024)(128)(2,1)S(1)}, bf16[2560]{0:T(1024)(128)(2,1)}, u32[]{:S(2)}) copy-start(bf16[2560]{0:T(1024)(128)(2,1)} %param.17) | copy-start | bytes 15364
  0.7 78.7 %copy-start.8 = (bf16[128]{0:T(256)(128)(2,1)S(1)}, bf16[128]{0:T(256)(128)(2,1)}, u32[]{:S(2)}) copy-start(bf16[128]{0:T(256)(128)(2,1)} %param.22) | copy-start | bytes 772
  3.2 75.8 %copy-start.2 = (bf16[2560,128]{1,0:T(8,128)(2,1)S(1)}, bf16[2560,128]{1,0:T(8,128)(2,1)}, u32[]{:S(2)}) copy-start(bf16[2560,128]{1,0:T(8,128)(2,1)} %param.19) | copy-start | bytes 1966084
  40.0 108.8 %collective-permute-start = (bf16[8,1,128,256]{3,2,0,1:T(8,128)(2,1)}, bf16[8,1,128,256]{3,2,0,1:T(8,128)(2,1)}, u32[]{:S(2)}, u32[]{:S(2)}) collective-permute-start(bf16[8,1,128,256]{3,2,0,1:T(8,128)(2,1)} %bitcast.255), channel_id=1, source_target_pairs={{0,8},{8,16},{16,24},{24,32},{32,40},{40,48},{48,56},{56,64},{64,7... | collective-permute-start | bytes 1572872 | tf_op jit(solution)/shard_map/ppermute | solution.py:209
  45.2 105.5 %collective-permute-start.1 = (bf16[8,1,128,256]{3,2,0,1:T(8,128)(2,1)}, bf16[8,1,128,256]{3,2,0,1:T(8,128)(2,1)}, u32[]{:S(2)}, u32[]{:S(2)}) collective-permute-start(bf16[8,1,128,256]{3,2,0,1:T(8,128)(2,1)} %bitcast.256), channel_id=1, source_target_pairs={{0,16},{8,24},{16,32},{24,40},{32,48},{40,56},{48,64},{56,72},{64,... | collective-permute-start | bytes 1572872 | tf_op jit(solution)/shard_map/ppermute | solution.py:209
  51.5 101.1 %collective-permute-start.2 = (bf16[8,1,128,256]{3,2,0,1:T(8,128)(2,1)}, bf16[8,1,128,256]{3,2,0,1:T(8,128)(2,1)}, u32[]{:S(2)}, u32[]{:S(2)}) collective-permute-start(bf16[8,1,128,256]{3,2,0,1:T(8,128)(2,1)} %bitcast.257), channel_id=1, source_target_pairs={{0,24},{8,32},{16,40},{24,48},{32,56},{40,64},{48,72},{56,80},{64,... | collective-permute-start | bytes 1572872 | tf_op jit(solution)/shard_map/ppermute | solution.py:209
  57.5 96.9 %collective-permute-start.3 = (bf16[8,1,128,256]{3,2,0,1:T(8,128)(2,1)}, bf16[8,1,128,256]{3,2,0,1:T(8,128)(2,1)}, u32[]{:S(2)}, u32[]{:S(2)}) collective-permute-start(bf16[8,1,128,256]{3,2,0,1:T(8,128)(2,1)} %bitcast.258), channel_id=1, source_target_pairs={{0,32},{8,40},{16,48},{24,56},{32,64},{40,72},{48,80},{56,88},{64,... | collective-permute-start | bytes 1572872 | tf_op jit(solution)/shard_map/ppermute | solution.py:209
  62.7 119.7 %collective-permute-start.4 = (bf16[8,1,128,256]{3,2,0,1:T(8,128)(2,1)}, bf16[8,1,128,256]{3,2,0,1:T(8,128)(2,1)}, u32[]{:S(2)}, u32[]{:S(2)}) collective-permute-start(bf16[8,1,128,256]{3,2,0,1:T(8,128)(2,1)} %bitcast.254), channel_id=1, source_target_pairs={{0,40},{8,48},{16,56},{24,64},{32,72},{40,80},{48,88},{56,96},{64,... | collective-permute-start | bytes 1572872 | tf_op jit(solution)/shard_map/ppermute | solution.py:209
  81.3 7.4 %copy-start.9 = (bf16[128]{0:T(256)(128)(2,1)S(1)}, bf16[128]{0:T(256)(128)(2,1)}, u32[]{:S(2)}) copy-start(bf16[128]{0:T(256)(128)(2,1)} %param.21) | copy-start | bytes 772
  102.4 53.9 %all-to-all-start = ((f32[8,8,2560]{2,1,0:T(8,128)}), f32[8,8,2560]{2,1,0:T(8,128)S(1)}, u32[]{:S(2)}, u32[]{:S(2)}) async-start(f32[8,8,2560]{2,1,0:T(8,128)} %broadcast_in_dim.139), calls=%async_computation | async-start | bytes 1310720 | tf_op jit(solution)/shard_map/all_to_all | solution.py:150
  120.2 28.6 %copy-start.7 = (bf16[320]{0:T(512)(128)(2,1)S(1)}, bf16[320]{0:T(512)(128)(2,1)}, u32[]{:S(2)}) copy-start(bf16[320]{0:T(512)(128)(2,1)} %param.24) | copy-start | bytes 1924
  180.5 22.0 %collective-permute-start.5 = (bf16[8,1,128,256]{3,2,0,1:T(8,128)(2,1)}, bf16[8,1,128,256]{3,2,0,1:T(8,128)(2,1)}, u32[]{:S(2)}, u32[]{:S(2)}) collective-permute-start(bf16[8,1,128,256]{3,2,0,1:T(8,128)(2,1)} %bitcast.268), channel_id=1, source_target_pairs={{0,48},{8,56},{16,64},{24,72},{32,80},{40,88},{48,96},{56,104},{64... | collective-permute-start | bytes 1572872 | tf_op jit(solution)/shard_map/ppermute | solution.py:209
  184.3 48.4 %collective-permute-start.6 = (bf16[8,1,128,256]{3,2,0,1:T(8,128)(2,1)}, bf16[8,1,128,256]{3,2,0,1:T(8,128)(2,1)}, u32[]{:S(2)}, u32[]{:S(2)}) collective-permute-start(bf16[8,1,128,256]{3,2,0,1:T(8,128)(2,1)} %bitcast.267), channel_id=1, source_target_pairs={{0,56},{8,64},{16,72},{24,80},{32,88},{40,96},{48,104},{56,112},{6... | collective-permute-start | bytes 1572872 | tf_op jit(solution)/shard_map/ppermute | solution.py:209
  186.8 47.7 %collective-permute-start.7 = (bf16[8,1,128,256]{3,2,0,1:T(8,128)(2,1)}, bf16[8,1,128,256]{3,2,0,1:T(8,128)(2,1)}, u32[]{:S(2)}, u32[]{:S(2)}) collective-permute-start(bf16[8,1,128,256]{3,2,0,1:T(8,128)(2,1)} %bitcast.266), channel_id=1, source_target_pairs={{0,64},{8,72},{16,80},{24,88},{32,96},{40,104},{48,112},{56,120},{... | collective-permute-start | bytes 1572872 | tf_op jit(solution)/shard_map/ppermute | solution.py:209
  188.9 64.9 %collective-permute-start.8 = (bf16[8,1,128,256]{3,2,0,1:T(8,128)(2,1)}, bf16[8,1,128,256]{3,2,0,1:T(8,128)(2,1)}, u32[]{:S(2)}, u32[]{:S(2)}) collective-permute-start(bf16[8,1,128,256]{3,2,0,1:T(8,128)(2,1)} %bitcast.265), channel_id=1, source_target_pairs={{0,72},{8,80},{16,88},{24,96},{32,104},{40,112},{48,120},{56,0},{6... | collective-permute-start | bytes 1572872 | tf_op jit(solution)/shard_map/ppermute | solution.py:209
  191.4 73.1 %collective-permute-start.9 = (bf16[8,1,128,256]{3,2,0,1:T(8,128)(2,1)}, bf16[8,1,128,256]{3,2,0,1:T(8,128)(2,1)}, u32[]{:S(2)}, u32[]{:S(2)}) collective-permute-start(bf16[8,1,128,256]{3,2,0,1:T(8,128)(2,1)} %bitcast.264), channel_id=1, source_target_pairs={{0,80},{8,88},{16,96},{24,104},{32,112},{40,120},{48,0},{56,8},{64... | collective-permute-start | bytes 1572872 | tf_op jit(solution)/shard_map/ppermute | solution.py:209
  197.7 94.9 %all-to-all-start.1 = ((f32[8,16,1216]{2,1,0:T(8,128)}), f32[8,16,1216]{2,1,0:T(8,128)S(1)}, u32[]{:S(2)}, u32[]{:S(2)}) async-start(f32[8,16,1216]{2,1,0:T(8,128)} %bitcast.253), calls=%async_computation.1 | async-start | bytes 1310720 | tf_op jit(solution)/shard_map/all_to_all | solution.py:183
  202.5 62.1 %copy-start.3 = (bf16[8,128,256]{2,1,0:T(8,128)(2,1)S(1)}, bf16[8,128,256]{2,1,0:T(8,128)(2,1)}, u32[]{:S(2)}) copy-start(bf16[8,128,256]{2,1,0:T(8,128)(2,1)} %gather_fusion.12) | copy-start | bytes 1572868
  202.5 63.9 %collective-permute-start.10 = (bf16[8,1,128,256]{3,2,0,1:T(8,128)(2,1)}, bf16[8,1,128,256]{3,2,0,1:T(8,128)(2,1)S(1)}, u32[]{:S(2)}, u32[]{:S(2)}) collective-permute-start(bf16[8,1,128,256]{3,2,0,1:T(8,128)(2,1)} %bitcast.263), channel_id=1, source_target_pairs={{0,88},{8,96},{16,104},{24,112},{32,120},{40,0},{48,8},{56,16},{64... | collective-permute-start | bytes 1572872 | tf_op jit(solution)/shard_map/ppermute | solution.py:209
  232.6 34.7 %collective-permute-start.11 = (bf16[8,1,128,256]{3,2,0,1:T(8,128)(2,1)}, bf16[8,1,128,256]{3,2,0,1:T(8,128)(2,1)S(1)}, u32[]{:S(2)}, u32[]{:S(2)}) collective-permute-start(bf16[8,1,128,256]{3,2,0,1:T(8,128)(2,1)} %bitcast.262), channel_id=1, source_target_pairs={{0,96},{8,104},{16,112},{24,120},{32,0},{40,8},{48,16},{56,24},{64... | collective-permute-start | bytes 1572872 | tf_op jit(solution)/shard_map/ppermute | solution.py:209
  234.5 45.7 %collective-permute-start.12 = (bf16[8,1,128,256]{3,2,0,1:T(8,128)(2,1)}, bf16[8,1,128,256]{3,2,0,1:T(8,128)(2,1)S(1)}, u32[]{:S(2)}, u32[]{:S(2)}) collective-permute-start(bf16[8,1,128,256]{3,2,0,1:T(8,128)(2,1)} %bitcast.261), channel_id=1, source_target_pairs={{0,104},{8,112},{16,120},{24,0},{32,8},{40,16},{48,24},{56,32},{64... | collective-permute-start | bytes 1572872 | tf_op jit(solution)/shard_map/ppermute | solution.py:209
  253.8 27.3 %collective-permute-start.13 = (bf16[8,1,128,256]{3,2,0,1:T(8,128)(2,1)}, bf16[8,1,128,256]{3,2,0,1:T(8,128)(2,1)S(1)}, u32[]{:S(2)}, u32[]{:S(2)}) collective-permute-start(bf16[8,1,128,256]{3,2,0,1:T(8,128)(2,1)} %bitcast.260), channel_id=1, source_target_pairs={{0,112},{8,120},{16,0},{24,8},{32,16},{40,24},{48,32},{56,40},{64,... | collective-permute-start | bytes 1572872 | tf_op jit(solution)/shard_map/ppermute | solution.py:209
  264.5 20.9 %collective-permute-start.14 = (bf16[8,1,128,256]{3,2,0,1:T(8,128)(2,1)S(1)}, bf16[8,1,128,256]{3,2,0,1:T(8,128)(2,1)S(1)}, u32[]{:S(2)}, u32[]{:S(2)}) collective-permute-start(bf16[8,1,128,256]{3,2,0,1:T(8,128)(2,1)S(1)} %bitcast.259), channel_id=1, source_target_pairs={{0,120},{8,0},{16,8},{24,16},{32,24},{40,32},{48,40},{56,48},{64,5... | collective-permute-start | bytes 1572872 | tf_op jit(solution)/shard_map/ppermute | solution.py:209
  307.7 21.0 %all-to-all-start.2 = ((f32[16,8,320]{2,1,0:T(8,128)}), f32[16,8,320]{2,1,0:T(8,128)S(1)}, u32[]{:S(2)}, u32[]{:S(2)}) async-start(f32[16,8,320]{2,1,0:T(8,128)} %convolution_bitcast_fusion), calls=%async_computation.2 | async-start | bytes 393216 | tf_op jit(solution)/shard_map/all_to_all | solution.py:197

commit v4 on v2

--- a/solution.py
+++ b/solution.py
@@ -142,16 +142,13 @@
     mixed = attend(query, sequence, positions_home)
     partial_out = jnp.dot(mixed, w_output, preferred_element_type=jnp.float32)
     devices_kvh = lax.axis_size("kvh")
-    attn_out = jnp.sum(
-        lax.all_to_all(
-            jnp.broadcast_to(partial_out[None], (devices_kvh,) + partial_out.shape),
-            "kvh",
-            split_axis=0,
-            concat_axis=0,
-            tiled=True,
-        ),
-        axis=0,
-    )
+    attn_out = partial_out
+    step = 1
+    while step < devices_kvh:
+        attn_out = attn_out + lax.ppermute(
+            attn_out, "kvh", [(i, i ^ step) for i in range(devices_kvh)]
+        )
+        step *= 2
     residual_full = (full_states.astype(jnp.float32) + attn_out).astype(jnp.bfloat16)
     residual_wide_full = residual_full.astype(jnp.float32)
     total_sq = jnp.sum(residual_wide_full * residual_wide_full, axis=-1, keepdims=True)
@@ -163,9 +160,9 @@
     ).astype(jnp.bfloat16)
 
     fresh_flat = fresh.reshape(row_count, kv_local * channels)
-    gathered = lax.all_gather(
-        jnp.concatenate([normed_two, fresh_flat], axis=1), "req", axis=0, tiled=True
-    )
+    outgoing = jnp.concatenate([normed_two, fresh_flat], axis=1)
+    received, outgoing = lax.optimization_barrier((received, outgoing))
+    gathered = lax.all_gather(outgoing, "req", axis=0, tiled=True)
     normed_all = gathered[:, :width_local]
     fresh_all = gathered[:, width_local:].reshape(total_rows, kv_local, channels)
     ffn_width = w_gate.shape[1]

time: 277 us -> 219 us (0.79)
  waiting for transfers between devices: 141 us -> 85.6 us
    all_to_all x1, waiting for transfers between devices: 121 us -> 73.4 us  [per_device(): lax.all_to_all(parcels, 'req', split_axis=0, concat_axis=0, tiled=True)]
    all_to_all x1 -> x0, waiting for transfers between devices: 10 us -> none  [per_device(): lax.all_to_all(jnp.broadcast_to(partial_out[None], (devices_kvh,) + parti...]
    ppermute x0 -> x3, waiting for transfers between devices: none -> 6.54 us  [per_device(): lax.ppermute(attn_out, 'kvh', [(i, i ^ step) for i in range(devices_kvh)])]
    all_to_all x1, waiting for transfers between devices: 10.4 us -> 4.74 us  [per_device(): lax.all_to_all(partial_both.reshape(devices_kvh, group_rows, 2 * ffn_widt...]
    ppermute x0 -> x3, starting transfers between devices: none -> 4.66 us  [per_device(): lax.ppermute(attn_out, 'kvh', [(i, i ^ step) for i in range(devices_kvh)])]
    all_to_all x1 -> x0, starting transfers between devices: 4.03 us -> none  [per_device(): lax.all_to_all(jnp.broadcast_to(partial_out[None], (devices_kvh,) + parti...]
  transfers between devices with their start and end apart: 4 -> 6, of which waited for: 3 -> 6; matrix products, arithmetic and copies ran while one was open for 5% -> 18% of each run, Pallas kernels for 0% -> 0%
where the time goes in v4:
time: 219 us; the launch traced here: 218 us
  waiting for transfers between devices  85.6 us (39%)
  blocking collectives  50.1 us (23%)
  local copies, waits for them, and re-layouts  26 us (12%)
  starting transfers between devices  22 us (10%)
  other arithmetic  19.8 us (9%)
  matrix products  13.2 us (6%)
    all_to_all x1, waiting for transfers between devices, per_device(): lax.all_to_all(parcels, 'req', split_axis=0, concat_axis=0, tiled=True)  73.4 us
    all_gather x1, blocking collectives, per_device(): gathered = lax.all_gather(outgoing, 'req', axis=0, tiled=True)  23.2 us
    select_n x2, other arithmetic, mask_blocks(): jnp.where(kept, blocks, jnp.where(placed, fresh[:, None, :, None, :], jnp...  15.3 us
    all_gather x1, blocking collectives, per_device(): full_states = lax.all_gather(states, 'kvh', axis=1, tiled=True)  14 us
    all_gather x1, blocking collectives, per_device(): hidden = lax.all_gather(hidden_part, 'kvh', axis=0, tiled=True)  12.8 us
    gather x3, local copies, waits for them, and re-layouts, per_device(): parcels = kv_pool[page_table[picked]]  9.9 us
    all_to_all x1, starting transfers between devices, per_device(): lax.all_to_all(parcels, 'req', split_axis=0, concat_axis=0, tiled=True)  7.38 us
    ppermute x3, waiting for transfers between devices, per_device(): lax.ppermute(attn_out, 'kvh', [(i, i ^ step) for i in range(devices_kvh)])  6.54 us
  transfers between devices with their start and end apart: 6, of which 6 were waited for; matrix products, arithmetic and copies ran while one was open for 18% of the time, Pallas kernels for 0%

profile of v4, /device:TPU:0, one launch (start us, length us, event | category | flops | bytes accessed | tf_op | source)
XLA Modules:
  0.0 217.5 jit_solution(9439197116256583357)
XLA Ops:
  0.7 0.8 compare_select_fusion.4
  1.5 1.0 scatter_custom_fusion
  2.5 0.6 gather_fusion.2
  3.7 1.2 gather_fusion.3
  5.3 8.6 %gather_fusion.4 = bf16[128,128,256]{2,1,0:T(8,128)(2,1)} fusion(bf16[64,128,256]{2,1,0:T(8,128)(2,1)} %bitcast.81, s32[1024]{0:T(1024)S(1)} %pad_clamp_fusion.2), kind=kCustom, calls=%fused_computation.4 | custom fusion | bytes 16777728 | tf_op jit(solution)/shard_map/gather | solution.py:112
  13.9 7.4 %all-to-all-start = ((bf16[16,8,1,128,256]{4,3,1,2,0:T(8,128)(2,1)}), bf16[16,8,1,128,256]{4,3,1,2,0:T(8,128)(2,1)}, u32[]{:S(2)}, u32[]{:S(2)}) async-start(bf16[16,8,1,128,256]{4,3,1,2,0:T(8,128)(2,1)} %bitcast.83), calls=%async_computation | async-start | bytes 16777216 | tf_op jit(solution)/shard_map/all_to_all | solution.py:113
  21.3 14.0 %all-gather = bf16[8,320,8]{1,2,0:T(8,128)(2,1)S(1)} all-gather(bf16[1,320,8]{1,2,0:T(8,128)(2,1)S(1)} %bitcast.87), channel_id=1, replica_groups=mesh['req'=16,'kvh'=8] {'kvh'}, dimensions={0}, use_global_device_ids=true | all-gather | bytes 46080 | tf_op jit(solution)/shard_map/all_gather | solution.py:117
  35.5 0.6 gather_fusion
  36.2 5.1 %gather_fusion.1 = bf16[64,128,256]{2,1,0:T(8,128)(2,1)} fusion(bf16[64,128,256]{2,1,0:T(8,128)(2,1)} %bitcast.82, s32[1024]{0:T(1024)S(1)} %pad_clamp_fusion.4), kind=kCustom, calls=%fused_computation.1 | custom fusion | bytes 8388864 | tf_op jit(solution)/shard_map/gather | solution.py:138
  41.6 2.3 %multiply_reduce_fusion.1 = (f32[8,4]{0,1:T(4,128)S(1)}, f32[8,4,128]{2,0,1:T(8,128)S(1)}) fusion(bf16[8,2560]{1,0:T(8,128)(2,1)S(1)} %fusion.17, bf16[2560,512]{1,0:T(8,128)(2,1)} %param.18), kind=kOutput, calls=%fused_computation.54 | convolution fusion | flops 20979680 | bytes 2678912 | tf_op jit(solution)/shard_map/dot_general | solution.py:121
  44.2 1.4 multiply_reduce_fusion.2
  46.3 7.6 %select_select_fusion.1 = bf16[8,1,1024,256]{3,2,0,1:T(8,128)(2,1)} fusion(bf16[8,1,1024,256]{3,2,0,1:T(8,128)(2,1)} %bitcast.85, pred[8,1024]{1,0:T(8,128)(4,1)S(1)} %get-tuple-element.17, pred[8,1024]{1,0:T(8,128)(4,1)S(1)} %get-tuple-element.16, bf16[8,256]{1,0:T(8,128)(2,1)S(1)} %maximum_bitcast_fusion), kind=kLoop, calls=%fused_computation.11 | loop fusion | flops 4194304 | bytes 8409088 | tf_op jit(solution)/shard_map/jit(_where)/select_n | solution.py:48
  54.0 2.5 %fusion.44 = (f32[8,4]{1,0:T(8,128)S(1)}, f32[8,4,1024]{2,1,0:T(4,128)S(1)}) fusion(bf16[8,1,1024,256]{3,2,0,1:T(8,128)(2,1)} %select_select_fusion.1, pred[8,1024]{1,0:T(8,128)(4,1)S(1)} %get-tuple-element.24, bf16[8,4,64]{2,1,0:T(4,128)(2,1)S(1)} %get-tuple-element.11, bf16[8,4,64]{2,1,0:T(4,128)(2,1)S(1)} %get-tuple-element.10), kind=kOutput, calls=%fused_computation.115 | convolution fusion | flops 8537087 | bytes 2244736 | tf_op jit(solution)/shard_map/sub | solution.py:67
  56.4 2.0 fusion.8
  59.3 0.9 collective-permute-done
  60.2 1.7 collective-permute-start.1
  62.0 3.0 %collective-permute-done.1 = f32[8,2560]{1,0:T(8,128)S(1)} collective-permute-done((f32[8,2560]{1,0:T(8,128)S(1)}, f32[8,2560]{1,0:T(8,128)S(1)}, u32[]{:S(2)}, u32[]{:S(2)}) %collective-permute-start.1) | collective-permute-done | bytes 81952 | tf_op jit(solution)/shard_map/ppermute | solution.py:148
  65.0 2.6 %collective-permute-start.2 = (f32[8,2560]{1,0:T(8,128)S(1)}, f32[8,2560]{1,0:T(8,128)S(1)}, u32[]{:S(2)}, u32[]{:S(2)}) collective-permute-start(f32[8,2560]{1,0:T(8,128)S(1)} %add.195), channel_id=1, source_target_pairs={{0,4},{1,5},{2,6},{3,7},{4,0},{5,1},{6,2},{7,3},{8,12},{9,13},{10,... | collective-permute-start | bytes 245768 | tf_op jit(solution)/shard_map/ppermute | solution.py:148
  67.7 0.6 gather_fusion.5
  68.5 2.6 %collective-permute-done.2 = f32[8,2560]{1,0:T(8,128)S(1)} collective-permute-done((f32[8,2560]{1,0:T(8,128)S(1)}, f32[8,2560]{1,0:T(8,128)S(1)}, u32[]{:S(2)}, u32[]{:S(2)}) %collective-permute-start.2) | collective-permute-done | bytes 81952 | tf_op jit(solution)/shard_map/ppermute | solution.py:148
  72.0 73.4 %all-to-all-done = bf16[16,8,1,128,256]{4,3,1,2,0:T(8,128)(2,1)} async-done(((bf16[16,8,1,128,256]{4,3,1,2,0:T(8,128)(2,1)}), bf16[16,8,1,128,256]{4,3,1,2,0:T(8,128)(2,1)}, u32[]{:S(2)}, u32[]{:S(2)}) %all-to-all-start) | async-done | bytes 8388640 | tf_op jit(solution)/shard_map/all_to_all | solution.py:113
  145.4 23.2 %all_gather.10 = bf16[128,576]{1,0:T(8,128)(2,1)S(1)} all-gather(bf16[8,576]{1,0:T(8,128)(2,1)S(1)} %pad_maximum_fusion), channel_id=1, replica_groups=mesh['req'=16,'kvh'=8] {'req'}, dimensions={0}, use_global_device_ids=true | all-gather | bytes 156672 | tf_op jit(solution)/shard_map/all_gather | solution.py:165
  168.7 2.4 %fusion.10 = f32[128,1216]{1,0:T(8,128)} fusion(bf16[320,608]{1,0:T(8,128)(2,1)} %param.26, bf16[320,608]{1,0:T(8,128)(2,1)} %param.25, bf16[128,576]{1,0:T(8,128)(2,1)S(1)} %all_gather.10), kind=kOutput, calls=%fused_computation.26 | convolution fusion | flops 101171200 | bytes 1499136 | tf_op jit(solution)/shard_map/dot_general | solution.py:170
  171.1 5.3 %all-to-all-start.1 = ((f32[8,16,1216]{2,1,0:T(8,128)}), f32[8,16,1216]{2,1,0:T(8,128)S(1)}, u32[]{:S(2)}, u32[]{:S(2)}) async-start(f32[8,16,1216]{2,1,0:T(8,128)} %bitcast.86), calls=%async_computation.1 | async-start | bytes 1310720 | tf_op jit(solution)/shard_map/all_to_all | solution.py:173
  177.1 6.2 %gather_fusion.6 = bf16[8,8,128,256]{3,2,1,0:T(8,128)(2,1)} fusion(bf16[16,8,128,256]{3,2,1,0:T(8,128)(2,1)} %bitcast.18, s32[1024]{0:T(1024)S(1)} %pad_clamp_fusion), kind=kCustom, calls=%fused_computation.6 | custom fusion | bytes 8388640 | tf_op jit(solution)/shard_map/gather | solution.py:199
  183.4 4.7 %all-to-all-done.1 = f32[8,16,1216]{2,1,0:T(8,128)S(1)} async-done(((f32[8,16,1216]{2,1,0:T(8,128)}), f32[8,16,1216]{2,1,0:T(8,128)S(1)}, u32[]{:S(2)}, u32[]{:S(2)}) %all-to-all-start.1) | async-done | bytes 622624 | tf_op jit(solution)/shard_map/all_to_all | solution.py:173
  188.2 12.8 %all_gather.11 = bf16[128,608]{1,0:T(8,128)(2,1)S(1)} all-gather(bf16[16,608]{1,0:T(8,128)(2,1)S(1)} %fusion.21), channel_id=1, replica_groups=mesh['req'=16,'kvh'=8] {'kvh'}, dimensions={0}, use_global_device_ids=true | all-gather | bytes 175104 | tf_op jit(solution)/shard_map/all_gather | solution.py:185
  201.0 2.0 convolution_bitcast_fusion
  203.0 4.7 %all-to-all-start.2 = ((f32[16,8,320]{2,1,0:T(8,128)}), f32[16,8,320]{2,1,0:T(8,128)S(1)}, u32[]{:S(2)}, u32[]{:S(2)}) async-start(f32[16,8,320]{2,1,0:T(8,128)} %convolution_bitcast_fusion), calls=%async_computation.2 | async-start | bytes 393216 | tf_op jit(solution)/shard_map/all_to_all | solution.py:188
  207.6 7.6 %select_select_fusion = bf16[64,1,128,256]{3,2,1,0:T(8,128)(2,1)} fusion(bf16[64,1,128,256]{3,2,1,0:T(8,128)(2,1)} %bitcast.84, pred[64,128]{1,0:T(8,128)(4,1)S(1)} %get-tuple-element.15, pred[64,128]{1,0:T(8,128)(4,1)S(1)} %get-tuple-element.14, bf16[64,256]{1,0:T(8,128)(2,1)S(1)} %broadcast_bitcast_fusion), kind=kLoop, calls=%fused_computation.10 | loop fusion | flops 4194304 | bytes 8437760 | tf_op jit(solution)/shard_map/jit(_where)/select_n | solution.py:48
  215.3 0.9 all-to-all-done.2
  216.1 1.4 add_convert_fusion.1
  (81 shorter events, 5.2 us)
Async XLA Ops:
  0.6 57.8 %copy-start = (bf16[512,2560]{1,0:T(8,128)(2,1)S(1)}, bf16[512,2560]{1,0:T(8,128)(2,1)}, u32[]{:S(2)}) copy-start(bf16[512,2560]{1,0:T(8,128)(2,1)} %param.23) | copy-start | bytes 7864324
  13.8 7.4 %copy-start.5 = (bf16[8,320]{1,0:T(8,128)(2,1)S(1)}, bf16[8,320]{1,0:T(8,128)(2,1)}, u32[]{:S(2)}) copy-start(bf16[8,320]{1,0:T(8,128)(2,1)} %param.16) | copy-start | bytes 15364
  13.8 21.6 %copy-start.6 = (bf16[2560]{0:T(1024)(128)(2,1)S(1)}, bf16[2560]{0:T(1024)(128)(2,1)}, u32[]{:S(2)}) copy-start(bf16[2560]{0:T(1024)(128)(2,1)} %param.17) | copy-start | bytes 15364
  13.8 21.6 %copy-start.9 = (bf16[128]{0:T(256)(128)(2,1)S(1)}, bf16[128]{0:T(256)(128)(2,1)}, u32[]{:S(2)}) copy-start(bf16[128]{0:T(256)(128)(2,1)} %param.22) | copy-start | bytes 772
  13.8 21.6 %copy-start.1 = (s32[128]{0:T(128)S(1)}, s32[128]{0:T(128)}, u32[]{:S(2)}) copy-start(s32[128]{0:T(128)} %param.29) | copy-start | bytes 1540
  13.9 22.3 %copy-start.2 = (s32[8,8]{1,0:T(8,128)S(1)}, s32[8,8]{1,0:T(8,128)}, u32[]{:S(2)}) copy-start(s32[8,8]{1,0:T(8,128)} %param.30) | copy-start | bytes 772
  13.9 131.5 %all-to-all-start = ((bf16[16,8,1,128,256]{4,3,1,2,0:T(8,128)(2,1)}), bf16[16,8,1,128,256]{4,3,1,2,0:T(8,128)(2,1)}, u32[]{:S(2)}, u32[]{:S(2)}) async-start(bf16[16,8,1,128,256]{4,3,1,2,0:T(8,128)(2,1)} %bitcast.83), calls=%async_computation | async-start | bytes 16777216 | tf_op jit(solution)/shard_map/all_to_all | solution.py:113
  36.2 7.7 %copy-start.10 = (bf16[128]{0:T(256)(128)(2,1)S(1)}, bf16[128]{0:T(256)(128)(2,1)}, u32[]{:S(2)}) copy-start(bf16[128]{0:T(256)(128)(2,1)} %param.21) | copy-start | bytes 772
  36.2 7.7 %copy-start.3 = (bf16[2560,128]{1,0:T(8,128)(2,1)S(1)}, bf16[2560,128]{1,0:T(8,128)(2,1)}, u32[]{:S(2)}) copy-start(bf16[2560,128]{1,0:T(8,128)(2,1)} %param.20) | copy-start | bytes 1966084
  53.9 5.3 %copy-start.7 = (bf16[320]{0:T(512)(128)(2,1)S(1)}, bf16[320]{0:T(512)(128)(2,1)}, u32[]{:S(2)}) copy-start(bf16[320]{0:T(512)(128)(2,1)} %param.24) | copy-start | bytes 1924
  54.0 7.9 %copy-start.8 = (s32[128]{0:T(128)S(1)}, s32[128]{0:T(128)}, u32[]{:S(2)}) copy-start(s32[128]{0:T(128)} %param.31) | copy-start | bytes 1540
  58.9 1.3 collective-permute-start
  60.2 4.8 %collective-permute-start.1 = (f32[8,2560]{1,0:T(8,128)S(1)}, f32[8,2560]{1,0:T(8,128)S(1)}, u32[]{:S(2)}, u32[]{:S(2)}) collective-permute-start(f32[8,2560]{1,0:T(8,128)S(1)} %add.194), channel_id=1, source_target_pairs={{0,2},{1,3},{2,0},{3,1},{4,6},{5,7},{6,4},{7,5},{8,10},{9,11},{10,... | collective-permute-start | bytes 245768 | tf_op jit(solution)/shard_map/ppermute | solution.py:148
  65.0 6.0 %collective-permute-start.2 = (f32[8,2560]{1,0:T(8,128)S(1)}, f32[8,2560]{1,0:T(8,128)S(1)}, u32[]{:S(2)}, u32[]{:S(2)}) collective-permute-start(f32[8,2560]{1,0:T(8,128)S(1)} %add.195), channel_id=1, source_target_pairs={{0,4},{1,5},{2,6},{3,7},{4,0},{5,1},{6,2},{7,3},{8,12},{9,13},{10,... | collective-permute-start | bytes 245768 | tf_op jit(solution)/shard_map/ppermute | solution.py:148
  71.2 0.6 copy-start.4
  171.1 17.0 %all-to-all-start.1 = ((f32[8,16,1216]{2,1,0:T(8,128)}), f32[8,16,1216]{2,1,0:T(8,128)S(1)}, u32[]{:S(2)}, u32[]{:S(2)}) async-start(f32[8,16,1216]{2,1,0:T(8,128)} %bitcast.86), calls=%async_computation.1 | async-start | bytes 1310720 | tf_op jit(solution)/shard_map/all_to_all | solution.py:173
  203.0 13.2 %all-to-all-start.2 = ((f32[16,8,320]{2,1,0:T(8,128)}), f32[16,8,320]{2,1,0:T(8,128)S(1)}, u32[]{:S(2)}, u32[]{:S(2)}) async-start(f32[16,8,320]{2,1,0:T(8,128)} %convolution_bitcast_fusion), calls=%async_computation.2 | async-start | bytes 393216 | tf_op jit(solution)/shard_map/all_to_all | solution.py:188

commit v5 on v4

--- a/solution.py
+++ b/solution.py
@@ -162,7 +162,13 @@
     fresh_flat = fresh.reshape(row_count, kv_local * channels)
     outgoing = jnp.concatenate([normed_two, fresh_flat], axis=1)
     received, outgoing = lax.optimization_barrier((received, outgoing))
-    gathered = lax.all_gather(outgoing, "req", axis=0, tiled=True)
+    gathered = lax.all_to_all(
+        jnp.broadcast_to(outgoing[None], (devices_req,) + outgoing.shape),
+        "req",
+        split_axis=0,
+        concat_axis=0,
+        tiled=True,
+    ).reshape(total_rows, outgoing.shape[1])
     normed_all = gathered[:, :width_local]
     fresh_all = gathered[:, width_local:].reshape(total_rows, kv_local, channels)
     ffn_width = w_gate.shape[1]
@@ -182,7 +188,13 @@
     hidden_part = (jax.nn.silu(summed[:, :ffn_width]) * summed[:, ffn_width:]).astype(
         jnp.bfloat16
     )
-    hidden = lax.all_gather(hidden_part, "kvh", axis=0, tiled=True)
+    hidden = lax.all_to_all(
+        jnp.broadcast_to(hidden_part[None], (devices_kvh,) + hidden_part.shape),
+        "kvh",
+        split_axis=0,
+        concat_axis=0,
+        tiled=True,
+    ).reshape(total_rows, ffn_width)
     lowered_parts = jnp.dot(hidden, w_down, preferred_element_type=jnp.float32)
     lowered = jnp.sum(
         lax.all_to_all(

time: 219 us -> 206 us (0.941)
  blocking collectives: 50.1 us -> 14 us
  waiting for transfers between devices: 85.6 us -> 99.9 us
  starting transfers between devices: 22 us -> 29.8 us
    all_gather x2 -> x0, blocking collectives: 36 us -> none  [the longest x1 23.2 us: per_device(): gathered = lax.all_gather(outgoing, 'req', axis=0, tiled=True)]
    all_to_all x0 -> x2, waiting for transfers between devices: none -> 14.5 us  [the longest x1 8.16 us: per_device(): lax.all_to_all(jnp.broadcast_to(outgoing[None], (devices_req,) + outgoing...]
    all_to_all x0 -> x2, starting transfers between devices: none -> 8.98 us  [the longest x1 5.6 us: per_device(): lax.all_to_all(jnp.broadcast_to(outgoing[None], (devices_req,) + outgoing...]
  transfers between devices with their start and end apart: 6 -> 8, of which waited for: 6 -> 8; matrix products, arithmetic and copies ran while one was open for 18% -> 19% of each run, Pallas kernels for 0% -> 0%
where the time goes in v5:
time: 206 us; the launch traced here: 205 us
  waiting for transfers between devices  99.9 us (48%)
  starting transfers between devices  29.8 us (14%)
  local copies, waits for them, and re-layouts  27.4 us (13%)
  other arithmetic  19.8 us (10%)
  blocking collectives  14 us (7%)
  matrix products  13.2 us (6%)
    all_to_all x1, waiting for transfers between devices, per_device(): lax.all_to_all(parcels, 'req', split_axis=0, concat_axis=0, tiled=True)  73.5 us
    select_n x2, other arithmetic, mask_blocks(): jnp.where(kept, blocks, jnp.where(placed, fresh[:, None, :, None, :], jnp...  15.3 us
    all_gather x1, blocking collectives, per_device(): full_states = lax.all_gather(states, 'kvh', axis=1, tiled=True)  14 us
    gather x3, local copies, waits for them, and re-layouts, per_device(): parcels = kv_pool[page_table[picked]]  9.99 us
    all_to_all x1, waiting for transfers between devices, per_device(): lax.all_to_all(jnp.broadcast_to(outgoing[None], (devices_req,) + outgoing...  8.16 us
    ppermute x3, waiting for transfers between devices, per_device(): lax.ppermute(attn_out, 'kvh', [(i, i ^ step) for i in range(devices_kvh)])  7.43 us
    all_to_all x1, starting transfers between devices, per_device(): lax.all_to_all(parcels, 'req', split_axis=0, concat_axis=0, tiled=True)  7.3 us
    all_to_all x1, waiting for transfers between devices, per_device(): lax.all_to_all(jnp.broadcast_to(hidden_part[None], (devices_kvh,) + hidde...  6.36 us
  transfers between devices with their start and end apart: 8, of which 8 were waited for; matrix products, arithmetic and copies ran while one was open for 19% of the time, Pallas kernels for 0%

profile of v5, /device:TPU:0, one launch (start us, length us, event | category | flops | bytes accessed | tf_op | source)
XLA Modules:
  0.0 205.1 jit_solution(9589806891497311579)
XLA Ops:
  0.7 0.8 compare_select_fusion.4
  1.5 1.0 scatter_custom_fusion
  3.7 1.2 gather_fusion.3
  5.3 8.7 %gather_fusion.4 = bf16[128,128,256]{2,1,0:T(8,128)(2,1)} fusion(bf16[64,128,256]{2,1,0:T(8,128)(2,1)} %bitcast.83, s32[1024]{0:T(1024)S(1)} %pad_clamp_fusion.2), kind=kCustom, calls=%fused_computation.4 | custom fusion | bytes 16777728 | tf_op jit(solution)/shard_map/gather | solution.py:112
  14.0 7.3 %all-to-all-start = ((bf16[16,8,1,128,256]{4,3,1,2,0:T(8,128)(2,1)}), bf16[16,8,1,128,256]{4,3,1,2,0:T(8,128)(2,1)}, u32[]{:S(2)}, u32[]{:S(2)}) async-start(bf16[16,8,1,128,256]{4,3,1,2,0:T(8,128)(2,1)} %bitcast.85), calls=%async_computation | async-start | bytes 16777216 | tf_op jit(solution)/shard_map/all_to_all | solution.py:113
  21.3 14.0 %all-gather = bf16[8,320,8]{1,2,0:T(8,128)(2,1)S(1)} all-gather(bf16[1,320,8]{1,2,0:T(8,128)(2,1)S(1)} %bitcast.92), channel_id=1, replica_groups=mesh['req'=16,'kvh'=8] {'kvh'}, dimensions={0}, use_global_device_ids=true | all-gather | bytes 46080 | tf_op jit(solution)/shard_map/all_gather | solution.py:117
  36.2 5.1 %gather_fusion.1 = bf16[64,128,256]{2,1,0:T(8,128)(2,1)} fusion(bf16[64,128,256]{2,1,0:T(8,128)(2,1)} %bitcast.84, s32[1024]{0:T(1024)S(1)} %pad_clamp_fusion.4), kind=kCustom, calls=%fused_computation.1 | custom fusion | bytes 8388864 | tf_op jit(solution)/shard_map/gather | solution.py:138
  41.6 2.3 %multiply_reduce_fusion.1 = (f32[8,4]{0,1:T(4,128)S(1)}, f32[8,4,128]{2,0,1:T(8,128)S(1)}) fusion(bf16[8,2560]{1,0:T(8,128)(2,1)S(1)} %fusion.19, bf16[2560,512]{1,0:T(8,128)(2,1)} %param.18), kind=kOutput, calls=%fused_computation.55 | convolution fusion | flops 20979680 | bytes 2678912 | tf_op jit(solution)/shard_map/dot_general | solution.py:121
  44.2 1.4 multiply_reduce_fusion.2
  46.3 7.6 %select_select_fusion.1 = bf16[8,1,1024,256]{3,2,0,1:T(8,128)(2,1)} fusion(bf16[8,1,1024,256]{3,2,0,1:T(8,128)(2,1)} %bitcast.87, pred[8,1024]{1,0:T(8,128)(4,1)S(1)} %get-tuple-element.17, pred[8,1024]{1,0:T(8,128)(4,1)S(1)} %get-tuple-element.16, bf16[8,256]{1,0:T(8,128)(2,1)S(1)} %maximum_bitcast_fusion), kind=kLoop, calls=%fused_computation.11 | loop fusion | flops 4194304 | bytes 8409088 | tf_op jit(solution)/shard_map/jit(_where)/select_n | solution.py:48
  54.0 2.5 %fusion.46 = (f32[8,4]{1,0:T(8,128)S(1)}, f32[8,4,1024]{2,1,0:T(4,128)S(1)}) fusion(bf16[8,1,1024,256]{3,2,0,1:T(8,128)(2,1)} %select_select_fusion.1, pred[8,1024]{1,0:T(8,128)(4,1)S(1)} %get-tuple-element.24, bf16[8,4,64]{2,1,0:T(4,128)(2,1)S(1)} %get-tuple-element.11, bf16[8,4,64]{2,1,0:T(4,128)(2,1)S(1)} %get-tuple-element.10), kind=kOutput, calls=%fused_computation.116 | convolution fusion | flops 8537087 | bytes 2244736 | tf_op jit(solution)/shard_map/sub | solution.py:67
  56.4 2.0 fusion.8
  59.3 0.9 collective-permute-done
  60.2 1.7 collective-permute-start.1
  61.9 3.1 %collective-permute-done.1 = f32[8,2560]{1,0:T(8,128)S(1)} collective-permute-done((f32[8,2560]{1,0:T(8,128)S(1)}, f32[8,2560]{1,0:T(8,128)S(1)}, u32[]{:S(2)}, u32[]{:S(2)}) %collective-permute-start.1) | collective-permute-done | bytes 81952 | tf_op jit(solution)/shard_map/ppermute | solution.py:148
  65.0 2.6 %collective-permute-start.2 = (f32[8,2560]{1,0:T(8,128)S(1)}, f32[8,2560]{1,0:T(8,128)S(1)}, u32[]{:S(2)}, u32[]{:S(2)}) collective-permute-start(f32[8,2560]{1,0:T(8,128)S(1)} %add.195), channel_id=1, source_target_pairs={{0,4},{1,5},{2,6},{3,7},{4,0},{5,1},{6,2},{7,3},{8,12},{9,13},{10,... | collective-permute-start | bytes 245768 | tf_op jit(solution)/shard_map/ppermute | solution.py:148
  67.6 3.4 %collective-permute-done.2 = f32[8,2560]{1,0:T(8,128)S(1)} collective-permute-done((f32[8,2560]{1,0:T(8,128)S(1)}, f32[8,2560]{1,0:T(8,128)S(1)}, u32[]{:S(2)}, u32[]{:S(2)}) %collective-permute-start.2) | collective-permute-done | bytes 81952 | tf_op jit(solution)/shard_map/ppermute | solution.py:148
  72.0 73.5 %all-to-all-done = bf16[16,8,1,128,256]{4,3,1,2,0:T(8,128)(2,1)} async-done(((bf16[16,8,1,128,256]{4,3,1,2,0:T(8,128)(2,1)}), bf16[16,8,1,128,256]{4,3,1,2,0:T(8,128)(2,1)}, u32[]{:S(2)}, u32[]{:S(2)}) %all-to-all-start) | async-done | bytes 8388640 | tf_op jit(solution)/shard_map/all_to_all | solution.py:113
  145.4 0.7 broadcast_in_dim.135
  146.1 5.6 %all-to-all-start.1 = ((bf16[16,8,576]{2,1,0:T(8,128)(2,1)}), bf16[16,8,576]{2,1,0:T(8,128)(2,1)S(1)}, u32[]{:S(2)}, u32[]{:S(2)}) async-start(bf16[16,8,576]{2,1,0:T(8,128)(2,1)} %broadcast_in_dim.135), calls=%async_computation.1 | async-start | bytes 327680 | tf_op jit(solution)/shard_map/all_to_all | solution.py:165
  151.7 8.2 %all-to-all-done.1 = bf16[16,8,576]{2,1,0:T(8,128)(2,1)S(1)} async-done(((bf16[16,8,576]{2,1,0:T(8,128)(2,1)}), bf16[16,8,576]{2,1,0:T(8,128)(2,1)S(1)}, u32[]{:S(2)}, u32[]{:S(2)}) %all-to-all-start.1) | async-done | bytes 147488 | tf_op jit(solution)/shard_map/all_to_all | solution.py:165
  159.9 2.4 %fusion.10 = f32[128,1216]{1,0:T(8,128)} fusion(bf16[320,608]{1,0:T(8,128)(2,1)} %param.26, bf16[320,608]{1,0:T(8,128)(2,1)} %param.25, bf16[128,576]{1,0:T(8,128)(2,1)S(1)} %bitcast.90), kind=kOutput, calls=%fused_computation.25 | convolution fusion | flops 101171200 | bytes 1499136 | tf_op jit(solution)/shard_map/dot_general | solution.py:176
  162.3 5.3 %all-to-all-start.2 = ((f32[8,16,1216]{2,1,0:T(8,128)}), f32[8,16,1216]{2,1,0:T(8,128)S(1)}, u32[]{:S(2)}, u32[]{:S(2)}) async-start(f32[8,16,1216]{2,1,0:T(8,128)} %bitcast.88), calls=%async_computation.2 | async-start | bytes 1310720 | tf_op jit(solution)/shard_map/all_to_all | solution.py:179
  168.6 6.2 %gather_fusion.6 = bf16[8,8,128,256]{3,2,1,0:T(8,128)(2,1)} fusion(bf16[16,8,128,256]{3,2,1,0:T(8,128)(2,1)} %bitcast.20, s32[1024]{0:T(1024)S(1)} %pad_clamp_fusion), kind=kCustom, calls=%fused_computation.6 | custom fusion | bytes 8388640 | tf_op jit(solution)/shard_map/gather | solution.py:211
  175.5 3.8 %all-to-all-done.2 = f32[8,16,1216]{2,1,0:T(8,128)S(1)} async-done(((f32[8,16,1216]{2,1,0:T(8,128)}), f32[8,16,1216]{2,1,0:T(8,128)S(1)}, u32[]{:S(2)}, u32[]{:S(2)}) %all-to-all-start.2) | async-done | bytes 622624 | tf_op jit(solution)/shard_map/all_to_all | solution.py:179
  180.1 3.4 %all-to-all-start.3 = ((bf16[8,16,608]{2,1,0:T(8,128)(2,1)}), bf16[8,16,608]{2,1,0:T(8,128)(2,1)S(1)}, u32[]{:S(2)}, u32[]{:S(2)}) async-start(bf16[8,16,608]{2,1,0:T(8,128)(2,1)} %broadcast_in_dim.136), calls=%async_computation.3 | async-start | bytes 327680 | tf_op jit(solution)/shard_map/all_to_all | solution.py:191
  183.5 6.4 %all-to-all-done.3 = bf16[8,16,608]{2,1,0:T(8,128)(2,1)S(1)} async-done(((bf16[8,16,608]{2,1,0:T(8,128)(2,1)}), bf16[8,16,608]{2,1,0:T(8,128)(2,1)S(1)}, u32[]{:S(2)}, u32[]{:S(2)}) %all-to-all-start.3) | async-done | bytes 155680 | tf_op jit(solution)/shard_map/all_to_all | solution.py:191
  189.9 2.0 fusion.14
  191.8 3.5 %all-to-all-start.4 = ((f32[16,8,320]{2,1,0:T(8,128)}), f32[16,8,320]{2,1,0:T(8,128)S(1)}, u32[]{:S(2)}, u32[]{:S(2)}) async-start(f32[16,8,320]{2,1,0:T(8,128)} %fusion.14), calls=%async_computation.4 | async-start | bytes 393216 | tf_op jit(solution)/shard_map/all_to_all | solution.py:200
  195.4 7.6 %select_select_fusion = bf16[64,1,128,256]{3,2,1,0:T(8,128)(2,1)} fusion(bf16[64,1,128,256]{3,2,1,0:T(8,128)(2,1)} %bitcast.86, pred[64,128]{1,0:T(8,128)(4,1)S(1)} %get-tuple-element.15, pred[64,128]{1,0:T(8,128)(4,1)S(1)} %get-tuple-element.14, bf16[64,256]{1,0:T(8,128)(2,1)S(1)} %broadcast_bitcast_fusion), kind=kLoop, calls=%fused_computation.10 | loop fusion | flops 4194304 | bytes 8437760 | tf_op jit(solution)/shard_map/jit(_where)/select_n | solution.py:48
  203.0 0.7 all-to-all-done.4
  203.7 1.4 add_convert_fusion.1
  (85 shorter events, 7.8 us)
Async XLA Ops:
  0.6 57.8 %copy-start = (bf16[512,2560]{1,0:T(8,128)(2,1)S(1)}, bf16[512,2560]{1,0:T(8,128)(2,1)}, u32[]{:S(2)}) copy-start(bf16[512,2560]{1,0:T(8,128)(2,1)} %param.23) | copy-start | bytes 7864324
  13.9 7.3 %copy-start.5 = (bf16[8,320]{1,0:T(8,128)(2,1)S(1)}, bf16[8,320]{1,0:T(8,128)(2,1)}, u32[]{:S(2)}) copy-start(bf16[8,320]{1,0:T(8,128)(2,1)} %param.16) | copy-start | bytes 15364
  13.9 21.5 %copy-start.6 = (bf16[2560]{0:T(1024)(128)(2,1)S(1)}, bf16[2560]{0:T(1024)(128)(2,1)}, u32[]{:S(2)}) copy-start(bf16[2560]{0:T(1024)(128)(2,1)} %param.17) | copy-start | bytes 15364
  13.9 21.5 %copy-start.9 = (bf16[128]{0:T(256)(128)(2,1)S(1)}, bf16[128]{0:T(256)(128)(2,1)}, u32[]{:S(2)}) copy-start(bf16[128]{0:T(256)(128)(2,1)} %param.22) | copy-start | bytes 772
  13.9 21.5 %copy-start.1 = (s32[128]{0:T(128)S(1)}, s32[128]{0:T(128)}, u32[]{:S(2)}) copy-start(s32[128]{0:T(128)} %param.29) | copy-start | bytes 1540
  13.9 22.2 %copy-start.2 = (s32[8,8]{1,0:T(8,128)S(1)}, s32[8,8]{1,0:T(8,128)}, u32[]{:S(2)}) copy-start(s32[8,8]{1,0:T(8,128)} %param.30) | copy-start | bytes 772
  14.0 131.5 %all-to-all-start = ((bf16[16,8,1,128,256]{4,3,1,2,0:T(8,128)(2,1)}), bf16[16,8,1,128,256]{4,3,1,2,0:T(8,128)(2,1)}, u32[]{:S(2)}, u32[]{:S(2)}) async-start(bf16[16,8,1,128,256]{4,3,1,2,0:T(8,128)(2,1)} %bitcast.85), calls=%async_computation | async-start | bytes 16777216 | tf_op jit(solution)/shard_map/all_to_all | solution.py:113
  36.2 7.7 %copy-start.10 = (bf16[128]{0:T(256)(128)(2,1)S(1)}, bf16[128]{0:T(256)(128)(2,1)}, u32[]{:S(2)}) copy-start(bf16[128]{0:T(256)(128)(2,1)} %param.21) | copy-start | bytes 772
  36.2 7.7 %copy-start.3 = (bf16[2560,128]{1,0:T(8,128)(2,1)S(1)}, bf16[2560,128]{1,0:T(8,128)(2,1)}, u32[]{:S(2)}) copy-start(bf16[2560,128]{1,0:T(8,128)(2,1)} %param.20) | copy-start | bytes 1966084
  54.0 13.7 %copy-start.7 = (bf16[320]{0:T(512)(128)(2,1)S(1)}, bf16[320]{0:T(512)(128)(2,1)}, u32[]{:S(2)}) copy-start(bf16[320]{0:T(512)(128)(2,1)} %param.24) | copy-start | bytes 1924
  58.5 109.1 %copy-start.8 = (s32[128]{0:T(128)S(1)}, s32[128]{0:T(128)}, u32[]{:S(2)}) copy-start(s32[128]{0:T(128)} %param.31) | copy-start | bytes 1540
  58.9 1.3 collective-permute-start
  60.2 4.8 %collective-permute-start.1 = (f32[8,2560]{1,0:T(8,128)S(1)}, f32[8,2560]{1,0:T(8,128)S(1)}, u32[]{:S(2)}, u32[]{:S(2)}) collective-permute-start(f32[8,2560]{1,0:T(8,128)S(1)} %add.194), channel_id=1, source_target_pairs={{0,2},{1,3},{2,0},{3,1},{4,6},{5,7},{6,4},{7,5},{8,10},{9,11},{10,... | collective-permute-start | bytes 245768 | tf_op jit(solution)/shard_map/ppermute | solution.py:148
  65.0 6.0 %collective-permute-start.2 = (f32[8,2560]{1,0:T(8,128)S(1)}, f32[8,2560]{1,0:T(8,128)S(1)}, u32[]{:S(2)}, u32[]{:S(2)}) collective-permute-start(f32[8,2560]{1,0:T(8,128)S(1)} %add.195), channel_id=1, source_target_pairs={{0,4},{1,5},{2,6},{3,7},{4,0},{5,1},{6,2},{7,3},{8,12},{9,13},{10,... | collective-permute-start | bytes 245768 | tf_op jit(solution)/shard_map/ppermute | solution.py:148
  71.2 0.6 copy-start.4
  146.1 13.8 %all-to-all-start.1 = ((bf16[16,8,576]{2,1,0:T(8,128)(2,1)}), bf16[16,8,576]{2,1,0:T(8,128)(2,1)S(1)}, u32[]{:S(2)}, u32[]{:S(2)}) async-start(bf16[16,8,576]{2,1,0:T(8,128)(2,1)} %broadcast_in_dim.135), calls=%async_computation.1 | async-start | bytes 327680 | tf_op jit(solution)/shard_map/all_to_all | solution.py:165
  162.3 17.0 %all-to-all-start.2 = ((f32[8,16,1216]{2,1,0:T(8,128)}), f32[8,16,1216]{2,1,0:T(8,128)S(1)}, u32[]{:S(2)}, u32[]{:S(2)}) async-start(f32[8,16,1216]{2,1,0:T(8,128)} %bitcast.88), calls=%async_computation.2 | async-start | bytes 1310720 | tf_op jit(solution)/shard_map/all_to_all | solution.py:179
  180.1 9.8 %all-to-all-start.3 = ((bf16[8,16,608]{2,1,0:T(8,128)(2,1)}), bf16[8,16,608]{2,1,0:T(8,128)(2,1)S(1)}, u32[]{:S(2)}, u32[]{:S(2)}) async-start(bf16[8,16,608]{2,1,0:T(8,128)(2,1)} %broadcast_in_dim.136), calls=%async_computation.3 | async-start | bytes 327680 | tf_op jit(solution)/shard_map/all_to_all | solution.py:191
  191.8 11.8 %all-to-all-start.4 = ((f32[16,8,320]{2,1,0:T(8,128)}), f32[16,8,320]{2,1,0:T(8,128)S(1)}, u32[]{:S(2)}, u32[]{:S(2)}) async-start(f32[16,8,320]{2,1,0:T(8,128)} %fusion.14), calls=%async_computation.4 | async-start | bytes 393216 | tf_op jit(solution)/shard_map/all_to_all | solution.py:200

commit v6 on v5

--- a/solution.py
+++ b/solution.py
@@ -3,6 +3,8 @@
 import jax
 import jax.numpy as jnp
 from jax import lax
+from jax.experimental import pallas as pl
+from jax.experimental.pallas import tpu as pltpu
 from jax.sharding import PartitionSpec as P
 
 D = 2560
@@ -50,6 +52,39 @@
         blocks,
         jnp.where(placed, fresh[:, None, :, None, :], jnp.zeros((), jnp.bfloat16)),
     )
+
+
+def pack_parcels(kv_pool, page_table, destination, slots):
+    rows, kv_local, page_len, channels = kv_pool.shape
+    reqs, pages_per = page_table.shape
+
+    def kernel(table_ref, dest_ref, pool_ref, out_ref, sems):
+        copies = []
+        for j in range(reqs):
+            for p in range(pages_per):
+                copy = pltpu.make_async_copy(
+                    pool_ref.at[table_ref[j, p]],
+                    out_ref.at[dest_ref[j], p],
+                    sems.at[j * pages_per + p],
+                )
+                copy.start()
+                copies.append(copy)
+        for copy in copies:
+            copy.wait()
+
+    return pl.pallas_call(
+        kernel,
+        out_shape=jax.ShapeDtypeStruct(
+            (slots, pages_per, kv_local, page_len, channels), kv_pool.dtype
+        ),
+        in_specs=[
+            pl.BlockSpec(memory_space=pltpu.SMEM),
+            pl.BlockSpec(memory_space=pltpu.SMEM),
+            pl.BlockSpec(memory_space=pl.ANY),
+        ],
+        out_specs=pl.BlockSpec(memory_space=pl.ANY),
+        scratch_shapes=[pltpu.SemaphoreType.DMA((reqs * pages_per,))],
+    )(page_table, destination, kv_pool)
 
 
 def attend(query, sequence, lengths_now):
@@ -102,14 +137,10 @@
     channels = 2 * head_dim
     total_rows = new_order.shape[0]
 
-    everyone = jnp.arange(total_rows, dtype=jnp.int32)
-    new_position = jnp.zeros((total_rows,), jnp.int32).at[new_order].set(everyone)
     home = my_index * row_count + jnp.arange(row_count, dtype=jnp.int32)
-    destination = new_position[home] // row_count
-    peer_ids = jnp.arange(devices_req, dtype=jnp.int32)
-    matches = destination[None, :] == peer_ids[:, None]
-    picked = jnp.argmax(matches.astype(jnp.int32), axis=1)
-    parcels = kv_pool[page_table[picked]]
+    new_slot = jnp.argmax((new_order[None, :] == home[:, None]).astype(jnp.int32), axis=1)
+    destination = (new_slot // row_count).astype(jnp.int32)
+    parcels = pack_parcels(kv_pool, page_table, destination, devices_req)
     received = lax.all_to_all(parcels, "req", split_axis=0, concat_axis=0, tiled=True)
     arriving = lax.dynamic_slice_in_dim(new_order, my_index * row_count, row_count)
     source_owner = arriving // row_count

time: 206 us -> 325 us (1.58)
  Pallas kernels: 0 us -> 129 us
  local copies, waits for them, and re-layouts: 27.4 us -> 15.7 us
    pallas_call x0 -> x1, Pallas kernels: none -> 129 us  [pack_parcels(): pl.pallas_call(kernel, out_shape=jax.ShapeDtypeStruct((slots, pages_per,...]
    gather x4 -> x0, local copies, waits for them, and re-layouts: 10.6 us -> none  [the longest x3 9.99 us: per_device(): parcels = kv_pool[page_table[picked]]]
  transfers between devices with their start and end apart: 8 -> 8, of which waited for: 8 -> 8; matrix products, arithmetic and copies ran while one was open for 19% -> 12% of each run, Pallas kernels for 0% -> 0%
where the time goes in v6:
time: 325 us; the launch traced here: 323 us
  Pallas kernels  129 us (40%)
  waiting for transfers between devices  99.9 us (31%)
  starting transfers between devices  29.8 us (9%)
  other arithmetic  20.3 us (6%)
  local copies, waits for them, and re-layouts  15.7 us (5%)
  blocking collectives  14 us (4%)
  matrix products  13.2 us (4%)
    pallas_call x1, Pallas kernels, pack_parcels(): pl.pallas_call(kernel, out_shape=jax.ShapeDtypeStruct((slots, pages_per,...  129 us
    all_to_all x1, waiting for transfers between devices, per_device(): lax.all_to_all(parcels, 'req', split_axis=0, concat_axis=0, tiled=True)  73.5 us
    select_n x2, other arithmetic, mask_blocks(): jnp.where(kept, blocks, jnp.where(placed, fresh[:, None, :, None, :], jnp...  15.3 us
    all_gather x1, blocking collectives, per_device(): full_states = lax.all_gather(states, 'kvh', axis=1, tiled=True)  14 us
    all_to_all x1, waiting for transfers between devices, per_device(): lax.all_to_all(jnp.broadcast_to(outgoing[None], (devices_req,) + outgoing...  8.16 us
    ppermute x3, waiting for transfers between devices, per_device(): lax.ppermute(attn_out, 'kvh', [(i, i ^ step) for i in range(devices_kvh)])  7.43 us
    all_to_all x1, starting transfers between devices, per_device(): lax.all_to_all(parcels, 'req', split_axis=0, concat_axis=0, tiled=True)  7.34 us
  transfers between devices with their start and end apart: 8, of which 8 were waited for; matrix products, arithmetic and copies ran while one was open for 12% of the time, Pallas kernels for 0%

profile of v6, /device:TPU:0, one launch (start us, length us, event | category | flops | bytes accessed | tf_op | source)
XLA Modules:
  0.0 323.4 jit_solution(9109982053077546093)
XLA Ops:
  0.7 1.5 iota_reduce_fusion
  2.7 129.5 %shard_map.167 = bf16[16,8,1,128,256]{4,3,2,1,0:T(8,128)(2,1)} custom-call(s32[8,8]{1,0:T(8,128)} %table_ref.1, s32[8]{0:T(128)} %and_select_fusion.1.dest_ref, bf16[64,1,128,256]{3,2,1,0:T(8,128)(2,1)} %pool_ref.1), custom_call_target="tpu_custom_call" | custom-call | tf_op jit(solution)/shard_map/pallas_call | solution.py:75
  132.2 7.3 %all-to-all-start = ((bf16[16,8,1,128,256]{4,3,2,1,0:T(8,128)(2,1)}), bf16[16,8,1,128,256]{4,3,2,1,0:T(8,128)(2,1)}, u32[]{:S(2)}, u32[]{:S(2)}) async-start(bf16[16,8,1,128,256]{4,3,2,1,0:T(8,128)(2,1)} %shard_map.167), calls=%async_computation | async-start | bytes 16777216 | tf_op jit(solution)/shard_map/all_to_all | solution.py:144
  139.6 14.0 %all-gather = bf16[8,320,8]{1,2,0:T(8,128)(2,1)S(1)} all-gather(bf16[1,320,8]{1,2,0:T(8,128)(2,1)S(1)} %bitcast.85), channel_id=1, replica_groups=mesh['req'=16,'kvh'=8] {'kvh'}, dimensions={0}, use_global_device_ids=true | all-gather | bytes 46080 | tf_op jit(solution)/shard_map/all_gather | solution.py:148
  153.8 0.6 gather_fusion
  154.8 2.3 multiply_reduce_fusion.1
  157.2 5.1 %gather_fusion.1 = bf16[64,128,256]{2,1,0:T(8,128)(2,1)} fusion(bf16[64,128,256]{2,1,0:T(8,128)(2,1)} %bitcast.78, s32[1024]{0:T(1024)S(1)} %pad_clamp_fusion.2), kind=kCustom, calls=%fused_computation.1 | custom fusion | bytes 8388864 | tf_op jit(solution)/shard_map/gather | solution.py:169
  162.5 1.4 multiply_reduce_fusion.2
  164.6 7.6 %select_select_fusion.1 = bf16[8,1,1024,256]{3,2,0,1:T(8,128)(2,1)} fusion(bf16[8,1,1024,256]{3,2,0,1:T(8,128)(2,1)} %bitcast.80, pred[8,1024]{1,0:T(8,128)(4,1)S(1)} %get-tuple-element.17, pred[8,1024]{1,0:T(8,128)(4,1)S(1)} %get-tuple-element.16, bf16[8,256]{1,0:T(8,128)(2,1)S(1)} %maximum_bitcast_fusion), kind=kLoop, calls=%fused_computation.7 | loop fusion | flops 4194304 | bytes 8409088 | tf_op jit(solution)/shard_map/jit(_where)/select_n | solution.py:50
  172.3 2.5 fusion.44
  174.7 2.0 fusion.8
  177.6 0.9 collective-permute-done
  178.5 1.7 collective-permute-start.1
  180.2 3.1 collective-permute-done.1
  183.3 2.6 collective-permute-start.2
  186.0 3.4 %collective-permute-done.2 = f32[8,2560]{1,0:T(8,128)S(1)} collective-permute-done((f32[8,2560]{1,0:T(8,128)S(1)}, f32[8,2560]{1,0:T(8,128)S(1)}, u32[]{:S(2)}, u32[]{:S(2)}) %collective-permute-start.2) | collective-permute-done | bytes 81952 | tf_op jit(solution)/shard_map/ppermute | solution.py:179
  190.3 73.5 %all-to-all-done = bf16[16,8,1,128,256]{4,3,2,1,0:T(8,128)(2,1)} async-done(((bf16[16,8,1,128,256]{4,3,2,1,0:T(8,128)(2,1)}), bf16[16,8,1,128,256]{4,3,2,1,0:T(8,128)(2,1)}, u32[]{:S(2)}, u32[]{:S(2)}) %all-to-all-start) | async-done | bytes 8388640 | tf_op jit(solution)/shard_map/all_to_all | solution.py:144
  263.7 0.7 broadcast_in_dim.125
  264.4 5.6 %all-to-all-start.1 = ((bf16[16,8,576]{2,1,0:T(8,128)(2,1)}), bf16[16,8,576]{2,1,0:T(8,128)(2,1)S(1)}, u32[]{:S(2)}, u32[]{:S(2)}) async-start(bf16[16,8,576]{2,1,0:T(8,128)(2,1)} %broadcast_in_dim.125), calls=%async_computation.1 | async-start | bytes 327680 | tf_op jit(solution)/shard_map/all_to_all | solution.py:196
  270.0 8.2 %all-to-all-done.1 = bf16[16,8,576]{2,1,0:T(8,128)(2,1)S(1)} async-done(((bf16[16,8,576]{2,1,0:T(8,128)(2,1)}), bf16[16,8,576]{2,1,0:T(8,128)(2,1)S(1)}, u32[]{:S(2)}, u32[]{:S(2)}) %all-to-all-start.1) | async-done | bytes 147488 | tf_op jit(solution)/shard_map/all_to_all | solution.py:196
  278.2 2.4 fusion.10
  280.6 5.3 %all-to-all-start.2 = ((f32[8,16,1216]{2,1,0:T(8,128)}), f32[8,16,1216]{2,1,0:T(8,128)S(1)}, u32[]{:S(2)}, u32[]{:S(2)}) async-start(f32[8,16,1216]{2,1,0:T(8,128)} %bitcast.81), calls=%async_computation.2 | async-start | bytes 1310720 | tf_op jit(solution)/shard_map/all_to_all | solution.py:210
  286.9 6.2 %gather_fusion.3 = bf16[8,8,128,256]{3,2,1,0:T(8,128)(2,1)} fusion(bf16[16,8,128,256]{3,2,1,0:T(8,128)(2,1)} %bitcast.18, s32[1024]{0:T(1024)S(1)} %pad_clamp_fusion), kind=kCustom, calls=%fused_computation.3 | custom fusion | bytes 8388640 | tf_op jit(solution)/shard_map/gather | solution.py:242
  293.8 3.8 %all-to-all-done.2 = f32[8,16,1216]{2,1,0:T(8,128)S(1)} async-done(((f32[8,16,1216]{2,1,0:T(8,128)}), f32[8,16,1216]{2,1,0:T(8,128)S(1)}, u32[]{:S(2)}, u32[]{:S(2)}) %all-to-all-start.2) | async-done | bytes 622624 | tf_op jit(solution)/shard_map/all_to_all | solution.py:210
  297.8 0.7 broadcast_in_dim.126
  298.4 3.4 %all-to-all-start.3 = ((bf16[8,16,608]{2,1,0:T(8,128)(2,1)}), bf16[8,16,608]{2,1,0:T(8,128)(2,1)S(1)}, u32[]{:S(2)}, u32[]{:S(2)}) async-start(bf16[8,16,608]{2,1,0:T(8,128)(2,1)} %broadcast_in_dim.126), calls=%async_computation.3 | async-start | bytes 327680 | tf_op jit(solution)/shard_map/all_to_all | solution.py:222
  301.8 6.4 %all-to-all-done.3 = bf16[8,16,608]{2,1,0:T(8,128)(2,1)S(1)} async-done(((bf16[8,16,608]{2,1,0:T(8,128)(2,1)}), bf16[8,16,608]{2,1,0:T(8,128)(2,1)S(1)}, u32[]{:S(2)}, u32[]{:S(2)}) %all-to-all-start.3) | async-done | bytes 155680 | tf_op jit(solution)/shard_map/all_to_all | solution.py:222
  308.2 2.0 fusion.14
  310.2 3.5 %all-to-all-start.4 = ((f32[16,8,320]{2,1,0:T(8,128)}), f32[16,8,320]{2,1,0:T(8,128)S(1)}, u32[]{:S(2)}, u32[]{:S(2)}) async-start(f32[16,8,320]{2,1,0:T(8,128)} %fusion.14), calls=%async_computation.4 | async-start | bytes 393216 | tf_op jit(solution)/shard_map/all_to_all | solution.py:231
  313.7 7.6 %select_select_fusion = bf16[64,1,128,256]{3,2,1,0:T(8,128)(2,1)} fusion(bf16[64,1,128,256]{3,2,1,0:T(8,128)(2,1)} %bitcast.79, pred[64,128]{1,0:T(8,128)(4,1)S(1)} %get-tuple-element.15, pred[64,128]{1,0:T(8,128)(4,1)S(1)} %get-tuple-element.14, bf16[64,256]{1,0:T(8,128)(2,1)S(1)} %broadcast_bitcast_fusion), kind=kLoop, calls=%fused_computation.6 | loop fusion | flops 4194304 | bytes 8437760 | tf_op jit(solution)/shard_map/jit(_where)/select_n | solution.py:50
  321.3 0.7 all-to-all-done.4
  322.0 1.4 add_convert_fusion.1
  (74 shorter events, 5.5 us)
Async XLA Ops:
  0.6 176.2 %copy-start = (bf16[512,2560]{1,0:T(8,128)(2,1)S(1)}, bf16[512,2560]{1,0:T(8,128)(2,1)}, u32[]{:S(2)}) copy-start(bf16[512,2560]{1,0:T(8,128)(2,1)} %param.23) | copy-start | bytes 7864324
  132.2 7.4 %copy-start.5 = (bf16[8,320]{1,0:T(8,128)(2,1)S(1)}, bf16[8,320]{1,0:T(8,128)(2,1)}, u32[]{:S(2)}) copy-start(bf16[8,320]{1,0:T(8,128)(2,1)} %param.16) | copy-start | bytes 15364
  132.2 21.6 %copy-start.6 = (bf16[2560]{0:T(1024)(128)(2,1)S(1)}, bf16[2560]{0:T(1024)(128)(2,1)}, u32[]{:S(2)}) copy-start(bf16[2560]{0:T(1024)(128)(2,1)} %param.17) | copy-start | bytes 15364
  132.2 21.6 %copy-start.9 = (bf16[128]{0:T(256)(128)(2,1)S(1)}, bf16[128]{0:T(256)(128)(2,1)}, u32[]{:S(2)}) copy-start(bf16[128]{0:T(256)(128)(2,1)} %param.22) | copy-start | bytes 772
  132.2 21.6 %copy-start.1 = (s32[128]{0:T(128)S(1)}, s32[128]{0:T(128)}, u32[]{:S(2)}) copy-start(s32[128]{0:T(128)} %param.29) | copy-start | bytes 1540
  132.2 22.3 %copy-start.4 = (s32[8,8]{1,0:T(8,128)S(1)}, s32[8,8]{1,0:T(8,128)}, u32[]{:S(2)}) copy-start(s32[8,8]{1,0:T(8,128)} %table_ref.1) | copy-start | bytes 772
  132.2 24.9 %copy-start.10 = (bf16[128]{0:T(256)(128)(2,1)S(1)}, bf16[128]{0:T(256)(128)(2,1)}, u32[]{:S(2)}) copy-start(bf16[128]{0:T(256)(128)(2,1)} %param.21) | copy-start | bytes 772
  132.2 131.5 %all-to-all-start = ((bf16[16,8,1,128,256]{4,3,2,1,0:T(8,128)(2,1)}), bf16[16,8,1,128,256]{4,3,2,1,0:T(8,128)(2,1)}, u32[]{:S(2)}, u32[]{:S(2)}) async-start(bf16[16,8,1,128,256]{4,3,2,1,0:T(8,128)(2,1)} %shard_map.167), calls=%async_computation | async-start | bytes 16777216 | tf_op jit(solution)/shard_map/all_to_all | solution.py:144
  157.2 5.1 %copy-start.2 = (bf16[2560,128]{1,0:T(8,128)(2,1)S(1)}, bf16[2560,128]{1,0:T(8,128)(2,1)}, u32[]{:S(2)}) copy-start(bf16[2560,128]{1,0:T(8,128)(2,1)} %param.20) | copy-start | bytes 1966084
  172.3 13.7 %copy-start.8 = (bf16[320]{0:T(512)(128)(2,1)S(1)}, bf16[320]{0:T(512)(128)(2,1)}, u32[]{:S(2)}) copy-start(bf16[320]{0:T(512)(128)(2,1)} %param.24) | copy-start | bytes 1924
  176.8 109.1 %copy-start.7 = (s32[128]{0:T(128)S(1)}, s32[128]{0:T(128)}, u32[]{:S(2)}) copy-start(s32[128]{0:T(128)} %param.31) | copy-start | bytes 1540
  177.2 1.3 collective-permute-start
  178.5 4.8 %collective-permute-start.1 = (f32[8,2560]{1,0:T(8,128)S(1)}, f32[8,2560]{1,0:T(8,128)S(1)}, u32[]{:S(2)}, u32[]{:S(2)}) collective-permute-start(f32[8,2560]{1,0:T(8,128)S(1)} %add.174), channel_id=1, source_target_pairs={{0,2},{1,3},{2,0},{3,1},{4,6},{5,7},{6,4},{7,5},{8,10},{9,11},{10,... | collective-permute-start | bytes 245768 | tf_op jit(solution)/shard_map/ppermute | solution.py:179
  183.3 6.0 %collective-permute-start.2 = (f32[8,2560]{1,0:T(8,128)S(1)}, f32[8,2560]{1,0:T(8,128)S(1)}, u32[]{:S(2)}, u32[]{:S(2)}) collective-permute-start(f32[8,2560]{1,0:T(8,128)S(1)} %add.175), channel_id=1, source_target_pairs={{0,4},{1,5},{2,6},{3,7},{4,0},{5,1},{6,2},{7,3},{8,12},{9,13},{10,... | collective-permute-start | bytes 245768 | tf_op jit(solution)/shard_map/ppermute | solution.py:179
  189.5 0.6 copy-start.3
  264.4 13.8 %all-to-all-start.1 = ((bf16[16,8,576]{2,1,0:T(8,128)(2,1)}), bf16[16,8,576]{2,1,0:T(8,128)(2,1)S(1)}, u32[]{:S(2)}, u32[]{:S(2)}) async-start(bf16[16,8,576]{2,1,0:T(8,128)(2,1)} %broadcast_in_dim.125), calls=%async_computation.1 | async-start | bytes 327680 | tf_op jit(solution)/shard_map/all_to_all | solution.py:196
  280.6 17.0 %all-to-all-start.2 = ((f32[8,16,1216]{2,1,0:T(8,128)}), f32[8,16,1216]{2,1,0:T(8,128)S(1)}, u32[]{:S(2)}, u32[]{:S(2)}) async-start(f32[8,16,1216]{2,1,0:T(8,128)} %bitcast.81), calls=%async_computation.2 | async-start | bytes 1310720 | tf_op jit(solution)/shard_map/all_to_all | solution.py:210
  298.4 9.8 %all-to-all-start.3 = ((bf16[8,16,608]{2,1,0:T(8,128)(2,1)}), bf16[8,16,608]{2,1,0:T(8,128)(2,1)S(1)}, u32[]{:S(2)}, u32[]{:S(2)}) async-start(bf16[8,16,608]{2,1,0:T(8,128)(2,1)} %broadcast_in_dim.126), calls=%async_computation.3 | async-start | bytes 327680 | tf_op jit(solution)/shard_map/all_to_all | solution.py:222
  310.2 11.8 %all-to-all-start.4 = ((f32[16,8,320]{2,1,0:T(8,128)}), f32[16,8,320]{2,1,0:T(8,128)S(1)}, u32[]{:S(2)}, u32[]{:S(2)}) async-start(f32[16,8,320]{2,1,0:T(8,128)} %fusion.14), calls=%async_computation.4 | async-start | bytes 393216 | tf_op jit(solution)/shard_map/all_to_all | solution.py:231

commit v7 on v5

--- a/solution.py
+++ b/solution.py
@@ -102,15 +102,21 @@
     channels = 2 * head_dim
     total_rows = new_order.shape[0]
 
-    everyone = jnp.arange(total_rows, dtype=jnp.int32)
-    new_position = jnp.zeros((total_rows,), jnp.int32).at[new_order].set(everyone)
     home = my_index * row_count + jnp.arange(row_count, dtype=jnp.int32)
-    destination = new_position[home] // row_count
+    new_slot = jnp.argmax((new_order[None, :] == home[:, None]).astype(jnp.int32), axis=1)
+    destination = new_slot // row_count
     peer_ids = jnp.arange(devices_req, dtype=jnp.int32)
     matches = destination[None, :] == peer_ids[:, None]
     picked = jnp.argmax(matches.astype(jnp.int32), axis=1)
-    parcels = kv_pool[page_table[picked]]
-    received = lax.all_to_all(parcels, "req", split_axis=0, concat_axis=0, tiled=True)
+    picked_pages = page_table[picked]
+    first_pages = pages_per // 2
+    parcels_first = kv_pool[picked_pages[:, :first_pages]]
+    received_first = lax.all_to_all(
+        parcels_first, "req", split_axis=0, concat_axis=0, tiled=True
+    )
+    parcels_second = kv_pool[picked_pages[:, first_pages:]]
+    page_block = kv_local * page_len * channels
+    second_pages_flat = (pages_per - first_pages) * page_block
     arriving = lax.dynamic_slice_in_dim(new_order, my_index * row_count, row_count)
     source_owner = arriving // row_count
 
@@ -161,14 +167,36 @@
 
     fresh_flat = fresh.reshape(row_count, kv_local * channels)
     outgoing = jnp.concatenate([normed_two, fresh_flat], axis=1)
-    received, outgoing = lax.optimization_barrier((received, outgoing))
-    gathered = lax.all_to_all(
-        jnp.broadcast_to(outgoing[None], (devices_req,) + outgoing.shape),
-        "req",
-        split_axis=0,
-        concat_axis=0,
-        tiled=True,
-    ).reshape(total_rows, outgoing.shape[1])
+    outgoing_width = outgoing.shape[1]
+    second_buffer = jnp.concatenate(
+        [
+            parcels_second.reshape(devices_req, second_pages_flat),
+            jnp.zeros((devices_req, row_count * outgoing_width), jnp.bfloat16),
+        ],
+        axis=1,
+    )
+    received_first, second_buffer = lax.optimization_barrier((received_first, second_buffer))
+    second_buffer = lax.dynamic_update_slice(
+        second_buffer,
+        jnp.broadcast_to(
+            outgoing.reshape(1, row_count * outgoing_width),
+            (devices_req, row_count * outgoing_width),
+        ),
+        (0, second_pages_flat),
+    )
+    received_second = lax.all_to_all(
+        second_buffer, "req", split_axis=0, concat_axis=0, tiled=True
+    )
+    gathered = received_second[:, second_pages_flat:].reshape(total_rows, outgoing_width)
+    received = jnp.concatenate(
+        [
+            received_first,
+            received_second[:, :second_pages_flat].reshape(
+                (devices_req, pages_per - first_pages) + parcels_second.shape[2:]
+            ),
+        ],
+        axis=1,
+    )
     normed_all = gathered[:, :width_local]
     fresh_all = gathered[:, width_local:].reshape(total_rows, kv_local, channels)
     ffn_width = w_gate.shape[1]

time: 206 us -> 235 us (1.14)
  local copies, waits for them, and re-layouts: 27.4 us -> 66.6 us
  waiting for transfers between devices: 99.9 us -> 76.5 us
  other arithmetic: 19.8 us -> 34.5 us
    unnamed x22 -> x32, local copies, waits for them, and re-layouts: 0.67 us -> 28.4 us
    all_to_all x2, waiting for transfers between devices: 81.6 us -> 65.6 us  [the longest x1 62.6 us: per_device(): lax.all_to_all(second_buffer, 'req', split_axis=0, concat_axis=0, tiled=T...]
    concatenate x0 -> x1, other arithmetic: none -> 7.41 us  [per_device(): jnp.concatenate([received_first, received_second[:, :second_pages_flat].r...]
    dynamic_update_slice x0 -> x1, other arithmetic: none -> 6.52 us  [per_device(): lax.dynamic_update_slice(second_buffer, jnp.broadcast_to(outgoing.reshape...]
    reshape x0 -> x2, local copies, waits for them, and re-layouts: none -> 4.99 us  [the longest x1 4.84 us: per_device(): parcels_second.reshape(devices_req, second_pages_flat)]
    all_to_all x1, waiting for transfers between devices: 3.84 us -> 0.01 us  [per_device(): lax.all_to_all(partial_both.reshape(devices_kvh, group_rows, 2 * ffn_widt...]
    concatenate x0 -> x1, local copies, waits for them, and re-layouts: none -> 3.75 us  [per_device(): jnp.concatenate([parcels_second.reshape(devices_req, second_pages_flat),...]
    ppermute x3, waiting for transfers between devices: 7.43 us -> 3.96 us  [per_device(): lax.ppermute(attn_out, 'kvh', [(i, i ^ step) for i in range(devices_kvh)])]
  transfers between devices with their start and end apart: 8 -> 8, of which waited for: 8 -> 6; matrix products, arithmetic and copies ran while one was open for 19% -> 28% of each run, Pallas kernels for 0% -> 0%
where the time goes in v7:
time: 235 us; the launch traced here: 234 us
  waiting for transfers between devices  76.5 us (33%)
  local copies, waits for them, and re-layouts  66.6 us (28%)
  other arithmetic  34.5 us (15%)
  starting transfers between devices  30.2 us (13%)
  blocking collectives  14 us (6%)
  matrix products  11.1 us (5%)
    all_to_all x1, waiting for transfers between devices, per_device(): lax.all_to_all(second_buffer, 'req', split_axis=0, concat_axis=0, tiled=T...  62.6 us
    unnamed x32, local copies, waits for them, and re-layouts  28.4 us
    select_n x2, other arithmetic, mask_blocks(): jnp.where(kept, blocks, jnp.where(placed, fresh[:, None, :, None, :], jnp...  15.4 us
    all_gather x1, blocking collectives, per_device(): full_states = lax.all_gather(states, 'kvh', axis=1, tiled=True)  14 us
    concatenate x1, other arithmetic, per_device(): jnp.concatenate([received_first, received_second[:, :second_pages_flat].r...  7.41 us
    all_to_all x1, starting transfers between devices, per_device(): lax.all_to_all(parcels_first, 'req', split_axis=0, concat_axis=0, tiled=T...  7.34 us
    dynamic_update_slice x1, other arithmetic, per_device(): lax.dynamic_update_slice(second_buffer, jnp.broadcast_to(outgoing.reshape...  6.52 us
    all_to_all x1, waiting for transfers between devices, per_device(): lax.all_to_all(jnp.broadcast_to(hidden_part[None], (devices_kvh,) + hidde...  6.44 us
  transfers between devices with their start and end apart: 8, of which 6 were waited for; matrix products, arithmetic and copies ran while one was open for 28% of the time, Pallas kernels for 0%

profile of v7, /device:TPU:0, one launch (start us, length us, event | category | flops | bytes accessed | tf_op | source)
XLA Modules:
  0.0 234.0 jit_solution(8167310871446195642)
XLA Ops:
  0.7 1.5 iota_reduce_fusion.1
  4.9 5.0 %gather_fusion.3 = bf16[64,128,256]{2,1,0:T(8,128)(2,1)} fusion(bf16[64,128,256]{2,1,0:T(8,128)(2,1)} %bitcast.89, s32[1024]{0:T(1024)S(1)} %pad_clamp_fusion.3), kind=kCustom, calls=%fused_computation.3 | custom fusion | bytes 8388864 | tf_op jit(solution)/shard_map/gather | solution.py:113
  10.0 7.3 %all-to-all-start = ((bf16[16,4,1,128,256]{4,3,1,2,0:T(8,128)(2,1)}), bf16[16,4,1,128,256]{4,3,1,2,0:T(8,128)(2,1)}, u32[]{:S(2)}, u32[]{:S(2)}) async-start(bf16[16,4,1,128,256]{4,3,1,2,0:T(8,128)(2,1)} %bitcast.95), calls=%async_computation | async-start | bytes 8388608 | tf_op jit(solution)/shard_map/all_to_all | solution.py:114
  17.4 14.0 %all-gather = bf16[8,320,8]{1,2,0:T(8,128)(2,1)S(1)} all-gather(bf16[1,320,8]{1,2,0:T(8,128)(2,1)S(1)} %bitcast.101), channel_id=1, replica_groups=mesh['req'=16,'kvh'=8] {'kvh'}, dimensions={0}, use_global_device_ids=true | all-gather | bytes 46080 | tf_op jit(solution)/shard_map/all_gather | solution.py:123
  34.2 5.0 %gather_fusion.1 = bf16[64,128,256]{2,1,0:T(8,128)(2,1)} fusion(bf16[64,128,256]{2,1,0:T(8,128)(2,1)} %bitcast.90, s32[1024]{0:T(1024)S(1)} %pad_clamp_fusion.5), kind=kCustom, calls=%fused_computation.1 | custom fusion | bytes 8388864 | tf_op jit(solution)/shard_map/gather | solution.py:144
  39.2 2.3 multiply_reduce_fusion.1
  42.3 7.6 %select_select_fusion.1 = bf16[8,1,1024,256]{3,2,0,1:T(8,128)(2,1)} fusion(bf16[8,1,1024,256]{3,2,0,1:T(8,128)(2,1)} %bitcast.98, pred[8,1024]{1,0:T(8,128)(4,1)S(1)} %get-tuple-element.21, pred[8,1024]{1,0:T(8,128)(4,1)S(1)} %get-tuple-element.20, bf16[8,256]{1,0:T(8,128)(2,1)S(1)} %maximum_bitcast_fusion.1), kind=kLoop, calls=%fused_computation.12 | loop fusion | flops 4194304 | bytes 8409088 | tf_op jit(solution)/shard_map/jit(_where)/select_n | solution.py:48
  49.9 2.5 %fusion.44 = (f32[8,4]{1,0:T(8,128)S(1)}, f32[8,4,1024]{2,1,0:T(4,128)S(1)}) fusion(bf16[8,1,1024,256]{3,2,0,1:T(8,128)(2,1)} %select_select_fusion.1, pred[8,1024]{1,0:T(8,128)(4,1)S(1)} %get-tuple-element.28, bf16[8,4,64]{2,1,0:T(4,128)(2,1)S(1)} %get-tuple-element.13, bf16[8,4,64]{2,1,0:T(4,128)(2,1)S(1)} %get-tuple-element.12), kind=kOutput, calls=%fused_computation.119 | convolution fusion | flops 8537087 | bytes 2244736 | tf_op jit(solution)/shard_map/sub | solution.py:67
  52.4 2.0 fusion.8
  56.2 1.7 collective-permute-start.1
  57.9 3.0 %collective-permute-done.1 = f32[8,2560]{1,0:T(8,128)S(1)} collective-permute-done((f32[8,2560]{1,0:T(8,128)S(1)}, f32[8,2560]{1,0:T(8,128)S(1)}, u32[]{:S(2)}, u32[]{:S(2)}) %collective-permute-start.1) | collective-permute-done | bytes 81952 | tf_op jit(solution)/shard_map/ppermute | solution.py:154
  61.0 2.6 %collective-permute-start.2 = (f32[8,2560]{1,0:T(8,128)S(1)}, f32[8,2560]{1,0:T(8,128)S(1)}, u32[]{:S(2)}, u32[]{:S(2)}) collective-permute-start(f32[8,2560]{1,0:T(8,128)S(1)} %add.186), channel_id=1, source_target_pairs={{0,4},{1,5},{2,6},{3,7},{4,0},{5,1},{6,2},{7,3},{8,12},{9,13},{10,... | collective-permute-start | bytes 245768 | tf_op jit(solution)/shard_map/ppermute | solution.py:154
  63.6 5.0 %gather_fusion.4 = bf16[64,128,256]{2,1,0:T(8,128)(2,1)} fusion(bf16[64,128,256]{2,1,0:T(8,128)(2,1)} %bitcast.91, s32[1024]{0:T(1024)S(1)} %pad_clamp_fusion.2), kind=kCustom, calls=%fused_computation.4 | custom fusion | bytes 8388864 | tf_op jit(solution)/shard_map/gather | solution.py:117
  68.6 4.8 %reshape.417 = bf16[16,131072]{1,0:T(8,128)(2,1)} reshape(bf16[64,128,256]{2,1,0:T(8,128)(2,1)} %gather_fusion.4) | data formatting | bytes 8388608 | tf_op jit(solution)/shard_map/reshape | solution.py:173
  73.5 3.8 %concatenate.34 = bf16[16,135680]{1,0:T(8,128)(2,1)} pad(bf16[16,131072]{1,0:T(8,128)(2,1)} %reshape.417, bf16[]{:T(256)} %constant.78.clone.1), padding=0_0x0_4608 | pad | bytes 8536066 | tf_op jit(solution)/shard_map/concatenate | solution.py:171
  77.6 3.0 %all-to-all-done = bf16[16,4,1,128,256]{4,3,1,2,0:T(8,128)(2,1)} async-done(((bf16[16,4,1,128,256]{4,3,1,2,0:T(8,128)(2,1)}), bf16[16,4,1,128,256]{4,3,1,2,0:T(8,128)(2,1)}, u32[]{:S(2)}, u32[]{:S(2)}) %all-to-all-start) | async-done | bytes 4194336 | tf_op jit(solution)/shard_map/all_to_all | solution.py:114
  81.8 6.5 %reduce.44 = bf16[16,135680]{1,0:T(8,128)(2,1)} reduce(bf16[16,1,135680]{2,0,1:T(8,128)(2,1)} %broadcast_dynamic-update-slice_fusion, bf16[]{:T(256)} %broadcast.450), dimensions={1}, to_apply=%copy.38.reduce_sub_computation | reduce | bytes 8683522 | tf_op jit(solution)/shard_map/dynamic_update_slice | solution.py:179
  88.3 4.1 %reshape.518 = bf16[16,2,67840]{2,1,0:T(2,128)(2,1)} reshape(bf16[16,135680]{1,0:T(8,128)(2,1)} %reduce.44) | data formatting | bytes 8683520
  92.4 4.7 %all-to-all-start.1 = ((bf16[16,2,67840]{2,1,0:T(2,128)(2,1)}), bf16[16,2,67840]{2,1,0:T(2,128)(2,1)}, u32[]{:S(2)}, u32[]{:S(2)}) async-start(bf16[16,2,67840]{2,1,0:T(2,128)(2,1)} %reshape.518), calls=%async_computation.1 | async-start | bytes 8683520 | tf_op jit(solution)/shard_map/all_to_all | solution.py:187
  98.1 62.6 %all-to-all-done.1 = bf16[16,2,67840]{2,1,0:T(2,128)(2,1)} async-done(((bf16[16,2,67840]{2,1,0:T(2,128)(2,1)}), bf16[16,2,67840]{2,1,0:T(2,128)(2,1)}, u32[]{:S(2)}, u32[]{:S(2)}) %all-to-all-start.1) | async-done | bytes 4341792 | tf_op jit(solution)/shard_map/all_to_all | solution.py:187
  160.7 14.5 %reshape.519 = bf16[16,1,135680]{2,1,0:T(2,128)(2,1)} reshape(bf16[16,2,67840]{2,1,0:T(2,128)(2,1)} %all-to-all-done.1) | data formatting | bytes 8683520
  175.2 4.7 %copy.54 = bf16[16,1,135680]{2,0,1:T(8,128)(2,1)S(1)} copy(bf16[16,1,135680]{2,1,0:T(2,128)(2,1)} %reshape.519) | data formatting | bytes 8683520
  180.0 2.0 copy-done.3
  183.4 4.4 %all-to-all-start.2 = ((f32[8,16,1216]{2,1,0:T(8,128)}), f32[8,16,1216]{2,1,0:T(8,128)S(1)}, u32[]{:S(2)}, u32[]{:S(2)}) async-start(f32[8,16,1216]{2,1,0:T(8,128)} %bitcast.15), calls=%async_computation.2 | async-start | bytes 1310720 | tf_op jit(solution)/shard_map/all_to_all | solution.py:207
  187.9 2.5 %slice.82 = bf16[16,131072]{1,0:T(8,128)(2,1)S(1)} slice(bf16[16,135680]{1,0:T(8,128)(2,1)} %bitcast.93), slice={[0:16], [0:131072]} | slice | bytes 8388608 | tf_op jit(solution)/shard_map/slice | solution.py:194
  190.4 3.0 %copy.45 = bf16[2,8,512,256]{3,2,1,0:T(8,128)(2,1)} copy(bf16[2,8,512,256]{3,1,2,0:T(8,128)(2,1)S(1)} %bitcast.97) | data formatting | bytes 8388608
  193.9 7.4 %maximum_bitcast_fusion = bf16[16,8,128,256]{3,2,1,0:T(8,128)(2,1)} fusion(bf16[16,4,1,128,256]{4,3,1,2,0:T(8,128)(2,1)} %bitcast.99, bf16[16,4,1,128,256]{4,3,1,2,0:T(8,128)(2,1)} %all-to-all-done), kind=kLoop, calls=%fused_computation.9 | loop fusion | flops 4194304 | bytes 16777216 | tf_op jit(solution)/shard_map/concatenate | solution.py:191
  201.4 6.3 %gather_fusion.6 = bf16[8,8,128,256]{3,2,1,0:T(8,128)(2,1)} fusion(bf16[16,8,128,256]{3,2,1,0:T(8,128)(2,1)} %maximum_bitcast_fusion, s32[1024]{0:T(1024)S(1)} %pad_clamp_fusion), kind=kCustom, calls=%fused_computation.6 | custom fusion | bytes 8388640 | tf_op jit(solution)/shard_map/gather | solution.py:239
  208.4 4.8 %all-to-all-start.3 = ((bf16[8,16,608]{2,1,0:T(8,128)(2,1)}), bf16[8,16,608]{2,1,0:T(8,128)(2,1)S(1)}, u32[]{:S(2)}, u32[]{:S(2)}) async-start(bf16[8,16,608]{2,1,0:T(8,128)(2,1)} %broadcast_in_dim.140), calls=%async_computation.3 | async-start | bytes 327680 | tf_op jit(solution)/shard_map/all_to_all | solution.py:219
  213.2 6.4 %all-to-all-done.3 = bf16[8,16,608]{2,1,0:T(8,128)(2,1)S(1)} async-done(((bf16[8,16,608]{2,1,0:T(8,128)(2,1)}), bf16[8,16,608]{2,1,0:T(8,128)(2,1)S(1)}, u32[]{:S(2)}, u32[]{:S(2)}) %all-to-all-start.3) | async-done | bytes 155680 | tf_op jit(solution)/shard_map/all_to_all | solution.py:219
  220.6 4.3 %all-to-all-start.4 = ((f32[16,8,320]{2,1,0:T(8,128)}), f32[16,8,320]{2,1,0:T(8,128)S(1)}, u32[]{:S(2)}, u32[]{:S(2)}) async-start(f32[16,8,320]{2,1,0:T(8,128)} %fusion.14), calls=%async_computation.4 | async-start | bytes 393216 | tf_op jit(solution)/shard_map/all_to_all | solution.py:228
  224.9 7.8 %select_select_fusion = bf16[64,1,128,256]{3,2,1,0:T(8,128)(2,1)} fusion(bf16[64,1,128,256]{3,2,1,0:T(8,128)(2,1)} %bitcast.96, pred[64,128]{1,0:T(8,128)(4,1)S(1)} %get-tuple-element.19, pred[64,128]{1,0:T(8,128)(4,1)S(1)} %get-tuple-element.18, bf16[64,256]{1,0:T(8,128)(2,1)S(1)} %broadcast_bitcast_fusion), kind=kLoop, calls=%fused_computation.11 | loop fusion | flops 4194304 | bytes 8437760 | tf_op jit(solution)/shard_map/jit(_where)/select_n | solution.py:48
  (102 shorter events, 15.8 us)
Async XLA Ops:
  0.6 53.8 %copy-start = (bf16[512,2560]{1,0:T(8,128)(2,1)S(1)}, bf16[512,2560]{1,0:T(8,128)(2,1)}, u32[]{:S(2)}) copy-start(bf16[512,2560]{1,0:T(8,128)(2,1)} %param.23) | copy-start | bytes 7864324
  9.9 7.4 %copy-start.4 = (s32[8,8]{1,0:T(8,128)S(1)}, s32[8,8]{1,0:T(8,128)}, u32[]{:S(2)}) copy-start(s32[8,8]{1,0:T(8,128)} %param.30) | copy-start | bytes 772
  9.9 7.4 %copy-start.7 = (bf16[8,320]{1,0:T(8,128)(2,1)S(1)}, bf16[8,320]{1,0:T(8,128)(2,1)}, u32[]{:S(2)}) copy-start(bf16[8,320]{1,0:T(8,128)(2,1)} %param.16) | copy-start | bytes 15364
  9.9 21.6 %copy-start.8 = (bf16[2560]{0:T(1024)(128)(2,1)S(1)}, bf16[2560]{0:T(1024)(128)(2,1)}, u32[]{:S(2)}) copy-start(bf16[2560]{0:T(1024)(128)(2,1)} %param.17) | copy-start | bytes 15364
  9.9 21.8 %copy-start.5 = (bf16[2560,128]{1,0:T(8,128)(2,1)S(1)}, bf16[2560,128]{1,0:T(8,128)(2,1)}, u32[]{:S(2)}) copy-start(bf16[2560,128]{1,0:T(8,128)(2,1)} %param.20) | copy-start | bytes 1966084
  9.9 23.4 %copy-start.12 = (bf16[128]{0:T(256)(128)(2,1)S(1)}, bf16[128]{0:T(256)(128)(2,1)}, u32[]{:S(2)}) copy-start(bf16[128]{0:T(256)(128)(2,1)} %param.22) | copy-start | bytes 772
  10.0 23.5 %copy-start.2 = (s32[128]{0:T(128)S(1)}, s32[128]{0:T(128)}, u32[]{:S(2)}) copy-start(s32[128]{0:T(128)} %param.29) | copy-start | bytes 1540
  10.0 70.6 %all-to-all-start = ((bf16[16,4,1,128,256]{4,3,1,2,0:T(8,128)(2,1)}), bf16[16,4,1,128,256]{4,3,1,2,0:T(8,128)(2,1)}, u32[]{:S(2)}, u32[]{:S(2)}) async-start(bf16[16,4,1,128,256]{4,3,1,2,0:T(8,128)(2,1)} %bitcast.95), calls=%async_computation | async-start | bytes 8388608 | tf_op jit(solution)/shard_map/all_to_all | solution.py:114
  34.2 7.3 %copy-start.13 = (bf16[128]{0:T(256)(128)(2,1)S(1)}, bf16[128]{0:T(256)(128)(2,1)}, u32[]{:S(2)}) copy-start(bf16[128]{0:T(256)(128)(2,1)} %param.21) | copy-start | bytes 772
  54.9 1.3 collective-permute-start
  56.2 4.8 %collective-permute-start.1 = (f32[8,2560]{1,0:T(8,128)S(1)}, f32[8,2560]{1,0:T(8,128)S(1)}, u32[]{:S(2)}, u32[]{:S(2)}) collective-permute-start(f32[8,2560]{1,0:T(8,128)S(1)} %add.185), channel_id=1, source_target_pairs={{0,2},{1,3},{2,0},{3,1},{4,6},{5,7},{6,4},{7,5},{8,10},{9,11},{10,... | collective-permute-start | bytes 245768 | tf_op jit(solution)/shard_map/ppermute | solution.py:154
  61.0 16.3 %collective-permute-start.2 = (f32[8,2560]{1,0:T(8,128)S(1)}, f32[8,2560]{1,0:T(8,128)S(1)}, u32[]{:S(2)}, u32[]{:S(2)}) collective-permute-start(f32[8,2560]{1,0:T(8,128)S(1)} %add.186), channel_id=1, source_target_pairs={{0,4},{1,5},{2,6},{3,7},{4,0},{5,1},{6,2},{7,3},{8,12},{9,13},{10,... | collective-permute-start | bytes 245768 | tf_op jit(solution)/shard_map/ppermute | solution.py:154
  68.6 4.8 %copy-start.9 = (bf16[320]{0:T(512)(128)(2,1)S(1)}, bf16[320]{0:T(512)(128)(2,1)}, u32[]{:S(2)}) copy-start(bf16[320]{0:T(512)(128)(2,1)} %param.24) | copy-start | bytes 1924
  92.4 68.3 %all-to-all-start.1 = ((bf16[16,2,67840]{2,1,0:T(2,128)(2,1)}), bf16[16,2,67840]{2,1,0:T(2,128)(2,1)}, u32[]{:S(2)}, u32[]{:S(2)}) async-start(bf16[16,2,67840]{2,1,0:T(2,128)(2,1)} %reshape.518), calls=%async_computation.1 | async-start | bytes 8683520 | tf_op jit(solution)/shard_map/all_to_all | solution.py:187
  175.2 6.9 %copy-start.10 = (bf16[320,608]{1,0:T(8,128)(2,1)S(1)}, bf16[320,608]{1,0:T(8,128)(2,1)}, u32[]{:S(2)}) copy-start(bf16[320,608]{1,0:T(8,128)(2,1)} %param.26) | copy-start | bytes 1167364
  175.2 6.9 %copy-start.11 = (bf16[320,608]{1,0:T(8,128)(2,1)S(1)}, bf16[320,608]{1,0:T(8,128)(2,1)}, u32[]{:S(2)}) copy-start(bf16[320,608]{1,0:T(8,128)(2,1)} %param.25) | copy-start | bytes 1167364
  179.9 2.0 copy-start.3
  183.4 24.2 %all-to-all-start.2 = ((f32[8,16,1216]{2,1,0:T(8,128)}), f32[8,16,1216]{2,1,0:T(8,128)S(1)}, u32[]{:S(2)}, u32[]{:S(2)}) async-start(f32[8,16,1216]{2,1,0:T(8,128)} %bitcast.15), calls=%async_computation.2 | async-start | bytes 1310720 | tf_op jit(solution)/shard_map/all_to_all | solution.py:207
  201.4 18.3 %copy-start.6 = (bf16[608,320]{0,1:T(8,128)(2,1)S(1)}, bf16[608,320]{0,1:T(8,128)(2,1)}, u32[]{:S(2)}) copy-start(bf16[608,320]{0,1:T(8,128)(2,1)} %param.27) | copy-start | bytes 1167364
  208.4 11.3 %all-to-all-start.3 = ((bf16[8,16,608]{2,1,0:T(8,128)(2,1)}), bf16[8,16,608]{2,1,0:T(8,128)(2,1)S(1)}, u32[]{:S(2)}, u32[]{:S(2)}) async-start(bf16[8,16,608]{2,1,0:T(8,128)(2,1)} %broadcast_in_dim.140), calls=%async_computation.3 | async-start | bytes 327680 | tf_op jit(solution)/shard_map/all_to_all | solution.py:219
  220.6 12.6 %all-to-all-start.4 = ((f32[16,8,320]{2,1,0:T(8,128)}), f32[16,8,320]{2,1,0:T(8,128)S(1)}, u32[]{:S(2)}, u32[]{:S(2)}) async-start(f32[16,8,320]{2,1,0:T(8,128)} %fusion.14), calls=%async_computation.4 | async-start | bytes 393216 | tf_op jit(solution)/shard_map/all_to_all | solution.py:228
  224.9 9.0 %copy-start.1 = (bf16[512,2560]{1,0:T(8,128)(2,1)S(1)}, bf16[512,2560]{1,0:T(8,128)(2,1)}, u32[]{:S(2)}) copy-start(bf16[512,2560]{1,0:T(8,128)(2,1)} %param.23) | copy-start | bytes 7864324

commit v8 on v7

--- a/solution.py
+++ b/solution.py
@@ -35,10 +35,10 @@
     )
 
 
-def mask_blocks(blocks, lengths_now, fresh):
+def mask_blocks(blocks, lengths_now, fresh, first_page=0):
     row_count, pages_per, kv_local, page_len, channels = blocks.shape
     positions = (
-        jnp.arange(pages_per, dtype=jnp.int32)[:, None] * page_len
+        (first_page + jnp.arange(pages_per, dtype=jnp.int32))[:, None] * page_len
         + jnp.arange(page_len, dtype=jnp.int32)[None, :]
     )
     positions = positions[None, :, None, :, None]
@@ -110,13 +110,15 @@
     picked = jnp.argmax(matches.astype(jnp.int32), axis=1)
     picked_pages = page_table[picked]
     first_pages = pages_per // 2
+    second_pages = pages_per - first_pages
     parcels_first = kv_pool[picked_pages[:, :first_pages]]
     received_first = lax.all_to_all(
         parcels_first, "req", split_axis=0, concat_axis=0, tiled=True
     )
-    parcels_second = kv_pool[picked_pages[:, first_pages:]]
-    page_block = kv_local * page_len * channels
-    second_pages_flat = (pages_per - first_pages) * page_block
+    second_span = second_pages * page_len
+    parcels_second = kv_pool[picked_pages[:, first_pages:]].reshape(
+        devices_req, second_span, channels
+    )
     arriving = lax.dynamic_slice_in_dim(new_order, my_index * row_count, row_count)
     source_owner = arriving // row_count
 
@@ -168,34 +170,29 @@
     fresh_flat = fresh.reshape(row_count, kv_local * channels)
     outgoing = jnp.concatenate([normed_two, fresh_flat], axis=1)
     outgoing_width = outgoing.shape[1]
+    extra_rows = -(-(row_count * outgoing_width) // channels)
+    extra_padded = -(-extra_rows // 32) * 32
     second_buffer = jnp.concatenate(
-        [
-            parcels_second.reshape(devices_req, second_pages_flat),
-            jnp.zeros((devices_req, row_count * outgoing_width), jnp.bfloat16),
-        ],
+        [parcels_second, jnp.zeros((devices_req, extra_padded, channels), jnp.bfloat16)],
         axis=1,
     )
     received_first, second_buffer = lax.optimization_barrier((received_first, second_buffer))
+    extra = jnp.pad(
+        outgoing.reshape(row_count * outgoing_width),
+        (0, extra_padded * channels - row_count * outgoing_width),
+    ).reshape(1, extra_padded, channels)
     second_buffer = lax.dynamic_update_slice(
         second_buffer,
-        jnp.broadcast_to(
-            outgoing.reshape(1, row_count * outgoing_width),
-            (devices_req, row_count * outgoing_width),
-        ),
-        (0, second_pages_flat),
+        jnp.broadcast_to(extra, (devices_req, extra_padded, channels)),
+        (0, second_span, 0),
     )
     received_second = lax.all_to_all(
         second_buffer, "req", split_axis=0, concat_axis=0, tiled=True
     )
-    gathered = received_second[:, second_pages_flat:].reshape(total_rows, outgoing_width)
-    received = jnp.concatenate(
-        [
-            received_first,
-            received_second[:, :second_pages_flat].reshape(
-                (devices_req, pages_per - first_pages) + parcels_second.shape[2:]
-            ),
-        ],
-        axis=1,
+    gathered = (
+        received_second[:, second_span:, :]
+        .reshape(devices_req, extra_padded * channels)[:, : row_count * outgoing_width]
+        .reshape(total_rows, outgoing_width)
     )
     normed_all = gathered[:, :width_local]
     fresh_all = gathered[:, width_local:].reshape(total_rows, kv_local, channels)
@@ -236,8 +233,17 @@
     )
     result = (residual_wide + lowered).astype(jnp.bfloat16)
 
-    arrived = received[source_owner]
-    new_blocks = mask_blocks(arrived, lengths[arriving], fresh_all[arriving])
+    lengths_new = lengths[arriving]
+    fresh_new = fresh_all[arriving]
+    blocks_first = mask_blocks(received_first[source_owner], lengths_new, fresh_new, 0)
+    blocks_second = mask_blocks(
+        received_second[:, :second_span, :]
+        .reshape(devices_req, second_pages, kv_local, page_len, channels)[source_owner],
+        lengths_new,
+        fresh_new,
+        first_pages,
+    )
+    new_blocks = jnp.concatenate([blocks_first, blocks_second], axis=1)
     new_pool = new_blocks.reshape(row_count * pages_per, kv_local, page_len, channels)
     return (result, new_pool)
 

time: 235 us -> 204 us (0.87)
  local copies, waits for them, and re-layouts: 66.6 us -> 39.8 us
  other arithmetic: 34.5 us -> 25.8 us
    unnamed x32 -> x25, local copies, waits for them, and re-layouts: 28.4 us -> 0.83 us
    dynamic_update_slice x1 -> x0, other arithmetic: 6.52 us -> none  [per_device(): lax.dynamic_update_slice(second_buffer, jnp.broadcast_to(outgoing.reshape...]
    all_to_all x1, waiting for transfers between devices: 6.44 us -> 0.01 us  [per_device(): lax.all_to_all(jnp.broadcast_to(hidden_part[None], (devices_kvh,) + hidde...]
    reshape x2, local copies, waits for them, and re-layouts: 4.99 us -> 0.25 us  [the longest x1 0.16 us: per_device(): gathered = received_second[:, second_span:, :].reshape(devices_req, extra...]
    all_to_all x1, waiting for transfers between devices: 0.54 us -> 4.04 us  [per_device(): lax.all_to_all(lowered_parts.reshape(devices_req, row_count, width_local)...]
    all_to_all x1, waiting for transfers between devices: 2.96 us -> 6.25 us  [per_device(): lax.all_to_all(parcels_first, 'req', split_axis=0, concat_axis=0, tiled=T...]
    slice x2 -> x3, local copies, waits for them, and re-layouts: 2.47 us -> 5.56 us  [the longest x1 4.58 us: per_device(): received_second[:, :second_span, :]]
    concatenate x1, other arithmetic: 7.41 us -> 4.6 us  [per_device(): new_blocks = jnp.concatenate([blocks_first, blocks_second], axis=1)]
  transfers between devices with their start and end apart: 8 -> 8, of which waited for: 6 -> 5; matrix products, arithmetic and copies ran while one was open for 28% -> 30% of each run, Pallas kernels for 0% -> 0%
where the time goes in v8:
time: 204 us; the launch traced here: 202 us
  waiting for transfers between devices  77.9 us (38%)
  local copies, waits for them, and re-layouts  39.8 us (20%)
  starting transfers between devices  31.4 us (15%)
  other arithmetic  25.8 us (13%)
  blocking collectives  14 us (7%)
  matrix products  12 us (6%)
    all_to_all x1, waiting for transfers between devices, per_device(): lax.all_to_all(second_buffer, 'req', split_axis=0, concat_axis=0, tiled=T...  63.7 us
    select_n x2, other arithmetic, mask_blocks(): jnp.where(kept, blocks, jnp.where(placed, fresh[:, None, :, None, :], jnp...  15.3 us
    all_gather x1, blocking collectives, per_device(): full_states = lax.all_gather(states, 'kvh', axis=1, tiled=True)  14 us
    all_to_all x1, starting transfers between devices, per_device(): lax.all_to_all(parcels_first, 'req', split_axis=0, concat_axis=0, tiled=T...  7.34 us
    all_to_all x1, waiting for transfers between devices, per_device(): lax.all_to_all(parcels_first, 'req', split_axis=0, concat_axis=0, tiled=T...  6.25 us
    all_to_all x1, starting transfers between devices, per_device(): lax.all_to_all(partial_both.reshape(devices_kvh, group_rows, 2 * ffn_widt...  5.31 us
    gather x1, local copies, waits for them, and re-layouts, per_device(): home_blocks = mask_blocks(kv_pool[page_table], positions_home, fresh)  5.02 us
    gather x1, local copies, waits for them, and re-layouts, per_device(): kv_pool[picked_pages[:, first_pages:]]  5.01 us
  transfers between devices with their start and end apart: 8, of which 5 were waited for; matrix products, arithmetic and copies ran while one was open for 30% of the time, Pallas kernels for 0%

profile of v8, /device:TPU:0, one launch (start us, length us, event | category | flops | bytes accessed | tf_op | source)
XLA Modules:
  0.0 201.9 jit_solution(4701029273907070588)
XLA Ops:
  0.7 1.5 iota_reduce_fusion.1
  3.5 1.2 gather_fusion.2
  4.9 4.9 %gather_fusion.3 = bf16[64,128,256]{2,1,0:T(8,128)(2,1)} fusion(bf16[64,128,256]{2,1,0:T(8,128)(2,1)} %bitcast.81, s32[1024]{0:T(1024)S(1)} %pad_clamp_fusion.3), kind=kCustom, calls=%fused_computation.3 | custom fusion | bytes 8388864 | tf_op jit(solution)/shard_map/gather | solution.py:114
  9.9 7.3 %all-to-all-start = ((bf16[16,4,1,128,256]{4,3,1,2,0:T(8,128)(2,1)}), bf16[16,4,1,128,256]{4,3,1,2,0:T(8,128)(2,1)}, u32[]{:S(2)}, u32[]{:S(2)}) async-start(bf16[16,4,1,128,256]{4,3,1,2,0:T(8,128)(2,1)} %bitcast.84), calls=%async_computation | async-start | bytes 8388608 | tf_op jit(solution)/shard_map/all_to_all | solution.py:115
  17.3 14.0 %all-gather = bf16[8,320,8]{1,2,0:T(8,128)(2,1)S(1)} all-gather(bf16[1,320,8]{1,2,0:T(8,128)(2,1)S(1)} %bitcast.93), channel_id=1, replica_groups=mesh['req'=16,'kvh'=8] {'kvh'}, dimensions={0}, use_global_device_ids=true | all-gather | bytes 46080 | tf_op jit(solution)/shard_map/all_gather | solution.py:125
  32.7 1.3 fusion.9
  34.1 5.0 %gather_fusion.1 = bf16[64,128,256]{2,1,0:T(8,128)(2,1)} fusion(bf16[64,128,256]{2,1,0:T(8,128)(2,1)} %bitcast.82, s32[1024]{0:T(1024)S(1)} %pad_clamp_fusion.5), kind=kCustom, calls=%fused_computation.1 | custom fusion | bytes 8388864 | tf_op jit(solution)/shard_map/gather | solution.py:146
  39.1 2.3 %multiply_reduce_fusion.1 = (f32[8,4]{0,1:T(4,128)S(1)}, f32[8,4,128]{2,0,1:T(8,128)S(1)}) fusion(bf16[8,2560]{1,0:T(8,128)(2,1)S(1)} %fusion.19, bf16[2560,512]{1,0:T(8,128)(2,1)} %param.18), kind=kOutput, calls=%fused_computation.57 | convolution fusion | flops 20979680 | bytes 2678912 | tf_op jit(solution)/shard_map/dot_general | solution.py:129
  42.2 7.6 %select_select_fusion = bf16[8,1,1024,256]{3,2,0,1:T(8,128)(2,1)} fusion(bf16[8,1,1024,256]{3,2,0,1:T(8,128)(2,1)} %bitcast.86, pred[8,1024]{1,0:T(8,128)(4,1)S(1)} %get-tuple-element.23, pred[8,1024]{1,0:T(8,128)(4,1)S(1)} %get-tuple-element.22, bf16[8,256]{1,0:T(8,128)(2,1)S(1)} %maximum_bitcast_fusion), kind=kLoop, calls=%fused_computation.11 | loop fusion | flops 4194304 | bytes 8409088 | tf_op jit(solution)/shard_map/jit(_where)/select_n | solution.py:48
  49.9 2.5 %fusion.43 = (f32[8,4]{1,0:T(8,128)S(1)}, f32[8,4,1024]{2,1,0:T(4,128)S(1)}) fusion(bf16[8,1,1024,256]{3,2,0,1:T(8,128)(2,1)} %select_select_fusion, pred[8,1024]{1,0:T(8,128)(4,1)S(1)} %get-tuple-element.36, bf16[8,4,64]{2,1,0:T(4,128)(2,1)S(1)} %get-tuple-element.17, bf16[8,4,64]{2,1,0:T(4,128)(2,1)S(1)} %get-tuple-element.16), kind=kOutput, calls=%fused_computation.124 | convolution fusion | flops 8537087 | bytes 2244736 | tf_op jit(solution)/shard_map/sub | solution.py:67
  52.3 2.0 %fusion.8 = bf16[1,8,4,128]{3,2,1,0:T(4,128)(2,1)S(1)} fusion(bf16[8,1,1024,256]{3,2,0,1:T(8,128)(2,1)} %select_select_fusion, f32[8,4,1024]{2,1,0:T(4,128)S(1)} %get-tuple-element.42, f32[8,4]{1,0:T(8,128)S(1)} %get-tuple-element.41), kind=kOutput, calls=%fused_computation.24 | convolution fusion | flops 8458240 | bytes 2236544 | tf_op jit(solution)/shard_map/rkgt,rktd->rkgd/dot_general | solution.py:68
  56.1 1.7 collective-permute-start.1
  57.9 3.0 %collective-permute-done.1 = f32[8,2560]{1,0:T(8,128)S(1)} collective-permute-done((f32[8,2560]{1,0:T(8,128)S(1)}, f32[8,2560]{1,0:T(8,128)S(1)}, u32[]{:S(2)}, u32[]{:S(2)}) %collective-permute-start.1) | collective-permute-done | bytes 81952 | tf_op jit(solution)/shard_map/ppermute | solution.py:156
  60.9 2.6 %collective-permute-start.2 = (f32[8,2560]{1,0:T(8,128)S(1)}, f32[8,2560]{1,0:T(8,128)S(1)}, u32[]{:S(2)}, u32[]{:S(2)}) collective-permute-start(f32[8,2560]{1,0:T(8,128)S(1)} %add.225), channel_id=1, source_target_pairs={{0,4},{1,5},{2,6},{3,7},{4,0},{5,1},{6,2},{7,3},{8,12},{9,13},{10,... | collective-permute-start | bytes 245768 | tf_op jit(solution)/shard_map/ppermute | solution.py:156
  63.6 5.0 %gather_fusion.4 = bf16[64,128,256]{2,1,0:T(8,128)(2,1)} fusion(bf16[64,128,256]{2,1,0:T(8,128)(2,1)} %bitcast.83, s32[1024]{0:T(1024)S(1)} %pad_clamp_fusion.2), kind=kCustom, calls=%fused_computation.4 | custom fusion | bytes 8388864 | tf_op jit(solution)/shard_map/gather | solution.py:119
  68.6 4.7 %concatenate.34 = bf16[16,544,256]{2,1,0:T(8,128)(2,1)} pad(bf16[16,512,256]{2,1,0:T(8,128)(2,1)} %bitcast.85, bf16[]{:T(256)} %constant.43.clone.1), padding=0_0x0_32x0_0 | pad | bytes 8650754 | tf_op jit(solution)/shard_map/concatenate | solution.py:175
  74.3 6.2 %all-to-all-done = bf16[16,4,1,128,256]{4,3,1,2,0:T(8,128)(2,1)} async-done(((bf16[16,4,1,128,256]{4,3,1,2,0:T(8,128)(2,1)}), bf16[16,4,1,128,256]{4,3,1,2,0:T(8,128)(2,1)}, u32[]{:S(2)}, u32[]{:S(2)}) %all-to-all-start) | async-done | bytes 4194336 | tf_op jit(solution)/shard_map/all_to_all | solution.py:115
  81.3 4.8 %all-to-all-start.1 = ((bf16[16,544,256]{2,1,0:T(8,128)(2,1)}), bf16[16,544,256]{2,1,0:T(8,128)(2,1)}, u32[]{:S(2)}, u32[]{:S(2)}) async-start(bf16[16,544,256]{2,1,0:T(8,128)(2,1)} %broadcast_dynamic-update-slice_fusion), calls=%async_computation.1 | async-start | bytes 8912896 | tf_op jit(solution)/shard_map/all_to_all | solution.py:189
  86.8 63.7 %all-to-all-done.1 = bf16[16,544,256]{2,1,0:T(8,128)(2,1)} async-done(((bf16[16,544,256]{2,1,0:T(8,128)(2,1)}), bf16[16,544,256]{2,1,0:T(8,128)(2,1)}, u32[]{:S(2)}, u32[]{:S(2)}) %all-to-all-start.1) | async-done | bytes 4456480 | tf_op jit(solution)/shard_map/all_to_all | solution.py:189
  150.5 1.0 slice.84
  151.8 2.2 %fusion.10 = f32[128,1216]{1,0:T(8,128)} fusion(bf16[320,608]{1,0:T(8,128)(2,1)S(1)} %copy-done.9, bf16[320,608]{1,0:T(8,128)(2,1)} %param.25, bf16[128,576]{1,0:T(8,128)(2,1)S(1)} %reshape.488), kind=kOutput, calls=%fused_computation.27 | convolution fusion | flops 101171200 | bytes 1519616 | tf_op jit(solution)/shard_map/dot_general | solution.py:201
  154.1 5.3 %all-to-all-start.2 = ((f32[8,16,1216]{2,1,0:T(8,128)}), f32[8,16,1216]{2,1,0:T(8,128)S(1)}, u32[]{:S(2)}, u32[]{:S(2)}) async-start(f32[8,16,1216]{2,1,0:T(8,128)} %bitcast.90), calls=%async_computation.2 | async-start | bytes 1310720 | tf_op jit(solution)/shard_map/all_to_all | solution.py:204
  159.5 4.2 %gather_fusion.6 = bf16[8,4,128,256]{3,2,1,0:T(8,128)(2,1)} fusion(bf16[16,4,128,256]{3,2,1,0:T(8,128)(2,1)} %bitcast.18, s32[1024]{0:T(1024)S(1)} %pad_clamp_fusion), kind=kCustom, calls=%fused_computation.6 | custom fusion | bytes 4194336 | tf_op jit(solution)/shard_map/gather | solution.py:238
  163.8 4.6 %slice.90 = bf16[16,512,256]{2,1,0:T(8,128)(2,1)} slice(bf16[16,544,256]{2,1,0:T(8,128)(2,1)} %all-to-all-done.1), slice={[0:16], [0:512], [0:256]} | slice | bytes 8388608 | tf_op jit(solution)/shard_map/slice | solution.py:240
  168.4 4.2 %gather_fusion.8 = bf16[8,4,128,256]{3,2,1,0:T(8,128)(2,1)} fusion(bf16[16,4,128,256]{3,2,1,0:T(8,128)(2,1)} %bitcast.87, s32[1024]{0:T(1024)S(1)} %pad_clamp_fusion), kind=kCustom, calls=%fused_computation.8 | custom fusion | bytes 4194336 | tf_op jit(solution)/shard_map/gather | solution.py:240
  174.0 4.8 %all-to-all-start.3 = ((bf16[8,16,608]{2,1,0:T(8,128)(2,1)}), bf16[8,16,608]{2,1,0:T(8,128)(2,1)S(1)}, u32[]{:S(2)}, u32[]{:S(2)}) async-start(bf16[8,16,608]{2,1,0:T(8,128)(2,1)} %broadcast_in_dim.169), calls=%async_computation.3 | async-start | bytes 327680 | tf_op jit(solution)/shard_map/all_to_all | solution.py:216
  178.8 7.6 %bitcast_select_fusion.1 = (bf16[8,4,1,128,256]{4,3,1,0,2:T(8,128)(2,1)}, bf16[8,4,1,128,256]{4,3,1,0,2:T(8,128)(2,1)}) fusion(bf16[8,4,128,256]{3,2,1,0:T(8,128)(2,1)} %gather_fusion.6, pred[8,4,128]{2,1,0:T(4,128)(4,1)S(1)} %get-tuple-element.27, pred[8,4,128]{2,1,0:T(4,128)(4,1)S(1)} %get-tuple-element.26, bf16[8,256]{1,0:T(8,128)(2,1)S(1)} %gather_fusion.7, ...), kind=kLoop, calls=%fused_computation.17 | loop fusion | flops 4194304 | bytes 8409088 | tf_op jit(solution)/shard_map/jit(_where)/select_n | solution.py:48
  186.5 1.0 fusion.14
  187.5 4.4 %all-to-all-start.4 = ((f32[16,8,320]{2,1,0:T(8,128)}), f32[16,8,320]{2,1,0:T(8,128)S(1)}, u32[]{:S(2)}, u32[]{:S(2)}) async-start(f32[16,8,320]{2,1,0:T(8,128)} %fusion.14), calls=%async_computation.4 | async-start | bytes 393216 | tf_op jit(solution)/shard_map/all_to_all | solution.py:225
  191.9 4.6 %pad_maximum_fusion = bf16[8,8,1,128,256]{4,3,1,0,2:T(8,128)(2,1)} fusion(bf16[8,4,1,128,256]{4,3,1,0,2:T(8,128)(2,1)} %get-tuple-element.25, bf16[8,4,1,128,256]{4,3,1,0,2:T(8,128)(2,1)} %get-tuple-element.24), kind=kLoop, calls=%fused_computation.10 | loop fusion | flops 2097152 | bytes 8388608 | tf_op jit(solution)/shard_map/concatenate | solution.py:246
  196.5 4.0 %all-to-all-done.4 = f32[16,8,320]{2,1,0:T(8,128)S(1)} async-done(((f32[16,8,320]{2,1,0:T(8,128)}), f32[16,8,320]{2,1,0:T(8,128)S(1)}, u32[]{:S(2)}, u32[]{:S(2)}) %all-to-all-start.4) | async-done | bytes 163872 | tf_op jit(solution)/shard_map/all_to_all | solution.py:225
  200.5 1.4 add_convert_fusion.1
  (96 shorter events, 10.0 us)
Async XLA Ops:
  0.6 53.7 %copy-start = (bf16[512,2560]{1,0:T(8,128)(2,1)S(1)}, bf16[512,2560]{1,0:T(8,128)(2,1)}, u32[]{:S(2)}) copy-start(bf16[512,2560]{1,0:T(8,128)(2,1)} %param.23) | copy-start | bytes 7864324
  9.9 7.4 %copy-start.2 = (s32[8,8]{1,0:T(8,128)S(1)}, s32[8,8]{1,0:T(8,128)}, u32[]{:S(2)}) copy-start(s32[8,8]{1,0:T(8,128)} %param.30) | copy-start | bytes 772
  9.9 7.4 %copy-start.6 = (bf16[8,320]{1,0:T(8,128)(2,1)S(1)}, bf16[8,320]{1,0:T(8,128)(2,1)}, u32[]{:S(2)}) copy-start(bf16[8,320]{1,0:T(8,128)(2,1)} %param.16) | copy-start | bytes 15364
  9.9 21.7 %copy-start.7 = (bf16[2560]{0:T(1024)(128)(2,1)S(1)}, bf16[2560]{0:T(1024)(128)(2,1)}, u32[]{:S(2)}) copy-start(bf16[2560]{0:T(1024)(128)(2,1)} %param.17) | copy-start | bytes 15364
  9.9 21.8 %copy-start.3 = (bf16[2560,128]{1,0:T(8,128)(2,1)S(1)}, bf16[2560,128]{1,0:T(8,128)(2,1)}, u32[]{:S(2)}) copy-start(bf16[2560,128]{1,0:T(8,128)(2,1)} %param.19) | copy-start | bytes 1966084
  9.9 22.1 %copy-start.10 = (bf16[128]{0:T(256)(128)(2,1)S(1)}, bf16[128]{0:T(256)(128)(2,1)}, u32[]{:S(2)}) copy-start(bf16[128]{0:T(256)(128)(2,1)} %param.22) | copy-start | bytes 772
  9.9 22.2 %copy-start.1 = (s32[128]{0:T(128)S(1)}, s32[128]{0:T(128)}, u32[]{:S(2)}) copy-start(s32[128]{0:T(128)} %param.29) | copy-start | bytes 1540
  9.9 70.6 %all-to-all-start = ((bf16[16,4,1,128,256]{4,3,1,2,0:T(8,128)(2,1)}), bf16[16,4,1,128,256]{4,3,1,2,0:T(8,128)(2,1)}, u32[]{:S(2)}, u32[]{:S(2)}) async-start(bf16[16,4,1,128,256]{4,3,1,2,0:T(8,128)(2,1)} %bitcast.84), calls=%async_computation | async-start | bytes 8388608 | tf_op jit(solution)/shard_map/all_to_all | solution.py:115
  34.1 7.4 %copy-start.11 = (bf16[128]{0:T(256)(128)(2,1)S(1)}, bf16[128]{0:T(256)(128)(2,1)}, u32[]{:S(2)}) copy-start(bf16[128]{0:T(256)(128)(2,1)} %param.21) | copy-start | bytes 772
  49.9 7.9 %copy-start.8 = (bf16[320]{0:T(512)(128)(2,1)S(1)}, bf16[320]{0:T(512)(128)(2,1)}, u32[]{:S(2)}) copy-start(bf16[320]{0:T(512)(128)(2,1)} %param.24) | copy-start | bytes 1924
  54.8 1.3 collective-permute-start
  56.1 4.8 %collective-permute-start.1 = (f32[8,2560]{1,0:T(8,128)S(1)}, f32[8,2560]{1,0:T(8,128)S(1)}, u32[]{:S(2)}, u32[]{:S(2)}) collective-permute-start(f32[8,2560]{1,0:T(8,128)S(1)} %add.224), channel_id=1, source_target_pairs={{0,2},{1,3},{2,0},{3,1},{4,6},{5,7},{6,4},{7,5},{8,10},{9,11},{10,... | collective-permute-start | bytes 245768 | tf_op jit(solution)/shard_map/ppermute | solution.py:156
  60.9 12.3 %collective-permute-start.2 = (f32[8,2560]{1,0:T(8,128)S(1)}, f32[8,2560]{1,0:T(8,128)S(1)}, u32[]{:S(2)}, u32[]{:S(2)}) collective-permute-start(f32[8,2560]{1,0:T(8,128)S(1)} %add.225), channel_id=1, source_target_pairs={{0,4},{1,5},{2,6},{3,7},{4,0},{5,1},{6,2},{7,3},{8,12},{9,13},{10,... | collective-permute-start | bytes 245768 | tf_op jit(solution)/shard_map/ppermute | solution.py:156
  73.4 0.6 copy-start.5
  81.3 70.5 %copy-start.9 = (bf16[320,608]{1,0:T(8,128)(2,1)S(1)}, bf16[320,608]{1,0:T(8,128)(2,1)}, u32[]{:S(2)}) copy-start(bf16[320,608]{1,0:T(8,128)(2,1)} %param.26) | copy-start | bytes 1167364
  81.3 69.2 %all-to-all-start.1 = ((bf16[16,544,256]{2,1,0:T(8,128)(2,1)}), bf16[16,544,256]{2,1,0:T(8,128)(2,1)}, u32[]{:S(2)}, u32[]{:S(2)}) async-start(bf16[16,544,256]{2,1,0:T(8,128)(2,1)} %broadcast_dynamic-update-slice_fusion), calls=%async_computation.1 | async-start | bytes 8912896 | tf_op jit(solution)/shard_map/all_to_all | solution.py:189
  154.1 19.2 %all-to-all-start.2 = ((f32[8,16,1216]{2,1,0:T(8,128)}), f32[8,16,1216]{2,1,0:T(8,128)S(1)}, u32[]{:S(2)}, u32[]{:S(2)}) async-start(f32[8,16,1216]{2,1,0:T(8,128)} %bitcast.90), calls=%async_computation.2 | async-start | bytes 1310720 | tf_op jit(solution)/shard_map/all_to_all | solution.py:204
  174.0 12.4 %all-to-all-start.3 = ((bf16[8,16,608]{2,1,0:T(8,128)(2,1)}), bf16[8,16,608]{2,1,0:T(8,128)(2,1)S(1)}, u32[]{:S(2)}, u32[]{:S(2)}) async-start(bf16[8,16,608]{2,1,0:T(8,128)(2,1)} %broadcast_in_dim.169), calls=%async_computation.3 | async-start | bytes 327680 | tf_op jit(solution)/shard_map/all_to_all | solution.py:216
  178.8 7.6 %copy-start.4 = (bf16[608,320]{0,1:T(8,128)(2,1)S(1)}, bf16[608,320]{0,1:T(8,128)(2,1)}, u32[]{:S(2)}) copy-start(bf16[608,320]{0,1:T(8,128)(2,1)} %param.27) | copy-start | bytes 1167364
  187.5 13.1 %all-to-all-start.4 = ((f32[16,8,320]{2,1,0:T(8,128)}), f32[16,8,320]{2,1,0:T(8,128)S(1)}, u32[]{:S(2)}, u32[]{:S(2)}) async-start(f32[16,8,320]{2,1,0:T(8,128)} %fusion.14), calls=%async_computation.4 | async-start | bytes 393216 | tf_op jit(solution)/shard_map/all_to_all | solution.py:225

commit v9 on v8

--- a/solution.py
+++ b/solution.py
@@ -189,6 +189,22 @@
     received_second = lax.all_to_all(
         second_buffer, "req", split_axis=0, concat_axis=0, tiled=True
     )
+    lengths_new = lengths[arriving]
+    first_span = first_pages * page_len
+    span_first = received_first.reshape(devices_req, first_span, channels)[source_owner]
+    span_first = jnp.where(
+        jnp.arange(first_span, dtype=jnp.int32)[None, :, None] < lengths_new[:, None, None],
+        span_first,
+        jnp.zeros((), jnp.bfloat16),
+    )
+    span_first, received_second = lax.optimization_barrier((span_first, received_second))
+    span_second = received_second[source_owner][:, :second_span, :]
+    span_second = jnp.where(
+        first_span + jnp.arange(second_span, dtype=jnp.int32)[None, :, None]
+        < lengths_new[:, None, None],
+        span_second,
+        jnp.zeros((), jnp.bfloat16),
+    )
     gathered = (
         received_second[:, second_span:, :]
         .reshape(devices_req, extra_padded * channels)[:, : row_count * outgoing_width]
@@ -233,18 +249,11 @@
     )
     result = (residual_wide + lowered).astype(jnp.bfloat16)
 
-    lengths_new = lengths[arriving]
-    fresh_new = fresh_all[arriving]
-    blocks_first = mask_blocks(received_first[source_owner], lengths_new, fresh_new, 0)
-    blocks_second = mask_blocks(
-        received_second[:, :second_span, :]
-        .reshape(devices_req, second_pages, kv_local, page_len, channels)[source_owner],
-        lengths_new,
-        fresh_new,
-        first_pages,
-    )
-    new_blocks = jnp.concatenate([blocks_first, blocks_second], axis=1)
-    new_pool = new_blocks.reshape(row_count * pages_per, kv_local, page_len, channels)
+    new_seq = jnp.concatenate([span_first, span_second], axis=1)
+    new_seq = new_seq.at[jnp.arange(row_count), lengths_new].set(
+        fresh_all[arriving].reshape(row_count, channels)
+    )
+    new_pool = new_seq.reshape(row_count * pages_per, kv_local, page_len, channels)
     return (result, new_pool)
 
 

time: 204 us -> 198 us (0.971)
  local copies, waits for them, and re-layouts: 39.8 us -> 37.4 us
    select_n x2 -> x1, other arithmetic: 15.3 us -> 7.64 us  [mask_blocks(): jnp.where(kept, blocks, jnp.where(placed, fresh[:, None, :, None, :], jnp...]
    all_to_all x1, waiting for transfers between devices: 0.01 us -> 7.4 us  [per_device(): lax.all_to_all(partial_both.reshape(devices_kvh, group_rows, 2 * ffn_widt...]
    all_to_all x1, waiting for transfers between devices: 63.7 us -> 56.4 us  [per_device(): lax.all_to_all(second_buffer, 'req', split_axis=0, concat_axis=0, tiled=T...]
    select_n x0 -> x2, other arithmetic: none -> 5.91 us  [the longest x1 2.97 us: per_device(): jnp.where(first_span + jnp.arange(second_span, dtype=jnp.int32)[None, :,...]
    slice x1 -> x0, local copies, waits for them, and re-layouts: 4.58 us -> none  [per_device(): received_second[:, :second_span, :]]
    all_to_all x1, waiting for transfers between devices: 0.01 us -> 2.74 us  [per_device(): lax.all_to_all(jnp.broadcast_to(hidden_part[None], (devices_kvh,) + hidde...]
    all_to_all x1, waiting for transfers between devices: 4.04 us -> 1.74 us  [per_device(): lax.all_to_all(lowered_parts.reshape(devices_req, row_count, width_local)...]
    scatter x0 -> x1, local copies, waits for them, and re-layouts: none -> 2.08 us  [per_device(): new_seq.at[jnp.arange(row_count), lengths_new]]
  transfers between devices with their start and end apart: 8 -> 8, of which waited for: 5 -> 7; matrix products, arithmetic and copies ran while one was open for 30% -> 28% of each run, Pallas kernels for 0% -> 0%
where the time goes in v9:
time: 198 us; the launch traced here: 197 us
  waiting for transfers between devices  78.5 us (40%)
  local copies, waits for them, and re-layouts  37.4 us (19%)
  starting transfers between devices  29.8 us (15%)
  other arithmetic  24 us (12%)
  blocking collectives  14 us (7%)
  matrix products  12 us (6%)
    all_to_all x1, waiting for transfers between devices, per_device(): lax.all_to_all(second_buffer, 'req', split_axis=0, concat_axis=0, tiled=T...  56.4 us
    all_gather x1, blocking collectives, per_device(): full_states = lax.all_gather(states, 'kvh', axis=1, tiled=True)  14 us
    select_n x1, other arithmetic, mask_blocks(): jnp.where(kept, blocks, jnp.where(placed, fresh[:, None, :, None, :], jnp...  7.64 us
    all_to_all x1, waiting for transfers between devices, per_device(): lax.all_to_all(partial_both.reshape(devices_kvh, group_rows, 2 * ffn_widt...  7.4 us
    all_to_all x1, starting transfers between devices, per_device(): lax.all_to_all(parcels_first, 'req', split_axis=0, concat_axis=0, tiled=T...  7.34 us
    all_to_all x1, waiting for transfers between devices, per_device(): lax.all_to_all(parcels_first, 'req', split_axis=0, concat_axis=0, tiled=T...  6.25 us
    all_to_all x1, starting transfers between devices, per_device(): lax.all_to_all(partial_both.reshape(devices_kvh, group_rows, 2 * ffn_widt...  5.31 us
    gather x1, local copies, waits for them, and re-layouts, per_device(): home_blocks = mask_blocks(kv_pool[page_table], positions_home, fresh)  5.02 us
  transfers between devices with their start and end apart: 8, of which 7 were waited for; matrix products, arithmetic and copies ran while one was open for 28% of the time, Pallas kernels for 0%

profile of v9, /device:TPU:0, one launch (start us, length us, event | category | flops | bytes accessed | tf_op | source)
XLA Modules:
  0.0 196.7 jit_solution(635425155920157197)
XLA Ops:
  0.7 1.5 iota_reduce_fusion.1
  4.9 4.9 %gather_fusion.4 = bf16[64,128,256]{2,1,0:T(8,128)(2,1)} fusion(bf16[64,128,256]{2,1,0:T(8,128)(2,1)} %bitcast.78, s32[1024]{0:T(1024)S(1)} %pad_clamp_fusion.2), kind=kCustom, calls=%fused_computation.4 | custom fusion | bytes 8388864 | tf_op jit(solution)/shard_map/gather | solution.py:114
  9.9 7.3 %all-to-all-start = ((bf16[16,4,1,128,256]{4,3,1,2,0:T(8,128)(2,1)}), bf16[16,4,1,128,256]{4,3,1,2,0:T(8,128)(2,1)}, u32[]{:S(2)}, u32[]{:S(2)}) async-start(bf16[16,4,1,128,256]{4,3,1,2,0:T(8,128)(2,1)} %bitcast.81), calls=%async_computation | async-start | bytes 8388608 | tf_op jit(solution)/shard_map/all_to_all | solution.py:115
  17.3 14.0 %all-gather = bf16[8,320,8]{1,2,0:T(8,128)(2,1)S(1)} all-gather(bf16[1,320,8]{1,2,0:T(8,128)(2,1)S(1)} %bitcast.89), channel_id=1, replica_groups=mesh['req'=16,'kvh'=8] {'kvh'}, dimensions={0}, use_global_device_ids=true | all-gather | bytes 46080 | tf_op jit(solution)/shard_map/all_gather | solution.py:125
  32.7 1.3 fusion.9
  34.1 5.0 %gather_fusion.1 = bf16[64,128,256]{2,1,0:T(8,128)(2,1)} fusion(bf16[64,128,256]{2,1,0:T(8,128)(2,1)} %bitcast.79, s32[1024]{0:T(1024)S(1)} %pad_clamp_fusion.5), kind=kCustom, calls=%fused_computation.1 | custom fusion | bytes 8388864 | tf_op jit(solution)/shard_map/gather | solution.py:146
  39.1 2.3 %multiply_reduce_fusion.1 = (f32[8,4]{0,1:T(4,128)S(1)}, f32[8,4,128]{2,0,1:T(8,128)S(1)}) fusion(bf16[8,2560]{1,0:T(8,128)(2,1)S(1)} %fusion.19, bf16[2560,512]{1,0:T(8,128)(2,1)} %param.18), kind=kOutput, calls=%fused_computation.59 | convolution fusion | flops 20979680 | bytes 2678912 | tf_op jit(solution)/shard_map/dot_general | solution.py:129
  42.2 7.6 %select_select_fusion = bf16[8,1,1024,256]{3,2,0,1:T(8,128)(2,1)} fusion(bf16[8,1,1024,256]{3,2,0,1:T(8,128)(2,1)} %bitcast.83, pred[8,1024]{1,0:T(8,128)(4,1)S(1)} %get-tuple-element.23, pred[8,1024]{1,0:T(8,128)(4,1)S(1)} %get-tuple-element.22, bf16[8,256]{1,0:T(8,128)(2,1)S(1)} %maximum_bitcast_fusion), kind=kLoop, calls=%fused_computation.12 | loop fusion | flops 4194304 | bytes 8409088 | tf_op jit(solution)/shard_map/jit(_where)/select_n | solution.py:48
  49.9 2.5 %fusion.46 = (f32[8,4]{1,0:T(8,128)S(1)}, f32[8,4,1024]{2,1,0:T(4,128)S(1)}) fusion(bf16[8,1,1024,256]{3,2,0,1:T(8,128)(2,1)} %select_select_fusion, pred[8,1024]{1,0:T(8,128)(4,1)S(1)} %get-tuple-element.28, bf16[8,4,64]{2,1,0:T(4,128)(2,1)S(1)} %get-tuple-element.17, bf16[8,4,64]{2,1,0:T(4,128)(2,1)S(1)} %get-tuple-element.16), kind=kOutput, calls=%fused_computation.127 | convolution fusion | flops 8537087 | bytes 2244736 | tf_op jit(solution)/shard_map/sub | solution.py:67
  52.3 2.0 %fusion.8 = bf16[1,8,4,128]{3,2,1,0:T(4,128)(2,1)S(1)} fusion(bf16[8,1,1024,256]{3,2,0,1:T(8,128)(2,1)} %select_select_fusion, f32[8,4,1024]{2,1,0:T(4,128)S(1)} %get-tuple-element.36, f32[8,4]{1,0:T(8,128)S(1)} %get-tuple-element.35), kind=kOutput, calls=%fused_computation.25 | convolution fusion | flops 8458240 | bytes 2236544 | tf_op jit(solution)/shard_map/rkgt,rktd->rkgd/dot_general | solution.py:68
  56.1 1.7 collective-permute-start.1
  57.9 3.0 %collective-permute-done.1 = f32[8,2560]{1,0:T(8,128)S(1)} collective-permute-done((f32[8,2560]{1,0:T(8,128)S(1)}, f32[8,2560]{1,0:T(8,128)S(1)}, u32[]{:S(2)}, u32[]{:S(2)}) %collective-permute-start.1) | collective-permute-done | bytes 81952 | tf_op jit(solution)/shard_map/ppermute | solution.py:156
  60.9 2.6 %collective-permute-start.2 = (f32[8,2560]{1,0:T(8,128)S(1)}, f32[8,2560]{1,0:T(8,128)S(1)}, u32[]{:S(2)}, u32[]{:S(2)}) collective-permute-start(f32[8,2560]{1,0:T(8,128)S(1)} %add.192), channel_id=1, source_target_pairs={{0,4},{1,5},{2,6},{3,7},{4,0},{5,1},{6,2},{7,3},{8,12},{9,13},{10,... | collective-permute-start | bytes 245768 | tf_op jit(solution)/shard_map/ppermute | solution.py:156
  63.6 5.0 %gather_fusion.5 = bf16[64,128,256]{2,1,0:T(8,128)(2,1)} fusion(bf16[64,128,256]{2,1,0:T(8,128)(2,1)} %bitcast.80, s32[1024]{0:T(1024)S(1)} %pad_clamp_fusion.1), kind=kCustom, calls=%fused_computation.5 | custom fusion | bytes 8388864 | tf_op jit(solution)/shard_map/gather | solution.py:119
  68.6 4.7 %concatenate.37 = bf16[16,544,256]{2,1,0:T(8,128)(2,1)} pad(bf16[16,512,256]{2,1,0:T(8,128)(2,1)} %bitcast.82, bf16[]{:T(256)} %constant.44.clone.1), padding=0_0x0_32x0_0 | pad | bytes 8650754 | tf_op jit(solution)/shard_map/concatenate | solution.py:175
  74.3 6.2 %all-to-all-done = bf16[16,4,1,128,256]{4,3,1,2,0:T(8,128)(2,1)} async-done(((bf16[16,4,1,128,256]{4,3,1,2,0:T(8,128)(2,1)}), bf16[16,4,1,128,256]{4,3,1,2,0:T(8,128)(2,1)}, u32[]{:S(2)}, u32[]{:S(2)}) %all-to-all-start) | async-done | bytes 4194336 | tf_op jit(solution)/shard_map/all_to_all | solution.py:115
  81.3 4.7 %all-to-all-start.1 = ((bf16[16,544,256]{2,1,0:T(8,128)(2,1)}), bf16[16,544,256]{2,1,0:T(8,128)(2,1)}, u32[]{:S(2)}, u32[]{:S(2)}) async-start(bf16[16,544,256]{2,1,0:T(8,128)(2,1)} %broadcast_dynamic-update-slice_fusion), calls=%async_computation.1 | async-start | bytes 8912896 | tf_op jit(solution)/shard_map/all_to_all | solution.py:189
  86.8 4.2 %gather_fusion.6 = bf16[8,512,256]{2,1,0:T(8,128)(2,1)} fusion(bf16[16,512,256]{2,1,0:T(8,128)(2,1)} %bitcast.15, s32[1024]{0:T(1024)S(1)} %pad_clamp_fusion), kind=kCustom, calls=%fused_computation.6 | custom fusion | bytes 4194336 | tf_op jit(solution)/shard_map/gather | solution.py:194
  91.0 2.9 %broadcast_select_fusion = bf16[8,512,256]{2,1,0:T(8,128)(2,1)} fusion(bf16[8,512,256]{2,1,0:T(8,128)(2,1)} %gather_fusion.6, pred[8,512]{1,0:T(8,128)(4,1)S(1)} %get-tuple-element.27), kind=kLoop, calls=%fused_computation.18 | loop fusion | flops 1048576 | bytes 4198400 | tf_op jit(solution)/shard_map/jit(_where)/select_n | solution.py:195
  93.9 56.4 %all-to-all-done.1 = bf16[16,544,256]{2,1,0:T(8,128)(2,1)} async-done(((bf16[16,544,256]{2,1,0:T(8,128)(2,1)}), bf16[16,544,256]{2,1,0:T(8,128)(2,1)}, u32[]{:S(2)}, u32[]{:S(2)}) %all-to-all-start.1) | async-done | bytes 4456480 | tf_op jit(solution)/shard_map/all_to_all | solution.py:189
  151.7 2.3 %fusion.10 = f32[128,1216]{1,0:T(8,128)} fusion(bf16[320,608]{1,0:T(8,128)(2,1)S(1)} %copy-done.9, bf16[320,608]{1,0:T(8,128)(2,1)} %param.25, bf16[128,576]{1,0:T(8,128)(2,1)S(1)} %reshape.461), kind=kOutput, calls=%fused_computation.28 | convolution fusion | flops 101171200 | bytes 1519616 | tf_op jit(solution)/shard_map/dot_general | solution.py:217
  153.9 5.3 %all-to-all-start.2 = ((f32[8,16,1216]{2,1,0:T(8,128)}), f32[8,16,1216]{2,1,0:T(8,128)S(1)}, u32[]{:S(2)}, u32[]{:S(2)}) async-start(f32[8,16,1216]{2,1,0:T(8,128)} %bitcast.86), calls=%async_computation.2 | async-start | bytes 1310720 | tf_op jit(solution)/shard_map/all_to_all | solution.py:220
  159.3 4.3 %gather_fusion.7 = bf16[8,544,256]{2,1,0:T(8,128)(2,1)} fusion(bf16[16,544,256]{2,1,0:T(8,128)(2,1)} %all-to-all-done.1, s32[1024]{0:T(1024)S(1)} %pad_clamp_fusion), kind=kCustom, calls=%fused_computation.7 | custom fusion | bytes 4456480 | tf_op jit(solution)/shard_map/gather | solution.py:201
  163.6 7.4 %all-to-all-done.2 = f32[8,16,1216]{2,1,0:T(8,128)S(1)} async-done(((f32[8,16,1216]{2,1,0:T(8,128)}), f32[8,16,1216]{2,1,0:T(8,128)S(1)}, u32[]{:S(2)}, u32[]{:S(2)}) %all-to-all-start.2) | async-done | bytes 622624 | tf_op jit(solution)/shard_map/all_to_all | solution.py:220
  171.8 3.4 %all-to-all-start.3 = ((bf16[8,16,608]{2,1,0:T(8,128)(2,1)}), bf16[8,16,608]{2,1,0:T(8,128)(2,1)S(1)}, u32[]{:S(2)}, u32[]{:S(2)}) async-start(bf16[8,16,608]{2,1,0:T(8,128)(2,1)} %broadcast_in_dim.143), calls=%async_computation.3 | async-start | bytes 327680 | tf_op jit(solution)/shard_map/all_to_all | solution.py:232
  175.2 3.0 %slice_select_fusion = bf16[8,512,256]{2,1,0:T(8,128)(2,1)} fusion(bf16[8,544,256]{2,1,0:T(8,128)(2,1)} %gather_fusion.7, pred[8,512]{1,0:T(8,128)(4,1)S(1)} %get-tuple-element.26), kind=kLoop, calls=%fused_computation.13 | loop fusion | flops 1048576 | bytes 4198400 | tf_op jit(solution)/shard_map/jit(_where)/select_n | solution.py:202
  178.8 2.7 %all-to-all-done.3 = bf16[8,16,608]{2,1,0:T(8,128)(2,1)S(1)} async-done(((bf16[8,16,608]{2,1,0:T(8,128)(2,1)}), bf16[8,16,608]{2,1,0:T(8,128)(2,1)S(1)}, u32[]{:S(2)}, u32[]{:S(2)}) %all-to-all-start.3) | async-done | bytes 155680 | tf_op jit(solution)/shard_map/all_to_all | solution.py:232
  182.5 4.4 %all-to-all-start.4 = ((f32[16,8,320]{2,1,0:T(8,128)}), f32[16,8,320]{2,1,0:T(8,128)S(1)}, u32[]{:S(2)}, u32[]{:S(2)}) async-start(f32[16,8,320]{2,1,0:T(8,128)} %fusion.14), calls=%async_computation.4 | async-start | bytes 393216 | tf_op jit(solution)/shard_map/all_to_all | solution.py:241
  187.0 4.5 %pad_maximum_fusion = bf16[8,1024,256]{2,1,0:T(8,128)(2,1)} fusion(bf16[8,512,256]{2,1,0:T(8,128)(2,1)} %slice_select_fusion, bf16[8,512,256]{2,1,0:T(8,128)(2,1)} %broadcast_select_fusion), kind=kLoop, calls=%fused_computation.11 | loop fusion | flops 8388608 | bytes 8388608 | tf_op jit(solution)/shard_map/concatenate | solution.py:252
  191.5 2.1 %scatter_fusion = bf16[8,1024,256]{2,1,0:T(8,128)(2,1)} fusion(bf16[8,1024,256]{2,1,0:T(8,128)(2,1)} %pad_maximum_fusion, s32[8]{0:T(128)S(1)} %fusion.41, bf16[8,256]{1,0:T(8,128)(2,1)S(1)} %gather_fusion.8), kind=kCustom, calls=%fused_computation.9 | custom fusion | bytes 12352 | tf_op jit(solution)/shard_map/scatter | solution.py:253
  193.6 1.7 all-to-all-done.4
  195.3 1.4 add_convert_fusion.1
  (96 shorter events, 13.2 us)
Async XLA Ops:
  0.6 53.7 %copy-start = (bf16[512,2560]{1,0:T(8,128)(2,1)S(1)}, bf16[512,2560]{1,0:T(8,128)(2,1)}, u32[]{:S(2)}) copy-start(bf16[512,2560]{1,0:T(8,128)(2,1)} %param.23) | copy-start | bytes 7864324
  9.9 7.4 %copy-start.2 = (s32[8,8]{1,0:T(8,128)S(1)}, s32[8,8]{1,0:T(8,128)}, u32[]{:S(2)}) copy-start(s32[8,8]{1,0:T(8,128)} %param.30) | copy-start | bytes 772
  9.9 7.4 %copy-start.6 = (bf16[8,320]{1,0:T(8,128)(2,1)S(1)}, bf16[8,320]{1,0:T(8,128)(2,1)}, u32[]{:S(2)}) copy-start(bf16[8,320]{1,0:T(8,128)(2,1)} %param.16) | copy-start | bytes 15364
  9.9 21.7 %copy-start.7 = (bf16[2560]{0:T(1024)(128)(2,1)S(1)}, bf16[2560]{0:T(1024)(128)(2,1)}, u32[]{:S(2)}) copy-start(bf16[2560]{0:T(1024)(128)(2,1)} %param.17) | copy-start | bytes 15364
  9.9 21.8 %copy-start.3 = (bf16[2560,128]{1,0:T(8,128)(2,1)S(1)}, bf16[2560,128]{1,0:T(8,128)(2,1)}, u32[]{:S(2)}) copy-start(bf16[2560,128]{1,0:T(8,128)(2,1)} %param.19) | copy-start | bytes 1966084
  9.9 22.1 %copy-start.10 = (bf16[128]{0:T(256)(128)(2,1)S(1)}, bf16[128]{0:T(256)(128)(2,1)}, u32[]{:S(2)}) copy-start(bf16[128]{0:T(256)(128)(2,1)} %param.22) | copy-start | bytes 772
  9.9 22.2 %copy-start.1 = (s32[128]{0:T(128)S(1)}, s32[128]{0:T(128)}, u32[]{:S(2)}) copy-start(s32[128]{0:T(128)} %param.29) | copy-start | bytes 1540
  9.9 70.6 %all-to-all-start = ((bf16[16,4,1,128,256]{4,3,1,2,0:T(8,128)(2,1)}), bf16[16,4,1,128,256]{4,3,1,2,0:T(8,128)(2,1)}, u32[]{:S(2)}, u32[]{:S(2)}) async-start(bf16[16,4,1,128,256]{4,3,1,2,0:T(8,128)(2,1)} %bitcast.81), calls=%async_computation | async-start | bytes 8388608 | tf_op jit(solution)/shard_map/all_to_all | solution.py:115
  34.1 7.4 %copy-start.11 = (bf16[128]{0:T(256)(128)(2,1)S(1)}, bf16[128]{0:T(256)(128)(2,1)}, u32[]{:S(2)}) copy-start(bf16[128]{0:T(256)(128)(2,1)} %param.21) | copy-start | bytes 772
  49.9 7.9 %copy-start.8 = (bf16[320]{0:T(512)(128)(2,1)S(1)}, bf16[320]{0:T(512)(128)(2,1)}, u32[]{:S(2)}) copy-start(bf16[320]{0:T(512)(128)(2,1)} %param.24) | copy-start | bytes 1924
  54.8 1.3 collective-permute-start
  56.1 4.8 %collective-permute-start.1 = (f32[8,2560]{1,0:T(8,128)S(1)}, f32[8,2560]{1,0:T(8,128)S(1)}, u32[]{:S(2)}, u32[]{:S(2)}) collective-permute-start(f32[8,2560]{1,0:T(8,128)S(1)} %add.191), channel_id=1, source_target_pairs={{0,2},{1,3},{2,0},{3,1},{4,6},{5,7},{6,4},{7,5},{8,10},{9,11},{10,... | collective-permute-start | bytes 245768 | tf_op jit(solution)/shard_map/ppermute | solution.py:156
  60.9 12.3 %collective-permute-start.2 = (f32[8,2560]{1,0:T(8,128)S(1)}, f32[8,2560]{1,0:T(8,128)S(1)}, u32[]{:S(2)}, u32[]{:S(2)}) collective-permute-start(f32[8,2560]{1,0:T(8,128)S(1)} %add.192), channel_id=1, source_target_pairs={{0,4},{1,5},{2,6},{3,7},{4,0},{5,1},{6,2},{7,3},{8,12},{9,13},{10,... | collective-permute-start | bytes 245768 | tf_op jit(solution)/shard_map/ppermute | solution.py:156
  73.4 0.6 copy-start.5
  81.3 69.1 %all-to-all-start.1 = ((bf16[16,544,256]{2,1,0:T(8,128)(2,1)}), bf16[16,544,256]{2,1,0:T(8,128)(2,1)}, u32[]{:S(2)}, u32[]{:S(2)}) async-start(bf16[16,544,256]{2,1,0:T(8,128)(2,1)} %broadcast_dynamic-update-slice_fusion), calls=%async_computation.1 | async-start | bytes 8912896 | tf_op jit(solution)/shard_map/all_to_all | solution.py:189
  86.8 64.9 %copy-start.9 = (bf16[320,608]{1,0:T(8,128)(2,1)S(1)}, bf16[320,608]{1,0:T(8,128)(2,1)}, u32[]{:S(2)}) copy-start(bf16[320,608]{1,0:T(8,128)(2,1)} %param.26) | copy-start | bytes 1167364
  153.9 17.0 %all-to-all-start.2 = ((f32[8,16,1216]{2,1,0:T(8,128)}), f32[8,16,1216]{2,1,0:T(8,128)S(1)}, u32[]{:S(2)}, u32[]{:S(2)}) async-start(f32[8,16,1216]{2,1,0:T(8,128)} %bitcast.86), calls=%async_computation.2 | async-start | bytes 1310720 | tf_op jit(solution)/shard_map/all_to_all | solution.py:220
  171.0 10.6 %copy-start.4 = (bf16[608,320]{0,1:T(8,128)(2,1)S(1)}, bf16[608,320]{0,1:T(8,128)(2,1)}, u32[]{:S(2)}) copy-start(bf16[608,320]{0,1:T(8,128)(2,1)} %param.27) | copy-start | bytes 1167364
  171.8 9.8 %all-to-all-start.3 = ((bf16[8,16,608]{2,1,0:T(8,128)(2,1)}), bf16[8,16,608]{2,1,0:T(8,128)(2,1)S(1)}, u32[]{:S(2)}, u32[]{:S(2)}) async-start(bf16[8,16,608]{2,1,0:T(8,128)(2,1)} %broadcast_in_dim.143), calls=%async_computation.3 | async-start | bytes 327680 | tf_op jit(solution)/shard_map/all_to_all | solution.py:232
  182.5 12.8 %all-to-all-start.4 = ((f32[16,8,320]{2,1,0:T(8,128)}), f32[16,8,320]{2,1,0:T(8,128)S(1)}, u32[]{:S(2)}, u32[]{:S(2)}) async-start(f32[16,8,320]{2,1,0:T(8,128)} %fusion.14), calls=%async_computation.4 | async-start | bytes 393216 | tf_op jit(solution)/shard_map/all_to_all | solution.py:241

commit v10 on v9

--- a/solution.py
+++ b/solution.py
@@ -111,7 +111,10 @@
     picked_pages = page_table[picked]
     first_pages = pages_per // 2
     second_pages = pages_per - first_pages
-    parcels_first = kv_pool[picked_pages[:, :first_pages]]
+    first_span = first_pages * page_len
+    parcels_first = kv_pool[picked_pages[:, :first_pages]].reshape(
+        devices_req, first_span, channels
+    )
     received_first = lax.all_to_all(
         parcels_first, "req", split_axis=0, concat_axis=0, tiled=True
     )
@@ -190,12 +193,13 @@
         second_buffer, "req", split_axis=0, concat_axis=0, tiled=True
     )
     lengths_new = lengths[arriving]
-    first_span = first_pages * page_len
-    span_first = received_first.reshape(devices_req, first_span, channels)[source_owner]
     span_first = jnp.where(
         jnp.arange(first_span, dtype=jnp.int32)[None, :, None] < lengths_new[:, None, None],
-        span_first,
+        received_first[source_owner],
         jnp.zeros((), jnp.bfloat16),
+    )
+    span_first = jnp.concatenate(
+        [span_first, jnp.zeros((row_count, second_span, channels), jnp.bfloat16)], axis=1
     )
     span_first, received_second = lax.optimization_barrier((span_first, received_second))
     span_second = received_second[source_owner][:, :second_span, :]
@@ -249,7 +253,7 @@
     )
     result = (residual_wide + lowered).astype(jnp.bfloat16)
 
-    new_seq = jnp.concatenate([span_first, span_second], axis=1)
+    new_seq = lax.dynamic_update_slice(span_first, span_second, (0, first_span, 0))
     new_seq = new_seq.at[jnp.arange(row_count), lengths_new].set(
         fresh_all[arriving].reshape(row_count, channels)
     )

time: 198 us -> 197 us (level)
  blocking collectives: 14 us -> 30.9 us
  waiting for transfers between devices: 78.5 us -> 70 us
  other arithmetic: 24 us -> 18.4 us
  starting transfers between devices: 29.8 us -> 24.5 us
  local copies, waits for them, and re-layouts: 37.4 us -> 39.7 us
    all_to_all x0 -> x1, blocking collectives: none -> 16.9 us  [per_device(): lax.all_to_all(partial_both.reshape(devices_kvh, group_rows, 2 * ffn_widt...]
    all_to_all x1 -> x0, waiting for transfers between devices: 7.4 us -> none  [per_device(): lax.all_to_all(partial_both.reshape(devices_kvh, group_rows, 2 * ffn_widt...]
    all_to_all x1 -> x0, starting transfers between devices: 5.31 us -> none  [per_device(): lax.all_to_all(partial_both.reshape(devices_kvh, group_rows, 2 * ffn_widt...]
    concatenate x1 -> x0, other arithmetic: 4.51 us -> none  [per_device(): new_seq = jnp.concatenate([span_first, span_second], axis=1)]
    select_n x1 -> x0, other arithmetic: 2.97 us -> none  [per_device(): jnp.where(first_span + jnp.arange(second_span, dtype=jnp.int32)[None, :,...]
    dynamic_update_slice x0 -> x1, other arithmetic: none -> 2.91 us  [per_device(): lax.dynamic_update_slice(span_first, span_second, (0, first_span, 0))]
    concatenate x0 -> x1, local copies, waits for them, and re-layouts: none -> 2.33 us  [per_device(): jnp.concatenate([span_first, jnp.zeros((row_count, second_span, channels)...]
  transfers between devices with their start and end apart: 8 -> 7, of which waited for: 7 -> 6; matrix products, arithmetic and copies ran while one was open for 28% -> 27% of each run, Pallas kernels for 0% -> 0%
where the time goes in v10:
time: 197 us; the launch traced here: 196 us
  waiting for transfers between devices  70 us (36%)
  local copies, waits for them, and re-layouts  39.7 us (20%)
  blocking collectives  30.9 us (16%)
  starting transfers between devices  24.5 us (12%)
  other arithmetic  18.4 us (9%)
  matrix products  11.2 us (6%)
    all_to_all x1, waiting for transfers between devices, per_device(): lax.all_to_all(second_buffer, 'req', split_axis=0, concat_axis=0, tiled=T...  55.1 us
    all_to_all x1, blocking collectives, per_device(): lax.all_to_all(partial_both.reshape(devices_kvh, group_rows, 2 * ffn_widt...  16.9 us
    all_gather x1, blocking collectives, per_device(): full_states = lax.all_gather(states, 'kvh', axis=1, tiled=True)  14 us
    select_n x1, other arithmetic, mask_blocks(): jnp.where(kept, blocks, jnp.where(placed, fresh[:, None, :, None, :], jnp...  7.64 us
    all_to_all x1, starting transfers between devices, per_device(): lax.all_to_all(parcels_first, 'req', split_axis=0, concat_axis=0, tiled=T...  7.34 us
    all_to_all x1, waiting for transfers between devices, per_device(): lax.all_to_all(parcels_first, 'req', split_axis=0, concat_axis=0, tiled=T...  6.25 us
    gather x1, local copies, waits for them, and re-layouts, per_device(): home_blocks = mask_blocks(kv_pool[page_table], positions_home, fresh)  5.02 us
    gather x1, local copies, waits for them, and re-layouts, per_device(): kv_pool[picked_pages[:, first_pages:]]  5.01 us
  transfers between devices with their start and end apart: 7, of which 6 were waited for; matrix products, arithmetic and copies ran while one was open for 27% of the time, Pallas kernels for 0%

profile of v10, /device:TPU:0, one launch (start us, length us, event | category | flops | bytes accessed | tf_op | source)
XLA Modules:
  0.0 195.7 jit_solution(14347031522312614849)
XLA Ops:
  0.7 1.5 iota_reduce_fusion.1
  3.5 1.2 gather_fusion.3
  4.9 4.9 %gather_fusion.4 = bf16[64,128,256]{2,1,0:T(8,128)(2,1)} fusion(bf16[64,128,256]{2,1,0:T(8,128)(2,1)} %bitcast.77, s32[1024]{0:T(1024)S(1)} %pad_clamp_fusion.2), kind=kCustom, calls=%fused_computation.4 | custom fusion | bytes 8388864 | tf_op jit(solution)/shard_map/gather | solution.py:115
  9.9 7.3 %all-to-all-start = ((bf16[16,512,256]{2,1,0:T(8,128)(2,1)}), bf16[16,512,256]{2,1,0:T(8,128)(2,1)}, u32[]{:S(2)}, u32[]{:S(2)}) async-start(bf16[16,512,256]{2,1,0:T(8,128)(2,1)} %bitcast.80), calls=%async_computation | async-start | bytes 8388608 | tf_op jit(solution)/shard_map/all_to_all | solution.py:118
  17.3 14.0 %all-gather = bf16[8,320,8]{1,2,0:T(8,128)(2,1)S(1)} all-gather(bf16[1,320,8]{1,2,0:T(8,128)(2,1)S(1)} %bitcast.88), channel_id=1, replica_groups=mesh['req'=16,'kvh'=8] {'kvh'}, dimensions={0}, use_global_device_ids=true | all-gather | bytes 46080 | tf_op jit(solution)/shard_map/all_gather | solution.py:128
  32.7 1.3 fusion.10
  34.1 5.0 %gather_fusion.1 = bf16[64,128,256]{2,1,0:T(8,128)(2,1)} fusion(bf16[64,128,256]{2,1,0:T(8,128)(2,1)} %bitcast.78, s32[1024]{0:T(1024)S(1)} %pad_clamp_fusion.5), kind=kCustom, calls=%fused_computation.1 | custom fusion | bytes 8388864 | tf_op jit(solution)/shard_map/gather | solution.py:149
  39.1 2.3 %multiply_reduce_fusion.1 = (f32[8,4]{0,1:T(4,128)S(1)}, f32[8,4,128]{2,0,1:T(8,128)S(1)}) fusion(bf16[8,2560]{1,0:T(8,128)(2,1)S(1)} %fusion.20, bf16[2560,512]{1,0:T(8,128)(2,1)} %param.18), kind=kOutput, calls=%fused_computation.59 | convolution fusion | flops 20979680 | bytes 2678912 | tf_op jit(solution)/shard_map/dot_general | solution.py:132
  42.2 7.6 %select_select_fusion = bf16[8,1,1024,256]{3,2,0,1:T(8,128)(2,1)} fusion(bf16[8,1,1024,256]{3,2,0,1:T(8,128)(2,1)} %bitcast.82, pred[8,1024]{1,0:T(8,128)(4,1)S(1)} %get-tuple-element.23, pred[8,1024]{1,0:T(8,128)(4,1)S(1)} %get-tuple-element.22, bf16[8,256]{1,0:T(8,128)(2,1)S(1)} %maximum_bitcast_fusion), kind=kLoop, calls=%fused_computation.11 | loop fusion | flops 4194304 | bytes 8409088 | tf_op jit(solution)/shard_map/jit(_where)/select_n | solution.py:48
  49.9 2.5 %fusion.47 = (f32[8,4]{1,0:T(8,128)S(1)}, f32[8,4,1024]{2,1,0:T(4,128)S(1)}) fusion(bf16[8,1,1024,256]{3,2,0,1:T(8,128)(2,1)} %select_select_fusion, pred[8,1024]{1,0:T(8,128)(4,1)S(1)} %get-tuple-element.28, bf16[8,4,64]{2,1,0:T(4,128)(2,1)S(1)} %get-tuple-element.17, bf16[8,4,64]{2,1,0:T(4,128)(2,1)S(1)} %get-tuple-element.16), kind=kOutput, calls=%fused_computation.127 | convolution fusion | flops 8537087 | bytes 2244736 | tf_op jit(solution)/shard_map/sub | solution.py:67
  52.3 2.0 %fusion.9 = bf16[1,8,4,128]{3,2,1,0:T(4,128)(2,1)S(1)} fusion(bf16[8,1,1024,256]{3,2,0,1:T(8,128)(2,1)} %select_select_fusion, f32[8,4,1024]{2,1,0:T(4,128)S(1)} %get-tuple-element.36, f32[8,4]{1,0:T(8,128)S(1)} %get-tuple-element.35), kind=kOutput, calls=%fused_computation.25 | convolution fusion | flops 8458240 | bytes 2236544 | tf_op jit(solution)/shard_map/rkgt,rktd->rkgd/dot_general | solution.py:68
  56.1 1.7 collective-permute-start.1
  57.9 3.0 %collective-permute-done.1 = f32[8,2560]{1,0:T(8,128)S(1)} collective-permute-done((f32[8,2560]{1,0:T(8,128)S(1)}, f32[8,2560]{1,0:T(8,128)S(1)}, u32[]{:S(2)}, u32[]{:S(2)}) %collective-permute-start.1) | collective-permute-done | bytes 81952 | tf_op jit(solution)/shard_map/ppermute | solution.py:159
  60.9 2.6 %collective-permute-start.2 = (f32[8,2560]{1,0:T(8,128)S(1)}, f32[8,2560]{1,0:T(8,128)S(1)}, u32[]{:S(2)}, u32[]{:S(2)}) collective-permute-start(f32[8,2560]{1,0:T(8,128)S(1)} %add.194), channel_id=1, source_target_pairs={{0,4},{1,5},{2,6},{3,7},{4,0},{5,1},{6,2},{7,3},{8,12},{9,13},{10,... | collective-permute-start | bytes 245768 | tf_op jit(solution)/shard_map/ppermute | solution.py:159
  63.6 5.0 %gather_fusion.5 = bf16[64,128,256]{2,1,0:T(8,128)(2,1)} fusion(bf16[64,128,256]{2,1,0:T(8,128)(2,1)} %bitcast.79, s32[1024]{0:T(1024)S(1)} %pad_clamp_fusion.1), kind=kCustom, calls=%fused_computation.5 | custom fusion | bytes 8388864 | tf_op jit(solution)/shard_map/gather | solution.py:122
  68.6 4.7 %concatenate.37 = bf16[16,544,256]{2,1,0:T(8,128)(2,1)} pad(bf16[16,512,256]{2,1,0:T(8,128)(2,1)} %bitcast.81, bf16[]{:T(256)} %constant.44.clone.1), padding=0_0x0_32x0_0 | pad | bytes 8650754 | tf_op jit(solution)/shard_map/concatenate | solution.py:178
  74.3 6.2 %all-to-all-done = bf16[16,512,256]{2,1,0:T(8,128)(2,1)} async-done(((bf16[16,512,256]{2,1,0:T(8,128)(2,1)}), bf16[16,512,256]{2,1,0:T(8,128)(2,1)}, u32[]{:S(2)}, u32[]{:S(2)}) %all-to-all-start) | async-done | bytes 4194336 | tf_op jit(solution)/shard_map/all_to_all | solution.py:118
  81.3 4.7 %all-to-all-start.1 = ((bf16[16,544,256]{2,1,0:T(8,128)(2,1)}), bf16[16,544,256]{2,1,0:T(8,128)(2,1)}, u32[]{:S(2)}, u32[]{:S(2)}) async-start(bf16[16,544,256]{2,1,0:T(8,128)(2,1)} %broadcast_dynamic-update-slice_fusion), calls=%async_computation.1 | async-start | bytes 8912896 | tf_op jit(solution)/shard_map/all_to_all | solution.py:192
  86.8 4.2 %gather_fusion.6 = bf16[8,512,256]{2,1,0:T(8,128)(2,1)} fusion(bf16[16,512,256]{2,1,0:T(8,128)(2,1)} %all-to-all-done, s32[1024]{0:T(1024)S(1)} %pad_clamp_fusion), kind=kCustom, calls=%fused_computation.6 | custom fusion | bytes 4194336 | tf_op jit(solution)/shard_map/gather | solution.py:198
  90.9 1.9 broadcast_select_fusion
  92.9 2.3 %concatenate.38 = bf16[8,1024,256]{2,1,0:T(8,128)(2,1)} pad(bf16[8,512,256]{2,1,0:T(8,128)(2,1)S(1)} %broadcast_select_fusion, bf16[]{:T(256)} %constant.44.clone.1), padding=0_0x0_512x0_0 | pad | bytes 6291458 | tf_op jit(solution)/shard_map/concatenate | solution.py:201
  95.2 55.1 %all-to-all-done.1 = bf16[16,544,256]{2,1,0:T(8,128)(2,1)} async-done(((bf16[16,544,256]{2,1,0:T(8,128)(2,1)}), bf16[16,544,256]{2,1,0:T(8,128)(2,1)}, u32[]{:S(2)}, u32[]{:S(2)}) %all-to-all-start.1) | async-done | bytes 4456480 | tf_op jit(solution)/shard_map/all_to_all | solution.py:192
  151.7 1.4 fusion.11
  153.1 16.9 %all_to_all.25 = f32[8,16,1216]{2,1,0:T(8,128)S(1)} all-to-all(f32[8,16,1216]{2,1,0:T(8,128)S(1)} %bitcast.85), channel_id=1, replica_groups=mesh['req'=16,'kvh'=8] {'kvh'}, dimensions={0} | all-to-all | bytes 1245184 | tf_op jit(solution)/shard_map/all_to_all | solution.py:224
  170.8 3.4 %all-to-all-start.3 = ((bf16[8,16,608]{2,1,0:T(8,128)(2,1)}), bf16[8,16,608]{2,1,0:T(8,128)(2,1)S(1)}, u32[]{:S(2)}, u32[]{:S(2)}) async-start(bf16[8,16,608]{2,1,0:T(8,128)(2,1)} %broadcast_in_dim.144), calls=%async_computation.3 | async-start | bytes 327680 | tf_op jit(solution)/shard_map/all_to_all | solution.py:236
  174.2 4.3 %gather_fusion.7 = bf16[8,544,256]{2,1,0:T(8,128)(2,1)} fusion(bf16[16,544,256]{2,1,0:T(8,128)(2,1)} %all-to-all-done.1, s32[1024]{0:T(1024)S(1)} %pad_clamp_fusion), kind=kCustom, calls=%fused_computation.7 | custom fusion | bytes 4456480 | tf_op jit(solution)/shard_map/gather | solution.py:205
  178.5 2.0 %all-to-all-done.3 = bf16[8,16,608]{2,1,0:T(8,128)(2,1)S(1)} async-done(((bf16[8,16,608]{2,1,0:T(8,128)(2,1)}), bf16[8,16,608]{2,1,0:T(8,128)(2,1)S(1)}, u32[]{:S(2)}, u32[]{:S(2)}) %all-to-all-start.3) | async-done | bytes 155680 | tf_op jit(solution)/shard_map/all_to_all | solution.py:236
  181.5 4.4 %all-to-all-start.4 = ((f32[16,8,320]{2,1,0:T(8,128)}), f32[16,8,320]{2,1,0:T(8,128)S(1)}, u32[]{:S(2)}, u32[]{:S(2)}) async-start(f32[16,8,320]{2,1,0:T(8,128)} %fusion.15), calls=%async_computation.4 | async-start | bytes 393216 | tf_op jit(solution)/shard_map/all_to_all | solution.py:245
  185.9 2.9 %fusion.1 = bf16[8,1024,256]{2,1,0:T(8,128)(2,1)} fusion(bf16[8,1024,256]{2,1,0:T(8,128)(2,1)} %concatenate.38, bf16[8,544,256]{2,1,0:T(8,128)(2,1)} %gather_fusion.7, pred[8,512]{1,0:T(8,128)(4,1)S(1)} %get-tuple-element.26), kind=kLoop, calls=%fused_computation.13 | loop fusion | flops 1048576 | bytes 4198400 | tf_op jit(solution)/shard_map/dynamic_update_slice | solution.py:256
  189.5 2.1 %scatter_fusion = bf16[8,1024,256]{2,1,0:T(8,128)(2,1)} fusion(bf16[8,1024,256]{2,1,0:T(8,128)(2,1)} %fusion.1, s32[8]{0:T(128)S(1)} %fusion.42, bf16[8,256]{1,0:T(8,128)(2,1)S(1)} %gather_fusion.8), kind=kCustom, calls=%fused_computation.9 | custom fusion | bytes 12352 | tf_op jit(solution)/shard_map/scatter | solution.py:257
  191.6 2.7 %all-to-all-done.4 = f32[16,8,320]{2,1,0:T(8,128)S(1)} async-done(((f32[16,8,320]{2,1,0:T(8,128)}), f32[16,8,320]{2,1,0:T(8,128)S(1)}, u32[]{:S(2)}, u32[]{:S(2)}) %all-to-all-start.4) | async-done | bytes 163872 | tf_op jit(solution)/shard_map/all_to_all | solution.py:245
  194.3 1.4 add_convert_fusion.1
  (95 shorter events, 11.9 us)
Async XLA Ops:
  0.6 53.7 %copy-start = (bf16[512,2560]{1,0:T(8,128)(2,1)S(1)}, bf16[512,2560]{1,0:T(8,128)(2,1)}, u32[]{:S(2)}) copy-start(bf16[512,2560]{1,0:T(8,128)(2,1)} %param.23) | copy-start | bytes 7864324
  9.9 7.4 %copy-start.2 = (s32[8,8]{1,0:T(8,128)S(1)}, s32[8,8]{1,0:T(8,128)}, u32[]{:S(2)}) copy-start(s32[8,8]{1,0:T(8,128)} %param.30) | copy-start | bytes 772
  9.9 7.4 %copy-start.6 = (bf16[8,320]{1,0:T(8,128)(2,1)S(1)}, bf16[8,320]{1,0:T(8,128)(2,1)}, u32[]{:S(2)}) copy-start(bf16[8,320]{1,0:T(8,128)(2,1)} %param.16) | copy-start | bytes 15364
  9.9 21.7 %copy-start.7 = (bf16[2560]{0:T(1024)(128)(2,1)S(1)}, bf16[2560]{0:T(1024)(128)(2,1)}, u32[]{:S(2)}) copy-start(bf16[2560]{0:T(1024)(128)(2,1)} %param.17) | copy-start | bytes 15364
  9.9 21.8 %copy-start.3 = (bf16[2560,128]{1,0:T(8,128)(2,1)S(1)}, bf16[2560,128]{1,0:T(8,128)(2,1)}, u32[]{:S(2)}) copy-start(bf16[2560,128]{1,0:T(8,128)(2,1)} %param.19) | copy-start | bytes 1966084
  9.9 22.1 %copy-start.10 = (bf16[128]{0:T(256)(128)(2,1)S(1)}, bf16[128]{0:T(256)(128)(2,1)}, u32[]{:S(2)}) copy-start(bf16[128]{0:T(256)(128)(2,1)} %param.22) | copy-start | bytes 772
  9.9 22.2 %copy-start.1 = (s32[128]{0:T(128)S(1)}, s32[128]{0:T(128)}, u32[]{:S(2)}) copy-start(s32[128]{0:T(128)} %param.29) | copy-start | bytes 1540
  9.9 70.6 %all-to-all-start = ((bf16[16,512,256]{2,1,0:T(8,128)(2,1)}), bf16[16,512,256]{2,1,0:T(8,128)(2,1)}, u32[]{:S(2)}, u32[]{:S(2)}) async-start(bf16[16,512,256]{2,1,0:T(8,128)(2,1)} %bitcast.80), calls=%async_computation | async-start | bytes 8388608 | tf_op jit(solution)/shard_map/all_to_all | solution.py:118
  34.1 7.4 %copy-start.11 = (bf16[128]{0:T(256)(128)(2,1)S(1)}, bf16[128]{0:T(256)(128)(2,1)}, u32[]{:S(2)}) copy-start(bf16[128]{0:T(256)(128)(2,1)} %param.21) | copy-start | bytes 772
  49.9 7.9 %copy-start.8 = (bf16[320]{0:T(512)(128)(2,1)S(1)}, bf16[320]{0:T(512)(128)(2,1)}, u32[]{:S(2)}) copy-start(bf16[320]{0:T(512)(128)(2,1)} %param.24) | copy-start | bytes 1924
  54.8 1.3 collective-permute-start
  56.1 4.8 %collective-permute-start.1 = (f32[8,2560]{1,0:T(8,128)S(1)}, f32[8,2560]{1,0:T(8,128)S(1)}, u32[]{:S(2)}, u32[]{:S(2)}) collective-permute-start(f32[8,2560]{1,0:T(8,128)S(1)} %add.193), channel_id=1, source_target_pairs={{0,2},{1,3},{2,0},{3,1},{4,6},{5,7},{6,4},{7,5},{8,10},{9,11},{10,... | collective-permute-start | bytes 245768 | tf_op jit(solution)/shard_map/ppermute | solution.py:159
  60.9 12.3 %collective-permute-start.2 = (f32[8,2560]{1,0:T(8,128)S(1)}, f32[8,2560]{1,0:T(8,128)S(1)}, u32[]{:S(2)}, u32[]{:S(2)}) collective-permute-start(f32[8,2560]{1,0:T(8,128)S(1)} %add.194), channel_id=1, source_target_pairs={{0,4},{1,5},{2,6},{3,7},{4,0},{5,1},{6,2},{7,3},{8,12},{9,13},{10,... | collective-permute-start | bytes 245768 | tf_op jit(solution)/shard_map/ppermute | solution.py:159
  73.4 0.6 copy-start.5
  81.3 69.1 %all-to-all-start.1 = ((bf16[16,544,256]{2,1,0:T(8,128)(2,1)}), bf16[16,544,256]{2,1,0:T(8,128)(2,1)}, u32[]{:S(2)}, u32[]{:S(2)}) async-start(bf16[16,544,256]{2,1,0:T(8,128)(2,1)} %broadcast_dynamic-update-slice_fusion), calls=%async_computation.1 | async-start | bytes 8912896 | tf_op jit(solution)/shard_map/all_to_all | solution.py:192
  92.9 58.8 %copy-start.9 = (bf16[320,608]{1,0:T(8,128)(2,1)S(1)}, bf16[320,608]{1,0:T(8,128)(2,1)}, u32[]{:S(2)}) copy-start(bf16[320,608]{1,0:T(8,128)(2,1)} %param.26) | copy-start | bytes 1167364
  170.0 10.5 %copy-start.4 = (bf16[608,320]{0,1:T(8,128)(2,1)S(1)}, bf16[608,320]{0,1:T(8,128)(2,1)}, u32[]{:S(2)}) copy-start(bf16[608,320]{0,1:T(8,128)(2,1)} %param.27) | copy-start | bytes 1167364
  170.8 9.8 %all-to-all-start.3 = ((bf16[8,16,608]{2,1,0:T(8,128)(2,1)}), bf16[8,16,608]{2,1,0:T(8,128)(2,1)S(1)}, u32[]{:S(2)}, u32[]{:S(2)}) async-start(bf16[8,16,608]{2,1,0:T(8,128)(2,1)} %broadcast_in_dim.144), calls=%async_computation.3 | async-start | bytes 327680 | tf_op jit(solution)/shard_map/all_to_all | solution.py:236
  181.5 12.8 %all-to-all-start.4 = ((f32[16,8,320]{2,1,0:T(8,128)}), f32[16,8,320]{2,1,0:T(8,128)S(1)}, u32[]{:S(2)}, u32[]{:S(2)}) async-start(f32[16,8,320]{2,1,0:T(8,128)} %fusion.15), calls=%async_computation.4 | async-start | bytes 393216 | tf_op jit(solution)/shard_map/all_to_all | solution.py:245

commit v11 on v10

--- a/solution.py
+++ b/solution.py
@@ -103,12 +103,18 @@
     total_rows = new_order.shape[0]
 
     home = my_index * row_count + jnp.arange(row_count, dtype=jnp.int32)
-    new_slot = jnp.argmax((new_order[None, :] == home[:, None]).astype(jnp.int32), axis=1)
+    new_slot = jnp.sum(
+        jnp.where(
+            new_order[None, :] == home[:, None],
+            jnp.arange(total_rows, dtype=jnp.int32)[None, :],
+            0,
+        ),
+        axis=1,
+    )
     destination = new_slot // row_count
     peer_ids = jnp.arange(devices_req, dtype=jnp.int32)
     matches = destination[None, :] == peer_ids[:, None]
-    picked = jnp.argmax(matches.astype(jnp.int32), axis=1)
-    picked_pages = page_table[picked]
+    picked_pages = jnp.sum(jnp.where(matches[:, :, None], page_table[None, :, :], 0), axis=1)
     first_pages = pages_per // 2
     second_pages = pages_per - first_pages
     first_span = first_pages * page_len
@@ -222,12 +228,12 @@
     group_rows = total_rows // devices_kvh
     summed = jnp.sum(
         lax.all_to_all(
-            partial_both.reshape(devices_kvh, group_rows, 2 * ffn_width),
+            partial_both.astype(jnp.bfloat16).reshape(devices_kvh, group_rows, 2 * ffn_width),
             "kvh",
             split_axis=0,
             concat_axis=0,
             tiled=True,
-        ),
+        ).astype(jnp.float32),
         axis=0,
     )
     hidden_part = (jax.nn.silu(summed[:, :ffn_width]) * summed[:, ffn_width:]).astype(

time: 197 us -> 194 us (0.985)
  blocking collectives: 30.9 us -> 27.4 us
    all_to_all x1, blocking collectives: 16.9 us -> 13.3 us  [per_device(): lax.all_to_all(partial_both.astype(jnp.bfloat16).reshape(devices_kvh, gro...]
    another operation x4 -> x2, other arithmetic: 2.31 us -> 0.21 us  [the longest x1 1.5 us: per_device(): jnp.argmax((new_order[None, :] == home[:, None]).astype(jnp.int32), axis=1)]
where the time goes in v11:
time: 194 us; the launch traced here: 193 us
  waiting for transfers between devices  69.9 us (36%)
  local copies, waits for them, and re-layouts  39.8 us (21%)
  blocking collectives  27.4 us (14%)
  starting transfers between devices  24.5 us (13%)
  other arithmetic  18 us (9%)
  matrix products  12.5 us (6%)
    all_to_all x1, waiting for transfers between devices, per_device(): lax.all_to_all(second_buffer, 'req', split_axis=0, concat_axis=0, tiled=T...  55.1 us
    all_gather x1, blocking collectives, per_device(): full_states = lax.all_gather(states, 'kvh', axis=1, tiled=True)  14 us
    all_to_all x1, blocking collectives, per_device(): lax.all_to_all(partial_both.astype(jnp.bfloat16).reshape(devices_kvh, gro...  13.3 us
    select_n x1, other arithmetic, mask_blocks(): jnp.where(kept, blocks, jnp.where(placed, fresh[:, None, :, None, :], jnp...  7.64 us
    all_to_all x1, starting transfers between devices, per_device(): lax.all_to_all(parcels_first, 'req', split_axis=0, concat_axis=0, tiled=T...  7.34 us
    all_to_all x1, waiting for transfers between devices, per_device(): lax.all_to_all(parcels_first, 'req', split_axis=0, concat_axis=0, tiled=T...  6.24 us
    gather x1, local copies, waits for them, and re-layouts, per_device(): home_blocks = mask_blocks(kv_pool[page_table], positions_home, fresh)  5.02 us
    gather x1, local copies, waits for them, and re-layouts, per_device(): kv_pool[picked_pages[:, first_pages:]]  5.01 us
  transfers between devices with their start and end apart: 7, of which 6 were waited for; matrix products, arithmetic and copies ran while one was open for 27% of the time, Pallas kernels for 0%

profile of v11, /device:TPU:0, one launch (start us, length us, event | category | flops | bytes accessed | tf_op | source)
XLA Modules:
  0.0 193.0 jit_solution(11261501397276235209)
XLA Ops:
  0.7 1.0 select_reduce_fusion.1
  3.4 4.9 %gather_fusion.3 = bf16[64,128,256]{2,1,0:T(8,128)(2,1)} fusion(bf16[64,128,256]{2,1,0:T(8,128)(2,1)} %bitcast.77, s32[1024]{0:T(1024)S(1)} %pad_clamp_fusion.2), kind=kCustom, calls=%fused_computation.3 | custom fusion | bytes 8388864 | tf_op jit(solution)/shard_map/gather | solution.py:121
  8.4 7.3 %all-to-all-start = ((bf16[16,512,256]{2,1,0:T(8,128)(2,1)}), bf16[16,512,256]{2,1,0:T(8,128)(2,1)}, u32[]{:S(2)}, u32[]{:S(2)}) async-start(bf16[16,512,256]{2,1,0:T(8,128)(2,1)} %bitcast.80), calls=%async_computation | async-start | bytes 8388608 | tf_op jit(solution)/shard_map/all_to_all | solution.py:124
  15.8 14.0 %all-gather = bf16[8,320,8]{1,2,0:T(8,128)(2,1)S(1)} all-gather(bf16[1,320,8]{1,2,0:T(8,128)(2,1)S(1)} %bitcast.88), channel_id=1, replica_groups=mesh['req'=16,'kvh'=8] {'kvh'}, dimensions={0}, use_global_device_ids=true | all-gather | bytes 46080 | tf_op jit(solution)/shard_map/all_gather | solution.py:134
  31.2 1.3 fusion.10
  32.6 5.0 %gather_fusion.1 = bf16[64,128,256]{2,1,0:T(8,128)(2,1)} fusion(bf16[64,128,256]{2,1,0:T(8,128)(2,1)} %bitcast.78, s32[1024]{0:T(1024)S(1)} %pad_clamp_fusion.4), kind=kCustom, calls=%fused_computation.1 | custom fusion | bytes 8388864 | tf_op jit(solution)/shard_map/gather | solution.py:155
  37.6 2.3 %multiply_reduce_fusion.1 = (f32[8,4]{0,1:T(4,128)S(1)}, f32[8,4,128]{2,0,1:T(8,128)S(1)}) fusion(bf16[8,2560]{1,0:T(8,128)(2,1)S(1)} %fusion.19, bf16[2560,512]{1,0:T(8,128)(2,1)} %param.18), kind=kOutput, calls=%fused_computation.58 | convolution fusion | flops 20979680 | bytes 2678912 | tf_op jit(solution)/shard_map/dot_general | solution.py:138
  40.7 7.6 %select_select_fusion = bf16[8,1,1024,256]{3,2,0,1:T(8,128)(2,1)} fusion(bf16[8,1,1024,256]{3,2,0,1:T(8,128)(2,1)} %bitcast.82, pred[8,1024]{1,0:T(8,128)(4,1)S(1)} %get-tuple-element.17, pred[8,1024]{1,0:T(8,128)(4,1)S(1)} %get-tuple-element.16, bf16[8,256]{1,0:T(8,128)(2,1)S(1)} %maximum_bitcast_fusion), kind=kLoop, calls=%fused_computation.10 | loop fusion | flops 4194304 | bytes 8409088 | tf_op jit(solution)/shard_map/jit(_where)/select_n | solution.py:48
  48.4 2.5 %fusion.46 = (f32[8,4]{1,0:T(8,128)S(1)}, f32[8,4,1024]{2,1,0:T(4,128)S(1)}) fusion(bf16[8,1,1024,256]{3,2,0,1:T(8,128)(2,1)} %select_select_fusion, pred[8,1024]{1,0:T(8,128)(4,1)S(1)} %get-tuple-element.24, bf16[8,4,64]{2,1,0:T(4,128)(2,1)S(1)} %get-tuple-element.13, bf16[8,4,64]{2,1,0:T(4,128)(2,1)S(1)} %get-tuple-element.12), kind=kOutput, calls=%fused_computation.125 | convolution fusion | flops 8537087 | bytes 2244736 | tf_op jit(solution)/shard_map/sub | solution.py:67
  50.8 2.0 %fusion.9 = bf16[1,8,4,128]{3,2,1,0:T(4,128)(2,1)S(1)} fusion(bf16[8,1,1024,256]{3,2,0,1:T(8,128)(2,1)} %select_select_fusion, f32[8,4,1024]{2,1,0:T(4,128)S(1)} %get-tuple-element.32, f32[8,4]{1,0:T(8,128)S(1)} %get-tuple-element.31), kind=kOutput, calls=%fused_computation.25 | convolution fusion | flops 8458240 | bytes 2236544 | tf_op jit(solution)/shard_map/rkgt,rktd->rkgd/dot_general | solution.py:68
  54.6 1.7 collective-permute-start.1
  56.5 2.9 %collective-permute-done.1 = f32[8,2560]{1,0:T(8,128)S(1)} collective-permute-done((f32[8,2560]{1,0:T(8,128)S(1)}, f32[8,2560]{1,0:T(8,128)S(1)}, u32[]{:S(2)}, u32[]{:S(2)}) %collective-permute-start.1) | collective-permute-done | bytes 81952 | tf_op jit(solution)/shard_map/ppermute | solution.py:165
  59.4 2.6 %collective-permute-start.2 = (f32[8,2560]{1,0:T(8,128)S(1)}, f32[8,2560]{1,0:T(8,128)S(1)}, u32[]{:S(2)}, u32[]{:S(2)}) collective-permute-start(f32[8,2560]{1,0:T(8,128)S(1)} %add.197), channel_id=1, source_target_pairs={{0,4},{1,5},{2,6},{3,7},{4,0},{5,1},{6,2},{7,3},{8,12},{9,13},{10,... | collective-permute-start | bytes 245768 | tf_op jit(solution)/shard_map/ppermute | solution.py:165
  62.1 5.0 %gather_fusion.4 = bf16[64,128,256]{2,1,0:T(8,128)(2,1)} fusion(bf16[64,128,256]{2,1,0:T(8,128)(2,1)} %bitcast.79, s32[1024]{0:T(1024)S(1)} %pad_clamp_fusion.1), kind=kCustom, calls=%fused_computation.4 | custom fusion | bytes 8388864 | tf_op jit(solution)/shard_map/gather | solution.py:128
  67.1 4.7 %concatenate.37 = bf16[16,544,256]{2,1,0:T(8,128)(2,1)} pad(bf16[16,512,256]{2,1,0:T(8,128)(2,1)} %bitcast.81, bf16[]{:T(256)} %constant.38.clone.1), padding=0_0x0_32x0_0 | pad | bytes 8650754 | tf_op jit(solution)/shard_map/concatenate | solution.py:184
  72.8 6.2 %all-to-all-done = bf16[16,512,256]{2,1,0:T(8,128)(2,1)} async-done(((bf16[16,512,256]{2,1,0:T(8,128)(2,1)}), bf16[16,512,256]{2,1,0:T(8,128)(2,1)}, u32[]{:S(2)}, u32[]{:S(2)}) %all-to-all-start) | async-done | bytes 4194336 | tf_op jit(solution)/shard_map/all_to_all | solution.py:124
  79.8 4.7 %all-to-all-start.1 = ((bf16[16,544,256]{2,1,0:T(8,128)(2,1)}), bf16[16,544,256]{2,1,0:T(8,128)(2,1)}, u32[]{:S(2)}, u32[]{:S(2)}) async-start(bf16[16,544,256]{2,1,0:T(8,128)(2,1)} %broadcast_dynamic-update-slice_fusion), calls=%async_computation.1 | async-start | bytes 8912896 | tf_op jit(solution)/shard_map/all_to_all | solution.py:198
  85.3 4.2 %gather_fusion.5 = bf16[8,512,256]{2,1,0:T(8,128)(2,1)} fusion(bf16[16,512,256]{2,1,0:T(8,128)(2,1)} %all-to-all-done, s32[1024]{0:T(1024)S(1)} %pad_clamp_fusion), kind=kCustom, calls=%fused_computation.5 | custom fusion | bytes 4194336 | tf_op jit(solution)/shard_map/gather | solution.py:204
  89.4 1.9 %broadcast_select_fusion = bf16[8,512,256]{2,1,0:T(8,128)(2,1)S(1)} fusion(bf16[8,512,256]{2,1,0:T(8,128)(2,1)} %gather_fusion.5, pred[8,512]{1,0:T(8,128)(4,1)S(1)} %get-tuple-element.23), kind=kLoop, calls=%fused_computation.18 | loop fusion | flops 1048576 | bytes 4198400 | tf_op jit(solution)/shard_map/jit(_where)/select_n | solution.py:202
  91.4 2.3 %concatenate.38 = bf16[8,1024,256]{2,1,0:T(8,128)(2,1)} pad(bf16[8,512,256]{2,1,0:T(8,128)(2,1)S(1)} %broadcast_select_fusion, bf16[]{:T(256)} %constant.38.clone.1), padding=0_0x0_512x0_0 | pad | bytes 6291458 | tf_op jit(solution)/shard_map/concatenate | solution.py:207
  93.7 55.1 %all-to-all-done.1 = bf16[16,544,256]{2,1,0:T(8,128)(2,1)} async-done(((bf16[16,544,256]{2,1,0:T(8,128)(2,1)}), bf16[16,544,256]{2,1,0:T(8,128)(2,1)}, u32[]{:S(2)}, u32[]{:S(2)}) %all-to-all-start.1) | async-done | bytes 4456480 | tf_op jit(solution)/shard_map/all_to_all | solution.py:198
  150.2 2.7 %convolution_convert_fusion = bf16[128,1216]{0,1:T(8,128)(2,1)} fusion(bf16[320,608]{1,0:T(8,128)(2,1)} %param.26, bf16[320,608]{1,0:T(8,128)(2,1)} %param.25, bf16[128,576]{1,0:T(8,128)(2,1)S(1)} %reshape.497), kind=kOutput, calls=%fused_computation.11 | convolution fusion | flops 101326848 | bytes 1187840 | tf_op jit(solution)/shard_map/dot_general | solution.py:227
  152.9 1.1 copy.32
  154.0 13.3 %all_to_all.25 = bf16[8,16,1216]{2,1,0:T(8,128)(2,1)S(1)} all-to-all(bf16[8,16,1216]{2,1,0:T(8,128)(2,1)S(1)} %bitcast.84), channel_id=1, replica_groups=mesh['req'=16,'kvh'=8] {'kvh'}, dimensions={0} | all-to-all | bytes 622592 | tf_op jit(solution)/shard_map/all_to_all | solution.py:230
  168.2 3.4 %all-to-all-start.3 = ((bf16[8,16,608]{2,1,0:T(8,128)(2,1)}), bf16[8,16,608]{2,1,0:T(8,128)(2,1)S(1)}, u32[]{:S(2)}, u32[]{:S(2)}) async-start(bf16[8,16,608]{2,1,0:T(8,128)(2,1)} %broadcast_in_dim.177), calls=%async_computation.3 | async-start | bytes 327680 | tf_op jit(solution)/shard_map/all_to_all | solution.py:242
  171.6 4.3 %gather_fusion.6 = bf16[8,544,256]{2,1,0:T(8,128)(2,1)} fusion(bf16[16,544,256]{2,1,0:T(8,128)(2,1)} %all-to-all-done.1, s32[1024]{0:T(1024)S(1)} %pad_clamp_fusion), kind=kCustom, calls=%fused_computation.6 | custom fusion | bytes 4456480 | tf_op jit(solution)/shard_map/gather | solution.py:211
  175.9 2.0 %all-to-all-done.3 = bf16[8,16,608]{2,1,0:T(8,128)(2,1)S(1)} async-done(((bf16[8,16,608]{2,1,0:T(8,128)(2,1)}), bf16[8,16,608]{2,1,0:T(8,128)(2,1)S(1)}, u32[]{:S(2)}, u32[]{:S(2)}) %all-to-all-start.3) | async-done | bytes 155680 | tf_op jit(solution)/shard_map/all_to_all | solution.py:242
  178.9 4.4 %all-to-all-start.4 = ((f32[16,8,320]{2,1,0:T(8,128)}), f32[16,8,320]{2,1,0:T(8,128)S(1)}, u32[]{:S(2)}, u32[]{:S(2)}) async-start(f32[16,8,320]{2,1,0:T(8,128)} %fusion.14), calls=%async_computation.4 | async-start | bytes 393216 | tf_op jit(solution)/shard_map/all_to_all | solution.py:251
  183.3 2.9 %fusion.1 = bf16[8,1024,256]{2,1,0:T(8,128)(2,1)} fusion(bf16[8,1024,256]{2,1,0:T(8,128)(2,1)} %concatenate.38, bf16[8,544,256]{2,1,0:T(8,128)(2,1)} %gather_fusion.6, pred[8,512]{1,0:T(8,128)(4,1)S(1)} %get-tuple-element.22), kind=kLoop, calls=%fused_computation.13 | loop fusion | flops 1048576 | bytes 4198400 | tf_op jit(solution)/shard_map/dynamic_update_slice | solution.py:262
  186.9 2.1 %scatter_fusion = bf16[8,1024,256]{2,1,0:T(8,128)(2,1)} fusion(bf16[8,1024,256]{2,1,0:T(8,128)(2,1)} %fusion.1, s32[8]{0:T(128)S(1)} %fusion.41, bf16[8,256]{1,0:T(8,128)(2,1)S(1)} %gather_fusion.7), kind=kCustom, calls=%fused_computation.8 | custom fusion | bytes 12352 | tf_op jit(solution)/shard_map/scatter | solution.py:263
  188.9 2.7 %all-to-all-done.4 = f32[16,8,320]{2,1,0:T(8,128)S(1)} async-done(((f32[16,8,320]{2,1,0:T(8,128)}), f32[16,8,320]{2,1,0:T(8,128)S(1)}, u32[]{:S(2)}, u32[]{:S(2)}) %all-to-all-start.4) | async-done | bytes 163872 | tf_op jit(solution)/shard_map/all_to_all | solution.py:251
  191.6 1.4 add_convert_fusion.1
  (94 shorter events, 12.2 us)
Async XLA Ops:
  0.6 52.2 %copy-start = (bf16[512,2560]{1,0:T(8,128)(2,1)S(1)}, bf16[512,2560]{1,0:T(8,128)(2,1)}, u32[]{:S(2)}) copy-start(bf16[512,2560]{1,0:T(8,128)(2,1)} %param.23) | copy-start | bytes 7864324
  8.4 7.4 %copy-start.5 = (s32[8,8]{1,0:T(8,128)S(1)}, s32[8,8]{1,0:T(8,128)}, u32[]{:S(2)}) copy-start(s32[8,8]{1,0:T(8,128)} %param.30) | copy-start | bytes 772
  8.4 7.4 %copy-start.6 = (bf16[8,320]{1,0:T(8,128)(2,1)S(1)}, bf16[8,320]{1,0:T(8,128)(2,1)}, u32[]{:S(2)}) copy-start(bf16[8,320]{1,0:T(8,128)(2,1)} %param.16) | copy-start | bytes 15364
  8.4 21.7 %copy-start.7 = (bf16[2560]{0:T(1024)(128)(2,1)S(1)}, bf16[2560]{0:T(1024)(128)(2,1)}, u32[]{:S(2)}) copy-start(bf16[2560]{0:T(1024)(128)(2,1)} %param.17) | copy-start | bytes 15364
  8.4 21.8 %copy-start.2 = (bf16[2560,128]{1,0:T(8,128)(2,1)S(1)}, bf16[2560,128]{1,0:T(8,128)(2,1)}, u32[]{:S(2)}) copy-start(bf16[2560,128]{1,0:T(8,128)(2,1)} %param.19) | copy-start | bytes 1966084
  8.4 22.1 %copy-start.9 = (bf16[128]{0:T(256)(128)(2,1)S(1)}, bf16[128]{0:T(256)(128)(2,1)}, u32[]{:S(2)}) copy-start(bf16[128]{0:T(256)(128)(2,1)} %param.22) | copy-start | bytes 772
  8.4 22.2 %copy-start.1 = (s32[128]{0:T(128)S(1)}, s32[128]{0:T(128)}, u32[]{:S(2)}) copy-start(s32[128]{0:T(128)} %param.29) | copy-start | bytes 1540
  8.4 70.6 %all-to-all-start = ((bf16[16,512,256]{2,1,0:T(8,128)(2,1)}), bf16[16,512,256]{2,1,0:T(8,128)(2,1)}, u32[]{:S(2)}, u32[]{:S(2)}) async-start(bf16[16,512,256]{2,1,0:T(8,128)(2,1)} %bitcast.80), calls=%async_computation | async-start | bytes 8388608 | tf_op jit(solution)/shard_map/all_to_all | solution.py:124
  32.6 7.4 %copy-start.10 = (bf16[128]{0:T(256)(128)(2,1)S(1)}, bf16[128]{0:T(256)(128)(2,1)}, u32[]{:S(2)}) copy-start(bf16[128]{0:T(256)(128)(2,1)} %param.21) | copy-start | bytes 772
  48.4 7.9 %copy-start.8 = (bf16[320]{0:T(512)(128)(2,1)S(1)}, bf16[320]{0:T(512)(128)(2,1)}, u32[]{:S(2)}) copy-start(bf16[320]{0:T(512)(128)(2,1)} %param.24) | copy-start | bytes 1924
  53.3 1.3 collective-permute-start
  54.6 4.8 %collective-permute-start.1 = (f32[8,2560]{1,0:T(8,128)S(1)}, f32[8,2560]{1,0:T(8,128)S(1)}, u32[]{:S(2)}, u32[]{:S(2)}) collective-permute-start(f32[8,2560]{1,0:T(8,128)S(1)} %add.196), channel_id=1, source_target_pairs={{0,2},{1,3},{2,0},{3,1},{4,6},{5,7},{6,4},{7,5},{8,10},{9,11},{10,... | collective-permute-start | bytes 245768 | tf_op jit(solution)/shard_map/ppermute | solution.py:165
  59.4 12.3 %collective-permute-start.2 = (f32[8,2560]{1,0:T(8,128)S(1)}, f32[8,2560]{1,0:T(8,128)S(1)}, u32[]{:S(2)}, u32[]{:S(2)}) collective-permute-start(f32[8,2560]{1,0:T(8,128)S(1)} %add.197), channel_id=1, source_target_pairs={{0,4},{1,5},{2,6},{3,7},{4,0},{5,1},{6,2},{7,3},{8,12},{9,13},{10,... | collective-permute-start | bytes 245768 | tf_op jit(solution)/shard_map/ppermute | solution.py:165
  71.9 0.6 copy-start.4
  79.8 69.0 %all-to-all-start.1 = ((bf16[16,544,256]{2,1,0:T(8,128)(2,1)}), bf16[16,544,256]{2,1,0:T(8,128)(2,1)}, u32[]{:S(2)}, u32[]{:S(2)}) async-start(bf16[16,544,256]{2,1,0:T(8,128)(2,1)} %broadcast_dynamic-update-slice_fusion), calls=%async_computation.1 | async-start | bytes 8912896 | tf_op jit(solution)/shard_map/all_to_all | solution.py:198
  150.1 27.8 %copy-start.3 = (bf16[608,320]{0,1:T(8,128)(2,1)S(1)}, bf16[608,320]{0,1:T(8,128)(2,1)}, u32[]{:S(2)}) copy-start(bf16[608,320]{0,1:T(8,128)(2,1)} %param.27) | copy-start | bytes 1167364
  168.2 9.8 %all-to-all-start.3 = ((bf16[8,16,608]{2,1,0:T(8,128)(2,1)}), bf16[8,16,608]{2,1,0:T(8,128)(2,1)S(1)}, u32[]{:S(2)}, u32[]{:S(2)}) async-start(bf16[8,16,608]{2,1,0:T(8,128)(2,1)} %broadcast_in_dim.177), calls=%async_computation.3 | async-start | bytes 327680 | tf_op jit(solution)/shard_map/all_to_all | solution.py:242
  178.9 12.7 %all-to-all-start.4 = ((f32[16,8,320]{2,1,0:T(8,128)}), f32[16,8,320]{2,1,0:T(8,128)S(1)}, u32[]{:S(2)}, u32[]{:S(2)}) async-start(f32[16,8,320]{2,1,0:T(8,128)} %fusion.14), calls=%async_computation.4 | async-start | bytes 393216 | tf_op jit(solution)/shard_map/all_to_all | solution.py:251

commit v12 on v11

--- a/solution.py
+++ b/solution.py
@@ -179,24 +179,17 @@
     fresh_flat = fresh.reshape(row_count, kv_local * channels)
     outgoing = jnp.concatenate([normed_two, fresh_flat], axis=1)
     outgoing_width = outgoing.shape[1]
-    extra_rows = -(-(row_count * outgoing_width) // channels)
-    extra_padded = -(-extra_rows // 32) * 32
-    second_buffer = jnp.concatenate(
-        [parcels_second, jnp.zeros((devices_req, extra_padded, channels), jnp.bfloat16)],
-        axis=1,
-    )
-    received_first, second_buffer = lax.optimization_barrier((received_first, second_buffer))
-    extra = jnp.pad(
-        outgoing.reshape(row_count * outgoing_width),
-        (0, extra_padded * channels - row_count * outgoing_width),
-    ).reshape(1, extra_padded, channels)
-    second_buffer = lax.dynamic_update_slice(
-        second_buffer,
-        jnp.broadcast_to(extra, (devices_req, extra_padded, channels)),
-        (0, second_span, 0),
-    )
+    received_first, outgoing = lax.optimization_barrier((received_first, outgoing))
+    gathered = lax.all_to_all(
+        jnp.broadcast_to(outgoing[None], (devices_req,) + outgoing.shape),
+        "req",
+        split_axis=0,
+        concat_axis=0,
+        tiled=True,
+    ).reshape(total_rows, outgoing_width)
+    gathered, parcels_second = lax.optimization_barrier((gathered, parcels_second))
     received_second = lax.all_to_all(
-        second_buffer, "req", split_axis=0, concat_axis=0, tiled=True
+        parcels_second, "req", split_axis=0, concat_axis=0, tiled=True
     )
     lengths_new = lengths[arriving]
     span_first = jnp.where(
@@ -208,17 +201,11 @@
         [span_first, jnp.zeros((row_count, second_span, channels), jnp.bfloat16)], axis=1
     )
     span_first, received_second = lax.optimization_barrier((span_first, received_second))
-    span_second = received_second[source_owner][:, :second_span, :]
     span_second = jnp.where(
         first_span + jnp.arange(second_span, dtype=jnp.int32)[None, :, None]
         < lengths_new[:, None, None],
-        span_second,
+        received_second[source_owner],
         jnp.zeros((), jnp.bfloat16),
-    )
-    gathered = (
-        received_second[:, second_span:, :]
-        .reshape(devices_req, extra_padded * channels)[:, : row_count * outgoing_width]
-        .reshape(total_rows, outgoing_width)
     )
     normed_all = gathered[:, :width_local]
     fresh_all = gathered[:, width_local:].reshape(total_rows, kv_local, channels)
@@ -226,27 +213,34 @@
     joined = jnp.concatenate([w_gate, w_up], axis=1)
     partial_both = jnp.dot(normed_all, joined, preferred_element_type=jnp.float32)
     group_rows = total_rows // devices_kvh
-    summed = jnp.sum(
-        lax.all_to_all(
-            partial_both.astype(jnp.bfloat16).reshape(devices_kvh, group_rows, 2 * ffn_width),
-            "kvh",
-            split_axis=0,
-            concat_axis=0,
-            tiled=True,
-        ).astype(jnp.float32),
-        axis=0,
-    )
+    current = partial_both.reshape(devices_kvh, group_rows, 2 * ffn_width)
+    step = devices_kvh // 2
+    while step >= 1:
+        upper = (kvh_index // step) % 2 == 1
+        half = current.shape[0] // 2
+        low, high = current[:half], current[half:]
+        keep = jnp.where(upper, high, low)
+        send = jnp.where(upper, low, high)
+        current = keep + lax.ppermute(
+            send, "kvh", [(i, i ^ step) for i in range(devices_kvh)]
+        )
+        step //= 2
+    summed = current[0]
     hidden_part = (jax.nn.silu(summed[:, :ffn_width]) * summed[:, ffn_width:]).astype(
         jnp.bfloat16
     )
-    hidden = lax.all_to_all(
-        jnp.broadcast_to(hidden_part[None], (devices_kvh,) + hidden_part.shape),
-        "kvh",
-        split_axis=0,
-        concat_axis=0,
-        tiled=True,
-    ).reshape(total_rows, ffn_width)
+    block = hidden_part[None]
+    step = 1
+    while step < devices_kvh:
+        upper = (kvh_index // step) % 2 == 1
+        other = lax.ppermute(block, "kvh", [(i, i ^ step) for i in range(devices_kvh)])
+        block = jnp.where(
+            upper, jnp.concatenate([other, block]), jnp.concatenate([block, other])
+        )
+        step *= 2
+    hidden = block.reshape(total_rows, ffn_width)
     lowered_parts = jnp.dot(hidden, w_down, preferred_element_type=jnp.float32)
+    lowered_parts, span_second = lax.optimization_barrier((lowered_parts, span_second))
     lowered = jnp.sum(
         lax.all_to_all(
             lowered_parts.reshape(devices_req, row_count, width_local),

time: 194 us -> 186 us (0.959)
  blocking collectives: 27.4 us -> 14 us
  starting transfers between devices: 24.5 us -> 36.4 us
  waiting for transfers between devices: 69.9 us -> 62.5 us
  other arithmetic: 18 us -> 21.5 us
    all_to_all x2, waiting for transfers between devices: 57.1 us -> 33 us  [the longest x1 30 us: per_device(): lax.all_to_all(parcels_second, 'req', split_axis=0, concat_axis=0, tiled=...]
    all_to_all x1 -> x0, blocking collectives: 13.3 us -> none  [per_device(): lax.all_to_all(partial_both.astype(jnp.bfloat16).reshape(devices_kvh, gro...]
    ppermute x0 -> x6, starting transfers between devices: none -> 10.8 us  [the longest x3 5.43 us: per_device(): lax.ppermute(send, 'kvh', [(i, i ^ step) for i in range(devices_kvh)])]
    all_to_all x1, waiting for transfers between devices: 6.24 us -> 13.3 us  [per_device(): lax.all_to_all(parcels_first, 'req', split_axis=0, concat_axis=0, tiled=T...]
    ppermute x0 -> x6, waiting for transfers between devices: none -> 5.6 us  [the longest x3 4.57 us: per_device(): lax.ppermute(send, 'kvh', [(i, i ^ step) for i in range(devices_kvh)])]
    select_n x0 -> x7, other arithmetic: none -> 5.08 us  [the longest x1 2.94 us: per_device(): jnp.where(first_span + jnp.arange(second_span, dtype=jnp.int32)[None, :,...]
    concatenate x1 -> x0, local copies, waits for them, and re-layouts: 4.67 us -> none  [per_device(): jnp.concatenate([parcels_second, jnp.zeros((devices_req, extra_padded, ch...]
    ppermute x3, waiting for transfers between devices: 3.86 us -> 7.43 us  [per_device(): lax.ppermute(attn_out, 'kvh', [(i, i ^ step) for i in range(devices_kvh)])]
  transfers between devices with their start and end apart: 7 -> 13, of which waited for: 6 -> 10; matrix products, arithmetic and copies ran while one was open for 27% -> 26% of each run, Pallas kernels for 0% -> 0%
where the time goes in v12:
time: 186 us; the launch traced here: 184 us
  waiting for transfers between devices  62.5 us (34%)
  local copies, waits for them, and re-layouts  37.9 us (20%)
  starting transfers between devices  36.4 us (20%)
  other arithmetic  21.5 us (12%)
  blocking collectives  14 us (8%)
  matrix products  10.9 us (6%)
    all_to_all x1, waiting for transfers between devices, per_device(): lax.all_to_all(parcels_second, 'req', split_axis=0, concat_axis=0, tiled=...  30 us
    all_gather x1, blocking collectives, per_device(): full_states = lax.all_gather(states, 'kvh', axis=1, tiled=True)  14 us
    all_to_all x1, waiting for transfers between devices, per_device(): lax.all_to_all(parcels_first, 'req', split_axis=0, concat_axis=0, tiled=T...  13.3 us
    select_n x1, other arithmetic, mask_blocks(): jnp.where(kept, blocks, jnp.where(placed, fresh[:, None, :, None, :], jnp...  7.64 us
    ppermute x3, waiting for transfers between devices, per_device(): lax.ppermute(attn_out, 'kvh', [(i, i ^ step) for i in range(devices_kvh)])  7.43 us
    all_to_all x1, starting transfers between devices, per_device(): lax.all_to_all(parcels_first, 'req', split_axis=0, concat_axis=0, tiled=T...  7.34 us
    ppermute x3, starting transfers between devices, per_device(): lax.ppermute(send, 'kvh', [(i, i ^ step) for i in range(devices_kvh)])  5.43 us
    ppermute x3, starting transfers between devices, per_device(): lax.ppermute(block, 'kvh', [(i, i ^ step) for i in range(devices_kvh)])  5.32 us
  transfers between devices with their start and end apart: 13, of which 10 were waited for; matrix products, arithmetic and copies ran while one was open for 26% of the time, Pallas kernels for 0%

profile of v12, /device:TPU:0, one launch (start us, length us, event | category | flops | bytes accessed | tf_op | source)
XLA Modules:
  0.0 184.3 jit_solution(7918469715409716625)
XLA Ops:
  3.4 5.0 %gather_fusion.2 = bf16[64,128,256]{2,1,0:T(8,128)(2,1)} fusion(bf16[64,128,256]{2,1,0:T(8,128)(2,1)} %bitcast.80, s32[1024]{0:T(1024)S(1)} %pad_clamp_fusion.3), kind=kCustom, calls=%fused_computation.2 | custom fusion | bytes 8388864 | tf_op jit(solution)/shard_map/gather | solution.py:121
  8.4 7.3 %all-to-all-start = ((bf16[16,512,256]{2,1,0:T(8,128)(2,1)}), bf16[16,512,256]{2,1,0:T(8,128)(2,1)}, u32[]{:S(2)}, u32[]{:S(2)}) async-start(bf16[16,512,256]{2,1,0:T(8,128)(2,1)} %bitcast.84), calls=%async_computation | async-start | bytes 8388608 | tf_op jit(solution)/shard_map/all_to_all | solution.py:124
  15.8 14.0 %all-gather = bf16[8,320,8]{1,2,0:T(8,128)(2,1)S(1)} all-gather(bf16[1,320,8]{1,2,0:T(8,128)(2,1)S(1)} %bitcast.92), channel_id=1, replica_groups=mesh['req'=16,'kvh'=8] {'kvh'}, dimensions={0}, use_global_device_ids=true | all-gather | bytes 46080 | tf_op jit(solution)/shard_map/all_gather | solution.py:134
  31.9 2.3 %multiply_reduce_fusion.1 = (f32[8,4]{0,1:T(4,128)S(1)}, f32[8,4,128]{2,0,1:T(8,128)S(1)}) fusion(bf16[8,2560]{1,0:T(8,128)(2,1)S(1)} %fusion.17, bf16[2560,512]{1,0:T(8,128)(2,1)} %param.18), kind=kOutput, calls=%fused_computation.63 | convolution fusion | flops 20979680 | bytes 2678912 | tf_op jit(solution)/shard_map/dot_general | solution.py:138
  35.0 5.0 %gather_fusion.1 = bf16[64,128,256]{2,1,0:T(8,128)(2,1)} fusion(bf16[64,128,256]{2,1,0:T(8,128)(2,1)} %bitcast.81, s32[1024]{0:T(1024)S(1)} %pad_clamp_fusion.4), kind=kCustom, calls=%fused_computation.1 | custom fusion | bytes 8388864 | tf_op jit(solution)/shard_map/gather | solution.py:155
  40.7 7.6 %select_select_fusion = bf16[8,1,1024,256]{3,2,0,1:T(8,128)(2,1)} fusion(bf16[8,1,1024,256]{3,2,0,1:T(8,128)(2,1)} %bitcast.85, pred[8,1024]{1,0:T(8,128)(4,1)S(1)} %get-tuple-element.27, pred[8,1024]{1,0:T(8,128)(4,1)S(1)} %get-tuple-element.26, bf16[8,256]{1,0:T(8,128)(2,1)S(1)} %maximum_bitcast_fusion), kind=kLoop, calls=%fused_computation.10 | loop fusion | flops 4194304 | bytes 8409088 | tf_op jit(solution)/shard_map/jit(_where)/select_n | solution.py:48
  48.4 2.5 %fusion.45 = (f32[8,4]{1,0:T(8,128)S(1)}, f32[8,4,1024]{2,1,0:T(4,128)S(1)}) fusion(bf16[8,1,1024,256]{3,2,0,1:T(8,128)(2,1)} %select_select_fusion, pred[8,1024]{1,0:T(8,128)(4,1)S(1)} %get-tuple-element.36, bf16[8,4,64]{2,1,0:T(4,128)(2,1)S(1)} %get-tuple-element.23, bf16[8,4,64]{2,1,0:T(4,128)(2,1)S(1)} %get-tuple-element.22), kind=kOutput, calls=%fused_computation.131 | convolution fusion | flops 8537087 | bytes 2244736 | tf_op jit(solution)/shard_map/sub | solution.py:67
  50.9 2.0 %fusion.8 = bf16[1,8,4,128]{3,2,1,0:T(4,128)(2,1)S(1)} fusion(bf16[8,1,1024,256]{3,2,0,1:T(8,128)(2,1)} %select_select_fusion, f32[8,4,1024]{2,1,0:T(4,128)S(1)} %get-tuple-element.42, f32[8,4]{1,0:T(8,128)S(1)} %get-tuple-element.41), kind=kOutput, calls=%fused_computation.23 | convolution fusion | flops 8458240 | bytes 2236544 | tf_op jit(solution)/shard_map/rkgt,rktd->rkgd/dot_general | solution.py:68
  54.6 1.7 collective-permute-start.1
  56.3 3.1 %collective-permute-done.1 = f32[8,2560]{1,0:T(8,128)S(1)} collective-permute-done((f32[8,2560]{1,0:T(8,128)S(1)}, f32[8,2560]{1,0:T(8,128)S(1)}, u32[]{:S(2)}, u32[]{:S(2)}) %collective-permute-start.1) | collective-permute-done | bytes 81952 | tf_op jit(solution)/shard_map/ppermute | solution.py:165
  59.4 2.6 %collective-permute-start.2 = (f32[8,2560]{1,0:T(8,128)S(1)}, f32[8,2560]{1,0:T(8,128)S(1)}, u32[]{:S(2)}, u32[]{:S(2)}) collective-permute-start(f32[8,2560]{1,0:T(8,128)S(1)} %add.218), channel_id=1, source_target_pairs={{0,4},{1,5},{2,6},{3,7},{4,0},{5,1},{6,2},{7,3},{8,12},{9,13},{10,... | collective-permute-start | bytes 245768 | tf_op jit(solution)/shard_map/ppermute | solution.py:165
  62.1 3.4 %collective-permute-done.2 = f32[8,2560]{1,0:T(8,128)S(1)} collective-permute-done((f32[8,2560]{1,0:T(8,128)S(1)}, f32[8,2560]{1,0:T(8,128)S(1)}, u32[]{:S(2)}, u32[]{:S(2)}) %collective-permute-start.2) | collective-permute-done | bytes 81952 | tf_op jit(solution)/shard_map/ppermute | solution.py:165
  65.8 13.3 %all-to-all-done = bf16[16,512,256]{2,1,0:T(8,128)(2,1)} async-done(((bf16[16,512,256]{2,1,0:T(8,128)(2,1)}), bf16[16,512,256]{2,1,0:T(8,128)(2,1)}, u32[]{:S(2)}, u32[]{:S(2)}) %all-to-all-start) | async-done | bytes 4194336 | tf_op jit(solution)/shard_map/all_to_all | solution.py:124
  79.7 4.7 %all-to-all-start.1 = ((bf16[16,8,576]{2,1,0:T(8,128)(2,1)}), bf16[16,8,576]{2,1,0:T(8,128)(2,1)S(1)}, u32[]{:S(2)}, u32[]{:S(2)}) async-start(bf16[16,8,576]{2,1,0:T(8,128)(2,1)} %broadcast_in_dim.165), calls=%async_computation.1 | async-start | bytes 327680 | tf_op jit(solution)/shard_map/all_to_all | solution.py:183
  84.6 5.0 %gather_fusion.3 = bf16[64,128,256]{2,1,0:T(8,128)(2,1)} fusion(bf16[64,128,256]{2,1,0:T(8,128)(2,1)} %bitcast.82, s32[1024]{0:T(1024)S(1)} %pad_clamp_fusion.2), kind=kCustom, calls=%fused_computation.3 | custom fusion | bytes 8388864 | tf_op jit(solution)/shard_map/gather | solution.py:128
  89.6 2.9 %all-to-all-done.1 = bf16[16,8,576]{2,1,0:T(8,128)(2,1)S(1)} async-done(((bf16[16,8,576]{2,1,0:T(8,128)(2,1)}), bf16[16,8,576]{2,1,0:T(8,128)(2,1)S(1)}, u32[]{:S(2)}, u32[]{:S(2)}) %all-to-all-start.1) | async-done | bytes 147488 | tf_op jit(solution)/shard_map/all_to_all | solution.py:183
  92.6 1.8 fusion.10
  95.5 2.0 %copy.37 = f32[64,1216]{1,0:T(8,128)} copy(f32[64,1216]{0,1:T(8,128)} %get-tuple-element.20) | data formatting | bytes 622592 | tf_op jit(solution)/shard_map/jit(_where)/select_n | solution.py:223
  97.5 3.9 %collective-permute-start.3 = (f32[4,16,1216]{2,1,0:T(8,128)}, f32[4,16,1216]{2,1,0:T(8,128)}, u32[]{:S(2)}, u32[]{:S(2)}) collective-permute-start(f32[4,16,1216]{2,1,0:T(8,128)} %bitcast.89), channel_id=1, source_target_pairs={{0,4},{1,5},{2,6},{3,7},{4,0},{5,1},{6,2},{7,3},{8,12},{9,13},{10,... | collective-permute-start | bytes 933896 | tf_op jit(solution)/shard_map/ppermute | solution.py:224
  101.4 4.6 %all-to-all-start.2 = ((bf16[16,512,256]{2,1,0:T(8,128)(2,1)}), bf16[16,512,256]{2,1,0:T(8,128)(2,1)}, u32[]{:S(2)}, u32[]{:S(2)}) async-start(bf16[16,512,256]{2,1,0:T(8,128)(2,1)} %bitcast.83), calls=%async_computation.2 | async-start | bytes 8388608 | tf_op jit(solution)/shard_map/all_to_all | solution.py:191
  110.2 3.4 %collective-permute-done.4 = f32[2,16,1216]{2,1,0:T(8,128)} collective-permute-done((f32[2,16,1216]{2,1,0:T(8,128)S(1)}, f32[2,16,1216]{2,1,0:T(8,128)}, u32[]{:S(2)}, u32[]{:S(2)}) %collective-permute-start.4) | collective-permute-done | bytes 155680 | tf_op jit(solution)/shard_map/ppermute | solution.py:224
  118.7 4.2 %gather_fusion.5 = bf16[8,512,256]{2,1,0:T(8,128)(2,1)} fusion(bf16[16,512,256]{2,1,0:T(8,128)(2,1)} %all-to-all-done, s32[1024]{0:T(1024)S(1)} %pad_clamp_fusion), kind=kCustom, calls=%fused_computation.5 | custom fusion | bytes 4194336 | tf_op jit(solution)/shard_map/gather | solution.py:197
  122.9 3.7 %collective-permute-start.8 = (bf16[4,16,608]{2,1,0:T(8,128)(2,1)S(1)}, bf16[4,16,608]{2,1,0:T(8,128)(2,1)}, u32[]{:S(2)}, u32[]{:S(2)}) collective-permute-start(bf16[4,16,608]{2,1,0:T(8,128)(2,1)S(1)} %maximum_select_fusion.1), channel_id=1, source_target_pairs={{0,4},{1,5},{2,6},{3,7},{4,0},{5,1},{6,2},{7,3},{8,12},{9,13},{10,... | collective-permute-start | bytes 233480 | tf_op jit(solution)/shard_map/ppermute | solution.py:236
  126.6 1.9 %broadcast_select_fusion = bf16[8,512,256]{2,1,0:T(8,128)(2,1)S(1)} fusion(bf16[8,512,256]{2,1,0:T(8,128)(2,1)} %gather_fusion.5, pred[8,512]{1,0:T(8,128)(4,1)S(1)} %get-tuple-element.33), kind=kLoop, calls=%fused_computation.15 | loop fusion | flops 1048576 | bytes 4198400 | tf_op jit(solution)/shard_map/jit(_where)/select_n | solution.py:195
  128.6 2.3 %concatenate.60 = bf16[8,1024,256]{2,1,0:T(8,128)(2,1)} pad(bf16[8,512,256]{2,1,0:T(8,128)(2,1)S(1)} %broadcast_select_fusion, bf16[]{:T(256)} %constant.129.clone.1), padding=0_0x0_512x0_0 | pad | bytes 6291458 | tf_op jit(solution)/shard_map/concatenate | solution.py:200
  132.9 30.0 %all-to-all-done.2 = bf16[16,512,256]{2,1,0:T(8,128)(2,1)} async-done(((bf16[16,512,256]{2,1,0:T(8,128)(2,1)}), bf16[16,512,256]{2,1,0:T(8,128)(2,1)}, u32[]{:S(2)}, u32[]{:S(2)}) %all-to-all-start.2) | async-done | bytes 4194336 | tf_op jit(solution)/shard_map/all_to_all | solution.py:191
  162.9 4.2 %gather_fusion.6 = bf16[8,512,256]{2,1,0:T(8,128)(2,1)} fusion(bf16[16,512,256]{2,1,0:T(8,128)(2,1)} %all-to-all-done.2, s32[1024]{0:T(1024)S(1)} %pad_clamp_fusion), kind=kCustom, calls=%fused_computation.6 | custom fusion | bytes 4194336 | tf_op jit(solution)/shard_map/gather | solution.py:207
  167.1 2.9 %broadcast_select_fusion.1 = bf16[8,512,256]{2,1,0:T(8,128)(2,1)} fusion(bf16[8,512,256]{2,1,0:T(8,128)(2,1)} %gather_fusion.6, pred[8,512]{1,0:T(8,128)(4,1)S(1)} %get-tuple-element.32), kind=kLoop, calls=%fused_computation.16 | loop fusion | flops 1048576 | bytes 4198400 | tf_op jit(solution)/shard_map/jit(_where)/select_n | solution.py:204
  170.8 4.4 %all-to-all-start.3 = ((f32[16,8,320]{2,1,0:T(8,128)}), f32[16,8,320]{2,1,0:T(8,128)S(1)}, u32[]{:S(2)}, u32[]{:S(2)}) async-start(f32[16,8,320]{2,1,0:T(8,128)} %bitcast.21), calls=%async_computation.3 | async-start | bytes 393216 | tf_op jit(solution)/shard_map/all_to_all | solution.py:245
  175.3 3.0 %constant_dynamic-update-slice_fusion = bf16[8,1024,256]{2,1,0:T(8,128)(2,1)} fusion(bf16[8,1024,256]{2,1,0:T(8,128)(2,1)} %concatenate.60, bf16[8,512,256]{2,1,0:T(8,128)(2,1)} %broadcast_select_fusion.1), kind=kLoop, calls=%fused_computation.128 | loop fusion | bytes 4194304 | tf_op jit(solution)/shard_map/dynamic_update_slice | solution.py:256
  178.3 2.1 %scatter_fusion = bf16[8,1024,256]{2,1,0:T(8,128)(2,1)} fusion(bf16[8,1024,256]{2,1,0:T(8,128)(2,1)} %constant_dynamic-update-slice_fusion, s32[8]{0:T(128)S(1)} %fusion.40, bf16[8,256]{1,0:T(8,128)(2,1)S(1)} %gather_fusion.7), kind=kCustom, calls=%fused_computation.8 | custom fusion | bytes 12352 | tf_op jit(solution)/shard_map/scatter | solution.py:257
  180.4 3.2 %all-to-all-done.3 = f32[16,8,320]{2,1,0:T(8,128)S(1)} async-done(((f32[16,8,320]{2,1,0:T(8,128)}), f32[16,8,320]{2,1,0:T(8,128)S(1)}, u32[]{:S(2)}, u32[]{:S(2)}) %all-to-all-start.3) | async-done | bytes 163872 | tf_op jit(solution)/shard_map/all_to_all | solution.py:245
  (107 shorter events, 23.1 us)
Async XLA Ops:
  0.6 52.3 %copy-start = (bf16[512,2560]{1,0:T(8,128)(2,1)S(1)}, bf16[512,2560]{1,0:T(8,128)(2,1)}, u32[]{:S(2)}) copy-start(bf16[512,2560]{1,0:T(8,128)(2,1)} %param.23) | copy-start | bytes 7864324
  8.4 7.4 %copy-start.4 = (s32[8,8]{1,0:T(8,128)S(1)}, s32[8,8]{1,0:T(8,128)}, u32[]{:S(2)}) copy-start(s32[8,8]{1,0:T(8,128)} %param.30) | copy-start | bytes 772
  8.4 7.4 %copy-start.5 = (bf16[8,320]{1,0:T(8,128)(2,1)S(1)}, bf16[8,320]{1,0:T(8,128)(2,1)}, u32[]{:S(2)}) copy-start(bf16[8,320]{1,0:T(8,128)(2,1)} %param.16) | copy-start | bytes 15364
  8.4 21.7 %copy-start.6 = (bf16[2560]{0:T(1024)(128)(2,1)S(1)}, bf16[2560]{0:T(1024)(128)(2,1)}, u32[]{:S(2)}) copy-start(bf16[2560]{0:T(1024)(128)(2,1)} %param.17) | copy-start | bytes 15364
  8.4 21.8 %copy-start.2 = (bf16[2560,128]{1,0:T(8,128)(2,1)S(1)}, bf16[2560,128]{1,0:T(8,128)(2,1)}, u32[]{:S(2)}) copy-start(bf16[2560,128]{1,0:T(8,128)(2,1)} %param.19) | copy-start | bytes 1966084
  8.4 22.1 %copy-start.9 = (bf16[128]{0:T(256)(128)(2,1)S(1)}, bf16[128]{0:T(256)(128)(2,1)}, u32[]{:S(2)}) copy-start(bf16[128]{0:T(256)(128)(2,1)} %param.22) | copy-start | bytes 772
  8.4 70.6 %all-to-all-start = ((bf16[16,512,256]{2,1,0:T(8,128)(2,1)}), bf16[16,512,256]{2,1,0:T(8,128)(2,1)}, u32[]{:S(2)}, u32[]{:S(2)}) async-start(bf16[16,512,256]{2,1,0:T(8,128)(2,1)} %bitcast.84), calls=%async_computation | async-start | bytes 8388608 | tf_op jit(solution)/shard_map/all_to_all | solution.py:124
  15.8 18.6 %copy-start.1 = (s32[128]{0:T(128)S(1)}, s32[128]{0:T(128)}, u32[]{:S(2)}) copy-start(s32[128]{0:T(128)} %param.29) | copy-start | bytes 1540
  35.0 5.1 %copy-start.10 = (bf16[128]{0:T(256)(128)(2,1)S(1)}, bf16[128]{0:T(256)(128)(2,1)}, u32[]{:S(2)}) copy-start(bf16[128]{0:T(256)(128)(2,1)} %param.21) | copy-start | bytes 772
  48.4 13.7 %copy-start.7 = (bf16[320]{0:T(512)(128)(2,1)S(1)}, bf16[320]{0:T(512)(128)(2,1)}, u32[]{:S(2)}) copy-start(bf16[320]{0:T(512)(128)(2,1)} %param.24) | copy-start | bytes 1924
  53.3 1.3 collective-permute-start
  54.6 4.8 %collective-permute-start.1 = (f32[8,2560]{1,0:T(8,128)S(1)}, f32[8,2560]{1,0:T(8,128)S(1)}, u32[]{:S(2)}, u32[]{:S(2)}) collective-permute-start(f32[8,2560]{1,0:T(8,128)S(1)} %add.217), channel_id=1, source_target_pairs={{0,2},{1,3},{2,0},{3,1},{4,6},{5,7},{6,4},{7,5},{8,10},{9,11},{10,... | collective-permute-start | bytes 245768 | tf_op jit(solution)/shard_map/ppermute | solution.py:165
  59.4 6.0 %collective-permute-start.2 = (f32[8,2560]{1,0:T(8,128)S(1)}, f32[8,2560]{1,0:T(8,128)S(1)}, u32[]{:S(2)}, u32[]{:S(2)}) collective-permute-start(f32[8,2560]{1,0:T(8,128)S(1)} %add.218), channel_id=1, source_target_pairs={{0,4},{1,5},{2,6},{3,7},{4,0},{5,1},{6,2},{7,3},{8,12},{9,13},{10,... | collective-permute-start | bytes 245768 | tf_op jit(solution)/shard_map/ppermute | solution.py:165
  79.7 12.8 %all-to-all-start.1 = ((bf16[16,8,576]{2,1,0:T(8,128)(2,1)}), bf16[16,8,576]{2,1,0:T(8,128)(2,1)S(1)}, u32[]{:S(2)}, u32[]{:S(2)}) async-start(bf16[16,8,576]{2,1,0:T(8,128)(2,1)} %broadcast_in_dim.165), calls=%async_computation.1 | async-start | bytes 327680 | tf_op jit(solution)/shard_map/all_to_all | solution.py:183
  84.6 8.0 %copy-start.8 = (bf16[320,608]{1,0:T(8,128)(2,1)S(1)}, bf16[320,608]{1,0:T(8,128)(2,1)}, u32[]{:S(2)}) copy-start(bf16[320,608]{1,0:T(8,128)(2,1)} %param.26) | copy-start | bytes 1167364
  97.5 9.4 %collective-permute-start.3 = (f32[4,16,1216]{2,1,0:T(8,128)}, f32[4,16,1216]{2,1,0:T(8,128)}, u32[]{:S(2)}, u32[]{:S(2)}) collective-permute-start(f32[4,16,1216]{2,1,0:T(8,128)} %bitcast.89), channel_id=1, source_target_pairs={{0,4},{1,5},{2,6},{3,7},{4,0},{5,1},{6,2},{7,3},{8,12},{9,13},{10,... | collective-permute-start | bytes 933896 | tf_op jit(solution)/shard_map/ppermute | solution.py:224
  101.4 61.5 %all-to-all-start.2 = ((bf16[16,512,256]{2,1,0:T(8,128)(2,1)}), bf16[16,512,256]{2,1,0:T(8,128)(2,1)}, u32[]{:S(2)}, u32[]{:S(2)}) async-start(bf16[16,512,256]{2,1,0:T(8,128)(2,1)} %bitcast.83), calls=%async_computation.2 | async-start | bytes 8388608 | tf_op jit(solution)/shard_map/all_to_all | solution.py:191
  108.1 5.5 %collective-permute-start.4 = (f32[2,16,1216]{2,1,0:T(8,128)S(1)}, f32[2,16,1216]{2,1,0:T(8,128)}, u32[]{:S(2)}, u32[]{:S(2)}) collective-permute-start(f32[2,16,1216]{2,1,0:T(8,128)S(1)} %slice_select_fusion.2), channel_id=1, source_target_pairs={{0,2},{1,3},{2,0},{3,1},{4,6},{5,7},{6,4},{7,5},{8,10},{9,11},{10,... | collective-permute-start | bytes 466952 | tf_op jit(solution)/shard_map/ppermute | solution.py:224
  114.5 1.4 collective-permute-start.5
  116.0 1.2 collective-permute-start.6
  117.3 5.7 %collective-permute-start.7 = (bf16[2,16,608]{2,1,0:T(8,128)(2,1)S(1)}, bf16[2,16,608]{2,1,0:T(8,128)(2,1)S(1)}, u32[]{:S(2)}, u32[]{:S(2)}) collective-permute-start(bf16[2,16,608]{2,1,0:T(8,128)(2,1)S(1)} %maximum_select_fusion.2), channel_id=1, source_target_pairs={{0,2},{1,3},{2,0},{3,1},{4,6},{5,7},{6,4},{7,5},{8,10},{9,11},{10,... | collective-permute-start | bytes 116744 | tf_op jit(solution)/shard_map/ppermute | solution.py:236
  122.9 8.6 %collective-permute-start.8 = (bf16[4,16,608]{2,1,0:T(8,128)(2,1)S(1)}, bf16[4,16,608]{2,1,0:T(8,128)(2,1)}, u32[]{:S(2)}, u32[]{:S(2)}) collective-permute-start(bf16[4,16,608]{2,1,0:T(8,128)(2,1)S(1)} %maximum_select_fusion.1), channel_id=1, source_target_pairs={{0,4},{1,5},{2,6},{3,7},{4,0},{5,1},{6,2},{7,3},{8,12},{9,13},{10,... | collective-permute-start | bytes 233480 | tf_op jit(solution)/shard_map/ppermute | solution.py:236
  128.6 4.0 %copy-start.3 = (bf16[608,320]{0,1:T(8,128)(2,1)S(1)}, bf16[608,320]{0,1:T(8,128)(2,1)}, u32[]{:S(2)}) copy-start(bf16[608,320]{0,1:T(8,128)(2,1)} %param.27) | copy-start | bytes 1167364
  170.8 12.8 %all-to-all-start.3 = ((f32[16,8,320]{2,1,0:T(8,128)}), f32[16,8,320]{2,1,0:T(8,128)S(1)}, u32[]{:S(2)}, u32[]{:S(2)}) async-start(f32[16,8,320]{2,1,0:T(8,128)} %bitcast.21), calls=%async_computation.3 | async-start | bytes 393216 | tf_op jit(solution)/shard_map/all_to_all | solution.py:245

commit v13 on v12

--- a/solution.py
+++ b/solution.py
@@ -240,7 +240,7 @@
         step *= 2
     hidden = block.reshape(total_rows, ffn_width)
     lowered_parts = jnp.dot(hidden, w_down, preferred_element_type=jnp.float32)
-    lowered_parts, span_second = lax.optimization_barrier((lowered_parts, span_second))
+    lowered_parts, _ = lax.optimization_barrier((lowered_parts, received_second))
     lowered = jnp.sum(
         lax.all_to_all(
             lowered_parts.reshape(devices_req, row_count, width_local),

time: 186 us -> 183 us (0.984)
  local copies, waits for them, and re-layouts: 37.9 us -> 34.9 us
    dynamic_update_slice x1 -> x0, local copies, waits for them, and re-layouts: 3.05 us -> none  [per_device(): lax.dynamic_update_slice(span_first, span_second, (0, first_span, 0))]
    select_n x1 -> x0, other arithmetic: 2.94 us -> none  [per_device(): jnp.where(first_span + jnp.arange(second_span, dtype=jnp.int32)[None, :,...]
    dynamic_update_slice x0 -> x1, other arithmetic: none -> 2.91 us  [per_device(): lax.dynamic_update_slice(span_first, span_second, (0, first_span, 0))]
  transfers between devices with their start and end apart: 13 -> 13, of which waited for: 10 -> 10; matrix products, arithmetic and copies ran while one was open for 26% -> 27% of each run, Pallas kernels for 0% -> 0%
where the time goes in v13:
time: 183 us; the launch traced here: 181 us
  waiting for transfers between devices  62.6 us (34%)
  starting transfers between devices  36.4 us (20%)
  local copies, waits for them, and re-layouts  34.9 us (19%)
  other arithmetic  21.5 us (12%)
  blocking collectives  14 us (8%)
  matrix products  10.9 us (6%)
    all_to_all x1, waiting for transfers between devices, per_device(): lax.all_to_all(parcels_second, 'req', split_axis=0, concat_axis=0, tiled=...  30 us
    all_gather x1, blocking collectives, per_device(): full_states = lax.all_gather(states, 'kvh', axis=1, tiled=True)  14 us
    all_to_all x1, waiting for transfers between devices, per_device(): lax.all_to_all(parcels_first, 'req', split_axis=0, concat_axis=0, tiled=T...  13.3 us
    select_n x1, other arithmetic, mask_blocks(): jnp.where(kept, blocks, jnp.where(placed, fresh[:, None, :, None, :], jnp...  7.64 us
    ppermute x3, waiting for transfers between devices, per_device(): lax.ppermute(attn_out, 'kvh', [(i, i ^ step) for i in range(devices_kvh)])  7.43 us
    all_to_all x1, starting transfers between devices, per_device(): lax.all_to_all(parcels_first, 'req', split_axis=0, concat_axis=0, tiled=T...  7.34 us
    ppermute x3, starting transfers between devices, per_device(): lax.ppermute(send, 'kvh', [(i, i ^ step) for i in range(devices_kvh)])  5.43 us
    ppermute x3, starting transfers between devices, per_device(): lax.ppermute(block, 'kvh', [(i, i ^ step) for i in range(devices_kvh)])  5.32 us
  transfers between devices with their start and end apart: 13, of which 10 were waited for; matrix products, arithmetic and copies ran while one was open for 27% of the time, Pallas kernels for 0%

profile of v13, /device:TPU:0, one launch (start us, length us, event | category | flops | bytes accessed | tf_op | source)
XLA Modules:
  0.0 181.4 jit_solution(6551271570232460741)
XLA Ops:
  3.4 5.0 %gather_fusion.2 = bf16[64,128,256]{2,1,0:T(8,128)(2,1)} fusion(bf16[64,128,256]{2,1,0:T(8,128)(2,1)} %bitcast.80, s32[1024]{0:T(1024)S(1)} %pad_clamp_fusion.3), kind=kCustom, calls=%fused_computation.2 | custom fusion | bytes 8388864 | tf_op jit(solution)/shard_map/gather | solution.py:121
  8.4 7.3 %all-to-all-start = ((bf16[16,512,256]{2,1,0:T(8,128)(2,1)}), bf16[16,512,256]{2,1,0:T(8,128)(2,1)}, u32[]{:S(2)}, u32[]{:S(2)}) async-start(bf16[16,512,256]{2,1,0:T(8,128)(2,1)} %bitcast.84), calls=%async_computation | async-start | bytes 8388608 | tf_op jit(solution)/shard_map/all_to_all | solution.py:124
  15.8 14.0 %all-gather = bf16[8,320,8]{1,2,0:T(8,128)(2,1)S(1)} all-gather(bf16[1,320,8]{1,2,0:T(8,128)(2,1)S(1)} %bitcast.92), channel_id=1, replica_groups=mesh['req'=16,'kvh'=8] {'kvh'}, dimensions={0}, use_global_device_ids=true | all-gather | bytes 46080 | tf_op jit(solution)/shard_map/all_gather | solution.py:134
  32.0 2.3 %multiply_reduce_fusion.1 = (f32[8,4]{0,1:T(4,128)S(1)}, f32[8,4,128]{2,0,1:T(8,128)S(1)}) fusion(bf16[8,2560]{1,0:T(8,128)(2,1)S(1)} %fusion.17, bf16[2560,512]{1,0:T(8,128)(2,1)} %param.18), kind=kOutput, calls=%fused_computation.63 | convolution fusion | flops 20979680 | bytes 2678912 | tf_op jit(solution)/shard_map/dot_general | solution.py:138
  35.0 5.0 %gather_fusion.1 = bf16[64,128,256]{2,1,0:T(8,128)(2,1)} fusion(bf16[64,128,256]{2,1,0:T(8,128)(2,1)} %bitcast.81, s32[1024]{0:T(1024)S(1)} %pad_clamp_fusion.4), kind=kCustom, calls=%fused_computation.1 | custom fusion | bytes 8388864 | tf_op jit(solution)/shard_map/gather | solution.py:155
  40.8 7.6 %select_select_fusion = bf16[8,1,1024,256]{3,2,0,1:T(8,128)(2,1)} fusion(bf16[8,1,1024,256]{3,2,0,1:T(8,128)(2,1)} %bitcast.85, pred[8,1024]{1,0:T(8,128)(4,1)S(1)} %get-tuple-element.25, pred[8,1024]{1,0:T(8,128)(4,1)S(1)} %get-tuple-element.24, bf16[8,256]{1,0:T(8,128)(2,1)S(1)} %maximum_bitcast_fusion), kind=kLoop, calls=%fused_computation.10 | loop fusion | flops 4194304 | bytes 8409088 | tf_op jit(solution)/shard_map/jit(_where)/select_n | solution.py:48
  48.4 2.5 %fusion.45 = (f32[8,4]{1,0:T(8,128)S(1)}, f32[8,4,1024]{2,1,0:T(4,128)S(1)}) fusion(bf16[8,1,1024,256]{3,2,0,1:T(8,128)(2,1)} %select_select_fusion, pred[8,1024]{1,0:T(8,128)(4,1)S(1)} %get-tuple-element.34, bf16[8,4,64]{2,1,0:T(4,128)(2,1)S(1)} %get-tuple-element.21, bf16[8,4,64]{2,1,0:T(4,128)(2,1)S(1)} %get-tuple-element.20), kind=kOutput, calls=%fused_computation.130 | convolution fusion | flops 8537087 | bytes 2244736 | tf_op jit(solution)/shard_map/sub | solution.py:67
  50.9 2.0 %fusion.8 = bf16[1,8,4,128]{3,2,1,0:T(4,128)(2,1)S(1)} fusion(bf16[8,1,1024,256]{3,2,0,1:T(8,128)(2,1)} %select_select_fusion, f32[8,4,1024]{2,1,0:T(4,128)S(1)} %get-tuple-element.40, f32[8,4]{1,0:T(8,128)S(1)} %get-tuple-element.39), kind=kOutput, calls=%fused_computation.23 | convolution fusion | flops 8458240 | bytes 2236544 | tf_op jit(solution)/shard_map/rkgt,rktd->rkgd/dot_general | solution.py:68
  54.7 1.7 collective-permute-start.1
  56.3 3.1 %collective-permute-done.1 = f32[8,2560]{1,0:T(8,128)S(1)} collective-permute-done((f32[8,2560]{1,0:T(8,128)S(1)}, f32[8,2560]{1,0:T(8,128)S(1)}, u32[]{:S(2)}, u32[]{:S(2)}) %collective-permute-start.1) | collective-permute-done | bytes 81952 | tf_op jit(solution)/shard_map/ppermute | solution.py:165
  59.4 2.6 %collective-permute-start.2 = (f32[8,2560]{1,0:T(8,128)S(1)}, f32[8,2560]{1,0:T(8,128)S(1)}, u32[]{:S(2)}, u32[]{:S(2)}) collective-permute-start(f32[8,2560]{1,0:T(8,128)S(1)} %add.218), channel_id=1, source_target_pairs={{0,4},{1,5},{2,6},{3,7},{4,0},{5,1},{6,2},{7,3},{8,12},{9,13},{10,... | collective-permute-start | bytes 245768 | tf_op jit(solution)/shard_map/ppermute | solution.py:165
  62.1 3.4 %collective-permute-done.2 = f32[8,2560]{1,0:T(8,128)S(1)} collective-permute-done((f32[8,2560]{1,0:T(8,128)S(1)}, f32[8,2560]{1,0:T(8,128)S(1)}, u32[]{:S(2)}, u32[]{:S(2)}) %collective-permute-start.2) | collective-permute-done | bytes 81952 | tf_op jit(solution)/shard_map/ppermute | solution.py:165
  65.8 13.3 %all-to-all-done = bf16[16,512,256]{2,1,0:T(8,128)(2,1)} async-done(((bf16[16,512,256]{2,1,0:T(8,128)(2,1)}), bf16[16,512,256]{2,1,0:T(8,128)(2,1)}, u32[]{:S(2)}, u32[]{:S(2)}) %all-to-all-start) | async-done | bytes 4194336 | tf_op jit(solution)/shard_map/all_to_all | solution.py:124
  79.7 4.7 %all-to-all-start.1 = ((bf16[16,8,576]{2,1,0:T(8,128)(2,1)}), bf16[16,8,576]{2,1,0:T(8,128)(2,1)S(1)}, u32[]{:S(2)}, u32[]{:S(2)}) async-start(bf16[16,8,576]{2,1,0:T(8,128)(2,1)} %broadcast_in_dim.165), calls=%async_computation.1 | async-start | bytes 327680 | tf_op jit(solution)/shard_map/all_to_all | solution.py:183
  84.6 5.0 %gather_fusion.3 = bf16[64,128,256]{2,1,0:T(8,128)(2,1)} fusion(bf16[64,128,256]{2,1,0:T(8,128)(2,1)} %bitcast.82, s32[1024]{0:T(1024)S(1)} %pad_clamp_fusion.2), kind=kCustom, calls=%fused_computation.3 | custom fusion | bytes 8388864 | tf_op jit(solution)/shard_map/gather | solution.py:128
  89.6 2.9 %all-to-all-done.1 = bf16[16,8,576]{2,1,0:T(8,128)(2,1)S(1)} async-done(((bf16[16,8,576]{2,1,0:T(8,128)(2,1)}), bf16[16,8,576]{2,1,0:T(8,128)(2,1)S(1)}, u32[]{:S(2)}, u32[]{:S(2)}) %all-to-all-start.1) | async-done | bytes 147488 | tf_op jit(solution)/shard_map/all_to_all | solution.py:183
  92.6 1.8 %fusion.10 = f32[128,1216]{0,1:T(8,128)S(1)} fusion(bf16[320,608]{1,0:T(8,128)(2,1)S(1)} %copy-done.8, bf16[320,608]{1,0:T(8,128)(2,1)} %param.25, bf16[128,576]{1,0:T(8,128)(2,1)S(1)} %bitcast.90), kind=kOutput, calls=%fused_computation.26 | convolution fusion | flops 101171200 | bytes 1519616 | tf_op jit(solution)/shard_map/dot_general | solution.py:214
  95.5 2.0 %copy.37 = f32[64,1216]{1,0:T(8,128)} copy(f32[64,1216]{0,1:T(8,128)} %get-tuple-element.18) | data formatting | bytes 622592 | tf_op jit(solution)/shard_map/jit(_where)/select_n | solution.py:223
  97.5 3.9 %collective-permute-start.3 = (f32[4,16,1216]{2,1,0:T(8,128)}, f32[4,16,1216]{2,1,0:T(8,128)}, u32[]{:S(2)}, u32[]{:S(2)}) collective-permute-start(f32[4,16,1216]{2,1,0:T(8,128)} %bitcast.89), channel_id=1, source_target_pairs={{0,4},{1,5},{2,6},{3,7},{4,0},{5,1},{6,2},{7,3},{8,12},{9,13},{10,... | collective-permute-start | bytes 933896 | tf_op jit(solution)/shard_map/ppermute | solution.py:224
  101.4 4.6 %all-to-all-start.2 = ((bf16[16,512,256]{2,1,0:T(8,128)(2,1)}), bf16[16,512,256]{2,1,0:T(8,128)(2,1)}, u32[]{:S(2)}, u32[]{:S(2)}) async-start(bf16[16,512,256]{2,1,0:T(8,128)(2,1)} %bitcast.83), calls=%async_computation.2 | async-start | bytes 8388608 | tf_op jit(solution)/shard_map/all_to_all | solution.py:191
  108.1 1.5 collective-permute-start.4
  110.2 3.4 %collective-permute-done.4 = f32[2,16,1216]{2,1,0:T(8,128)} collective-permute-done((f32[2,16,1216]{2,1,0:T(8,128)S(1)}, f32[2,16,1216]{2,1,0:T(8,128)}, u32[]{:S(2)}, u32[]{:S(2)}) %collective-permute-start.4) | collective-permute-done | bytes 155680 | tf_op jit(solution)/shard_map/ppermute | solution.py:224
  118.7 4.2 %gather_fusion.5 = bf16[8,512,256]{2,1,0:T(8,128)(2,1)} fusion(bf16[16,512,256]{2,1,0:T(8,128)(2,1)} %all-to-all-done, s32[1024]{0:T(1024)S(1)} %pad_clamp_fusion), kind=kCustom, calls=%fused_computation.5 | custom fusion | bytes 4194336 | tf_op jit(solution)/shard_map/gather | solution.py:197
  122.9 3.7 %collective-permute-start.8 = (bf16[4,16,608]{2,1,0:T(8,128)(2,1)S(1)}, bf16[4,16,608]{2,1,0:T(8,128)(2,1)}, u32[]{:S(2)}, u32[]{:S(2)}) collective-permute-start(bf16[4,16,608]{2,1,0:T(8,128)(2,1)S(1)} %maximum_select_fusion.1), channel_id=1, source_target_pairs={{0,4},{1,5},{2,6},{3,7},{4,0},{5,1},{6,2},{7,3},{8,12},{9,13},{10,... | collective-permute-start | bytes 233480 | tf_op jit(solution)/shard_map/ppermute | solution.py:236
  126.6 1.9 %broadcast_select_fusion = bf16[8,512,256]{2,1,0:T(8,128)(2,1)S(1)} fusion(bf16[8,512,256]{2,1,0:T(8,128)(2,1)} %gather_fusion.5, pred[8,512]{1,0:T(8,128)(4,1)S(1)} %get-tuple-element.31), kind=kLoop, calls=%fused_computation.16 | loop fusion | flops 1048576 | bytes 4198400 | tf_op jit(solution)/shard_map/jit(_where)/select_n | solution.py:195
  128.6 2.3 %concatenate.60 = bf16[8,1024,256]{2,1,0:T(8,128)(2,1)} pad(bf16[8,512,256]{2,1,0:T(8,128)(2,1)S(1)} %broadcast_select_fusion, bf16[]{:T(256)} %constant.129.clone.1), padding=0_0x0_512x0_0 | pad | bytes 6291458 | tf_op jit(solution)/shard_map/concatenate | solution.py:200
  132.9 30.0 %all-to-all-done.2 = bf16[16,512,256]{2,1,0:T(8,128)(2,1)} async-done(((bf16[16,512,256]{2,1,0:T(8,128)(2,1)}), bf16[16,512,256]{2,1,0:T(8,128)(2,1)}, u32[]{:S(2)}, u32[]{:S(2)}) %all-to-all-start.2) | async-done | bytes 4194336 | tf_op jit(solution)/shard_map/all_to_all | solution.py:191
  162.9 4.2 %gather_fusion.6 = bf16[8,512,256]{2,1,0:T(8,128)(2,1)} fusion(bf16[16,512,256]{2,1,0:T(8,128)(2,1)} %all-to-all-done.2, s32[1024]{0:T(1024)S(1)} %pad_clamp_fusion), kind=kCustom, calls=%fused_computation.6 | custom fusion | bytes 4194336 | tf_op jit(solution)/shard_map/gather | solution.py:207
  167.9 4.4 %all-to-all-start.3 = ((f32[16,8,320]{2,1,0:T(8,128)}), f32[16,8,320]{2,1,0:T(8,128)S(1)}, u32[]{:S(2)}, u32[]{:S(2)}) async-start(f32[16,8,320]{2,1,0:T(8,128)} %bitcast.21), calls=%async_computation.3 | async-start | bytes 393216 | tf_op jit(solution)/shard_map/all_to_all | solution.py:245
  172.3 2.9 %select_dynamic-update-slice_fusion = bf16[8,1024,256]{2,1,0:T(8,128)(2,1)} fusion(bf16[8,1024,256]{2,1,0:T(8,128)(2,1)} %concatenate.60, bf16[8,512,256]{2,1,0:T(8,128)(2,1)} %gather_fusion.6, pred[8,512]{1,0:T(8,128)(4,1)S(1)} %get-tuple-element.30), kind=kLoop, calls=%fused_computation.15 | loop fusion | flops 1048576 | bytes 4198400 | tf_op jit(solution)/shard_map/dynamic_update_slice | solution.py:256
  175.3 2.1 %scatter_fusion = bf16[8,1024,256]{2,1,0:T(8,128)(2,1)} fusion(bf16[8,1024,256]{2,1,0:T(8,128)(2,1)} %select_dynamic-update-slice_fusion, s32[8]{0:T(128)S(1)} %fusion.40, bf16[8,256]{1,0:T(8,128)(2,1)S(1)} %gather_fusion.7), kind=kCustom, calls=%fused_computation.8 | custom fusion | bytes 12352 | tf_op jit(solution)/shard_map/scatter | solution.py:257
  177.3 3.3 %all-to-all-done.3 = f32[16,8,320]{2,1,0:T(8,128)S(1)} async-done(((f32[16,8,320]{2,1,0:T(8,128)}), f32[16,8,320]{2,1,0:T(8,128)S(1)}, u32[]{:S(2)}, u32[]{:S(2)}) %all-to-all-start.3) | async-done | bytes 163872 | tf_op jit(solution)/shard_map/all_to_all | solution.py:245
  (106 shorter events, 21.6 us)
Async XLA Ops:
  0.6 52.3 %copy-start = (bf16[512,2560]{1,0:T(8,128)(2,1)S(1)}, bf16[512,2560]{1,0:T(8,128)(2,1)}, u32[]{:S(2)}) copy-start(bf16[512,2560]{1,0:T(8,128)(2,1)} %param.23) | copy-start | bytes 7864324
  8.4 7.4 %copy-start.4 = (s32[8,8]{1,0:T(8,128)S(1)}, s32[8,8]{1,0:T(8,128)}, u32[]{:S(2)}) copy-start(s32[8,8]{1,0:T(8,128)} %param.30) | copy-start | bytes 772
  8.4 7.4 %copy-start.5 = (bf16[8,320]{1,0:T(8,128)(2,1)S(1)}, bf16[8,320]{1,0:T(8,128)(2,1)}, u32[]{:S(2)}) copy-start(bf16[8,320]{1,0:T(8,128)(2,1)} %param.16) | copy-start | bytes 15364
  8.4 21.6 %copy-start.6 = (bf16[2560]{0:T(1024)(128)(2,1)S(1)}, bf16[2560]{0:T(1024)(128)(2,1)}, u32[]{:S(2)}) copy-start(bf16[2560]{0:T(1024)(128)(2,1)} %param.17) | copy-start | bytes 15364
  8.4 21.8 %copy-start.2 = (bf16[2560,128]{1,0:T(8,128)(2,1)S(1)}, bf16[2560,128]{1,0:T(8,128)(2,1)}, u32[]{:S(2)}) copy-start(bf16[2560,128]{1,0:T(8,128)(2,1)} %param.20) | copy-start | bytes 1966084
  8.4 23.4 %copy-start.9 = (bf16[128]{0:T(256)(128)(2,1)S(1)}, bf16[128]{0:T(256)(128)(2,1)}, u32[]{:S(2)}) copy-start(bf16[128]{0:T(256)(128)(2,1)} %param.22) | copy-start | bytes 772
  8.4 70.6 %all-to-all-start = ((bf16[16,512,256]{2,1,0:T(8,128)(2,1)}), bf16[16,512,256]{2,1,0:T(8,128)(2,1)}, u32[]{:S(2)}, u32[]{:S(2)}) async-start(bf16[16,512,256]{2,1,0:T(8,128)(2,1)} %bitcast.84), calls=%async_computation | async-start | bytes 8388608 | tf_op jit(solution)/shard_map/all_to_all | solution.py:124
  15.8 18.6 %copy-start.1 = (s32[128]{0:T(128)S(1)}, s32[128]{0:T(128)}, u32[]{:S(2)}) copy-start(s32[128]{0:T(128)} %param.29) | copy-start | bytes 1540
  35.0 5.0 %copy-start.10 = (bf16[128]{0:T(256)(128)(2,1)S(1)}, bf16[128]{0:T(256)(128)(2,1)}, u32[]{:S(2)}) copy-start(bf16[128]{0:T(256)(128)(2,1)} %param.21) | copy-start | bytes 772
  48.4 13.7 %copy-start.7 = (bf16[320]{0:T(512)(128)(2,1)S(1)}, bf16[320]{0:T(512)(128)(2,1)}, u32[]{:S(2)}) copy-start(bf16[320]{0:T(512)(128)(2,1)} %param.24) | copy-start | bytes 1924
  53.4 1.3 collective-permute-start
  54.7 4.8 %collective-permute-start.1 = (f32[8,2560]{1,0:T(8,128)S(1)}, f32[8,2560]{1,0:T(8,128)S(1)}, u32[]{:S(2)}, u32[]{:S(2)}) collective-permute-start(f32[8,2560]{1,0:T(8,128)S(1)} %add.217), channel_id=1, source_target_pairs={{0,2},{1,3},{2,0},{3,1},{4,6},{5,7},{6,4},{7,5},{8,10},{9,11},{10,... | collective-permute-start | bytes 245768 | tf_op jit(solution)/shard_map/ppermute | solution.py:165
  59.4 6.0 %collective-permute-start.2 = (f32[8,2560]{1,0:T(8,128)S(1)}, f32[8,2560]{1,0:T(8,128)S(1)}, u32[]{:S(2)}, u32[]{:S(2)}) collective-permute-start(f32[8,2560]{1,0:T(8,128)S(1)} %add.218), channel_id=1, source_target_pairs={{0,4},{1,5},{2,6},{3,7},{4,0},{5,1},{6,2},{7,3},{8,12},{9,13},{10,... | collective-permute-start | bytes 245768 | tf_op jit(solution)/shard_map/ppermute | solution.py:165
  79.7 12.8 %all-to-all-start.1 = ((bf16[16,8,576]{2,1,0:T(8,128)(2,1)}), bf16[16,8,576]{2,1,0:T(8,128)(2,1)S(1)}, u32[]{:S(2)}, u32[]{:S(2)}) async-start(bf16[16,8,576]{2,1,0:T(8,128)(2,1)} %broadcast_in_dim.165), calls=%async_computation.1 | async-start | bytes 327680 | tf_op jit(solution)/shard_map/all_to_all | solution.py:183
  84.6 8.0 %copy-start.8 = (bf16[320,608]{1,0:T(8,128)(2,1)S(1)}, bf16[320,608]{1,0:T(8,128)(2,1)}, u32[]{:S(2)}) copy-start(bf16[320,608]{1,0:T(8,128)(2,1)} %param.26) | copy-start | bytes 1167364
  97.5 9.4 %collective-permute-start.3 = (f32[4,16,1216]{2,1,0:T(8,128)}, f32[4,16,1216]{2,1,0:T(8,128)}, u32[]{:S(2)}, u32[]{:S(2)}) collective-permute-start(f32[4,16,1216]{2,1,0:T(8,128)} %bitcast.89), channel_id=1, source_target_pairs={{0,4},{1,5},{2,6},{3,7},{4,0},{5,1},{6,2},{7,3},{8,12},{9,13},{10,... | collective-permute-start | bytes 933896 | tf_op jit(solution)/shard_map/ppermute | solution.py:224
  101.4 61.5 %all-to-all-start.2 = ((bf16[16,512,256]{2,1,0:T(8,128)(2,1)}), bf16[16,512,256]{2,1,0:T(8,128)(2,1)}, u32[]{:S(2)}, u32[]{:S(2)}) async-start(bf16[16,512,256]{2,1,0:T(8,128)(2,1)} %bitcast.83), calls=%async_computation.2 | async-start | bytes 8388608 | tf_op jit(solution)/shard_map/all_to_all | solution.py:191
  108.1 5.5 %collective-permute-start.4 = (f32[2,16,1216]{2,1,0:T(8,128)S(1)}, f32[2,16,1216]{2,1,0:T(8,128)}, u32[]{:S(2)}, u32[]{:S(2)}) collective-permute-start(f32[2,16,1216]{2,1,0:T(8,128)S(1)} %slice_select_fusion.2), channel_id=1, source_target_pairs={{0,2},{1,3},{2,0},{3,1},{4,6},{5,7},{6,4},{7,5},{8,10},{9,11},{10,... | collective-permute-start | bytes 466952 | tf_op jit(solution)/shard_map/ppermute | solution.py:224
  114.5 1.4 collective-permute-start.5
  116.0 1.2 collective-permute-start.6
  117.3 5.7 %collective-permute-start.7 = (bf16[2,16,608]{2,1,0:T(8,128)(2,1)S(1)}, bf16[2,16,608]{2,1,0:T(8,128)(2,1)S(1)}, u32[]{:S(2)}, u32[]{:S(2)}) collective-permute-start(bf16[2,16,608]{2,1,0:T(8,128)(2,1)S(1)} %maximum_select_fusion.2), channel_id=1, source_target_pairs={{0,2},{1,3},{2,0},{3,1},{4,6},{5,7},{6,4},{7,5},{8,10},{9,11},{10,... | collective-permute-start | bytes 116744 | tf_op jit(solution)/shard_map/ppermute | solution.py:236
  122.9 8.6 %collective-permute-start.8 = (bf16[4,16,608]{2,1,0:T(8,128)(2,1)S(1)}, bf16[4,16,608]{2,1,0:T(8,128)(2,1)}, u32[]{:S(2)}, u32[]{:S(2)}) collective-permute-start(bf16[4,16,608]{2,1,0:T(8,128)(2,1)S(1)} %maximum_select_fusion.1), channel_id=1, source_target_pairs={{0,4},{1,5},{2,6},{3,7},{4,0},{5,1},{6,2},{7,3},{8,12},{9,13},{10,... | collective-permute-start | bytes 233480 | tf_op jit(solution)/shard_map/ppermute | solution.py:236
  128.6 4.0 %copy-start.3 = (bf16[608,320]{0,1:T(8,128)(2,1)S(1)}, bf16[608,320]{0,1:T(8,128)(2,1)}, u32[]{:S(2)}) copy-start(bf16[608,320]{0,1:T(8,128)(2,1)} %param.27) | copy-start | bytes 1167364
  167.9 12.8 %all-to-all-start.3 = ((f32[16,8,320]{2,1,0:T(8,128)}), f32[16,8,320]{2,1,0:T(8,128)S(1)}, u32[]{:S(2)}, u32[]{:S(2)}) async-start(f32[16,8,320]{2,1,0:T(8,128)} %bitcast.21), calls=%async_computation.3 | async-start | bytes 393216 | tf_op jit(solution)/shard_map/all_to_all | solution.py:245

commit v14 on v13

--- a/solution.py
+++ b/solution.py
@@ -201,12 +201,6 @@
         [span_first, jnp.zeros((row_count, second_span, channels), jnp.bfloat16)], axis=1
     )
     span_first, received_second = lax.optimization_barrier((span_first, received_second))
-    span_second = jnp.where(
-        first_span + jnp.arange(second_span, dtype=jnp.int32)[None, :, None]
-        < lengths_new[:, None, None],
-        received_second[source_owner],
-        jnp.zeros((), jnp.bfloat16),
-    )
     normed_all = gathered[:, :width_local]
     fresh_all = gathered[:, width_local:].reshape(total_rows, kv_local, channels)
     ffn_width = w_gate.shape[1]
@@ -253,7 +247,15 @@
     )
     result = (residual_wide + lowered).astype(jnp.bfloat16)
 
-    new_seq = lax.dynamic_update_slice(span_first, span_second, (0, first_span, 0))
+    new_seq = span_first
+    second_positions = first_span + jnp.arange(second_span, dtype=jnp.int32)[:, None]
+    for slot in range(row_count):
+        piece = jnp.where(
+            second_positions < lengths_new[slot],
+            lax.dynamic_index_in_dim(received_second, source_owner[slot], axis=0, keepdims=False),
+            jnp.zeros((), jnp.bfloat16),
+        )
+        new_seq = lax.dynamic_update_slice(new_seq, piece[None], (slot, first_span, 0))
     new_seq = new_seq.at[jnp.arange(row_count), lengths_new].set(
         fresh_all[arriving].reshape(row_count, channels)
     )

time: 183 us -> 181 us (0.989)
  waiting for transfers between devices: 62.6 us -> 31 us
  other arithmetic: 21.5 us -> 38 us
  between operations: 1.06 us -> 15.9 us
  local copies, waits for them, and re-layouts: 34.9 us -> 32 us
    all_to_all x1, waiting for transfers between devices: 30 us -> 2.34 us  [per_device(): lax.all_to_all(parcels_second, 'req', split_axis=0, concat_axis=0, tiled=...]
    dynamic_update_slice x1 -> x8, other arithmetic: 2.91 us -> 14.3 us  [per_device(): lax.dynamic_update_slice(new_seq, piece[None], (slot, first_span, 0))]
    lt x1 -> x9, other arithmetic: 0.08 us -> 5.24 us  [the longest x8 5.17 us: per_device(): second_positions < lengths_new[slot]]
    gather x1 -> x0, local copies, waits for them, and re-layouts: 4.2 us -> none  [per_device(): received_second[source_owner]]
    all_to_all x1, waiting for transfers between devices: 3.34 us -> 0.01 us  [per_device(): lax.all_to_all(lowered_parts.reshape(devices_req, row_count, width_local)...]
    ppermute x3, waiting for transfers between devices: 4.58 us -> 7.89 us  [per_device(): lax.ppermute(send, 'kvh', [(i, i ^ step) for i in range(devices_kvh)])]
    ppermute x3, waiting for transfers between devices: 7.43 us -> 5.04 us  [per_device(): lax.ppermute(attn_out, 'kvh', [(i, i ^ step) for i in range(devices_kvh)])]
  transfers between devices with their start and end apart: 13 -> 13, of which waited for: 10 -> 9; matrix products, arithmetic and copies ran while one was open for 27% -> 40% of each run, Pallas kernels for 0% -> 0%
where the time goes in v14:
time: 181 us; the launch traced here: 179 us
  other arithmetic  38 us (21%)
  starting transfers between devices  36.7 us (20%)
  local copies, waits for them, and re-layouts  32 us (18%)
  waiting for transfers between devices  31 us (17%)
  between operations  15.9 us (9%)
  blocking collectives  14 us (8%)
  matrix products  10.9 us (6%)
    dynamic_update_slice x8, other arithmetic, per_device(): lax.dynamic_update_slice(new_seq, piece[None], (slot, first_span, 0))  14.3 us
    all_gather x1, blocking collectives, per_device(): full_states = lax.all_gather(states, 'kvh', axis=1, tiled=True)  14 us
    all_to_all x1, waiting for transfers between devices, per_device(): lax.all_to_all(parcels_first, 'req', split_axis=0, concat_axis=0, tiled=T...  12.8 us
    ppermute x3, waiting for transfers between devices, per_device(): lax.ppermute(send, 'kvh', [(i, i ^ step) for i in range(devices_kvh)])  7.89 us
    select_n x1, other arithmetic, mask_blocks(): jnp.where(kept, blocks, jnp.where(placed, fresh[:, None, :, None, :], jnp...  7.64 us
    all_to_all x1, starting transfers between devices, per_device(): lax.all_to_all(parcels_first, 'req', split_axis=0, concat_axis=0, tiled=T...  7.34 us
    ppermute x3, starting transfers between devices, per_device(): lax.ppermute(send, 'kvh', [(i, i ^ step) for i in range(devices_kvh)])  5.33 us
    ppermute x3, starting transfers between devices, per_device(): lax.ppermute(block, 'kvh', [(i, i ^ step) for i in range(devices_kvh)])  5.23 us
  transfers between devices with their start and end apart: 13, of which 9 were waited for; matrix products, arithmetic and copies ran while one was open for 40% of the time, Pallas kernels for 0%

profile of v14, /device:TPU:0, one launch (start us, length us, event | category | flops | bytes accessed | tf_op | source)
XLA Modules:
  0.0 178.6 jit_solution(3087618088609787919)
XLA Ops:
  3.4 5.0 %gather_fusion.2 = bf16[64,128,256]{2,1,0:T(8,128)(2,1)} fusion(bf16[64,128,256]{2,1,0:T(8,128)(2,1)} %bitcast.96, s32[1024]{0:T(1024)S(1)} %pad_clamp_fusion.3), kind=kCustom, calls=%fused_computation.2 | custom fusion | bytes 8388864 | tf_op jit(solution)/shard_map/gather | solution.py:121
  8.4 7.3 %all-to-all-start = ((bf16[16,512,256]{2,1,0:T(8,128)(2,1)}), bf16[16,512,256]{2,1,0:T(8,128)(2,1)}, u32[]{:S(2)}, u32[]{:S(2)}) async-start(bf16[16,512,256]{2,1,0:T(8,128)(2,1)} %bitcast.100), calls=%async_computation | async-start | bytes 8388608 | tf_op jit(solution)/shard_map/all_to_all | solution.py:124
  15.8 14.0 %all-gather = bf16[8,320,8]{1,2,0:T(8,128)(2,1)S(1)} all-gather(bf16[1,320,8]{1,2,0:T(8,128)(2,1)S(1)} %bitcast.108), channel_id=1, replica_groups=mesh['req'=16,'kvh'=8] {'kvh'}, dimensions={0}, use_global_device_ids=true | all-gather | bytes 46080 | tf_op jit(solution)/shard_map/all_gather | solution.py:134
  32.7 2.3 %multiply_reduce_fusion.1 = (f32[8,4]{0,1:T(4,128)S(1)}, f32[8,4,128]{2,0,1:T(8,128)S(1)}) fusion(bf16[8,2560]{1,0:T(8,128)(2,1)S(1)} %fusion.17, bf16[2560,512]{1,0:T(8,128)(2,1)} %param.18), kind=kOutput, calls=%fused_computation.69 | convolution fusion | flops 20979680 | bytes 2678912 | tf_op jit(solution)/shard_map/dot_general | solution.py:138
  35.2 5.0 %gather_fusion.1 = bf16[64,128,256]{2,1,0:T(8,128)(2,1)} fusion(bf16[64,128,256]{2,1,0:T(8,128)(2,1)} %bitcast.97, s32[1024]{0:T(1024)S(1)} %pad_clamp_fusion.4), kind=kCustom, calls=%fused_computation.1 | custom fusion | bytes 8388864 | tf_op jit(solution)/shard_map/gather | solution.py:155
  40.8 7.6 %select_select_fusion = bf16[8,1,1024,256]{3,2,0,1:T(8,128)(2,1)} fusion(bf16[8,1,1024,256]{3,2,0,1:T(8,128)(2,1)} %bitcast.101, pred[8,1024]{1,0:T(8,128)(4,1)S(1)} %get-tuple-element.27, pred[8,1024]{1,0:T(8,128)(4,1)S(1)} %get-tuple-element.26, bf16[8,256]{1,0:T(8,128)(2,1)S(1)} %maximum_bitcast_fusion), kind=kLoop, calls=%fused_computation.9 | loop fusion | flops 4194304 | bytes 8409088 | tf_op jit(solution)/shard_map/jit(_where)/select_n | solution.py:48
  48.4 2.5 %fusion.55 = (f32[8,4]{1,0:T(8,128)S(1)}, f32[8,4,1024]{2,1,0:T(4,128)S(1)}) fusion(bf16[8,1,1024,256]{3,2,0,1:T(8,128)(2,1)} %select_select_fusion, pred[8,1024]{1,0:T(8,128)(4,1)S(1)} %get-tuple-element.49, bf16[8,4,64]{2,1,0:T(4,128)(2,1)S(1)} %get-tuple-element.23, bf16[8,4,64]{2,1,0:T(4,128)(2,1)S(1)} %get-tuple-element.22), kind=kOutput, calls=%fused_computation.145 | convolution fusion | flops 8537087 | bytes 2244736 | tf_op jit(solution)/shard_map/sub | solution.py:67
  50.9 2.0 %fusion.8 = bf16[1,8,4,128]{3,2,1,0:T(4,128)(2,1)S(1)} fusion(bf16[8,1,1024,256]{3,2,0,1:T(8,128)(2,1)} %select_select_fusion, f32[8,4,1024]{2,1,0:T(4,128)S(1)} %get-tuple-element.55, f32[8,4]{1,0:T(8,128)S(1)} %get-tuple-element.54), kind=kOutput, calls=%fused_computation.21 | convolution fusion | flops 8458240 | bytes 2236544 | tf_op jit(solution)/shard_map/rkgt,rktd->rkgd/dot_general | solution.py:68
  57.6 2.3 %collective-permute-done.1 = f32[8,2560]{1,0:T(8,128)S(1)} collective-permute-done((f32[8,2560]{1,0:T(8,128)S(1)}, f32[8,2560]{1,0:T(8,128)S(1)}, u32[]{:S(2)}, u32[]{:S(2)}) %collective-permute-start.1) | collective-permute-done | bytes 81952 | tf_op jit(solution)/shard_map/ppermute | solution.py:165
  59.9 2.6 %collective-permute-start.2 = (f32[8,2560]{1,0:T(8,128)S(1)}, f32[8,2560]{1,0:T(8,128)S(1)}, u32[]{:S(2)}, u32[]{:S(2)}) collective-permute-start(f32[8,2560]{1,0:T(8,128)S(1)} %add.277), channel_id=1, source_target_pairs={{0,4},{1,5},{2,6},{3,7},{4,0},{5,1},{6,2},{7,3},{8,12},{9,13},{10,... | collective-permute-start | bytes 245768 | tf_op jit(solution)/shard_map/ppermute | solution.py:165
  63.2 2.7 %collective-permute-done.2 = f32[8,2560]{1,0:T(8,128)S(1)} collective-permute-done((f32[8,2560]{1,0:T(8,128)S(1)}, f32[8,2560]{1,0:T(8,128)S(1)}, u32[]{:S(2)}, u32[]{:S(2)}) %collective-permute-start.2) | collective-permute-done | bytes 81952 | tf_op jit(solution)/shard_map/ppermute | solution.py:165
  66.2 12.8 %all-to-all-done = bf16[16,512,256]{2,1,0:T(8,128)(2,1)} async-done(((bf16[16,512,256]{2,1,0:T(8,128)(2,1)}), bf16[16,512,256]{2,1,0:T(8,128)(2,1)}, u32[]{:S(2)}, u32[]{:S(2)}) %all-to-all-start) | async-done | bytes 4194336 | tf_op jit(solution)/shard_map/all_to_all | solution.py:124
  79.7 4.7 %all-to-all-start.1 = ((bf16[16,8,576]{2,1,0:T(8,128)(2,1)}), bf16[16,8,576]{2,1,0:T(8,128)(2,1)S(1)}, u32[]{:S(2)}, u32[]{:S(2)}) async-start(bf16[16,8,576]{2,1,0:T(8,128)(2,1)} %broadcast_in_dim.219), calls=%async_computation.1 | async-start | bytes 327680 | tf_op jit(solution)/shard_map/all_to_all | solution.py:183
  85.2 5.0 %gather_fusion.3 = bf16[64,128,256]{2,1,0:T(8,128)(2,1)} fusion(bf16[64,128,256]{2,1,0:T(8,128)(2,1)} %bitcast.98, s32[1024]{0:T(1024)S(1)} %pad_clamp_fusion.2), kind=kCustom, calls=%fused_computation.3 | custom fusion | bytes 8388864 | tf_op jit(solution)/shard_map/gather | solution.py:128
  90.1 2.5 %all-to-all-done.1 = bf16[16,8,576]{2,1,0:T(8,128)(2,1)S(1)} async-done(((bf16[16,8,576]{2,1,0:T(8,128)(2,1)}), bf16[16,8,576]{2,1,0:T(8,128)(2,1)S(1)}, u32[]{:S(2)}, u32[]{:S(2)}) %all-to-all-start.1) | async-done | bytes 147488 | tf_op jit(solution)/shard_map/all_to_all | solution.py:183
  92.6 5.0 %all-to-all-start.2 = ((bf16[16,512,256]{2,1,0:T(8,128)(2,1)}), bf16[16,512,256]{2,1,0:T(8,128)(2,1)}, u32[]{:S(2)}, u32[]{:S(2)}) async-start(bf16[16,512,256]{2,1,0:T(8,128)(2,1)} %bitcast.99), calls=%async_computation.2 | async-start | bytes 8388608 | tf_op jit(solution)/shard_map/all_to_all | solution.py:191
  97.6 1.8 %fusion.10 = f32[128,1216]{0,1:T(8,128)S(1)} fusion(bf16[320,608]{1,0:T(8,128)(2,1)S(1)} %copy-done.8, bf16[320,608]{1,0:T(8,128)(2,1)} %param.25, bf16[128,576]{1,0:T(8,128)(2,1)S(1)} %bitcast.106), kind=kOutput, calls=%fused_computation.24 | convolution fusion | flops 101171200 | bytes 1519616 | tf_op jit(solution)/shard_map/dot_general | solution.py:208
  100.5 2.0 %copy.37 = f32[64,1216]{1,0:T(8,128)} copy(f32[64,1216]{0,1:T(8,128)} %get-tuple-element.20) | data formatting | bytes 622592 | tf_op jit(solution)/shard_map/jit(_where)/select_n | solution.py:217
  102.5 3.9 %collective-permute-start.3 = (f32[4,16,1216]{2,1,0:T(8,128)}, f32[4,16,1216]{2,1,0:T(8,128)}, u32[]{:S(2)}, u32[]{:S(2)}) collective-permute-start(f32[4,16,1216]{2,1,0:T(8,128)} %bitcast.105), channel_id=1, source_target_pairs={{0,4},{1,5},{2,6},{3,7},{4,0},{5,1},{6,2},{7,3},{8,12},{9,13},{10,... | collective-permute-start | bytes 933896 | tf_op jit(solution)/shard_map/ppermute | solution.py:218
  108.1 4.4 %collective-permute-done.3 = f32[4,16,1216]{2,1,0:T(8,128)} collective-permute-done((f32[4,16,1216]{2,1,0:T(8,128)}, f32[4,16,1216]{2,1,0:T(8,128)}, u32[]{:S(2)}, u32[]{:S(2)}) %collective-permute-start.3) | collective-permute-done | bytes 311328 | tf_op jit(solution)/shard_map/ppermute | solution.py:218
  116.3 2.8 %collective-permute-done.4 = f32[2,16,1216]{2,1,0:T(8,128)} collective-permute-done((f32[2,16,1216]{2,1,0:T(8,128)S(1)}, f32[2,16,1216]{2,1,0:T(8,128)}, u32[]{:S(2)}, u32[]{:S(2)}) %collective-permute-start.4) | collective-permute-done | bytes 155680 | tf_op jit(solution)/shard_map/ppermute | solution.py:218
  139.6 4.2 %gather_fusion.5 = bf16[8,512,256]{2,1,0:T(8,128)(2,1)} fusion(bf16[16,512,256]{2,1,0:T(8,128)(2,1)} %all-to-all-done, s32[1024]{0:T(1024)S(1)} %pad_clamp_fusion), kind=kCustom, calls=%fused_computation.5 | custom fusion | bytes 4194336 | tf_op jit(solution)/shard_map/gather | solution.py:197
  143.9 3.7 %collective-permute-start.8 = (bf16[4,16,608]{2,1,0:T(8,128)(2,1)S(1)}, bf16[4,16,608]{2,1,0:T(8,128)(2,1)}, u32[]{:S(2)}, u32[]{:S(2)}) collective-permute-start(bf16[4,16,608]{2,1,0:T(8,128)(2,1)S(1)} %maximum_select_fusion.1), channel_id=1, source_target_pairs={{0,4},{1,5},{2,6},{3,7},{4,0},{5,1},{6,2},{7,3},{8,12},{9,13},{10,... | collective-permute-start | bytes 233480 | tf_op jit(solution)/shard_map/ppermute | solution.py:230
  147.5 1.9 %broadcast_select_fusion = bf16[8,512,256]{2,1,0:T(8,128)(2,1)S(1)} fusion(bf16[8,512,256]{2,1,0:T(8,128)(2,1)} %gather_fusion.5, pred[8,512]{1,0:T(8,128)(4,1)S(1)} %iota_compare_fusion.1), kind=kLoop, calls=%fused_computation.14 | loop fusion | flops 1048576 | bytes 4198400 | tf_op jit(solution)/shard_map/jit(_where)/select_n | solution.py:195
  149.5 2.3 %concatenate.60 = bf16[8,1024,256]{2,1,0:T(8,128)(2,1)} pad(bf16[8,512,256]{2,1,0:T(8,128)(2,1)S(1)} %broadcast_select_fusion, bf16[]{:T(256)} %constant.151.clone.1), padding=0_0x0_512x0_0 | pad | bytes 6291458 | tf_op jit(solution)/shard_map/concatenate | solution.py:200
  153.8 2.3 %all-to-all-done.2 = bf16[16,512,256]{2,1,0:T(8,128)(2,1)} async-done(((bf16[16,512,256]{2,1,0:T(8,128)(2,1)}), bf16[16,512,256]{2,1,0:T(8,128)(2,1)}, u32[]{:S(2)}, u32[]{:S(2)}) %all-to-all-start.2) | async-done | bytes 4194336 | tf_op jit(solution)/shard_map/all_to_all | solution.py:191
  156.9 4.5 %all-to-all-start.3 = ((f32[16,8,320]{2,1,0:T(8,128)}), f32[16,8,320]{2,1,0:T(8,128)S(1)}, u32[]{:S(2)}, u32[]{:S(2)}) async-start(f32[16,8,320]{2,1,0:T(8,128)} %bitcast.21), calls=%async_computation.3 | async-start | bytes 393216 | tf_op jit(solution)/shard_map/all_to_all | solution.py:239
  161.5 1.8 %select_dynamic-update-slice_fusion.7 = bf16[8,1024,256]{2,1,0:T(8,128)(2,1)} fusion(bf16[8,1024,256]{2,1,0:T(8,128)(2,1)} %concatenate.60, bf16[16,512,256]{2,1,0:T(8,128)(2,1)} %all-to-all-done.2, s32[]{:T(128)S(6)} %select_n.297, pred[512]{0:T(512)(128)(4,1)S(1)} %fusion.45), kind=kLoop, calls=%fused_computation.37 | loop fusion | flops 131072 | bytes 524804 | tf_op jit(solution)/shard_map/dynamic_update_slice | solution.py:258
  163.3 1.8 %select_dynamic-update-slice_fusion.6 = bf16[8,1024,256]{2,1,0:T(8,128)(2,1)} fusion(bf16[8,1024,256]{2,1,0:T(8,128)(2,1)} %select_dynamic-update-slice_fusion.7, bf16[16,512,256]{2,1,0:T(8,128)(2,1)} %all-to-all-done.2, s32[]{:T(128)S(6)} %select_n.299, pred[512]{0:T(512)(128)(4,1)S(1)} %fusion.44), kind=kLoop, calls=%fused_computation.36 | loop fusion | flops 131072 | bytes 524804 | tf_op jit(solution)/shard_map/dynamic_update_slice | solution.py:258
  165.1 1.8 %select_dynamic-update-slice_fusion.5 = bf16[8,1024,256]{2,1,0:T(8,128)(2,1)} fusion(bf16[8,1024,256]{2,1,0:T(8,128)(2,1)} %select_dynamic-update-slice_fusion.6, bf16[16,512,256]{2,1,0:T(8,128)(2,1)} %all-to-all-done.2, s32[]{:T(128)S(6)} %select_n.301, pred[512]{0:T(512)(128)(4,1)S(1)} %fusion.43), kind=kLoop, calls=%fused_computation.35 | loop fusion | flops 131072 | bytes 524804 | tf_op jit(solution)/shard_map/dynamic_update_slice | solution.py:258
  174.0 1.8 %select_dynamic-update-slice_fusion = bf16[8,1024,256]{2,1,0:T(8,128)(2,1)} fusion(bf16[8,1024,256]{2,1,0:T(8,128)(2,1)} %select_dynamic-update-slice_fusion.1, bf16[16,512,256]{2,1,0:T(8,128)(2,1)} %all-to-all-done.2, s32[]{:T(128)S(6)} %select_n.311, pred[512]{0:T(512)(128)(4,1)S(1)} %fusion.38), kind=kLoop, calls=%fused_computation.30 | loop fusion | flops 131072 | bytes 524804 | tf_op jit(solution)/shard_map/dynamic_update_slice | solution.py:258
  175.8 2.1 %scatter_fusion = bf16[8,1024,256]{2,1,0:T(8,128)(2,1)} fusion(bf16[8,1024,256]{2,1,0:T(8,128)(2,1)} %select_dynamic-update-slice_fusion, s32[8]{0:T(128)S(1)} %fusion.48, bf16[8,256]{1,0:T(8,128)(2,1)S(1)} %gather_fusion.6), kind=kCustom, calls=%fused_computation.7 | custom fusion | bytes 12352 | tf_op jit(solution)/shard_map/scatter | solution.py:259
  (121 shorter events, 36.1 us)
Async XLA Ops:
  0.6 52.3 %copy-start = (bf16[512,2560]{1,0:T(8,128)(2,1)S(1)}, bf16[512,2560]{1,0:T(8,128)(2,1)}, u32[]{:S(2)}) copy-start(bf16[512,2560]{1,0:T(8,128)(2,1)} %param.23) | copy-start | bytes 7864324
  8.4 7.4 %copy-start.4 = (s32[8,8]{1,0:T(8,128)S(1)}, s32[8,8]{1,0:T(8,128)}, u32[]{:S(2)}) copy-start(s32[8,8]{1,0:T(8,128)} %param.30) | copy-start | bytes 772
  8.4 7.4 %copy-start.5 = (bf16[8,320]{1,0:T(8,128)(2,1)S(1)}, bf16[8,320]{1,0:T(8,128)(2,1)}, u32[]{:S(2)}) copy-start(bf16[8,320]{1,0:T(8,128)(2,1)} %param.16) | copy-start | bytes 15364
  8.4 21.7 %copy-start.6 = (bf16[2560]{0:T(1024)(128)(2,1)S(1)}, bf16[2560]{0:T(1024)(128)(2,1)}, u32[]{:S(2)}) copy-start(bf16[2560]{0:T(1024)(128)(2,1)} %param.17) | copy-start | bytes 15364
  8.4 21.8 %copy-start.2 = (bf16[2560,128]{1,0:T(8,128)(2,1)S(1)}, bf16[2560,128]{1,0:T(8,128)(2,1)}, u32[]{:S(2)}) copy-start(bf16[2560,128]{1,0:T(8,128)(2,1)} %param.19) | copy-start | bytes 1966084
  8.4 22.2 %copy-start.9 = (bf16[128]{0:T(256)(128)(2,1)S(1)}, bf16[128]{0:T(256)(128)(2,1)}, u32[]{:S(2)}) copy-start(bf16[128]{0:T(256)(128)(2,1)} %param.22) | copy-start | bytes 772
  8.4 22.2 %copy-start.1 = (s32[128]{0:T(128)S(1)}, s32[128]{0:T(128)}, u32[]{:S(2)}) copy-start(s32[128]{0:T(128)} %param.29) | copy-start | bytes 1540
  8.4 70.6 %all-to-all-start = ((bf16[16,512,256]{2,1,0:T(8,128)(2,1)}), bf16[16,512,256]{2,1,0:T(8,128)(2,1)}, u32[]{:S(2)}, u32[]{:S(2)}) async-start(bf16[16,512,256]{2,1,0:T(8,128)(2,1)} %bitcast.100), calls=%async_computation | async-start | bytes 8388608 | tf_op jit(solution)/shard_map/all_to_all | solution.py:124
  35.2 5.1 %copy-start.10 = (bf16[128]{0:T(256)(128)(2,1)S(1)}, bf16[128]{0:T(256)(128)(2,1)}, u32[]{:S(2)}) copy-start(bf16[128]{0:T(256)(128)(2,1)} %param.21) | copy-start | bytes 772
  48.4 5.3 %copy-start.7 = (bf16[320]{0:T(512)(128)(2,1)S(1)}, bf16[320]{0:T(512)(128)(2,1)}, u32[]{:S(2)}) copy-start(bf16[320]{0:T(512)(128)(2,1)} %param.24) | copy-start | bytes 1924
  53.4 1.9 %collective-permute-start = (f32[8,2560]{1,0:T(8,128)S(1)}, f32[8,2560]{1,0:T(8,128)S(1)}, u32[]{:S(2)}, u32[]{:S(2)}) collective-permute-start(f32[8,2560]{1,0:T(8,128)S(1)} %fusion.24), channel_id=1, source_target_pairs={{0,1},{1,0},{2,3},{3,2},{4,5},{5,4},{6,7},{7,6},{8,9},{9,8},{10,11... | collective-permute-start | bytes 245768 | tf_op jit(solution)/shard_map/ppermute | solution.py:165
  55.3 4.6 %collective-permute-start.1 = (f32[8,2560]{1,0:T(8,128)S(1)}, f32[8,2560]{1,0:T(8,128)S(1)}, u32[]{:S(2)}, u32[]{:S(2)}) collective-permute-start(f32[8,2560]{1,0:T(8,128)S(1)} %add.276), channel_id=1, source_target_pairs={{0,2},{1,3},{2,0},{3,1},{4,6},{5,7},{6,4},{7,5},{8,10},{9,11},{10,... | collective-permute-start | bytes 245768 | tf_op jit(solution)/shard_map/ppermute | solution.py:165
  59.9 6.0 %collective-permute-start.2 = (f32[8,2560]{1,0:T(8,128)S(1)}, f32[8,2560]{1,0:T(8,128)S(1)}, u32[]{:S(2)}, u32[]{:S(2)}) collective-permute-start(f32[8,2560]{1,0:T(8,128)S(1)} %add.277), channel_id=1, source_target_pairs={{0,4},{1,5},{2,6},{3,7},{4,0},{5,1},{6,2},{7,3},{8,12},{9,13},{10,... | collective-permute-start | bytes 245768 | tf_op jit(solution)/shard_map/ppermute | solution.py:165
  79.7 12.8 %all-to-all-start.1 = ((bf16[16,8,576]{2,1,0:T(8,128)(2,1)}), bf16[16,8,576]{2,1,0:T(8,128)(2,1)S(1)}, u32[]{:S(2)}, u32[]{:S(2)}) async-start(bf16[16,8,576]{2,1,0:T(8,128)(2,1)} %broadcast_in_dim.219), calls=%async_computation.1 | async-start | bytes 327680 | tf_op jit(solution)/shard_map/all_to_all | solution.py:183
  92.6 5.0 %copy-start.8 = (bf16[320,608]{1,0:T(8,128)(2,1)S(1)}, bf16[320,608]{1,0:T(8,128)(2,1)}, u32[]{:S(2)}) copy-start(bf16[320,608]{1,0:T(8,128)(2,1)} %param.26) | copy-start | bytes 1167364
  92.6 63.5 %all-to-all-start.2 = ((bf16[16,512,256]{2,1,0:T(8,128)(2,1)}), bf16[16,512,256]{2,1,0:T(8,128)(2,1)}, u32[]{:S(2)}, u32[]{:S(2)}) async-start(bf16[16,512,256]{2,1,0:T(8,128)(2,1)} %bitcast.99), calls=%async_computation.2 | async-start | bytes 8388608 | tf_op jit(solution)/shard_map/all_to_all | solution.py:191
  102.5 10.0 %collective-permute-start.3 = (f32[4,16,1216]{2,1,0:T(8,128)}, f32[4,16,1216]{2,1,0:T(8,128)}, u32[]{:S(2)}, u32[]{:S(2)}) collective-permute-start(f32[4,16,1216]{2,1,0:T(8,128)} %bitcast.105), channel_id=1, source_target_pairs={{0,4},{1,5},{2,6},{3,7},{4,0},{5,1},{6,2},{7,3},{8,12},{9,13},{10,... | collective-permute-start | bytes 933896 | tf_op jit(solution)/shard_map/ppermute | solution.py:218
  113.6 5.5 %collective-permute-start.4 = (f32[2,16,1216]{2,1,0:T(8,128)S(1)}, f32[2,16,1216]{2,1,0:T(8,128)}, u32[]{:S(2)}, u32[]{:S(2)}) collective-permute-start(f32[2,16,1216]{2,1,0:T(8,128)S(1)} %slice_select_fusion.2), channel_id=1, source_target_pairs={{0,2},{1,3},{2,0},{3,1},{4,6},{5,7},{6,4},{7,5},{8,10},{9,11},{10,... | collective-permute-start | bytes 466952 | tf_op jit(solution)/shard_map/ppermute | solution.py:218
  120.1 1.4 collective-permute-start.5
  121.6 1.2 collective-permute-start.6
  122.8 21.0 %collective-permute-start.7 = (bf16[2,16,608]{2,1,0:T(8,128)(2,1)S(1)}, bf16[2,16,608]{2,1,0:T(8,128)(2,1)S(1)}, u32[]{:S(2)}, u32[]{:S(2)}) collective-permute-start(bf16[2,16,608]{2,1,0:T(8,128)(2,1)S(1)} %maximum_select_fusion.2), channel_id=1, source_target_pairs={{0,2},{1,3},{2,0},{3,1},{4,6},{5,7},{6,4},{7,5},{8,10},{9,11},{10,... | collective-permute-start | bytes 116744 | tf_op jit(solution)/shard_map/ppermute | solution.py:230
  143.9 8.6 %collective-permute-start.8 = (bf16[4,16,608]{2,1,0:T(8,128)(2,1)S(1)}, bf16[4,16,608]{2,1,0:T(8,128)(2,1)}, u32[]{:S(2)}, u32[]{:S(2)}) collective-permute-start(bf16[4,16,608]{2,1,0:T(8,128)(2,1)S(1)} %maximum_select_fusion.1), channel_id=1, source_target_pairs={{0,4},{1,5},{2,6},{3,7},{4,0},{5,1},{6,2},{7,3},{8,12},{9,13},{10,... | collective-permute-start | bytes 233480 | tf_op jit(solution)/shard_map/ppermute | solution.py:230
  149.5 4.0 %copy-start.3 = (bf16[608,320]{0,1:T(8,128)(2,1)S(1)}, bf16[608,320]{0,1:T(8,128)(2,1)}, u32[]{:S(2)}) copy-start(bf16[608,320]{0,1:T(8,128)(2,1)} %param.27) | copy-start | bytes 1167364
  156.9 21.0 %all-to-all-start.3 = ((f32[16,8,320]{2,1,0:T(8,128)}), f32[16,8,320]{2,1,0:T(8,128)S(1)}, u32[]{:S(2)}, u32[]{:S(2)}) async-start(f32[16,8,320]{2,1,0:T(8,128)} %bitcast.21), calls=%async_computation.3 | async-start | bytes 393216 | tf_op jit(solution)/shard_map/all_to_all | solution.py:239

commit v15 on v14

--- a/solution.py
+++ b/solution.py
@@ -237,12 +237,12 @@
     lowered_parts, _ = lax.optimization_barrier((lowered_parts, received_second))
     lowered = jnp.sum(
         lax.all_to_all(
-            lowered_parts.reshape(devices_req, row_count, width_local),
+            lowered_parts.astype(jnp.bfloat16).reshape(devices_req, row_count, width_local),
             "req",
             split_axis=0,
             concat_axis=0,
             tiled=True,
-        ),
+        ).astype(jnp.float32),
         axis=0,
     )
     result = (residual_wide + lowered).astype(jnp.bfloat16)

time: 181 us -> 181 us (level)
  no operation moved by 1% of the time
where the time goes in v15:
time: 181 us; the launch traced here: 179 us
  other arithmetic  38 us (21%)
  starting transfers between devices  36.7 us (20%)
  local copies, waits for them, and re-layouts  31.9 us (18%)
  waiting for transfers between devices  31 us (17%)
  between operations  15.9 us (9%)
  blocking collectives  14 us (8%)
  matrix products  10.9 us (6%)
    dynamic_update_slice x8, other arithmetic, per_device(): lax.dynamic_update_slice(new_seq, piece[None], (slot, first_span, 0))  14.3 us
    all_gather x1, blocking collectives, per_device(): full_states = lax.all_gather(states, 'kvh', axis=1, tiled=True)  14 us
    all_to_all x1, waiting for transfers between devices, per_device(): lax.all_to_all(parcels_first, 'req', split_axis=0, concat_axis=0, tiled=T...  12.8 us
    ppermute x3, waiting for transfers between devices, per_device(): lax.ppermute(send, 'kvh', [(i, i ^ step) for i in range(devices_kvh)])  7.89 us
    select_n x1, other arithmetic, mask_blocks(): jnp.where(kept, blocks, jnp.where(placed, fresh[:, None, :, None, :], jnp...  7.64 us
    all_to_all x1, starting transfers between devices, per_device(): lax.all_to_all(parcels_first, 'req', split_axis=0, concat_axis=0, tiled=T...  7.34 us
    ppermute x3, starting transfers between devices, per_device(): lax.ppermute(send, 'kvh', [(i, i ^ step) for i in range(devices_kvh)])  5.33 us
    ppermute x3, starting transfers between devices, per_device(): lax.ppermute(block, 'kvh', [(i, i ^ step) for i in range(devices_kvh)])  5.23 us
  transfers between devices with their start and end apart: 13, of which 9 were waited for; matrix products, arithmetic and copies ran while one was open for 40% of the time, Pallas kernels for 0%

profile of v15, /device:TPU:0, one launch (start us, length us, event | category | flops | bytes accessed | tf_op | source)
XLA Modules:
  0.0 178.5 jit_solution(13392371185773123080)
XLA Ops:
  3.4 5.0 %gather_fusion.2 = bf16[64,128,256]{2,1,0:T(8,128)(2,1)} fusion(bf16[64,128,256]{2,1,0:T(8,128)(2,1)} %bitcast.96, s32[1024]{0:T(1024)S(1)} %pad_clamp_fusion.3), kind=kCustom, calls=%fused_computation.2 | custom fusion | bytes 8388864 | tf_op jit(solution)/shard_map/gather | solution.py:121
  8.4 7.3 %all-to-all-start = ((bf16[16,512,256]{2,1,0:T(8,128)(2,1)}), bf16[16,512,256]{2,1,0:T(8,128)(2,1)}, u32[]{:S(2)}, u32[]{:S(2)}) async-start(bf16[16,512,256]{2,1,0:T(8,128)(2,1)} %bitcast.100), calls=%async_computation | async-start | bytes 8388608 | tf_op jit(solution)/shard_map/all_to_all | solution.py:124
  15.8 14.0 %all-gather = bf16[8,320,8]{1,2,0:T(8,128)(2,1)S(1)} all-gather(bf16[1,320,8]{1,2,0:T(8,128)(2,1)S(1)} %bitcast.108), channel_id=1, replica_groups=mesh['req'=16,'kvh'=8] {'kvh'}, dimensions={0}, use_global_device_ids=true | all-gather | bytes 46080 | tf_op jit(solution)/shard_map/all_gather | solution.py:134
  32.7 2.3 %multiply_reduce_fusion.1 = (f32[8,4]{0,1:T(4,128)S(1)}, f32[8,4,128]{2,0,1:T(8,128)S(1)}) fusion(bf16[8,2560]{1,0:T(8,128)(2,1)S(1)} %fusion.17, bf16[2560,512]{1,0:T(8,128)(2,1)} %param.18), kind=kOutput, calls=%fused_computation.70 | convolution fusion | flops 20979680 | bytes 2678912 | tf_op jit(solution)/shard_map/dot_general | solution.py:138
  35.2 5.0 %gather_fusion.1 = bf16[64,128,256]{2,1,0:T(8,128)(2,1)} fusion(bf16[64,128,256]{2,1,0:T(8,128)(2,1)} %bitcast.97, s32[1024]{0:T(1024)S(1)} %pad_clamp_fusion.4), kind=kCustom, calls=%fused_computation.1 | custom fusion | bytes 8388864 | tf_op jit(solution)/shard_map/gather | solution.py:155
  40.8 7.6 %select_select_fusion = bf16[8,1,1024,256]{3,2,0,1:T(8,128)(2,1)} fusion(bf16[8,1,1024,256]{3,2,0,1:T(8,128)(2,1)} %bitcast.101, pred[8,1024]{1,0:T(8,128)(4,1)S(1)} %get-tuple-element.27, pred[8,1024]{1,0:T(8,128)(4,1)S(1)} %get-tuple-element.26, bf16[8,256]{1,0:T(8,128)(2,1)S(1)} %maximum_bitcast_fusion), kind=kLoop, calls=%fused_computation.9 | loop fusion | flops 4194304 | bytes 8409088 | tf_op jit(solution)/shard_map/jit(_where)/select_n | solution.py:48
  48.4 2.5 %fusion.55 = (f32[8,4]{1,0:T(8,128)S(1)}, f32[8,4,1024]{2,1,0:T(4,128)S(1)}) fusion(bf16[8,1,1024,256]{3,2,0,1:T(8,128)(2,1)} %select_select_fusion, pred[8,1024]{1,0:T(8,128)(4,1)S(1)} %get-tuple-element.49, bf16[8,4,64]{2,1,0:T(4,128)(2,1)S(1)} %get-tuple-element.23, bf16[8,4,64]{2,1,0:T(4,128)(2,1)S(1)} %get-tuple-element.22), kind=kOutput, calls=%fused_computation.146 | convolution fusion | flops 8537087 | bytes 2244736 | tf_op jit(solution)/shard_map/sub | solution.py:67
  50.9 2.0 %fusion.8 = bf16[1,8,4,128]{3,2,1,0:T(4,128)(2,1)S(1)} fusion(bf16[8,1,1024,256]{3,2,0,1:T(8,128)(2,1)} %select_select_fusion, f32[8,4,1024]{2,1,0:T(4,128)S(1)} %get-tuple-element.55, f32[8,4]{1,0:T(8,128)S(1)} %get-tuple-element.54), kind=kOutput, calls=%fused_computation.21 | convolution fusion | flops 8458240 | bytes 2236544 | tf_op jit(solution)/shard_map/rkgt,rktd->rkgd/dot_general | solution.py:68
  57.6 2.3 %collective-permute-done.1 = f32[8,2560]{1,0:T(8,128)S(1)} collective-permute-done((f32[8,2560]{1,0:T(8,128)S(1)}, f32[8,2560]{1,0:T(8,128)S(1)}, u32[]{:S(2)}, u32[]{:S(2)}) %collective-permute-start.1) | collective-permute-done | bytes 81952 | tf_op jit(solution)/shard_map/ppermute | solution.py:165
  59.9 2.6 %collective-permute-start.2 = (f32[8,2560]{1,0:T(8,128)S(1)}, f32[8,2560]{1,0:T(8,128)S(1)}, u32[]{:S(2)}, u32[]{:S(2)}) collective-permute-start(f32[8,2560]{1,0:T(8,128)S(1)} %add.277), channel_id=1, source_target_pairs={{0,4},{1,5},{2,6},{3,7},{4,0},{5,1},{6,2},{7,3},{8,12},{9,13},{10,... | collective-permute-start | bytes 245768 | tf_op jit(solution)/shard_map/ppermute | solution.py:165
  63.2 2.7 %collective-permute-done.2 = f32[8,2560]{1,0:T(8,128)S(1)} collective-permute-done((f32[8,2560]{1,0:T(8,128)S(1)}, f32[8,2560]{1,0:T(8,128)S(1)}, u32[]{:S(2)}, u32[]{:S(2)}) %collective-permute-start.2) | collective-permute-done | bytes 81952 | tf_op jit(solution)/shard_map/ppermute | solution.py:165
  66.2 12.8 %all-to-all-done = bf16[16,512,256]{2,1,0:T(8,128)(2,1)} async-done(((bf16[16,512,256]{2,1,0:T(8,128)(2,1)}), bf16[16,512,256]{2,1,0:T(8,128)(2,1)}, u32[]{:S(2)}, u32[]{:S(2)}) %all-to-all-start) | async-done | bytes 4194336 | tf_op jit(solution)/shard_map/all_to_all | solution.py:124
  79.7 4.7 %all-to-all-start.1 = ((bf16[16,8,576]{2,1,0:T(8,128)(2,1)}), bf16[16,8,576]{2,1,0:T(8,128)(2,1)S(1)}, u32[]{:S(2)}, u32[]{:S(2)}) async-start(bf16[16,8,576]{2,1,0:T(8,128)(2,1)} %broadcast_in_dim.219), calls=%async_computation.1 | async-start | bytes 327680 | tf_op jit(solution)/shard_map/all_to_all | solution.py:183
  85.2 5.0 %gather_fusion.3 = bf16[64,128,256]{2,1,0:T(8,128)(2,1)} fusion(bf16[64,128,256]{2,1,0:T(8,128)(2,1)} %bitcast.98, s32[1024]{0:T(1024)S(1)} %pad_clamp_fusion.2), kind=kCustom, calls=%fused_computation.3 | custom fusion | bytes 8388864 | tf_op jit(solution)/shard_map/gather | solution.py:128
  90.1 2.5 %all-to-all-done.1 = bf16[16,8,576]{2,1,0:T(8,128)(2,1)S(1)} async-done(((bf16[16,8,576]{2,1,0:T(8,128)(2,1)}), bf16[16,8,576]{2,1,0:T(8,128)(2,1)S(1)}, u32[]{:S(2)}, u32[]{:S(2)}) %all-to-all-start.1) | async-done | bytes 147488 | tf_op jit(solution)/shard_map/all_to_all | solution.py:183
  92.6 5.0 %all-to-all-start.2 = ((bf16[16,512,256]{2,1,0:T(8,128)(2,1)}), bf16[16,512,256]{2,1,0:T(8,128)(2,1)}, u32[]{:S(2)}, u32[]{:S(2)}) async-start(bf16[16,512,256]{2,1,0:T(8,128)(2,1)} %bitcast.99), calls=%async_computation.2 | async-start | bytes 8388608 | tf_op jit(solution)/shard_map/all_to_all | solution.py:191
  97.6 1.8 %fusion.10 = f32[128,1216]{0,1:T(8,128)S(1)} fusion(bf16[320,608]{1,0:T(8,128)(2,1)S(1)} %copy-done.8, bf16[320,608]{1,0:T(8,128)(2,1)} %param.25, bf16[128,576]{1,0:T(8,128)(2,1)S(1)} %bitcast.106), kind=kOutput, calls=%fused_computation.24 | convolution fusion | flops 101171200 | bytes 1519616 | tf_op jit(solution)/shard_map/dot_general | solution.py:208
  100.5 2.0 %copy.37 = f32[64,1216]{1,0:T(8,128)} copy(f32[64,1216]{0,1:T(8,128)} %get-tuple-element.20) | data formatting | bytes 622592 | tf_op jit(solution)/shard_map/jit(_where)/select_n | solution.py:217
  102.5 3.9 %collective-permute-start.3 = (f32[4,16,1216]{2,1,0:T(8,128)}, f32[4,16,1216]{2,1,0:T(8,128)}, u32[]{:S(2)}, u32[]{:S(2)}) collective-permute-start(f32[4,16,1216]{2,1,0:T(8,128)} %bitcast.105), channel_id=1, source_target_pairs={{0,4},{1,5},{2,6},{3,7},{4,0},{5,1},{6,2},{7,3},{8,12},{9,13},{10,... | collective-permute-start | bytes 933896 | tf_op jit(solution)/shard_map/ppermute | solution.py:218
  108.1 4.4 %collective-permute-done.3 = f32[4,16,1216]{2,1,0:T(8,128)} collective-permute-done((f32[4,16,1216]{2,1,0:T(8,128)}, f32[4,16,1216]{2,1,0:T(8,128)}, u32[]{:S(2)}, u32[]{:S(2)}) %collective-permute-start.3) | collective-permute-done | bytes 311328 | tf_op jit(solution)/shard_map/ppermute | solution.py:218
  116.3 2.8 %collective-permute-done.4 = f32[2,16,1216]{2,1,0:T(8,128)} collective-permute-done((f32[2,16,1216]{2,1,0:T(8,128)S(1)}, f32[2,16,1216]{2,1,0:T(8,128)}, u32[]{:S(2)}, u32[]{:S(2)}) %collective-permute-start.4) | collective-permute-done | bytes 155680 | tf_op jit(solution)/shard_map/ppermute | solution.py:218
  139.6 4.2 %gather_fusion.5 = bf16[8,512,256]{2,1,0:T(8,128)(2,1)} fusion(bf16[16,512,256]{2,1,0:T(8,128)(2,1)} %all-to-all-done, s32[1024]{0:T(1024)S(1)} %pad_clamp_fusion), kind=kCustom, calls=%fused_computation.5 | custom fusion | bytes 4194336 | tf_op jit(solution)/shard_map/gather | solution.py:197
  143.9 3.7 %collective-permute-start.8 = (bf16[4,16,608]{2,1,0:T(8,128)(2,1)S(1)}, bf16[4,16,608]{2,1,0:T(8,128)(2,1)}, u32[]{:S(2)}, u32[]{:S(2)}) collective-permute-start(bf16[4,16,608]{2,1,0:T(8,128)(2,1)S(1)} %maximum_select_fusion.1), channel_id=1, source_target_pairs={{0,4},{1,5},{2,6},{3,7},{4,0},{5,1},{6,2},{7,3},{8,12},{9,13},{10,... | collective-permute-start | bytes 233480 | tf_op jit(solution)/shard_map/ppermute | solution.py:230
  147.5 1.9 %broadcast_select_fusion = bf16[8,512,256]{2,1,0:T(8,128)(2,1)S(1)} fusion(bf16[8,512,256]{2,1,0:T(8,128)(2,1)} %gather_fusion.5, pred[8,512]{1,0:T(8,128)(4,1)S(1)} %iota_compare_fusion.1), kind=kLoop, calls=%fused_computation.14 | loop fusion | flops 1048576 | bytes 4198400 | tf_op jit(solution)/shard_map/jit(_where)/select_n | solution.py:195
  149.5 2.3 %concatenate.60 = bf16[8,1024,256]{2,1,0:T(8,128)(2,1)} pad(bf16[8,512,256]{2,1,0:T(8,128)(2,1)S(1)} %broadcast_select_fusion, bf16[]{:T(256)} %constant.151.clone.1), padding=0_0x0_512x0_0 | pad | bytes 6291458 | tf_op jit(solution)/shard_map/concatenate | solution.py:200
  153.8 2.3 %all-to-all-done.2 = bf16[16,512,256]{2,1,0:T(8,128)(2,1)} async-done(((bf16[16,512,256]{2,1,0:T(8,128)(2,1)}), bf16[16,512,256]{2,1,0:T(8,128)(2,1)}, u32[]{:S(2)}, u32[]{:S(2)}) %all-to-all-start.2) | async-done | bytes 4194336 | tf_op jit(solution)/shard_map/all_to_all | solution.py:191
  156.9 4.5 %all-to-all-start.3 = ((bf16[16,8,320]{2,1,0:T(8,128)(2,1)}), bf16[16,8,320]{2,1,0:T(8,128)(2,1)S(1)}, u32[]{:S(2)}, u32[]{:S(2)}) async-start(bf16[16,8,320]{2,1,0:T(8,128)(2,1)} %bitcast.21), calls=%async_computation.3 | async-start | bytes 196608 | tf_op jit(solution)/shard_map/all_to_all | solution.py:239
  161.4 1.8 %select_dynamic-update-slice_fusion.7 = bf16[8,1024,256]{2,1,0:T(8,128)(2,1)} fusion(bf16[8,1024,256]{2,1,0:T(8,128)(2,1)} %concatenate.60, bf16[16,512,256]{2,1,0:T(8,128)(2,1)} %all-to-all-done.2, s32[]{:T(128)S(6)} %select_n.297, pred[512]{0:T(512)(128)(4,1)S(1)} %fusion.45), kind=kLoop, calls=%fused_computation.37 | loop fusion | flops 131072 | bytes 524804 | tf_op jit(solution)/shard_map/dynamic_update_slice | solution.py:258
  163.2 1.8 %select_dynamic-update-slice_fusion.6 = bf16[8,1024,256]{2,1,0:T(8,128)(2,1)} fusion(bf16[8,1024,256]{2,1,0:T(8,128)(2,1)} %select_dynamic-update-slice_fusion.7, bf16[16,512,256]{2,1,0:T(8,128)(2,1)} %all-to-all-done.2, s32[]{:T(128)S(6)} %select_n.299, pred[512]{0:T(512)(128)(4,1)S(1)} %fusion.44), kind=kLoop, calls=%fused_computation.36 | loop fusion | flops 131072 | bytes 524804 | tf_op jit(solution)/shard_map/dynamic_update_slice | solution.py:258
  165.0 1.8 %select_dynamic-update-slice_fusion.5 = bf16[8,1024,256]{2,1,0:T(8,128)(2,1)} fusion(bf16[8,1024,256]{2,1,0:T(8,128)(2,1)} %select_dynamic-update-slice_fusion.6, bf16[16,512,256]{2,1,0:T(8,128)(2,1)} %all-to-all-done.2, s32[]{:T(128)S(6)} %select_n.301, pred[512]{0:T(512)(128)(4,1)S(1)} %fusion.43), kind=kLoop, calls=%fused_computation.35 | loop fusion | flops 131072 | bytes 524804 | tf_op jit(solution)/shard_map/dynamic_update_slice | solution.py:258
  174.0 1.8 %select_dynamic-update-slice_fusion = bf16[8,1024,256]{2,1,0:T(8,128)(2,1)} fusion(bf16[8,1024,256]{2,1,0:T(8,128)(2,1)} %select_dynamic-update-slice_fusion.1, bf16[16,512,256]{2,1,0:T(8,128)(2,1)} %all-to-all-done.2, s32[]{:T(128)S(6)} %select_n.311, pred[512]{0:T(512)(128)(4,1)S(1)} %fusion.38), kind=kLoop, calls=%fused_computation.30 | loop fusion | flops 131072 | bytes 524804 | tf_op jit(solution)/shard_map/dynamic_update_slice | solution.py:258
  175.7 2.1 %scatter_fusion = bf16[8,1024,256]{2,1,0:T(8,128)(2,1)} fusion(bf16[8,1024,256]{2,1,0:T(8,128)(2,1)} %select_dynamic-update-slice_fusion, s32[8]{0:T(128)S(1)} %fusion.48, bf16[8,256]{1,0:T(8,128)(2,1)S(1)} %gather_fusion.6), kind=kCustom, calls=%fused_computation.7 | custom fusion | bytes 12352 | tf_op jit(solution)/shard_map/scatter | solution.py:259
  (121 shorter events, 36.1 us)
Async XLA Ops:
  0.6 52.3 %copy-start = (bf16[512,2560]{1,0:T(8,128)(2,1)S(1)}, bf16[512,2560]{1,0:T(8,128)(2,1)}, u32[]{:S(2)}) copy-start(bf16[512,2560]{1,0:T(8,128)(2,1)} %param.23) | copy-start | bytes 7864324
  8.4 7.4 %copy-start.4 = (s32[8,8]{1,0:T(8,128)S(1)}, s32[8,8]{1,0:T(8,128)}, u32[]{:S(2)}) copy-start(s32[8,8]{1,0:T(8,128)} %param.30) | copy-start | bytes 772
  8.4 7.4 %copy-start.5 = (bf16[8,320]{1,0:T(8,128)(2,1)S(1)}, bf16[8,320]{1,0:T(8,128)(2,1)}, u32[]{:S(2)}) copy-start(bf16[8,320]{1,0:T(8,128)(2,1)} %param.16) | copy-start | bytes 15364
  8.4 21.7 %copy-start.6 = (bf16[2560]{0:T(1024)(128)(2,1)S(1)}, bf16[2560]{0:T(1024)(128)(2,1)}, u32[]{:S(2)}) copy-start(bf16[2560]{0:T(1024)(128)(2,1)} %param.17) | copy-start | bytes 15364
  8.4 21.8 %copy-start.2 = (bf16[2560,128]{1,0:T(8,128)(2,1)S(1)}, bf16[2560,128]{1,0:T(8,128)(2,1)}, u32[]{:S(2)}) copy-start(bf16[2560,128]{1,0:T(8,128)(2,1)} %param.19) | copy-start | bytes 1966084
  8.4 22.2 %copy-start.9 = (bf16[128]{0:T(256)(128)(2,1)S(1)}, bf16[128]{0:T(256)(128)(2,1)}, u32[]{:S(2)}) copy-start(bf16[128]{0:T(256)(128)(2,1)} %param.22) | copy-start | bytes 772
  8.4 22.2 %copy-start.1 = (s32[128]{0:T(128)S(1)}, s32[128]{0:T(128)}, u32[]{:S(2)}) copy-start(s32[128]{0:T(128)} %param.29) | copy-start | bytes 1540
  8.4 70.6 %all-to-all-start = ((bf16[16,512,256]{2,1,0:T(8,128)(2,1)}), bf16[16,512,256]{2,1,0:T(8,128)(2,1)}, u32[]{:S(2)}, u32[]{:S(2)}) async-start(bf16[16,512,256]{2,1,0:T(8,128)(2,1)} %bitcast.100), calls=%async_computation | async-start | bytes 8388608 | tf_op jit(solution)/shard_map/all_to_all | solution.py:124
  35.2 5.1 %copy-start.10 = (bf16[128]{0:T(256)(128)(2,1)S(1)}, bf16[128]{0:T(256)(128)(2,1)}, u32[]{:S(2)}) copy-start(bf16[128]{0:T(256)(128)(2,1)} %param.21) | copy-start | bytes 772
  48.4 5.3 %copy-start.7 = (bf16[320]{0:T(512)(128)(2,1)S(1)}, bf16[320]{0:T(512)(128)(2,1)}, u32[]{:S(2)}) copy-start(bf16[320]{0:T(512)(128)(2,1)} %param.24) | copy-start | bytes 1924
  53.4 1.9 %collective-permute-start = (f32[8,2560]{1,0:T(8,128)S(1)}, f32[8,2560]{1,0:T(8,128)S(1)}, u32[]{:S(2)}, u32[]{:S(2)}) collective-permute-start(f32[8,2560]{1,0:T(8,128)S(1)} %fusion.24), channel_id=1, source_target_pairs={{0,1},{1,0},{2,3},{3,2},{4,5},{5,4},{6,7},{7,6},{8,9},{9,8},{10,11... | collective-permute-start | bytes 245768 | tf_op jit(solution)/shard_map/ppermute | solution.py:165
  55.3 4.6 %collective-permute-start.1 = (f32[8,2560]{1,0:T(8,128)S(1)}, f32[8,2560]{1,0:T(8,128)S(1)}, u32[]{:S(2)}, u32[]{:S(2)}) collective-permute-start(f32[8,2560]{1,0:T(8,128)S(1)} %add.276), channel_id=1, source_target_pairs={{0,2},{1,3},{2,0},{3,1},{4,6},{5,7},{6,4},{7,5},{8,10},{9,11},{10,... | collective-permute-start | bytes 245768 | tf_op jit(solution)/shard_map/ppermute | solution.py:165
  59.9 6.0 %collective-permute-start.2 = (f32[8,2560]{1,0:T(8,128)S(1)}, f32[8,2560]{1,0:T(8,128)S(1)}, u32[]{:S(2)}, u32[]{:S(2)}) collective-permute-start(f32[8,2560]{1,0:T(8,128)S(1)} %add.277), channel_id=1, source_target_pairs={{0,4},{1,5},{2,6},{3,7},{4,0},{5,1},{6,2},{7,3},{8,12},{9,13},{10,... | collective-permute-start | bytes 245768 | tf_op jit(solution)/shard_map/ppermute | solution.py:165
  79.7 12.8 %all-to-all-start.1 = ((bf16[16,8,576]{2,1,0:T(8,128)(2,1)}), bf16[16,8,576]{2,1,0:T(8,128)(2,1)S(1)}, u32[]{:S(2)}, u32[]{:S(2)}) async-start(bf16[16,8,576]{2,1,0:T(8,128)(2,1)} %broadcast_in_dim.219), calls=%async_computation.1 | async-start | bytes 327680 | tf_op jit(solution)/shard_map/all_to_all | solution.py:183
  92.6 5.0 %copy-start.8 = (bf16[320,608]{1,0:T(8,128)(2,1)S(1)}, bf16[320,608]{1,0:T(8,128)(2,1)}, u32[]{:S(2)}) copy-start(bf16[320,608]{1,0:T(8,128)(2,1)} %param.26) | copy-start | bytes 1167364
  92.6 63.5 %all-to-all-start.2 = ((bf16[16,512,256]{2,1,0:T(8,128)(2,1)}), bf16[16,512,256]{2,1,0:T(8,128)(2,1)}, u32[]{:S(2)}, u32[]{:S(2)}) async-start(bf16[16,512,256]{2,1,0:T(8,128)(2,1)} %bitcast.99), calls=%async_computation.2 | async-start | bytes 8388608 | tf_op jit(solution)/shard_map/all_to_all | solution.py:191
  102.5 10.0 %collective-permute-start.3 = (f32[4,16,1216]{2,1,0:T(8,128)}, f32[4,16,1216]{2,1,0:T(8,128)}, u32[]{:S(2)}, u32[]{:S(2)}) collective-permute-start(f32[4,16,1216]{2,1,0:T(8,128)} %bitcast.105), channel_id=1, source_target_pairs={{0,4},{1,5},{2,6},{3,7},{4,0},{5,1},{6,2},{7,3},{8,12},{9,13},{10,... | collective-permute-start | bytes 933896 | tf_op jit(solution)/shard_map/ppermute | solution.py:218
  113.6 5.5 %collective-permute-start.4 = (f32[2,16,1216]{2,1,0:T(8,128)S(1)}, f32[2,16,1216]{2,1,0:T(8,128)}, u32[]{:S(2)}, u32[]{:S(2)}) collective-permute-start(f32[2,16,1216]{2,1,0:T(8,128)S(1)} %slice_select_fusion.2), channel_id=1, source_target_pairs={{0,2},{1,3},{2,0},{3,1},{4,6},{5,7},{6,4},{7,5},{8,10},{9,11},{10,... | collective-permute-start | bytes 466952 | tf_op jit(solution)/shard_map/ppermute | solution.py:218
  120.1 1.4 collective-permute-start.5
  121.6 1.2 collective-permute-start.6
  122.8 21.0 %collective-permute-start.7 = (bf16[2,16,608]{2,1,0:T(8,128)(2,1)S(1)}, bf16[2,16,608]{2,1,0:T(8,128)(2,1)S(1)}, u32[]{:S(2)}, u32[]{:S(2)}) collective-permute-start(bf16[2,16,608]{2,1,0:T(8,128)(2,1)S(1)} %maximum_select_fusion.2), channel_id=1, source_target_pairs={{0,2},{1,3},{2,0},{3,1},{4,6},{5,7},{6,4},{7,5},{8,10},{9,11},{10,... | collective-permute-start | bytes 116744 | tf_op jit(solution)/shard_map/ppermute | solution.py:230
  143.9 8.6 %collective-permute-start.8 = (bf16[4,16,608]{2,1,0:T(8,128)(2,1)S(1)}, bf16[4,16,608]{2,1,0:T(8,128)(2,1)}, u32[]{:S(2)}, u32[]{:S(2)}) collective-permute-start(bf16[4,16,608]{2,1,0:T(8,128)(2,1)S(1)} %maximum_select_fusion.1), channel_id=1, source_target_pairs={{0,4},{1,5},{2,6},{3,7},{4,0},{5,1},{6,2},{7,3},{8,12},{9,13},{10,... | collective-permute-start | bytes 233480 | tf_op jit(solution)/shard_map/ppermute | solution.py:230
  149.5 4.0 %copy-start.3 = (bf16[608,320]{0,1:T(8,128)(2,1)S(1)}, bf16[608,320]{0,1:T(8,128)(2,1)}, u32[]{:S(2)}) copy-start(bf16[608,320]{0,1:T(8,128)(2,1)} %param.27) | copy-start | bytes 1167364
  156.9 21.0 %all-to-all-start.3 = ((bf16[16,8,320]{2,1,0:T(8,128)(2,1)}), bf16[16,8,320]{2,1,0:T(8,128)(2,1)S(1)}, u32[]{:S(2)}, u32[]{:S(2)}) async-start(bf16[16,8,320]{2,1,0:T(8,128)(2,1)} %bitcast.21), calls=%async_computation.3 | async-start | bytes 196608 | tf_op jit(solution)/shard_map/all_to_all | solution.py:239

commit v16 on v14

--- a/solution.py
+++ b/solution.py
@@ -115,7 +115,7 @@
     peer_ids = jnp.arange(devices_req, dtype=jnp.int32)
     matches = destination[None, :] == peer_ids[:, None]
     picked_pages = jnp.sum(jnp.where(matches[:, :, None], page_table[None, :, :], 0), axis=1)
-    first_pages = pages_per // 2
+    first_pages = (pages_per * 5) // 8
     second_pages = pages_per - first_pages
     first_span = first_pages * page_len
     parcels_first = kv_pool[picked_pages[:, :first_pages]].reshape(

time: 181 us -> 198 us (1.094)
  waiting for transfers between devices: 31 us -> 44.6 us
  local copies, waits for them, and re-layouts: 32 us -> 35.1 us
    all_to_all x1, waiting for transfers between devices: 12.8 us -> 27.8 us  [per_device(): lax.all_to_all(parcels_first, 'req', split_axis=0, concat_axis=0, tiled=T...]
    ppermute x3, waiting for transfers between devices: 7.89 us -> 4.62 us  [per_device(): lax.ppermute(send, 'kvh', [(i, i ^ step) for i in range(devices_kvh)])]
    gather x1, local copies, waits for them, and re-layouts: 4.97 us -> 7.87 us  [per_device(): kv_pool[picked_pages[:, :first_pages]]]
  transfers between devices with their start and end apart: 13 -> 13, of which waited for: 9 -> 8; matrix products, arithmetic and copies ran while one was open for 40% -> 33% of each run, Pallas kernels for 0% -> 0%
where the time goes in v16:
time: 198 us; the launch traced here: 196 us
  waiting for transfers between devices  44.6 us (23%)
  other arithmetic  38.4 us (19%)
  starting transfers between devices  36.6 us (18%)
  local copies, waits for them, and re-layouts  35.1 us (18%)
  between operations  16.3 us (8%)
  blocking collectives  14 us (7%)
  matrix products  11 us (6%)
    all_to_all x1, waiting for transfers between devices, per_device(): lax.all_to_all(parcels_first, 'req', split_axis=0, concat_axis=0, tiled=T...  27.8 us
    all_gather x1, blocking collectives, per_device(): full_states = lax.all_gather(states, 'kvh', axis=1, tiled=True)  14 us
    dynamic_update_slice x8, other arithmetic, per_device(): lax.dynamic_update_slice(new_seq, piece[None], (slot, first_span, 0))  13.8 us
    gather x1, local copies, waits for them, and re-layouts, per_device(): kv_pool[picked_pages[:, :first_pages]]  7.87 us
    select_n x1, other arithmetic, mask_blocks(): jnp.where(kept, blocks, jnp.where(placed, fresh[:, None, :, None, :], jnp...  7.64 us
    all_to_all x1, starting transfers between devices, per_device(): lax.all_to_all(parcels_first, 'req', split_axis=0, concat_axis=0, tiled=T...  7.33 us
    all_to_all x1, starting transfers between devices, per_device(): lax.all_to_all(parcels_second, 'req', split_axis=0, concat_axis=0, tiled=...  5.93 us
    ppermute x3, waiting for transfers between devices, per_device(): lax.ppermute(attn_out, 'kvh', [(i, i ^ step) for i in range(devices_kvh)])  5.66 us
  transfers between devices with their start and end apart: 13, of which 8 were waited for; matrix products, arithmetic and copies ran while one was open for 33% of the time, Pallas kernels for 0%

profile of v16, /device:TPU:0, one launch (start us, length us, event | category | flops | bytes accessed | tf_op | source)
XLA Modules:
  0.0 196.1 jit_solution(12313433770426757104)
XLA Ops:
  3.4 7.9 %gather_fusion.2 = bf16[80,128,256]{2,1,0:T(8,128)(2,1)} fusion(bf16[64,128,256]{2,1,0:T(8,128)(2,1)} %bitcast.96, s32[1024]{0:T(1024)S(1)} %pad_clamp_fusion.3), kind=kCustom, calls=%fused_computation.2 | custom fusion | bytes 10486080 | tf_op jit(solution)/shard_map/gather | solution.py:121
  11.3 7.3 %all-to-all-start = ((bf16[16,640,256]{2,1,0:T(8,128)(2,1)}), bf16[16,640,256]{2,1,0:T(8,128)(2,1)}, u32[]{:S(2)}, u32[]{:S(2)}) async-start(bf16[16,640,256]{2,1,0:T(8,128)(2,1)} %bitcast.99), calls=%async_computation | async-start | bytes 10485760 | tf_op jit(solution)/shard_map/all_to_all | solution.py:124
  18.7 14.0 %all-gather = bf16[8,320,8]{1,2,0:T(8,128)(2,1)S(1)} all-gather(bf16[1,320,8]{1,2,0:T(8,128)(2,1)S(1)} %bitcast.108), channel_id=1, replica_groups=mesh['req'=16,'kvh'=8] {'kvh'}, dimensions={0}, use_global_device_ids=true | all-gather | bytes 46080 | tf_op jit(solution)/shard_map/all_gather | solution.py:134
  35.5 5.0 %gather_fusion.1 = bf16[64,128,256]{2,1,0:T(8,128)(2,1)} fusion(bf16[64,128,256]{2,1,0:T(8,128)(2,1)} %bitcast.97, s32[1024]{0:T(1024)S(1)} %pad_clamp_fusion.4), kind=kCustom, calls=%fused_computation.1 | custom fusion | bytes 8388864 | tf_op jit(solution)/shard_map/gather | solution.py:155
  40.6 2.3 %multiply_reduce_fusion.1 = (f32[8,4]{0,1:T(4,128)S(1)}, f32[8,4,128]{2,0,1:T(8,128)S(1)}) fusion(bf16[8,2560]{1,0:T(8,128)(2,1)S(1)} %fusion.17, bf16[2560,512]{1,0:T(8,128)(2,1)} %param.18), kind=kOutput, calls=%fused_computation.69 | convolution fusion | flops 20979680 | bytes 2678912 | tf_op jit(solution)/shard_map/dot_general | solution.py:138
  43.6 7.6 %select_select_fusion = bf16[8,1,1024,256]{3,2,0,1:T(8,128)(2,1)} fusion(bf16[8,1,1024,256]{3,2,0,1:T(8,128)(2,1)} %bitcast.100, pred[8,1024]{1,0:T(8,128)(4,1)S(1)} %get-tuple-element.27, pred[8,1024]{1,0:T(8,128)(4,1)S(1)} %get-tuple-element.26, bf16[8,256]{1,0:T(8,128)(2,1)S(1)} %maximum_bitcast_fusion), kind=kLoop, calls=%fused_computation.9 | loop fusion | flops 4194304 | bytes 8409088 | tf_op jit(solution)/shard_map/jit(_where)/select_n | solution.py:48
  51.3 2.5 %fusion.55 = (f32[8,4]{1,0:T(8,128)S(1)}, f32[8,4,1024]{2,1,0:T(4,128)S(1)}) fusion(bf16[8,1,1024,256]{3,2,0,1:T(8,128)(2,1)} %select_select_fusion, pred[8,1024]{1,0:T(8,128)(4,1)S(1)} %get-tuple-element.47, bf16[8,4,64]{2,1,0:T(4,128)(2,1)S(1)} %get-tuple-element.23, bf16[8,4,64]{2,1,0:T(4,128)(2,1)S(1)} %get-tuple-element.22), kind=kOutput, calls=%fused_computation.145 | convolution fusion | flops 8537087 | bytes 2244736 | tf_op jit(solution)/shard_map/sub | solution.py:67
  53.8 2.0 %fusion.8 = bf16[1,8,4,128]{3,2,1,0:T(4,128)(2,1)S(1)} fusion(bf16[8,1,1024,256]{3,2,0,1:T(8,128)(2,1)} %select_select_fusion, f32[8,4,1024]{2,1,0:T(4,128)S(1)} %get-tuple-element.53, f32[8,4]{1,0:T(8,128)S(1)} %get-tuple-element.52), kind=kOutput, calls=%fused_computation.21 | convolution fusion | flops 8458240 | bytes 2236544 | tf_op jit(solution)/shard_map/rkgt,rktd->rkgd/dot_general | solution.py:68
  59.8 2.9 %collective-permute-done.1 = f32[8,2560]{1,0:T(8,128)S(1)} collective-permute-done((f32[8,2560]{1,0:T(8,128)S(1)}, f32[8,2560]{1,0:T(8,128)S(1)}, u32[]{:S(2)}, u32[]{:S(2)}) %collective-permute-start.1) | collective-permute-done | bytes 81952 | tf_op jit(solution)/shard_map/ppermute | solution.py:165
  62.8 2.6 %collective-permute-start.2 = (f32[8,2560]{1,0:T(8,128)S(1)}, f32[8,2560]{1,0:T(8,128)S(1)}, u32[]{:S(2)}, u32[]{:S(2)}) collective-permute-start(f32[8,2560]{1,0:T(8,128)S(1)} %add.283), channel_id=1, source_target_pairs={{0,4},{1,5},{2,6},{3,7},{4,0},{5,1},{6,2},{7,3},{8,12},{9,13},{10,... | collective-permute-start | bytes 245768 | tf_op jit(solution)/shard_map/ppermute | solution.py:165
  66.1 2.7 %collective-permute-done.2 = f32[8,2560]{1,0:T(8,128)S(1)} collective-permute-done((f32[8,2560]{1,0:T(8,128)S(1)}, f32[8,2560]{1,0:T(8,128)S(1)}, u32[]{:S(2)}, u32[]{:S(2)}) %collective-permute-start.2) | collective-permute-done | bytes 81952 | tf_op jit(solution)/shard_map/ppermute | solution.py:165
  69.1 27.8 %all-to-all-done = bf16[16,640,256]{2,1,0:T(8,128)(2,1)} async-done(((bf16[16,640,256]{2,1,0:T(8,128)(2,1)}), bf16[16,640,256]{2,1,0:T(8,128)(2,1)}, u32[]{:S(2)}, u32[]{:S(2)}) %all-to-all-start) | async-done | bytes 5242912 | tf_op jit(solution)/shard_map/all_to_all | solution.py:124
  97.6 5.3 %all-to-all-start.1 = ((bf16[16,8,576]{2,1,0:T(8,128)(2,1)}), bf16[16,8,576]{2,1,0:T(8,128)(2,1)S(1)}, u32[]{:S(2)}, u32[]{:S(2)}) async-start(bf16[16,8,576]{2,1,0:T(8,128)(2,1)} %broadcast_in_dim.219), calls=%async_computation.1 | async-start | bytes 327680 | tf_op jit(solution)/shard_map/all_to_all | solution.py:183
  103.6 4.7 %gather_fusion.3 = bf16[48,128,256]{2,1,0:T(8,128)(2,1)} fusion(bf16[64,128,256]{2,1,0:T(8,128)(2,1)} %bitcast.98, s32[1024]{0:T(1024)S(1)} %pad_clamp_fusion.2), kind=kCustom, calls=%fused_computation.3 | custom fusion | bytes 6291648 | tf_op jit(solution)/shard_map/gather | solution.py:128
  109.0 2.1 %all-to-all-done.1 = bf16[16,8,576]{2,1,0:T(8,128)(2,1)S(1)} async-done(((bf16[16,8,576]{2,1,0:T(8,128)(2,1)}), bf16[16,8,576]{2,1,0:T(8,128)(2,1)S(1)}, u32[]{:S(2)}, u32[]{:S(2)}) %all-to-all-start.1) | async-done | bytes 147488 | tf_op jit(solution)/shard_map/all_to_all | solution.py:183
  111.1 1.9 fusion.10
  114.1 2.1 %copy.37 = f32[64,1216]{1,0:T(8,128)} copy(f32[64,1216]{0,1:T(8,128)} %get-tuple-element.20) | data formatting | bytes 622592 | tf_op jit(solution)/shard_map/jit(_where)/select_n | solution.py:217
  116.2 3.9 %collective-permute-start.3 = (f32[4,16,1216]{2,1,0:T(8,128)}, f32[4,16,1216]{2,1,0:T(8,128)}, u32[]{:S(2)}, u32[]{:S(2)}) collective-permute-start(f32[4,16,1216]{2,1,0:T(8,128)} %bitcast.105), channel_id=1, source_target_pairs={{0,4},{1,5},{2,6},{3,7},{4,0},{5,1},{6,2},{7,3},{8,12},{9,13},{10,... | collective-permute-start | bytes 933896 | tf_op jit(solution)/shard_map/ppermute | solution.py:218
  121.6 3.9 %collective-permute-done.3 = f32[4,16,1216]{2,1,0:T(8,128)} collective-permute-done((f32[4,16,1216]{2,1,0:T(8,128)}, f32[4,16,1216]{2,1,0:T(8,128)}, u32[]{:S(2)}, u32[]{:S(2)}) %collective-permute-start.3) | collective-permute-done | bytes 311328 | tf_op jit(solution)/shard_map/ppermute | solution.py:218
  128.8 5.9 %all-to-all-start.2 = ((bf16[16,384,256]{2,1,0:T(8,128)(2,1)}), bf16[16,384,256]{2,1,0:T(8,128)(2,1)}, u32[]{:S(2)}, u32[]{:S(2)}) async-start(bf16[16,384,256]{2,1,0:T(8,128)(2,1)} %bitcast.101), calls=%async_computation.2 | async-start | bytes 6291456 | tf_op jit(solution)/shard_map/all_to_all | solution.py:191
  155.7 4.7 %gather_fusion.5 = bf16[8,640,256]{2,1,0:T(8,128)(2,1)} fusion(bf16[16,640,256]{2,1,0:T(8,128)(2,1)} %all-to-all-done, s32[1024]{0:T(1024)S(1)} %pad_clamp_fusion), kind=kCustom, calls=%fused_computation.5 | custom fusion | bytes 5242912 | tf_op jit(solution)/shard_map/gather | solution.py:197
  160.4 3.3 %collective-permute-start.8 = (bf16[4,16,608]{2,1,0:T(8,128)(2,1)S(1)}, bf16[4,16,608]{2,1,0:T(8,128)(2,1)}, u32[]{:S(2)}, u32[]{:S(2)}) collective-permute-start(bf16[4,16,608]{2,1,0:T(8,128)(2,1)S(1)} %maximum_select_fusion.1), channel_id=1, source_target_pairs={{0,4},{1,5},{2,6},{3,7},{4,0},{5,1},{6,2},{7,3},{8,12},{9,13},{10,... | collective-permute-start | bytes 233480 | tf_op jit(solution)/shard_map/ppermute | solution.py:230
  163.7 3.1 %broadcast_select_fusion = bf16[8,640,256]{2,1,0:T(8,128)(2,1)S(1)} fusion(bf16[8,640,256]{2,1,0:T(8,128)(2,1)} %gather_fusion.5, pred[8,640]{1,0:T(8,128)(4,1)S(1)} %iota_compare_fusion.1), kind=kLoop, calls=%fused_computation.10 | loop fusion | flops 1310720 | bytes 5248000 | tf_op jit(solution)/shard_map/jit(_where)/select_n | solution.py:195
  166.8 2.3 %concatenate.60 = bf16[8,1024,256]{2,1,0:T(8,128)(2,1)} pad(bf16[8,640,256]{2,1,0:T(8,128)(2,1)S(1)} %broadcast_select_fusion, bf16[]{:T(256)} %constant.153.clone.1), padding=0_0x0_384x0_0 | pad | bytes 6815746 | tf_op jit(solution)/shard_map/concatenate | solution.py:200
  171.1 4.1 %all-to-all-done.2 = bf16[16,384,256]{2,1,0:T(8,128)(2,1)} async-done(((bf16[16,384,256]{2,1,0:T(8,128)(2,1)}), bf16[16,384,256]{2,1,0:T(8,128)(2,1)}, u32[]{:S(2)}, u32[]{:S(2)}) %all-to-all-start.2) | async-done | bytes 3145760 | tf_op jit(solution)/shard_map/all_to_all | solution.py:191
  176.0 3.5 %all-to-all-start.3 = ((f32[16,8,320]{2,1,0:T(8,128)}), f32[16,8,320]{2,1,0:T(8,128)S(1)}, u32[]{:S(2)}, u32[]{:S(2)}) async-start(f32[16,8,320]{2,1,0:T(8,128)} %bitcast.21), calls=%async_computation.3 | async-start | bytes 393216 | tf_op jit(solution)/shard_map/all_to_all | solution.py:239
  179.5 1.7 select_dynamic-update-slice_fusion.7
  183.0 1.7 select_dynamic-update-slice_fusion.5
  186.4 1.7 select_dynamic-update-slice_fusion.3
  188.2 1.7 select_dynamic-update-slice_fusion.2
  191.6 1.7 select_dynamic-update-slice_fusion
  193.3 2.1 %scatter_fusion = bf16[8,1024,256]{2,1,0:T(8,128)(2,1)} fusion(bf16[8,1024,256]{2,1,0:T(8,128)(2,1)} %select_dynamic-update-slice_fusion, s32[8]{0:T(128)S(1)} %fusion.48, bf16[8,256]{1,0:T(8,128)(2,1)S(1)} %gather_fusion.6), kind=kCustom, calls=%fused_computation.7 | custom fusion | bytes 12352 | tf_op jit(solution)/shard_map/scatter | solution.py:259
  (120 shorter events, 33.5 us)
Async XLA Ops:
  0.6 55.2 %copy-start = (bf16[512,2560]{1,0:T(8,128)(2,1)S(1)}, bf16[512,2560]{1,0:T(8,128)(2,1)}, u32[]{:S(2)}) copy-start(bf16[512,2560]{1,0:T(8,128)(2,1)} %param.23) | copy-start | bytes 7864324
  11.3 7.4 %copy-start.4 = (s32[8,8]{1,0:T(8,128)S(1)}, s32[8,8]{1,0:T(8,128)}, u32[]{:S(2)}) copy-start(s32[8,8]{1,0:T(8,128)} %param.30) | copy-start | bytes 772
  11.3 7.4 %copy-start.5 = (bf16[8,320]{1,0:T(8,128)(2,1)S(1)}, bf16[8,320]{1,0:T(8,128)(2,1)}, u32[]{:S(2)}) copy-start(bf16[8,320]{1,0:T(8,128)(2,1)} %param.16) | copy-start | bytes 15364
  11.3 21.7 %copy-start.6 = (bf16[2560]{0:T(1024)(128)(2,1)S(1)}, bf16[2560]{0:T(1024)(128)(2,1)}, u32[]{:S(2)}) copy-start(bf16[2560]{0:T(1024)(128)(2,1)} %param.17) | copy-start | bytes 15364
  11.3 21.8 %copy-start.2 = (bf16[2560,128]{1,0:T(8,128)(2,1)S(1)}, bf16[2560,128]{1,0:T(8,128)(2,1)}, u32[]{:S(2)}) copy-start(bf16[2560,128]{1,0:T(8,128)(2,1)} %param.19) | copy-start | bytes 1966084
  11.3 22.1 %copy-start.8 = (bf16[128]{0:T(256)(128)(2,1)S(1)}, bf16[128]{0:T(256)(128)(2,1)}, u32[]{:S(2)}) copy-start(bf16[128]{0:T(256)(128)(2,1)} %param.22) | copy-start | bytes 772
  11.3 22.2 %copy-start.1 = (s32[128]{0:T(128)S(1)}, s32[128]{0:T(128)}, u32[]{:S(2)}) copy-start(s32[128]{0:T(128)} %param.29) | copy-start | bytes 1540
  11.3 85.6 %all-to-all-start = ((bf16[16,640,256]{2,1,0:T(8,128)(2,1)}), bf16[16,640,256]{2,1,0:T(8,128)(2,1)}, u32[]{:S(2)}, u32[]{:S(2)}) async-start(bf16[16,640,256]{2,1,0:T(8,128)(2,1)} %bitcast.99), calls=%async_computation | async-start | bytes 10485760 | tf_op jit(solution)/shard_map/all_to_all | solution.py:124
  35.5 7.4 %copy-start.9 = (bf16[128]{0:T(256)(128)(2,1)S(1)}, bf16[128]{0:T(256)(128)(2,1)}, u32[]{:S(2)}) copy-start(bf16[128]{0:T(256)(128)(2,1)} %param.21) | copy-start | bytes 772
  51.3 5.3 %copy-start.7 = (bf16[320]{0:T(512)(128)(2,1)S(1)}, bf16[320]{0:T(512)(128)(2,1)}, u32[]{:S(2)}) copy-start(bf16[320]{0:T(512)(128)(2,1)} %param.24) | copy-start | bytes 1924
  56.2 1.9 collective-permute-start
  58.2 4.6 %collective-permute-start.1 = (f32[8,2560]{1,0:T(8,128)S(1)}, f32[8,2560]{1,0:T(8,128)S(1)}, u32[]{:S(2)}, u32[]{:S(2)}) collective-permute-start(f32[8,2560]{1,0:T(8,128)S(1)} %add.282), channel_id=1, source_target_pairs={{0,2},{1,3},{2,0},{3,1},{4,6},{5,7},{6,4},{7,5},{8,10},{9,11},{10,... | collective-permute-start | bytes 245768 | tf_op jit(solution)/shard_map/ppermute | solution.py:165
  62.8 6.0 %collective-permute-start.2 = (f32[8,2560]{1,0:T(8,128)S(1)}, f32[8,2560]{1,0:T(8,128)S(1)}, u32[]{:S(2)}, u32[]{:S(2)}) collective-permute-start(f32[8,2560]{1,0:T(8,128)S(1)} %add.283), channel_id=1, source_target_pairs={{0,4},{1,5},{2,6},{3,7},{4,0},{5,1},{6,2},{7,3},{8,12},{9,13},{10,... | collective-permute-start | bytes 245768 | tf_op jit(solution)/shard_map/ppermute | solution.py:165
  97.6 13.5 %all-to-all-start.1 = ((bf16[16,8,576]{2,1,0:T(8,128)(2,1)}), bf16[16,8,576]{2,1,0:T(8,128)(2,1)S(1)}, u32[]{:S(2)}, u32[]{:S(2)}) async-start(bf16[16,8,576]{2,1,0:T(8,128)(2,1)} %broadcast_in_dim.219), calls=%async_computation.1 | async-start | bytes 327680 | tf_op jit(solution)/shard_map/all_to_all | solution.py:183
  116.2 9.4 %collective-permute-start.3 = (f32[4,16,1216]{2,1,0:T(8,128)}, f32[4,16,1216]{2,1,0:T(8,128)}, u32[]{:S(2)}, u32[]{:S(2)}) collective-permute-start(f32[4,16,1216]{2,1,0:T(8,128)} %bitcast.105), channel_id=1, source_target_pairs={{0,4},{1,5},{2,6},{3,7},{4,0},{5,1},{6,2},{7,3},{8,12},{9,13},{10,... | collective-permute-start | bytes 933896 | tf_op jit(solution)/shard_map/ppermute | solution.py:218
  126.7 8.7 %collective-permute-start.4 = (f32[2,16,1216]{2,1,0:T(8,128)S(1)}, f32[2,16,1216]{2,1,0:T(8,128)}, u32[]{:S(2)}, u32[]{:S(2)}) collective-permute-start(f32[2,16,1216]{2,1,0:T(8,128)S(1)} %slice_select_fusion.2), channel_id=1, source_target_pairs={{0,2},{1,3},{2,0},{3,1},{4,6},{5,7},{6,4},{7,5},{8,10},{9,11},{10,... | collective-permute-start | bytes 466952 | tf_op jit(solution)/shard_map/ppermute | solution.py:218
  128.8 46.4 %all-to-all-start.2 = ((bf16[16,384,256]{2,1,0:T(8,128)(2,1)}), bf16[16,384,256]{2,1,0:T(8,128)(2,1)}, u32[]{:S(2)}, u32[]{:S(2)}) async-start(bf16[16,384,256]{2,1,0:T(8,128)(2,1)} %bitcast.101), calls=%async_computation.2 | async-start | bytes 6291456 | tf_op jit(solution)/shard_map/all_to_all | solution.py:191
  136.4 1.4 collective-permute-start.5
  137.8 1.2 collective-permute-start.6
  139.1 21.3 %collective-permute-start.7 = (bf16[2,16,608]{2,1,0:T(8,128)(2,1)S(1)}, bf16[2,16,608]{2,1,0:T(8,128)(2,1)S(1)}, u32[]{:S(2)}, u32[]{:S(2)}) collective-permute-start(bf16[2,16,608]{2,1,0:T(8,128)(2,1)S(1)} %maximum_select_fusion.2), channel_id=1, source_target_pairs={{0,2},{1,3},{2,0},{3,1},{4,6},{5,7},{6,4},{7,5},{8,10},{9,11},{10,... | collective-permute-start | bytes 116744 | tf_op jit(solution)/shard_map/ppermute | solution.py:230
  160.4 9.4 %collective-permute-start.8 = (bf16[4,16,608]{2,1,0:T(8,128)(2,1)S(1)}, bf16[4,16,608]{2,1,0:T(8,128)(2,1)}, u32[]{:S(2)}, u32[]{:S(2)}) collective-permute-start(bf16[4,16,608]{2,1,0:T(8,128)(2,1)S(1)} %maximum_select_fusion.1), channel_id=1, source_target_pairs={{0,4},{1,5},{2,6},{3,7},{4,0},{5,1},{6,2},{7,3},{8,12},{9,13},{10,... | collective-permute-start | bytes 233480 | tf_op jit(solution)/shard_map/ppermute | solution.py:230
  166.8 4.0 %copy-start.3 = (bf16[608,320]{0,1:T(8,128)(2,1)S(1)}, bf16[608,320]{0,1:T(8,128)(2,1)}, u32[]{:S(2)}) copy-start(bf16[608,320]{0,1:T(8,128)(2,1)} %param.27) | copy-start | bytes 1167364
  176.0 19.4 %all-to-all-start.3 = ((f32[16,8,320]{2,1,0:T(8,128)}), f32[16,8,320]{2,1,0:T(8,128)S(1)}, u32[]{:S(2)}, u32[]{:S(2)}) async-start(f32[16,8,320]{2,1,0:T(8,128)} %bitcast.21), calls=%async_computation.3 | async-start | bytes 393216 | tf_op jit(solution)/shard_map/all_to_all | solution.py:239

commit v17 on v16

--- a/solution.py
+++ b/solution.py
@@ -115,7 +115,7 @@
     peer_ids = jnp.arange(devices_req, dtype=jnp.int32)
     matches = destination[None, :] == peer_ids[:, None]
     picked_pages = jnp.sum(jnp.where(matches[:, :, None], page_table[None, :, :], 0), axis=1)
-    first_pages = (pages_per * 5) // 8
+    first_pages = (pages_per * 3) // 8
     second_pages = pages_per - first_pages
     first_span = first_pages * page_len
     parcels_first = kv_pool[picked_pages[:, :first_pages]].reshape(

time: 198 us -> 188 us (0.949)
  waiting for transfers between devices: 44.6 us -> 31.6 us
  starting transfers between devices: 36.6 us -> 40.5 us
    all_to_all x1, waiting for transfers between devices: 27.8 us -> 0.01 us  [per_device(): lax.all_to_all(parcels_first, 'req', split_axis=0, concat_axis=0, tiled=T...]
    all_to_all x1, waiting for transfers between devices: 4.08 us -> 17.9 us  [per_device(): lax.all_to_all(parcels_second, 'req', split_axis=0, concat_axis=0, tiled=...]
    gather x1, local copies, waits for them, and re-layouts: 7.87 us -> 4.67 us  [per_device(): kv_pool[picked_pages[:, :first_pages]]]
    gather x1, local copies, waits for them, and re-layouts: 4.7 us -> 7.86 us  [per_device(): kv_pool[picked_pages[:, first_pages:]]]
    ppermute x3, waiting for transfers between devices: 4.62 us -> 7.75 us  [per_device(): lax.ppermute(send, 'kvh', [(i, i ^ step) for i in range(devices_kvh)])]
    all_to_all x1, waiting for transfers between devices: 2.07 us -> 0.01 us  [per_device(): lax.all_to_all(jnp.broadcast_to(outgoing[None], (devices_req,) + outgoing...]
  transfers between devices with their start and end apart: 13 -> 13, of which waited for: 8 -> 7; matrix products, arithmetic and copies ran while one was open for 33% -> 40% of each run, Pallas kernels for 0% -> 0%
where the time goes in v17:
time: 188 us; the launch traced here: 186 us
  starting transfers between devices  40.5 us (22%)
  other arithmetic  38.5 us (20%)
  local copies, waits for them, and re-layouts  34.1 us (18%)
  waiting for transfers between devices  31.6 us (17%)
  between operations  16.3 us (9%)
  blocking collectives  14 us (7%)
  matrix products  10.9 us (6%)
    all_to_all x1, waiting for transfers between devices, per_device(): lax.all_to_all(parcels_second, 'req', split_axis=0, concat_axis=0, tiled=...  17.9 us
    dynamic_update_slice x8, other arithmetic, per_device(): lax.dynamic_update_slice(new_seq, piece[None], (slot, first_span, 0))  14.8 us
    all_gather x1, blocking collectives, per_device(): full_states = lax.all_gather(states, 'kvh', axis=1, tiled=True)  14 us
    gather x1, local copies, waits for them, and re-layouts, per_device(): kv_pool[picked_pages[:, first_pages:]]  7.86 us
    ppermute x3, waiting for transfers between devices, per_device(): lax.ppermute(send, 'kvh', [(i, i ^ step) for i in range(devices_kvh)])  7.75 us
    select_n x1, other arithmetic, mask_blocks(): jnp.where(kept, blocks, jnp.where(placed, fresh[:, None, :, None, :], jnp...  7.63 us
    all_to_all x1, starting transfers between devices, per_device(): lax.all_to_all(parcels_second, 'req', split_axis=0, concat_axis=0, tiled=...  7.41 us
    all_to_all x1, starting transfers between devices, per_device(): lax.all_to_all(parcels_first, 'req', split_axis=0, concat_axis=0, tiled=T...  7.33 us
  transfers between devices with their start and end apart: 13, of which 7 were waited for; matrix products, arithmetic and copies ran while one was open for 40% of the time, Pallas kernels for 0%

profile of v17, /device:TPU:0, one launch (start us, length us, event | category | flops | bytes accessed | tf_op | source)
XLA Modules:
  0.0 185.9 jit_solution(15492602347200768916)
XLA Ops:
  3.4 4.7 %gather_fusion.2 = bf16[48,128,256]{2,1,0:T(8,128)(2,1)} fusion(bf16[64,128,256]{2,1,0:T(8,128)(2,1)} %bitcast.96, s32[1024]{0:T(1024)S(1)} %pad_clamp_fusion.3), kind=kCustom, calls=%fused_computation.2 | custom fusion | bytes 6291648 | tf_op jit(solution)/shard_map/gather | solution.py:121
  8.1 7.3 %all-to-all-start = ((bf16[16,384,256]{2,1,0:T(8,128)(2,1)}), bf16[16,384,256]{2,1,0:T(8,128)(2,1)}, u32[]{:S(2)}, u32[]{:S(2)}) async-start(bf16[16,384,256]{2,1,0:T(8,128)(2,1)} %bitcast.101), calls=%async_computation | async-start | bytes 6291456 | tf_op jit(solution)/shard_map/all_to_all | solution.py:124
  15.6 14.0 %all-gather = bf16[8,320,8]{1,2,0:T(8,128)(2,1)S(1)} all-gather(bf16[1,320,8]{1,2,0:T(8,128)(2,1)S(1)} %bitcast.108), channel_id=1, replica_groups=mesh['req'=16,'kvh'=8] {'kvh'}, dimensions={0}, use_global_device_ids=true | all-gather | bytes 46080 | tf_op jit(solution)/shard_map/all_gather | solution.py:134
  32.8 2.3 %multiply_reduce_fusion.1 = (f32[8,4]{0,1:T(4,128)S(1)}, f32[8,4,128]{2,0,1:T(8,128)S(1)}) fusion(bf16[8,2560]{1,0:T(8,128)(2,1)S(1)} %fusion.17, bf16[2560,512]{1,0:T(8,128)(2,1)} %param.18), kind=kOutput, calls=%fused_computation.68 | convolution fusion | flops 20979680 | bytes 2678912 | tf_op jit(solution)/shard_map/dot_general | solution.py:138
  35.4 5.0 %gather_fusion.1 = bf16[64,128,256]{2,1,0:T(8,128)(2,1)} fusion(bf16[64,128,256]{2,1,0:T(8,128)(2,1)} %bitcast.97, s32[1024]{0:T(1024)S(1)} %pad_clamp_fusion.4), kind=kCustom, calls=%fused_computation.1 | custom fusion | bytes 8388864 | tf_op jit(solution)/shard_map/gather | solution.py:155
  40.5 7.6 %select_select_fusion = bf16[8,1,1024,256]{3,2,0,1:T(8,128)(2,1)} fusion(bf16[8,1,1024,256]{3,2,0,1:T(8,128)(2,1)} %bitcast.100, pred[8,1024]{1,0:T(8,128)(4,1)S(1)} %get-tuple-element.27, pred[8,1024]{1,0:T(8,128)(4,1)S(1)} %get-tuple-element.26, bf16[8,256]{1,0:T(8,128)(2,1)S(1)} %maximum_bitcast_fusion), kind=kLoop, calls=%fused_computation.9 | loop fusion | flops 4194304 | bytes 8409088 | tf_op jit(solution)/shard_map/jit(_where)/select_n | solution.py:48
  48.1 2.5 %fusion.55 = (f32[8,4]{1,0:T(8,128)S(1)}, f32[8,4,1024]{2,1,0:T(4,128)S(1)}) fusion(bf16[8,1,1024,256]{3,2,0,1:T(8,128)(2,1)} %select_select_fusion, pred[8,1024]{1,0:T(8,128)(4,1)S(1)} %get-tuple-element.47, bf16[8,4,64]{2,1,0:T(4,128)(2,1)S(1)} %get-tuple-element.23, bf16[8,4,64]{2,1,0:T(4,128)(2,1)S(1)} %get-tuple-element.22), kind=kOutput, calls=%fused_computation.145 | convolution fusion | flops 8537087 | bytes 2244736 | tf_op jit(solution)/shard_map/sub | solution.py:67
  50.6 2.0 %fusion.8 = bf16[1,8,4,128]{3,2,1,0:T(4,128)(2,1)S(1)} fusion(bf16[8,1,1024,256]{3,2,0,1:T(8,128)(2,1)} %select_select_fusion, f32[8,4,1024]{2,1,0:T(4,128)S(1)} %get-tuple-element.53, f32[8,4]{1,0:T(8,128)S(1)} %get-tuple-element.52), kind=kOutput, calls=%fused_computation.21 | convolution fusion | flops 8458240 | bytes 2236544 | tf_op jit(solution)/shard_map/rkgt,rktd->rkgd/dot_general | solution.py:68
  56.6 2.9 %collective-permute-done.1 = f32[8,2560]{1,0:T(8,128)S(1)} collective-permute-done((f32[8,2560]{1,0:T(8,128)S(1)}, f32[8,2560]{1,0:T(8,128)S(1)}, u32[]{:S(2)}, u32[]{:S(2)}) %collective-permute-start.1) | collective-permute-done | bytes 81952 | tf_op jit(solution)/shard_map/ppermute | solution.py:165
  59.6 2.6 %collective-permute-start.2 = (f32[8,2560]{1,0:T(8,128)S(1)}, f32[8,2560]{1,0:T(8,128)S(1)}, u32[]{:S(2)}, u32[]{:S(2)}) collective-permute-start(f32[8,2560]{1,0:T(8,128)S(1)} %add.283), channel_id=1, source_target_pairs={{0,4},{1,5},{2,6},{3,7},{4,0},{5,1},{6,2},{7,3},{8,12},{9,13},{10,... | collective-permute-start | bytes 245768 | tf_op jit(solution)/shard_map/ppermute | solution.py:165
  62.9 2.7 %collective-permute-done.2 = f32[8,2560]{1,0:T(8,128)S(1)} collective-permute-done((f32[8,2560]{1,0:T(8,128)S(1)}, f32[8,2560]{1,0:T(8,128)S(1)}, u32[]{:S(2)}, u32[]{:S(2)}) %collective-permute-start.2) | collective-permute-done | bytes 81952 | tf_op jit(solution)/shard_map/ppermute | solution.py:165
  66.6 7.2 %all-to-all-start.1 = ((bf16[16,8,576]{2,1,0:T(8,128)(2,1)}), bf16[16,8,576]{2,1,0:T(8,128)(2,1)S(1)}, u32[]{:S(2)}, u32[]{:S(2)}) async-start(bf16[16,8,576]{2,1,0:T(8,128)(2,1)} %broadcast_in_dim.219), calls=%async_computation.1 | async-start | bytes 327680 | tf_op jit(solution)/shard_map/all_to_all | solution.py:183
  74.5 7.9 %gather_fusion.3 = bf16[80,128,256]{2,1,0:T(8,128)(2,1)} fusion(bf16[64,128,256]{2,1,0:T(8,128)(2,1)} %bitcast.98, s32[1024]{0:T(1024)S(1)} %pad_clamp_fusion.2), kind=kCustom, calls=%fused_computation.3 | custom fusion | bytes 10486080 | tf_op jit(solution)/shard_map/gather | solution.py:128
  82.4 7.4 %all-to-all-start.2 = ((bf16[16,640,256]{2,1,0:T(8,128)(2,1)}), bf16[16,640,256]{2,1,0:T(8,128)(2,1)}, u32[]{:S(2)}, u32[]{:S(2)}) async-start(bf16[16,640,256]{2,1,0:T(8,128)(2,1)} %bitcast.99), calls=%async_computation.2 | async-start | bytes 10485760 | tf_op jit(solution)/shard_map/all_to_all | solution.py:191
  93.3 2.0 %copy.37 = f32[64,1216]{1,0:T(8,128)} copy(f32[64,1216]{0,1:T(8,128)} %get-tuple-element.20) | data formatting | bytes 622592 | tf_op jit(solution)/shard_map/jit(_where)/select_n | solution.py:217
  95.3 2.6 %collective-permute-start.3 = (f32[4,16,1216]{2,1,0:T(8,128)}, f32[4,16,1216]{2,1,0:T(8,128)}, u32[]{:S(2)}, u32[]{:S(2)}) collective-permute-start(f32[4,16,1216]{2,1,0:T(8,128)} %bitcast.105), channel_id=1, source_target_pairs={{0,4},{1,5},{2,6},{3,7},{4,0},{5,1},{6,2},{7,3},{8,12},{9,13},{10,... | collective-permute-start | bytes 933896 | tf_op jit(solution)/shard_map/ppermute | solution.py:218
  99.6 4.6 %collective-permute-done.3 = f32[4,16,1216]{2,1,0:T(8,128)} collective-permute-done((f32[4,16,1216]{2,1,0:T(8,128)}, f32[4,16,1216]{2,1,0:T(8,128)}, u32[]{:S(2)}, u32[]{:S(2)}) %collective-permute-start.3) | collective-permute-done | bytes 311328 | tf_op jit(solution)/shard_map/ppermute | solution.py:218
  108.4 2.5 %collective-permute-done.4 = f32[2,16,1216]{2,1,0:T(8,128)} collective-permute-done((f32[2,16,1216]{2,1,0:T(8,128)S(1)}, f32[2,16,1216]{2,1,0:T(8,128)}, u32[]{:S(2)}, u32[]{:S(2)}) %collective-permute-start.4) | collective-permute-done | bytes 155680 | tf_op jit(solution)/shard_map/ppermute | solution.py:218
  132.0 3.7 %gather_fusion.5 = bf16[8,384,256]{2,1,0:T(8,128)(2,1)} fusion(bf16[16,384,256]{2,1,0:T(8,128)(2,1)} %all-to-all-done, s32[1024]{0:T(1024)S(1)} %pad_clamp_fusion), kind=kCustom, calls=%fused_computation.5 | custom fusion | bytes 3145760 | tf_op jit(solution)/shard_map/gather | solution.py:197
  135.7 2.8 %collective-permute-start.8 = (bf16[4,16,608]{2,1,0:T(8,128)(2,1)S(1)}, bf16[4,16,608]{2,1,0:T(8,128)(2,1)}, u32[]{:S(2)}, u32[]{:S(2)}) collective-permute-start(bf16[4,16,608]{2,1,0:T(8,128)(2,1)S(1)} %maximum_select_fusion.1), channel_id=1, source_target_pairs={{0,4},{1,5},{2,6},{3,7},{4,0},{5,1},{6,2},{7,3},{8,12},{9,13},{10,... | collective-permute-start | bytes 233480 | tf_op jit(solution)/shard_map/ppermute | solution.py:230
  140.4 2.3 %concatenate.60 = bf16[8,1024,256]{2,1,0:T(8,128)(2,1)} pad(bf16[8,384,256]{2,1,0:T(8,128)(2,1)S(1)} %broadcast_select_fusion, bf16[]{:T(256)} %constant.153.clone.1), padding=0_0x0_640x0_0 | pad | bytes 5767170 | tf_op jit(solution)/shard_map/concatenate | solution.py:200
  144.7 17.9 %all-to-all-done.2 = bf16[16,640,256]{2,1,0:T(8,128)(2,1)} async-done(((bf16[16,640,256]{2,1,0:T(8,128)(2,1)}), bf16[16,640,256]{2,1,0:T(8,128)(2,1)}, u32[]{:S(2)}, u32[]{:S(2)}) %all-to-all-start.2) | async-done | bytes 5242912 | tf_op jit(solution)/shard_map/all_to_all | solution.py:191
  163.4 4.9 %all-to-all-start.3 = ((f32[16,8,320]{2,1,0:T(8,128)}), f32[16,8,320]{2,1,0:T(8,128)S(1)}, u32[]{:S(2)}, u32[]{:S(2)}) async-start(f32[16,8,320]{2,1,0:T(8,128)} %bitcast.21), calls=%async_computation.3 | async-start | bytes 393216 | tf_op jit(solution)/shard_map/all_to_all | solution.py:239
  168.3 1.9 select_dynamic-update-slice_fusion.7
  170.2 1.8 select_dynamic-update-slice_fusion.6
  172.0 1.8 select_dynamic-update-slice_fusion.5
  173.9 1.8 select_dynamic-update-slice_fusion.4
  175.7 1.8 select_dynamic-update-slice_fusion.3
  177.6 1.8 select_dynamic-update-slice_fusion.2
  179.4 1.8 select_dynamic-update-slice_fusion.1
  181.3 1.8 select_dynamic-update-slice_fusion
  183.1 2.1 %scatter_fusion = bf16[8,1024,256]{2,1,0:T(8,128)(2,1)} fusion(bf16[8,1024,256]{2,1,0:T(8,128)(2,1)} %select_dynamic-update-slice_fusion, s32[8]{0:T(128)S(1)} %fusion.48, bf16[8,256]{1,0:T(8,128)(2,1)S(1)} %gather_fusion.6), kind=kCustom, calls=%fused_computation.7 | custom fusion | bytes 12352 | tf_op jit(solution)/shard_map/scatter | solution.py:259
  (122 shorter events, 33.2 us)
Async XLA Ops:
  0.6 52.0 %copy-start = (bf16[512,2560]{1,0:T(8,128)(2,1)S(1)}, bf16[512,2560]{1,0:T(8,128)(2,1)}, u32[]{:S(2)}) copy-start(bf16[512,2560]{1,0:T(8,128)(2,1)} %param.23) | copy-start | bytes 7864324
  8.1 7.4 %copy-start.4 = (s32[8,8]{1,0:T(8,128)S(1)}, s32[8,8]{1,0:T(8,128)}, u32[]{:S(2)}) copy-start(s32[8,8]{1,0:T(8,128)} %param.30) | copy-start | bytes 772
  8.1 7.4 %copy-start.5 = (bf16[8,320]{1,0:T(8,128)(2,1)S(1)}, bf16[8,320]{1,0:T(8,128)(2,1)}, u32[]{:S(2)}) copy-start(bf16[8,320]{1,0:T(8,128)(2,1)} %param.16) | copy-start | bytes 15364
  8.1 21.7 %copy-start.6 = (bf16[2560]{0:T(1024)(128)(2,1)S(1)}, bf16[2560]{0:T(1024)(128)(2,1)}, u32[]{:S(2)}) copy-start(bf16[2560]{0:T(1024)(128)(2,1)} %param.17) | copy-start | bytes 15364
  8.1 21.8 %copy-start.2 = (bf16[2560,128]{1,0:T(8,128)(2,1)S(1)}, bf16[2560,128]{1,0:T(8,128)(2,1)}, u32[]{:S(2)}) copy-start(bf16[2560,128]{1,0:T(8,128)(2,1)} %param.19) | copy-start | bytes 1966084
  8.1 22.2 %copy-start.9 = (bf16[128]{0:T(256)(128)(2,1)S(1)}, bf16[128]{0:T(256)(128)(2,1)}, u32[]{:S(2)}) copy-start(bf16[128]{0:T(256)(128)(2,1)} %param.22) | copy-start | bytes 772
  8.1 22.2 %copy-start.1 = (s32[128]{0:T(128)S(1)}, s32[128]{0:T(128)}, u32[]{:S(2)}) copy-start(s32[128]{0:T(128)} %param.29) | copy-start | bytes 1540
  8.1 57.8 %all-to-all-start = ((bf16[16,384,256]{2,1,0:T(8,128)(2,1)}), bf16[16,384,256]{2,1,0:T(8,128)(2,1)}, u32[]{:S(2)}, u32[]{:S(2)}) async-start(bf16[16,384,256]{2,1,0:T(8,128)(2,1)} %bitcast.101), calls=%async_computation | async-start | bytes 6291456 | tf_op jit(solution)/shard_map/all_to_all | solution.py:124
  15.5 19.7 %copy-start.10 = (bf16[128]{0:T(256)(128)(2,1)S(1)}, bf16[128]{0:T(256)(128)(2,1)}, u32[]{:S(2)}) copy-start(bf16[128]{0:T(256)(128)(2,1)} %param.21) | copy-start | bytes 772
  48.1 5.3 %copy-start.7 = (bf16[320]{0:T(512)(128)(2,1)S(1)}, bf16[320]{0:T(512)(128)(2,1)}, u32[]{:S(2)}) copy-start(bf16[320]{0:T(512)(128)(2,1)} %param.24) | copy-start | bytes 1924
  53.1 1.9 %collective-permute-start = (f32[8,2560]{1,0:T(8,128)S(1)}, f32[8,2560]{1,0:T(8,128)S(1)}, u32[]{:S(2)}, u32[]{:S(2)}) collective-permute-start(f32[8,2560]{1,0:T(8,128)S(1)} %fusion.24), channel_id=1, source_target_pairs={{0,1},{1,0},{2,3},{3,2},{4,5},{5,4},{6,7},{7,6},{8,9},{9,8},{10,11... | collective-permute-start | bytes 245768 | tf_op jit(solution)/shard_map/ppermute | solution.py:165
  55.0 4.6 %collective-permute-start.1 = (f32[8,2560]{1,0:T(8,128)S(1)}, f32[8,2560]{1,0:T(8,128)S(1)}, u32[]{:S(2)}, u32[]{:S(2)}) collective-permute-start(f32[8,2560]{1,0:T(8,128)S(1)} %add.282), channel_id=1, source_target_pairs={{0,2},{1,3},{2,0},{3,1},{4,6},{5,7},{6,4},{7,5},{8,10},{9,11},{10,... | collective-permute-start | bytes 245768 | tf_op jit(solution)/shard_map/ppermute | solution.py:165
  59.6 6.0 %collective-permute-start.2 = (f32[8,2560]{1,0:T(8,128)S(1)}, f32[8,2560]{1,0:T(8,128)S(1)}, u32[]{:S(2)}, u32[]{:S(2)}) collective-permute-start(f32[8,2560]{1,0:T(8,128)S(1)} %add.283), channel_id=1, source_target_pairs={{0,4},{1,5},{2,6},{3,7},{4,0},{5,1},{6,2},{7,3},{8,12},{9,13},{10,... | collective-permute-start | bytes 245768 | tf_op jit(solution)/shard_map/ppermute | solution.py:165
  66.6 15.8 %all-to-all-start.1 = ((bf16[16,8,576]{2,1,0:T(8,128)(2,1)}), bf16[16,8,576]{2,1,0:T(8,128)(2,1)S(1)}, u32[]{:S(2)}, u32[]{:S(2)}) async-start(bf16[16,8,576]{2,1,0:T(8,128)(2,1)} %broadcast_in_dim.219), calls=%async_computation.1 | async-start | bytes 327680 | tf_op jit(solution)/shard_map/all_to_all | solution.py:183
  82.4 8.0 %copy-start.8 = (bf16[320,608]{1,0:T(8,128)(2,1)S(1)}, bf16[320,608]{1,0:T(8,128)(2,1)}, u32[]{:S(2)}) copy-start(bf16[320,608]{1,0:T(8,128)(2,1)} %param.26) | copy-start | bytes 1167364
  82.4 80.1 %all-to-all-start.2 = ((bf16[16,640,256]{2,1,0:T(8,128)(2,1)}), bf16[16,640,256]{2,1,0:T(8,128)(2,1)}, u32[]{:S(2)}, u32[]{:S(2)}) async-start(bf16[16,640,256]{2,1,0:T(8,128)(2,1)} %bitcast.99), calls=%async_computation.2 | async-start | bytes 10485760 | tf_op jit(solution)/shard_map/all_to_all | solution.py:191
  95.3 8.9 %collective-permute-start.3 = (f32[4,16,1216]{2,1,0:T(8,128)}, f32[4,16,1216]{2,1,0:T(8,128)}, u32[]{:S(2)}, u32[]{:S(2)}) collective-permute-start(f32[4,16,1216]{2,1,0:T(8,128)} %bitcast.105), channel_id=1, source_target_pairs={{0,4},{1,5},{2,6},{3,7},{4,0},{5,1},{6,2},{7,3},{8,12},{9,13},{10,... | collective-permute-start | bytes 933896 | tf_op jit(solution)/shard_map/ppermute | solution.py:218
  105.4 5.5 %collective-permute-start.4 = (f32[2,16,1216]{2,1,0:T(8,128)S(1)}, f32[2,16,1216]{2,1,0:T(8,128)}, u32[]{:S(2)}, u32[]{:S(2)}) collective-permute-start(f32[2,16,1216]{2,1,0:T(8,128)S(1)} %slice_select_fusion.2), channel_id=1, source_target_pairs={{0,2},{1,3},{2,0},{3,1},{4,6},{5,7},{6,4},{7,5},{8,10},{9,11},{10,... | collective-permute-start | bytes 466952 | tf_op jit(solution)/shard_map/ppermute | solution.py:218
  111.8 1.4 collective-permute-start.5
  113.3 1.2 collective-permute-start.6
  114.5 21.2 %collective-permute-start.7 = (bf16[2,16,608]{2,1,0:T(8,128)(2,1)S(1)}, bf16[2,16,608]{2,1,0:T(8,128)(2,1)S(1)}, u32[]{:S(2)}, u32[]{:S(2)}) collective-permute-start(bf16[2,16,608]{2,1,0:T(8,128)(2,1)S(1)} %maximum_select_fusion.2), channel_id=1, source_target_pairs={{0,2},{1,3},{2,0},{3,1},{4,6},{5,7},{6,4},{7,5},{8,10},{9,11},{10,... | collective-permute-start | bytes 116744 | tf_op jit(solution)/shard_map/ppermute | solution.py:230
  135.7 8.7 %copy-start.3 = (bf16[608,320]{0,1:T(8,128)(2,1)S(1)}, bf16[608,320]{0,1:T(8,128)(2,1)}, u32[]{:S(2)}) copy-start(bf16[608,320]{0,1:T(8,128)(2,1)} %param.27) | copy-start | bytes 1167364
  135.7 7.6 %collective-permute-start.8 = (bf16[4,16,608]{2,1,0:T(8,128)(2,1)S(1)}, bf16[4,16,608]{2,1,0:T(8,128)(2,1)}, u32[]{:S(2)}, u32[]{:S(2)}) collective-permute-start(bf16[4,16,608]{2,1,0:T(8,128)(2,1)S(1)} %maximum_select_fusion.1), channel_id=1, source_target_pairs={{0,4},{1,5},{2,6},{3,7},{4,0},{5,1},{6,2},{7,3},{8,12},{9,13},{10,... | collective-permute-start | bytes 233480 | tf_op jit(solution)/shard_map/ppermute | solution.py:230
  163.4 21.8 %all-to-all-start.3 = ((f32[16,8,320]{2,1,0:T(8,128)}), f32[16,8,320]{2,1,0:T(8,128)S(1)}, u32[]{:S(2)}, u32[]{:S(2)}) async-start(f32[16,8,320]{2,1,0:T(8,128)} %bitcast.21), calls=%async_computation.3 | async-start | bytes 393216 | tf_op jit(solution)/shard_map/all_to_all | solution.py:239
